TPU v7x, 32 devices: a whole 2x2x4 slice. The times are simulated.
32 devices in a mesh: groups: 2 (over x), ctx: 8 (over z, y), head: 2 (over core).
Axes of the slice: x: 2, y: 2, z: 4, core: 2. Of those that a mesh axis runs over, the one named last changes fastest.
Arguments:
- queries: bfloat16 [2048, 8192], P(('groups', 'ctx'), 'head'), parts along dimension 0, may hold values from -6 to 6
- key_rows: bfloat16 [2048, 1024], P(('groups', 'ctx'), 'head'), parts along dimension 0, may hold values from -6 to 6
- value_rows: bfloat16 [2048, 1024], P(('groups', 'ctx'), 'head'), parts along dimension 0, may hold values from -6 to 6
- out_grad: bfloat16 [2048, 8192], P(('groups', 'ctx'), 'head'), parts along dimension 0, may hold values from -6 to 6
- doc_start: int32 [2048], P(('groups', 'ctx')), parts along dimension 0, may hold values from 0 to 1023, as said below
- span_order: int32 [32], P('groups'), parts along dimension 0, may hold values from 0 to 15, as said below
Outputs:
- attended: bfloat16 [2048, 8192], P(('groups', 'ctx'), 'head'), parts along dimension 0
- query_grad: bfloat16 [2048, 8192], P(('groups', 'ctx'), 'head'), parts along dimension 0
- key_grad: bfloat16 [2048, 1024], P(('groups', 'ctx'), 'head'), parts along dimension 0
- value_grad: bfloat16 [2048, 1024], P(('groups', 'ctx'), 'head'), parts along dimension 0
There are 2 independent parts, one for each index of `groups`. A program takes and returns all parts, laid end to end along the dimension named above; each array names one. Nothing has to cross between parts.
Inputs may be any that keep to these rules, and one draw needn't show every extreme that they name: `span_order`: a permutation of the 16 spans. Documents are contiguous runs of sequence positions of at most 256, and one document is exactly 256 long; the last position is a document of its own; every row's doc_start is at most its own position.
All inputs are finite; a program needn't handle non-finite values.
Results may differ from a plain program's by a relative error of at most 0.0086.
Values may be sent and summed in bfloat16 or wider, within the bound.
No kernel may reach another device: no remote copies, remote signals or barrier semaphores. Data moves between devices by JAX's collectives and lax.ppermute only.
A program may use at most 64 MiB of HBM per device.

v0:
```python
import math

import jax
import jax.numpy as jnp
from jax import lax
from jax.sharding import PartitionSpec as P

DH = 128


masked_score = -1e30


def key_places(span_order, first_row, row_count, span_rows):
    row_ids = first_row + jnp.arange(row_count, dtype=jnp.int32)
    return span_order[row_ids // span_rows] * span_rows + row_ids % span_rows


def keep_state(tile_state):
    return tile_state


def local(queries, key_rows, value_rows, out_grad, doc_start, span_order):
    local_rows = queries.shape[0]
    span_rows = local_rows // 2
    head_count = queries.shape[1] // DH
    kv_count = key_rows.shape[1] // DH
    kv_cols = kv_count * DH
    group_size = head_count // kv_count
    score_scale = 1.0 / math.sqrt(DH)
    ctx_count = lax.axis_size("ctx")
    my_index = lax.axis_index("ctx")
    total_rows = local_rows * ctx_count
    first_row = my_index * local_rows
    query_places = key_places(span_order, first_row, local_rows, span_rows).reshape(2, span_rows)
    query_starts = doc_start.reshape(2, span_rows)
    query_tiles = queries.reshape(2, span_rows, kv_count, group_size, DH)
    grad_tiles = out_grad.reshape(2, span_rows, kv_count, group_size, DH)

    def visible(tile_index, places):
        lower = places[None, :] >= query_starts[tile_index][:, None]
        upper = places[None, :] <= query_places[tile_index][:, None]
        return lower & upper

    def raw_scores(tile_index, key_block):
        return (
            jnp.einsum(
                "tkgd,skd->ktgs",
                query_tiles[tile_index],
                key_block,
                preferred_element_type=jnp.float32,
            )
            * score_scale
        )

    def split_blocks(row_count):
        return row_count // local_rows

    def totals_update(tile_index, seen_mask, key_block, value_block, tile_state):
        running_max, denominator = tile_state
        wide_mask = seen_mask[None, :, None, :]
        scores = jnp.where(wide_mask, raw_scores(tile_index, key_block), masked_score)
        new_max = jnp.maximum(running_max, jnp.max(scores, axis=3))
        weights = jnp.where(wide_mask, jnp.exp(scores - new_max[..., None]), 0.0)
        denominator = denominator * jnp.exp(running_max - new_max) + jnp.sum(weights, axis=3)
        return (new_max, denominator)

    def make_pass(tile_update, with_values, state_in, shard_pair):
        if with_values:
            key_part, value_part = shard_pair
        else:
            key_part = shard_pair
            value_part = shard_pair
        block_count = split_blocks(key_part.shape[0])
        block_rows = key_part.shape[0] // block_count

        def make_one_block(block_index, state):
            row_at = block_index * block_rows
            key_block = lax.dynamic_slice_in_dim(key_part, row_at, block_rows, 0).reshape(
                block_rows, kv_count, DH
            )
            value_block = lax.dynamic_slice_in_dim(value_part, row_at, block_rows, 0).reshape(
                block_rows, kv_count, DH
            )
            places = key_places(span_order, row_at, block_rows, span_rows)
            updated = []
            for tile_index in range(2):
                seen_mask = visible(tile_index, places)

                def make_update(tile_state, tile_index=tile_index, seen_mask=seen_mask):
                    return tile_update(tile_index, seen_mask, key_block, value_block, tile_state)

                updated.append(
                    lax.cond(jnp.any(seen_mask), make_update, keep_state, state[tile_index])
                )
            return tuple(updated)

        return lax.fori_loop(0, block_count, make_one_block, state_in)

    tile_zero = jnp.zeros((kv_count, span_rows, group_size, DH), jnp.float32)
    stat_low = jnp.full((kv_count, span_rows, group_size), masked_score, jnp.float32)
    stat_zero = jnp.zeros((kv_count, span_rows, group_size), jnp.float32)
    totals_init = ((stat_low, stat_zero), (stat_low, stat_zero))
    totals_state = make_pass(
        totals_update, False, totals_init, lax.all_gather(key_rows, "ctx", axis=0, tiled=True)
    )
    log_totals = [totals_state[index][0] + jnp.log(totals_state[index][1]) for index in range(2)]

    def output_update(tile_index, seen_mask, key_block, value_block, weighted):
        wide_mask = seen_mask[None, :, None, :]
        scores = jnp.where(wide_mask, raw_scores(tile_index, key_block), masked_score)
        weights = jnp.where(wide_mask, jnp.exp(scores - log_totals[tile_index][..., None]), 0.0)
        return weighted + jnp.einsum(
            "ktgs,skd->ktgd",
            weights.astype(jnp.bfloat16),
            value_block,
            preferred_element_type=jnp.float32,
        )

    output_state = make_pass(
        output_update,
        True,
        (tile_zero, tile_zero),
        (
            lax.all_gather(key_rows, "ctx", axis=0, tiled=True),
            lax.all_gather(value_rows, "ctx", axis=0, tiled=True),
        ),
    )
    attended_tiles = jnp.stack([output_state[0], output_state[1]]).astype(jnp.bfloat16)
    attended_rows = attended_tiles.transpose(0, 2, 1, 3, 4)
    attended = attended_rows.reshape(local_rows, head_count * DH)
    row_dots = jnp.sum(
        attended_rows.astype(jnp.float32) * grad_tiles.astype(jnp.float32), axis=4
    ).transpose(0, 2, 1, 3)

    def block_grads(grads_query, key_flat, value_flat, block_offset):
        block_rows = key_flat.shape[0]
        key_block = key_flat.reshape(block_rows, kv_count, DH)
        value_block = value_flat.reshape(block_rows, kv_count, DH)
        places = key_places(span_order, block_offset, block_rows, span_rows)
        key_accum = jnp.zeros((block_rows, kv_count, DH), jnp.float32)
        value_accum = jnp.zeros((block_rows, kv_count, DH), jnp.float32)
        new_query = []
        for tile_index in range(2):
            seen_mask = visible(tile_index, places)

            def block_update(tile_args, tile_index=tile_index, seen_mask=seen_mask):
                query_accum, key_sum, value_sum = tile_args
                wide_mask = seen_mask[None, :, None, :]
                scores = jnp.where(wide_mask, raw_scores(tile_index, key_block), masked_score)
                weights = jnp.where(
                    wide_mask, jnp.exp(scores - log_totals[tile_index][..., None]), 0.0
                )
                weights_low = weights.astype(jnp.bfloat16)
                grad_weights = jnp.einsum(
                    "tkgd,skd->ktgs",
                    grad_tiles[tile_index],
                    value_block,
                    preferred_element_type=jnp.float32,
                )
                grad_scores = (weights * (grad_weights - row_dots[tile_index][..., None])).astype(
                    jnp.bfloat16
                )
                query_accum = query_accum + jnp.einsum(
                    "ktgs,skd->ktgd", grad_scores, key_block, preferred_element_type=jnp.float32
                )
                key_sum = key_sum + jnp.einsum(
                    "ktgs,tkgd->skd",
                    grad_scores,
                    query_tiles[tile_index],
                    preferred_element_type=jnp.float32,
                )
                value_sum = value_sum + jnp.einsum(
                    "ktgs,tkgd->skd",
                    weights_low,
                    grad_tiles[tile_index],
                    preferred_element_type=jnp.float32,
                )
                return (query_accum, key_sum, value_sum)

            result_tuple = lax.cond(
                jnp.any(seen_mask),
                block_update,
                keep_state,
                (grads_query[tile_index], key_accum, value_accum),
            )
            new_query.append(result_tuple[0])
            key_accum = result_tuple[1]
            value_accum = result_tuple[2]
        packed = jnp.concatenate(
            [
                key_accum.reshape(block_rows, kv_cols) * score_scale,
                value_accum.reshape(block_rows, kv_cols),
            ],
            axis=1,
        )
        return (tuple(new_query), packed)

    backward_init = ((tile_zero, tile_zero), jnp.zeros((total_rows, 2 * kv_cols), jnp.float32))
    key_part = lax.all_gather(key_rows, "ctx", axis=0, tiled=True)
    value_part = lax.all_gather(value_rows, "ctx", axis=0, tiled=True)
    block_count = split_blocks(key_part.shape[0])
    block_rows = key_part.shape[0] // block_count

    def backward_one_block(block_index, state):
        grads_query, buffer = state
        row_at = block_index * block_rows
        key_flat = lax.dynamic_slice_in_dim(key_part, row_at, block_rows, 0)
        value_flat = lax.dynamic_slice_in_dim(value_part, row_at, block_rows, 0)
        grads_query, packed = block_grads(grads_query, key_flat, value_flat, row_at)
        current = lax.dynamic_slice_in_dim(buffer, row_at, block_rows, 0)
        buffer = lax.dynamic_update_slice_in_dim(buffer, current + packed, row_at, 0)
        return (grads_query, buffer)

    grads_query, buffer = lax.fori_loop(0, block_count, backward_one_block, backward_init)
    summed = lax.psum_scatter(buffer, "ctx", scatter_dimension=0, tiled=True)
    query_stack = (jnp.stack([grads_query[0], grads_query[1]]) * score_scale).astype(jnp.bfloat16)
    query_grad = query_stack.transpose(0, 2, 1, 3, 4).reshape(local_rows, head_count * DH)
    key_grad = summed[:, :kv_cols].astype(jnp.bfloat16)
    value_grad = summed[:, kv_cols:].astype(jnp.bfloat16)
    return (attended, query_grad, key_grad, value_grad)


def solution(mesh):
    in_specs = (
        P(("groups", "ctx"), "head"),
        P(("groups", "ctx"), "head"),
        P(("groups", "ctx"), "head"),
        P(("groups", "ctx"), "head"),
        P(("groups", "ctx")),
        P("groups"),
    )
    out_specs = (
        P(("groups", "ctx"), "head"),
        P(("groups", "ctx"), "head"),
        P(("groups", "ctx"), "head"),
        P(("groups", "ctx"), "head"),
    )
    return jax.shard_map(local, mesh=mesh, in_specs=in_specs, out_specs=out_specs, check_vma=False)
```

profile of v0, /device:TPU:0, one launch (start us, length us, event | category | flops | bytes accessed | tf_op | source)
XLA Modules:
  0.0 649.5 jit_solution(15144263146200980459)
XLA Ops:
  14.0 10.2 %fusion.111 = s32[128]{0:T(128)S(1)} fusion(s32[]{:T(128)} %bitcast.148, s32[]{:T(128)} %bitcast.149, s32[]{:T(128)} %bitcast.150, s32[]{:T(128)} %bitcast.151, s32[]{:T(128)} %bitcast.152, s32[]{:T(128)} %bitcast.154, s32[]{:T(128)} %bitcast.153, s32[]{:T(128)} %bitcast.131, s32[]{:T(128)} %bitcast.133, s32[]{:T(128)} %bitcast.135, s32[]{:T(128)} %bitcast.137, ...), kind=kLoop, calls=%fused_computation.253 | loop fusion | flops 6400 | bytes 580 | tf_op jit(solution)/shard_map/mul | solution.py:16
  26.4 26.5 %all-gather.3.cloned.1.call-done = bf16[1024,512]{0,1:T(8,128)(2,1)} async-done(((bf16[128,512]{0,1:T(8,128)(2,1)}), bf16[1024,512]{0,1:T(8,128)(2,1)}) %all-gather.3.cloned.1.call-update) | async-done | bytes 1048592 | tf_op jit(solution)/shard_map/all_gather | solution.py:125
  54.3 140.8 %while.66 = (s32[]{:T(128)}, f32[4,64,8]{2,1,0:T(8,128)S(1)}, f32[4,64,8]{2,1,0:T(8,128)}, f32[4,64,8]{2,1,0:T(8,128)S(1)}, f32[4,64,8]{2,1,0:T(8,128)}, /*index...) while((s32[]{:T(128)}, f32[4,64,8]{2,1,0:T(8,128)S(1)}, ...), condition=%wide.region_11.12_spmd, body=%wide.region_0.11_spmd.sunk | while | flops 137445248 | bytes 6033959 | solution.py:98
  55.7 10.1 %fusion.133 = s32[128]{0:T(128)S(1)} fusion(s32[]{:T(128)} %bitcast.641, s32[]{:T(128)} %bitcast.642, s32[]{:T(128)} %bitcast.643, s32[]{:T(128)} %bitcast.644, s32[]{:T(128)} %bitcast.645, s32[]{:T(128)} %bitcast.646, s32[]{:T(128)} %bitcast.647, s32[]{:T(128)} %bitcast.648, s32[]{:T(128)} %bitcast.649, s32[]{:T(128)} %bitcast.650, s32[]{:T(128)} %bitcast.651, ...), kind=kLoop, calls=%fused_computation.39.clone.1 | loop fusion | flops 8064 | bytes 580 | tf_op jit(solution)/shard_map/while/body/eval_jaxpr/add | solution.py:16
  78.1 10.1 %fusion.133 = s32[128]{0:T(128)S(1)} fusion(s32[]{:T(128)} %bitcast.641, s32[]{:T(128)} %bitcast.642, s32[]{:T(128)} %bitcast.643, s32[]{:T(128)} %bitcast.644, s32[]{:T(128)} %bitcast.645, s32[]{:T(128)} %bitcast.646, s32[]{:T(128)} %bitcast.647, s32[]{:T(128)} %bitcast.648, s32[]{:T(128)} %bitcast.649, s32[]{:T(128)} %bitcast.650, s32[]{:T(128)} %bitcast.651, ...), kind=kLoop, calls=%fused_computation.39.clone.1 | loop fusion | flops 8064 | bytes 580 | tf_op jit(solution)/shard_map/while/body/eval_jaxpr/add | solution.py:16
  93.4 10.1 %fusion.133 = s32[128]{0:T(128)S(1)} fusion(s32[]{:T(128)} %bitcast.641, s32[]{:T(128)} %bitcast.642, s32[]{:T(128)} %bitcast.643, s32[]{:T(128)} %bitcast.644, s32[]{:T(128)} %bitcast.645, s32[]{:T(128)} %bitcast.646, s32[]{:T(128)} %bitcast.647, s32[]{:T(128)} %bitcast.648, s32[]{:T(128)} %bitcast.649, s32[]{:T(128)} %bitcast.650, s32[]{:T(128)} %bitcast.651, ...), kind=kLoop, calls=%fused_computation.39.clone.1 | loop fusion | flops 8064 | bytes 580 | tf_op jit(solution)/shard_map/while/body/eval_jaxpr/add | solution.py:16
  108.7 10.1 %fusion.133 = s32[128]{0:T(128)S(1)} fusion(s32[]{:T(128)} %bitcast.641, s32[]{:T(128)} %bitcast.642, s32[]{:T(128)} %bitcast.643, s32[]{:T(128)} %bitcast.644, s32[]{:T(128)} %bitcast.645, s32[]{:T(128)} %bitcast.646, s32[]{:T(128)} %bitcast.647, s32[]{:T(128)} %bitcast.648, s32[]{:T(128)} %bitcast.649, s32[]{:T(128)} %bitcast.650, s32[]{:T(128)} %bitcast.651, ...), kind=kLoop, calls=%fused_computation.39.clone.1 | loop fusion | flops 8064 | bytes 580 | tf_op jit(solution)/shard_map/while/body/eval_jaxpr/add | solution.py:16
  124.0 10.1 %fusion.133 = s32[128]{0:T(128)S(1)} fusion(s32[]{:T(128)} %bitcast.641, s32[]{:T(128)} %bitcast.642, s32[]{:T(128)} %bitcast.643, s32[]{:T(128)} %bitcast.644, s32[]{:T(128)} %bitcast.645, s32[]{:T(128)} %bitcast.646, s32[]{:T(128)} %bitcast.647, s32[]{:T(128)} %bitcast.648, s32[]{:T(128)} %bitcast.649, s32[]{:T(128)} %bitcast.650, s32[]{:T(128)} %bitcast.651, ...), kind=kLoop, calls=%fused_computation.39.clone.1 | loop fusion | flops 8064 | bytes 580 | tf_op jit(solution)/shard_map/while/body/eval_jaxpr/add | solution.py:16
  139.3 10.1 %fusion.133 = s32[128]{0:T(128)S(1)} fusion(s32[]{:T(128)} %bitcast.641, s32[]{:T(128)} %bitcast.642, s32[]{:T(128)} %bitcast.643, s32[]{:T(128)} %bitcast.644, s32[]{:T(128)} %bitcast.645, s32[]{:T(128)} %bitcast.646, s32[]{:T(128)} %bitcast.647, s32[]{:T(128)} %bitcast.648, s32[]{:T(128)} %bitcast.649, s32[]{:T(128)} %bitcast.650, s32[]{:T(128)} %bitcast.651, ...), kind=kLoop, calls=%fused_computation.39.clone.1 | loop fusion | flops 8064 | bytes 580 | tf_op jit(solution)/shard_map/while/body/eval_jaxpr/add | solution.py:16
  158.9 10.1 %fusion.133 = s32[128]{0:T(128)S(1)} fusion(s32[]{:T(128)} %bitcast.641, s32[]{:T(128)} %bitcast.642, s32[]{:T(128)} %bitcast.643, s32[]{:T(128)} %bitcast.644, s32[]{:T(128)} %bitcast.645, s32[]{:T(128)} %bitcast.646, s32[]{:T(128)} %bitcast.647, s32[]{:T(128)} %bitcast.648, s32[]{:T(128)} %bitcast.649, s32[]{:T(128)} %bitcast.650, s32[]{:T(128)} %bitcast.651, ...), kind=kLoop, calls=%fused_computation.39.clone.1 | loop fusion | flops 8064 | bytes 580 | tf_op jit(solution)/shard_map/while/body/eval_jaxpr/add | solution.py:16
  177.0 10.1 %fusion.133 = s32[128]{0:T(128)S(1)} fusion(s32[]{:T(128)} %bitcast.641, s32[]{:T(128)} %bitcast.642, s32[]{:T(128)} %bitcast.643, s32[]{:T(128)} %bitcast.644, s32[]{:T(128)} %bitcast.645, s32[]{:T(128)} %bitcast.646, s32[]{:T(128)} %bitcast.647, s32[]{:T(128)} %bitcast.648, s32[]{:T(128)} %bitcast.649, s32[]{:T(128)} %bitcast.650, s32[]{:T(128)} %bitcast.651, ...), kind=kLoop, calls=%fused_computation.39.clone.1 | loop fusion | flops 8064 | bytes 580 | tf_op jit(solution)/shard_map/while/body/eval_jaxpr/add | solution.py:16
  198.8 131.1 %while.67 = (s32[]{:T(128)}, f32[4,64,8,128]{3,2,1,0:T(8,128)}, f32[4,64,8,128]{3,2,1,0:T(8,128)}, s32[16]{0:T(128)S(1)}, s32[2,64]{1,0:T(2,128)}, /*index=5*/s3...) while((s32[]{:T(128)}, f32[4,64,8,128]{3,2,1,0:T(8,128)}, ...), condition=%wide.region_19.20_spmd, body=%wide.region_12.19_spmd.sunk | while | flops 271654784 | bytes 6345215 | solution.py:98
  200.3 10.1 %fusion.136 = s32[128]{0:T(128)S(1)} fusion(s32[]{:T(128)} %bitcast.669, s32[]{:T(128)} %bitcast.670, s32[]{:T(128)} %bitcast.671, s32[]{:T(128)} %bitcast.672, s32[]{:T(128)} %bitcast.673, s32[]{:T(128)} %bitcast.674, s32[]{:T(128)} %bitcast.675, s32[]{:T(128)} %bitcast.676, s32[]{:T(128)} %bitcast.677, s32[]{:T(128)} %bitcast.678, s32[]{:T(128)} %bitcast.679, ...), kind=kLoop, calls=%fused_computation.113.clone.1 | loop fusion | flops 8064 | bytes 580 | tf_op jit(solution)/shard_map/while/body/eval_jaxpr/add | solution.py:16
  220.5 10.1 %fusion.136 = s32[128]{0:T(128)S(1)} fusion(s32[]{:T(128)} %bitcast.669, s32[]{:T(128)} %bitcast.670, s32[]{:T(128)} %bitcast.671, s32[]{:T(128)} %bitcast.672, s32[]{:T(128)} %bitcast.673, s32[]{:T(128)} %bitcast.674, s32[]{:T(128)} %bitcast.675, s32[]{:T(128)} %bitcast.676, s32[]{:T(128)} %bitcast.677, s32[]{:T(128)} %bitcast.678, s32[]{:T(128)} %bitcast.679, ...), kind=kLoop, calls=%fused_computation.113.clone.1 | loop fusion | flops 8064 | bytes 580 | tf_op jit(solution)/shard_map/while/body/eval_jaxpr/add | solution.py:16
  235.2 10.1 %fusion.136 = s32[128]{0:T(128)S(1)} fusion(s32[]{:T(128)} %bitcast.669, s32[]{:T(128)} %bitcast.670, s32[]{:T(128)} %bitcast.671, s32[]{:T(128)} %bitcast.672, s32[]{:T(128)} %bitcast.673, s32[]{:T(128)} %bitcast.674, s32[]{:T(128)} %bitcast.675, s32[]{:T(128)} %bitcast.676, s32[]{:T(128)} %bitcast.677, s32[]{:T(128)} %bitcast.678, s32[]{:T(128)} %bitcast.679, ...), kind=kLoop, calls=%fused_computation.113.clone.1 | loop fusion | flops 8064 | bytes 580 | tf_op jit(solution)/shard_map/while/body/eval_jaxpr/add | solution.py:16
  249.8 10.1 %fusion.136 = s32[128]{0:T(128)S(1)} fusion(s32[]{:T(128)} %bitcast.669, s32[]{:T(128)} %bitcast.670, s32[]{:T(128)} %bitcast.671, s32[]{:T(128)} %bitcast.672, s32[]{:T(128)} %bitcast.673, s32[]{:T(128)} %bitcast.674, s32[]{:T(128)} %bitcast.675, s32[]{:T(128)} %bitcast.676, s32[]{:T(128)} %bitcast.677, s32[]{:T(128)} %bitcast.678, s32[]{:T(128)} %bitcast.679, ...), kind=kLoop, calls=%fused_computation.113.clone.1 | loop fusion | flops 8064 | bytes 580 | tf_op jit(solution)/shard_map/while/body/eval_jaxpr/add | solution.py:16
  264.5 10.1 %fusion.136 = s32[128]{0:T(128)S(1)} fusion(s32[]{:T(128)} %bitcast.669, s32[]{:T(128)} %bitcast.670, s32[]{:T(128)} %bitcast.671, s32[]{:T(128)} %bitcast.672, s32[]{:T(128)} %bitcast.673, s32[]{:T(128)} %bitcast.674, s32[]{:T(128)} %bitcast.675, s32[]{:T(128)} %bitcast.676, s32[]{:T(128)} %bitcast.677, s32[]{:T(128)} %bitcast.678, s32[]{:T(128)} %bitcast.679, ...), kind=kLoop, calls=%fused_computation.113.clone.1 | loop fusion | flops 8064 | bytes 580 | tf_op jit(solution)/shard_map/while/body/eval_jaxpr/add | solution.py:16
  279.1 10.1 %fusion.136 = s32[128]{0:T(128)S(1)} fusion(s32[]{:T(128)} %bitcast.669, s32[]{:T(128)} %bitcast.670, s32[]{:T(128)} %bitcast.671, s32[]{:T(128)} %bitcast.672, s32[]{:T(128)} %bitcast.673, s32[]{:T(128)} %bitcast.674, s32[]{:T(128)} %bitcast.675, s32[]{:T(128)} %bitcast.676, s32[]{:T(128)} %bitcast.677, s32[]{:T(128)} %bitcast.678, s32[]{:T(128)} %bitcast.679, ...), kind=kLoop, calls=%fused_computation.113.clone.1 | loop fusion | flops 8064 | bytes 580 | tf_op jit(solution)/shard_map/while/body/eval_jaxpr/add | solution.py:16
  296.5 10.1 %fusion.136 = s32[128]{0:T(128)S(1)} fusion(s32[]{:T(128)} %bitcast.669, s32[]{:T(128)} %bitcast.670, s32[]{:T(128)} %bitcast.671, s32[]{:T(128)} %bitcast.672, s32[]{:T(128)} %bitcast.673, s32[]{:T(128)} %bitcast.674, s32[]{:T(128)} %bitcast.675, s32[]{:T(128)} %bitcast.676, s32[]{:T(128)} %bitcast.677, s32[]{:T(128)} %bitcast.678, s32[]{:T(128)} %bitcast.679, ...), kind=kLoop, calls=%fused_computation.113.clone.1 | loop fusion | flops 8064 | bytes 580 | tf_op jit(solution)/shard_map/while/body/eval_jaxpr/add | solution.py:16
  314.0 10.1 %fusion.136 = s32[128]{0:T(128)S(1)} fusion(s32[]{:T(128)} %bitcast.669, s32[]{:T(128)} %bitcast.670, s32[]{:T(128)} %bitcast.671, s32[]{:T(128)} %bitcast.672, s32[]{:T(128)} %bitcast.673, s32[]{:T(128)} %bitcast.674, s32[]{:T(128)} %bitcast.675, s32[]{:T(128)} %bitcast.676, s32[]{:T(128)} %bitcast.677, s32[]{:T(128)} %bitcast.678, s32[]{:T(128)} %bitcast.679, ...), kind=kLoop, calls=%fused_computation.113.clone.1 | loop fusion | flops 8064 | bytes 580 | tf_op jit(solution)/shard_map/while/body/eval_jaxpr/add | solution.py:16
  338.4 180.4 %while.68 = (s32[]{:T(128)}, f32[4,64,8,128]{3,2,1,0:T(8,128)}, f32[4,64,8,128]{3,2,1,0:T(8,128)S(1)}, f32[1024,1024]{1,0:T(8,128)}, s32[16]{0:T(128)S(1)}, /*in...) while((s32[]{:T(128)}, f32[4,64,8,128]{3,2,1,0:T(8,128)}, ...), condition=%wide.region_28.29_spmd, body=%wide.region_21.28_spmd.sunk | while | flops 676339584 | bytes 45421300 | solution.py:215
  371.0 9.7 %fusion.139 = s32[128]{0:T(128)S(1)} fusion(s32[]{:T(128)} %bitcast.698, s32[]{:T(128)} %bitcast.699, s32[]{:T(128)} %bitcast.700, s32[]{:T(128)} %bitcast.701, s32[]{:T(128)} %bitcast.702, s32[]{:T(128)} %bitcast.703, s32[]{:T(128)} %bitcast.704, s32[]{:T(128)} %bitcast.705, s32[]{:T(128)} %bitcast.706, s32[]{:T(128)} %bitcast.707, s32[]{:T(128)} %bitcast.708, ...), kind=kLoop, calls=%fused_computation.206.clone.1 | loop fusion | flops 8064 | bytes 580 | tf_op jit(solution)/shard_map/while/body/eval_jaxpr/add | solution.py:16
  445.3 9.7 %fusion.139 = s32[128]{0:T(128)S(1)} fusion(s32[]{:T(128)} %bitcast.698, s32[]{:T(128)} %bitcast.699, s32[]{:T(128)} %bitcast.700, s32[]{:T(128)} %bitcast.701, s32[]{:T(128)} %bitcast.702, s32[]{:T(128)} %bitcast.703, s32[]{:T(128)} %bitcast.704, s32[]{:T(128)} %bitcast.705, s32[]{:T(128)} %bitcast.706, s32[]{:T(128)} %bitcast.707, s32[]{:T(128)} %bitcast.708, ...), kind=kLoop, calls=%fused_computation.206.clone.1 | loop fusion | flops 8064 | bytes 580 | tf_op jit(solution)/shard_map/while/body/eval_jaxpr/add | solution.py:16
  525.1 116.1 %reduce-scatter.2.cloned.1.call-done = f32[128,1024]{1,0:T(8,128)} async-done(((f32[1024,1024]{1,0:T(8,128)}), f32[128,1024]{1,0:T(8,128)}) %reduce-scatter.2.cloned.1.call-update) | async-done | bytes 524304 | tf_op jit(solution)/shard_map/reduce_scatter | solution.py:216
  (360 shorter events, 342.0 us)
Async XLA Ops:
  7.2 45.7 %all-gather.3.cloned.1.call-start = ((), (), s32[]{:S(2)}) async-start(), calls=%async_computation.1 | async-start | bytes 1179648 | tf_op jit(solution)/shard_map/all_gather | solution.py:125
  8.9 187.9 %all-gather.5.cloned.1.call-start = ((), (), s32[]{:S(2)}) async-start(), calls=%async_computation.2 | async-start | bytes 1179648 | tf_op jit(solution)/shard_map/all_gather | solution.py:126
  10.6 630.6 %reduce-scatter.2.cloned.1.call-start = ((), (), s32[]{:S(2)}) async-start(), calls=%async_computation.3 | async-start | bytes 4718592 | tf_op jit(solution)/shard_map/reduce_scatter | solution.py:216
  24.2 1.8 copy-start.11
  24.2 30.0 %copy-start.6 = (s32[16]{0:T(128)S(1)}, s32[16]{0:T(128)}, u32[]{:S(2)}) copy-start(s32[16]{0:T(128)} %param.29) | copy-start | bytes 196
  330.0 4.0 copy-start.3
  331.6 6.8 %copy-start.7 = (bf16[4,64,8,128]{3,2,0,1:T(8,128)(2,1)}, bf16[4,64,8,128]{3,2,0,1:T(8,128)(2,1)S(1)}, u32[]{:S(2)}) copy-start(bf16[4,64,8,128]{3,2,0,1:T(8,128)(2,1)S(1)} %copy.148) | copy-start | bytes 1572868
  333.2 5.3 copy-start.9
  356.7 1.2 copy-start.4
  357.9 1.2 copy-start
  359.6 1.0 copy-start.1
  361.5 5.0 copy-start.5
  462.1 1.2 copy-start.4
  463.3 1.2 copy-start
  465.0 1.0 copy-start.1
  485.5 5.0 copy-start.5
  511.8 1.2 copy-start.4
  513.0 1.2 copy-start
  514.7 1.0 copy-start.1
  518.8 1.0 copy-start.8
  518.8 1.2 copy-start.10
  518.8 4.6 copy-start.2
Sparse Core Ops, SparseCore 0:
  10.6 42.2 all-gather.2
  55.5 38.6 all-gather.4
  519.0 122.2 reduce-scatter.1
where the time goes:
time: 657 us; the launch traced here: 650 us
  other arithmetic  299 us (46%)
  waiting for transfers between devices  143 us (22%)
  local copies, waits for them, and re-layouts  123 us (19%)
  matrix products  37.5 us (6%)
  loops' own time  32.7 us (5%)
  between operations  13.9 us (2%)
    add x25, other arithmetic, key_places(): return span_order[row_ids // span_rows] * span_rows + row_ids % span_rows  239 us
    reduce_scatter x1, waiting for transfers between devices, local(): summed = lax.psum_scatter(buffer, 'ctx', scatter_dimension=0, tiled=True)  116 us
    all_gather x1, waiting for transfers between devices, local(): lax.all_gather(key_rows, 'ctx', axis=0, tiled=True)  26.5 us
    another operation x2, loops' own time, make_pass(): return lax.fori_loop(0, block_count, make_one_block, state_in)  21.6 us
    gather x25, local copies, waits for them, and re-layouts, key_places(): return span_order[row_ids // span_rows] * span_rows + row_ids % span_rows  18.9 us
    reduce_or x16, other arithmetic, make_one_block(): jnp.any(seen_mask)  17.7 us
    le x24, local copies, waits for them, and re-layouts, visible(): upper = places[None, :] <= query_places[tile_index][:, None]  17.7 us
    dot_general x5, matrix products, output_update(): jnp.einsum('ktgs,skd->ktgd', weights.astype(jnp.bfloat16), value_block, p...  14.2 us
  transfers between devices with their start and end apart: 3, of which 2 were waited for; matrix products, arithmetic and copies ran while one was open for 24% of the time, Pallas kernels for 0%

commit v1 on v0

v1 whole, which is shorter than its diff:
```python
import math

import jax
import jax.numpy as jnp
from jax import lax
from jax.experimental import pallas as pl
from jax.experimental.pallas import tpu as pltpu
from jax.sharding import PartitionSpec as P

DH = 128
SPAN = 64


def attention_kernel(qpos_ref, qstart_ref, kpos_ref, q_ref, do_ref, k_ref, v_ref,
                     out_ref, dq_ref, dk_ref, dv_ref, *, group_size, score_scale):
    qpos = qpos_ref[...]
    qstart = qstart_ref[...]
    kpos = kpos_ref[0]
    visible = (kpos >= qstart) & (kpos <= qpos)
    key_block = k_ref[0]
    value_block = v_ref[0]
    window = key_block.shape[0]
    key_sum = jnp.zeros((window, DH), jnp.float32)
    value_sum = jnp.zeros((window, DH), jnp.float32)
    contract_last = (((1,), (1,)), ((), ()))
    contract_first = (((0,), (0,)), ((), ()))
    for head in range(group_size):
        cols = slice(head * DH, (head + 1) * DH)
        query_head = q_ref[:, cols]
        grad_head = do_ref[:, cols]
        scores = lax.dot_general(query_head, key_block, contract_last,
                                 preferred_element_type=jnp.float32) * score_scale
        masked = jnp.where(visible, scores, -jnp.inf)
        row_max = jnp.max(masked, axis=1, keepdims=True)
        shifted = jnp.where(visible, jnp.exp(masked - row_max), 0.0)
        log_totals = row_max + jnp.log(jnp.sum(shifted, axis=1, keepdims=True))
        weights = jnp.where(visible, jnp.exp(masked - log_totals), 0.0)
        weights_low = weights.astype(jnp.bfloat16)
        attended = jnp.dot(weights_low, value_block,
                           preferred_element_type=jnp.float32).astype(jnp.bfloat16)
        out_ref[:, cols] = attended
        row_dots = jnp.sum(attended.astype(jnp.float32) * grad_head.astype(jnp.float32),
                           axis=1, keepdims=True)
        grad_weights = lax.dot_general(grad_head, value_block, contract_last,
                                       preferred_element_type=jnp.float32)
        grad_scores = (weights * (grad_weights - row_dots)).astype(jnp.bfloat16)
        query_grad = jnp.dot(grad_scores, key_block, preferred_element_type=jnp.float32)
        dq_ref[:, cols] = (query_grad * score_scale).astype(jnp.bfloat16)
        key_sum = key_sum + lax.dot_general(grad_scores, query_head, contract_first,
                                            preferred_element_type=jnp.float32)
        value_sum = value_sum + lax.dot_general(weights_low, grad_head, contract_first,
                                                preferred_element_type=jnp.float32)
    dk_ref[0] = key_sum * score_scale
    dv_ref[0] = value_sum


def local(queries, key_rows, value_rows, out_grad, doc_start, span_order):
    local_rows = queries.shape[0]
    tiles = local_rows // SPAN
    head_count = queries.shape[1] // DH
    kv_count = key_rows.shape[1] // DH
    kv_cols = kv_count * DH
    group_size = head_count // kv_count
    group_cols = group_size * DH
    score_scale = 1.0 / math.sqrt(DH)
    ctx_count = lax.axis_size("ctx")
    my_index = lax.axis_index("ctx")
    total_rows = local_rows * ctx_count
    slot_count = total_rows // SPAN
    reach = total_rows // 4 // SPAN
    window_spans = reach + 1
    window = window_spans * SPAN

    slot_of_span = jnp.zeros((slot_count,), jnp.int32).at[span_order].set(
        jnp.arange(slot_count, dtype=jnp.int32))
    my_spans = lax.dynamic_slice_in_dim(span_order, my_index * tiles, tiles)
    window_span = my_spans[:, None] - reach + jnp.arange(window_spans, dtype=jnp.int32)[None, :]
    window_slot = slot_of_span[jnp.clip(window_span, 0, slot_count - 1)]
    row_in_span = jnp.arange(SPAN, dtype=jnp.int32)
    key_pos = (window_span[:, :, None] * SPAN + row_in_span[None, None, :]).reshape(tiles, 1, window)
    query_pos = (my_spans[:, None] * SPAN + row_in_span[None, :]).reshape(local_rows, 1)
    query_start = doc_start.reshape(local_rows, 1)

    key_all = lax.all_gather(key_rows, "ctx", axis=0, tiled=True).reshape(slot_count, SPAN, kv_cols)
    value_all = lax.all_gather(value_rows, "ctx", axis=0, tiled=True).reshape(slot_count, SPAN, kv_cols)
    key_win = key_all[window_slot].reshape(tiles, window, kv_cols)
    value_win = value_all[window_slot].reshape(tiles, window, kv_cols)

    kernel = pl.pallas_call(
        lambda *refs: attention_kernel(*refs, group_size=group_size, score_scale=score_scale),
        grid=(tiles, kv_count),
        in_specs=[
            pl.BlockSpec((SPAN, 1), lambda t, c: (t, 0)),
            pl.BlockSpec((SPAN, 1), lambda t, c: (t, 0)),
            pl.BlockSpec((1, 1, window), lambda t, c: (t, 0, 0)),
            pl.BlockSpec((SPAN, group_cols), lambda t, c: (t, c)),
            pl.BlockSpec((SPAN, group_cols), lambda t, c: (t, c)),
            pl.BlockSpec((1, window, DH), lambda t, c: (t, 0, c)),
            pl.BlockSpec((1, window, DH), lambda t, c: (t, 0, c)),
        ],
        out_specs=[
            pl.BlockSpec((SPAN, group_cols), lambda t, c: (t, c)),
            pl.BlockSpec((SPAN, group_cols), lambda t, c: (t, c)),
            pl.BlockSpec((1, window, DH), lambda t, c: (t, 0, c)),
            pl.BlockSpec((1, window, DH), lambda t, c: (t, 0, c)),
        ],
        out_shape=[
            jax.ShapeDtypeStruct((local_rows, head_count * DH), jnp.bfloat16),
            jax.ShapeDtypeStruct((local_rows, head_count * DH), jnp.bfloat16),
            jax.ShapeDtypeStruct((tiles, window, kv_cols), jnp.float32),
            jax.ShapeDtypeStruct((tiles, window, kv_cols), jnp.float32),
        ],
    )
    attended, query_grad, key_part, value_part = kernel(
        query_pos, query_start, key_pos, queries, out_grad, key_win, value_win)

    packed = jnp.concatenate([key_part, value_part], axis=2).reshape(
        tiles * window_spans, SPAN, 2 * kv_cols)
    buffer = jnp.zeros((slot_count, SPAN, 2 * kv_cols), jnp.float32)
    buffer = buffer.at[window_slot.reshape(-1)].add(packed)
    summed = lax.psum_scatter(buffer.reshape(total_rows, 2 * kv_cols), "ctx",
                              scatter_dimension=0, tiled=True)
    key_grad = summed[:, :kv_cols].astype(jnp.bfloat16)
    value_grad = summed[:, kv_cols:].astype(jnp.bfloat16)
    return (attended, query_grad, key_grad, value_grad)


def solution(mesh):
    in_specs = (
        P(("groups", "ctx"), "head"),
        P(("groups", "ctx"), "head"),
        P(("groups", "ctx"), "head"),
        P(("groups", "ctx"), "head"),
        P(("groups", "ctx")),
        P("groups"),
    )
    out_specs = (
        P(("groups", "ctx"), "head"),
        P(("groups", "ctx"), "head"),
        P(("groups", "ctx"), "head"),
        P(("groups", "ctx"), "head"),
    )
    return jax.shard_map(local, mesh=mesh, in_specs=in_specs, out_specs=out_specs, check_vma=False)
```

time: 657 us -> 248 us (0.38); the launches traced: 650 us -> 248 us
  other arithmetic: 299 us -> 13.2 us
  local copies, waits for them, and re-layouts: 123 us -> 12.5 us
  Pallas kernels: 0 us -> 43.3 us
  matrix products: 37.5 us -> 0 us
  loops' own time: 32.7 us -> 0 us
  waiting for transfers between devices: 143 us -> 165 us
    add x39 -> x2, other arithmetic: 257 us -> 0.67 us  [the longest x1 0.6 us: local(): window_span[:, :, None] * SPAN + row_in_span[None, None, :]]
    pallas_call x0 -> x1, Pallas kernels: none -> 43.3 us  [local(): kernel(query_pos, query_start, key_pos, queries, out_grad, key_win, value...]
    all_gather x1, waiting for transfers between devices: 0.01 us -> 38.2 us  [local(): lax.all_gather(value_rows, 'ctx', axis=0, tiled=True)]
    dot_general x35 -> x0, matrix products: 37.5 us -> none  [the longest x5 14.2 us: output_update(): jnp.einsum('ktgs,skd->ktgd', weights.astype(jnp.bfloat16), value_block, p...]
    dynamic_slice x40 -> x0, local copies, waits for them, and re-layouts: 33.5 us -> none  [the longest x16 10.2 us: backward_one_block(): current = lax.dynamic_slice_in_dim(buffer, row_at, block_rows, 0)]
    another operation x51 -> x0, loops' own time: 32.7 us -> none  [the longest x2 21.6 us: make_pass(): return lax.fori_loop(0, block_count, make_one_block, state_in)]
    reduce_scatter x1, waiting for transfers between devices: 116 us -> 86.9 us  [local(): lax.psum_scatter(buffer.reshape(total_rows, 2 * kv_cols), 'ctx', scatter_...]
    reduce_or x24 -> x0, other arithmetic: 23.8 us -> none  [the longest x16 17.7 us: make_one_block(): jnp.any(seen_mask)]
  transfers between devices with their start and end apart: 3 -> 3, of which waited for: 2 -> 3; matrix products, arithmetic and copies ran while one was open for 24% -> 4% of each run, Pallas kernels for 0% -> 0%
where the time goes in v1:
time: 248 us
  waiting for transfers between devices  165 us (67%)
  Pallas kernels  43.3 us (17%)
  between operations  13.8 us (6%)
  other arithmetic  13.2 us (5%)
  local copies, waits for them, and re-layouts  12.5 us (5%)
    reduce_scatter x1, waiting for transfers between devices, local(): lax.psum_scatter(buffer.reshape(total_rows, 2 * kv_cols), 'ctx', scatter_...  86.9 us
    pallas_call x1, Pallas kernels, local(): kernel(query_pos, query_start, key_pos, queries, out_grad, key_win, value...  43.3 us
    all_gather x1, waiting for transfers between devices, local(): lax.all_gather(key_rows, 'ctx', axis=0, tiled=True)  38.4 us
    all_gather x1, waiting for transfers between devices, local(): lax.all_gather(value_rows, 'ctx', axis=0, tiled=True)  38.2 us
    scatter-add x1, other arithmetic, local(): buffer = buffer.at[window_slot.reshape(-1)].add(packed)  7.96 us
  transfers between devices with their start and end apart: 3, of which 3 were waited for; matrix products, arithmetic and copies ran while one was open for 4% of the time, Pallas kernels for 0%

profile of v1, /device:TPU:0, one launch (start us, length us, event | category | flops | bytes accessed | tf_op | source)
XLA Modules:
  0.0 247.6 jit_solution(15654404821302385170)
XLA Ops:
  7.2 0.7 all-gather.5.cloned.1.call-update
  7.9 0.7 all-gather.3.cloned.1.call-update
  8.7 0.7 broadcast_add_fusion.1
  9.5 0.1 reshape.206
  9.6 0.7 compare_select_fusion.3
  10.3 0.6 scatter_custom_fusion
  10.9 0.7 gather_fusion
  11.6 0.1 gather.12
  11.6 0.1 reshape.214
  12.0 0.1 add.143
  12.1 0.8 add.142.refs_0_
  12.9 1.4 copy.18.refs_1_
  14.3 0.6 broadcast_add_fusion.refs_2_
  14.9 38.2 %all-gather.5.cloned.1.call-done = bf16[1024,512]{1,0:T(8,128)(2,1)} async-done(((bf16[128,512]{1,0:T(8,128)(2,1)}), bf16[1024,512]{1,0:T(8,128)(2,1)}) %all-gather.5.cloned.1.call-update) | async-done | bytes 1048592 | tf_op jit(solution)/shard_map/all_gather | solution.py:85
  53.0 2.7 %gather_fusion.2 = bf16[10,64,512]{2,1,0:T(8,128)(2,1)} fusion(bf16[16,64,512]{2,1,0:T(8,128)(2,1)} %bitcast.20, s32[1024]{0:T(1024)S(1)} %pad_clamp_fusion), kind=kCustom, calls=%fused_computation.2 | custom fusion | bytes 1310760 | tf_op jit(solution)/shard_map/gather | solution.py:87
  55.7 38.4 %all-gather.3.cloned.1.call-done = bf16[1024,512]{1,0:T(8,128)(2,1)} async-done(((bf16[128,512]{1,0:T(8,128)(2,1)}), bf16[1024,512]{1,0:T(8,128)(2,1)}) %all-gather.3.cloned.1.call-update) | async-done | bytes 1048592 | tf_op jit(solution)/shard_map/all_gather | solution.py:84
  94.1 2.7 %gather_fusion.1 = bf16[10,64,512]{2,1,0:T(8,128)(2,1)} fusion(bf16[16,64,512]{2,1,0:T(8,128)(2,1)} %bitcast.21, s32[1024]{0:T(1024)S(1)} %pad_clamp_fusion), kind=kCustom, calls=%fused_computation.1 | custom fusion | bytes 1310760 | tf_op jit(solution)/shard_map/gather | solution.py:86
  96.8 43.3 %shard_map.93 = (bf16[128,4096]{1,0:T(8,128)(2,1)}, bf16[128,4096]{1,0:T(8,128)(2,1)}, f32[2,320,512]{2,1,0:T(8,128)}, f32[2,320,512]{2,1,0:T(8,128)}) custom-call(s32[128,1]{1,0:T(8,128)} %add.142.refs_0_, s32[128,1]{1,0:T(8,128)} %copy.18.refs_1_, s32[2,1,320]{2,1,0:T(1,128)} %broadcast_add_fusion.refs_2_, bf16[128,4096]{1,0:T(8,128)(2,1)} %refs_3_.1, ...), custom_call_target="tpu_custom_call" | custom-call | tf_op jit(solution)/shard_map/pallas_call | solution.py:114
  140.0 1.9 pad_maximum_fusion
  142.0 2.5 broadcast_in_dim.5
  144.4 8.0 %scatter_fusion = f32[16,64,1024]{2,1,0:T(8,128)} fusion(f32[16,64,1024]{2,1,0:T(8,128)} %broadcast_in_dim.5, s32[10]{0:T(128)S(1)} %fusion, f32[10,64,1024]{2,1,0:T(8,128)S(1)} %bitcast.17), kind=kCustom, calls=%fused_computation.4 | custom fusion | flops 655360 | bytes 7864360 | tf_op jit(solution)/shard_map/scatter-add | solution.py:120
  152.4 86.9 %reduce-scatter.2.cloned.1.call-done = f32[128,1024]{1,0:T(8,128)} async-done(((f32[1024,1024]{1,0:T(8,128)}), f32[128,1024]{1,0:T(8,128)}) %reduce-scatter.2.cloned.1.call-update) | async-done | bytes 524304 | tf_op jit(solution)/shard_map/reduce_scatter | solution.py:121
  239.3 1.1 convert.4
  240.4 0.7 fusion.3
  (15 shorter events, 0.5 us)
Async XLA Ops:
  7.2 45.9 %all-gather.5.cloned.1.call-start = ((), (), s32[]{:S(2)}) async-start(), calls=%async_computation.2 | async-start | bytes 1179648 | tf_op jit(solution)/shard_map/all_gather | solution.py:85
  7.9 86.2 %all-gather.3.cloned.1.call-start = ((), (), s32[]{:S(2)}) async-start(), calls=%async_computation.1 | async-start | bytes 1179648 | tf_op jit(solution)/shard_map/all_gather | solution.py:84
  8.6 230.7 %reduce-scatter.2.cloned.1.call-start = ((), (), s32[]{:S(2)}) async-start(), calls=%async_computation.3 | async-start | bytes 4718592 | tf_op jit(solution)/shard_map/reduce_scatter | solution.py:121
Sparse Core Ops, SparseCore 0:
  10.1 42.8 all-gather.4
  55.2 38.8 all-gather.2
  152.5 86.7 reduce-scatter.1

commit v2 on v1

--- a/solution.py
+++ b/solution.py
@@ -81,10 +81,17 @@
     query_pos = (my_spans[:, None] * SPAN + row_in_span[None, :]).reshape(local_rows, 1)
     query_start = doc_start.reshape(local_rows, 1)
 
-    key_all = lax.all_gather(key_rows, "ctx", axis=0, tiled=True).reshape(slot_count, SPAN, kv_cols)
-    value_all = lax.all_gather(value_rows, "ctx", axis=0, tiled=True).reshape(slot_count, SPAN, kv_cols)
-    key_win = key_all[window_slot].reshape(tiles, window, kv_cols)
-    value_win = value_all[window_slot].reshape(tiles, window, kv_cols)
+    pair = jnp.concatenate([key_rows, value_rows], axis=1)
+    pieces = [pair]
+    for shift in range(1, ctx_count):
+        pieces.append(lax.ppermute(
+            pair, "ctx", [(i, (i + shift) % ctx_count) for i in range(ctx_count)]))
+    pair_all = jnp.stack(pieces).reshape(ctx_count * tiles, SPAN, 2 * kv_cols)
+    window_owner = window_slot // tiles
+    window_piece = ((my_index - window_owner) % ctx_count) * tiles + window_slot % tiles
+    pair_win = pair_all[window_piece].reshape(tiles, window, 2 * kv_cols)
+    key_win = pair_win[:, :, :kv_cols]
+    value_win = pair_win[:, :, kv_cols:]
 
     kernel = pl.pallas_call(
         lambda *refs: attention_kernel(*refs, group_size=group_size, score_scale=score_scale),
@@ -118,8 +125,13 @@
         tiles * window_spans, SPAN, 2 * kv_cols)
     buffer = jnp.zeros((slot_count, SPAN, 2 * kv_cols), jnp.float32)
     buffer = buffer.at[window_slot.reshape(-1)].add(packed)
-    summed = lax.psum_scatter(buffer.reshape(total_rows, 2 * kv_cols), "ctx",
-                              scatter_dimension=0, tiled=True)
+    blocks = buffer.reshape(ctx_count, local_rows, 2 * kv_cols)
+    summed = lax.dynamic_index_in_dim(blocks, my_index, 0, keepdims=False)
+    for shift in range(1, ctx_count):
+        send = lax.dynamic_index_in_dim(blocks, (my_index + shift) % ctx_count, 0, keepdims=False)
+        summed = summed + lax.ppermute(
+            send.astype(jnp.bfloat16), "ctx",
+            [(i, (i + shift) % ctx_count) for i in range(ctx_count)]).astype(jnp.float32)
     key_grad = summed[:, :kv_cols].astype(jnp.bfloat16)
     value_grad = summed[:, kv_cols:].astype(jnp.bfloat16)
     return (attended, query_grad, key_grad, value_grad)

time: 248 us -> 165 us (0.67)
  waiting for transfers between devices: 165 us -> 59.1 us
  starting transfers between devices: 0.11 us -> 33.7 us
  between operations: 13.8 us -> 0.86 us
    reduce_scatter x1 -> x0, waiting for transfers between devices: 86.9 us -> none  [local(): lax.psum_scatter(buffer.reshape(total_rows, 2 * kv_cols), 'ctx', scatter_...]
    all_gather x2 -> x0, waiting for transfers between devices: 76.5 us -> none  [the longest x1 38.4 us: local(): lax.all_gather(key_rows, 'ctx', axis=0, tiled=True)]
    ppermute x0 -> x14, waiting for transfers between devices: none -> 59.1 us  [the longest x7 42.7 us: local(): lax.ppermute(send.astype(jnp.bfloat16), 'ctx', [(i, (i + shift) % ctx_cou...]
    ppermute x0 -> x14, starting transfers between devices: none -> 33.7 us  [the longest x7 19.9 us: local(): lax.ppermute(send.astype(jnp.bfloat16), 'ctx', [(i, (i + shift) % ctx_cou...]
    gather x2 -> x1, local copies, waits for them, and re-layouts: 5.38 us -> 0.63 us  [local(): pair_win = pair_all[window_piece].reshape(tiles, window, 2 * kv_cols)]
    unnamed x0 -> x10, local copies, waits for them, and re-layouts: none -> 2.95 us
  transfers between devices with their start and end apart: 3 -> 14, of which waited for: 3 -> 8; matrix products, arithmetic and copies ran while one was open for 4% -> 5% of each run, Pallas kernels for 0% -> 0%
where the time goes in v2:
time: 165 us
  waiting for transfers between devices  59.1 us (36%)
  Pallas kernels  43.3 us (26%)
  starting transfers between devices  33.7 us (20%)
  local copies, waits for them, and re-layouts  14.4 us (9%)
  other arithmetic  13.5 us (8%)
    pallas_call x1, Pallas kernels, local(): kernel(query_pos, query_start, key_pos, queries, out_grad, key_win, value...  43.3 us
    ppermute x7, waiting for transfers between devices, local(): lax.ppermute(send.astype(jnp.bfloat16), 'ctx', [(i, (i + shift) % ctx_cou...  42.7 us
    ppermute x7, starting transfers between devices, local(): lax.ppermute(send.astype(jnp.bfloat16), 'ctx', [(i, (i + shift) % ctx_cou...  19.9 us
    ppermute x7, waiting for transfers between devices, local(): lax.ppermute(pair, 'ctx', [(i, (i + shift) % ctx_count) for i in range(ct...  16.5 us
    ppermute x7, starting transfers between devices, local(): lax.ppermute(pair, 'ctx', [(i, (i + shift) % ctx_count) for i in range(ct...  13.8 us
    scatter-add x1, other arithmetic, local(): buffer = buffer.at[window_slot.reshape(-1)].add(packed)  7.98 us
  transfers between devices with their start and end apart: 14, of which 8 were waited for; matrix products, arithmetic and copies ran while one was open for 5% of the time, Pallas kernels for 0%

profile of v2, /device:TPU:0, one launch (start us, length us, event | category | flops | bytes accessed | tf_op | source)
XLA Modules:
  0.0 164.9 jit_solution(12921288453715332198)
XLA Ops:
  2.5 3.0 %collective-permute-start = (bf16[128,1024]{1,0:T(8,128)(2,1)S(1)}, bf16[128,1024]{1,0:T(8,128)(2,1)}, u32[]{:S(2)}, u32[]{:S(2)}) collective-permute-start(bf16[128,1024]{1,0:T(8,128)(2,1)S(1)} %constant_dynamic-update-slice_fusion), channel_id=1, source_target_pairs={{0,2},{2,4},{4,6},{6,8},{8,10},{10,12},{12,14},{14,0},{1,3},{3,5},... | collective-permute-start | bytes 786440 | tf_op jit(solution)/shard_map/ppermute | solution.py:87
  5.5 1.6 collective-permute-start.1
  7.1 2.5 %collective-permute-start.2 = (bf16[128,1024]{1,0:T(8,128)(2,1)S(1)}, bf16[128,1024]{1,0:T(8,128)(2,1)S(1)}, u32[]{:S(2)}, u32[]{:S(2)}) collective-permute-start(bf16[128,1024]{1,0:T(8,128)(2,1)S(1)} %constant_dynamic-update-slice_fusion), channel_id=1, source_target_pairs={{0,6},{2,8},{4,10},{6,12},{8,14},{10,0},{12,2},{14,4},{1,7},{3,9},... | collective-permute-start | bytes 786440 | tf_op jit(solution)/shard_map/ppermute | solution.py:87
  9.6 1.2 collective-permute-start.3
  10.8 2.6 %collective-permute-start.4 = (bf16[128,1024]{1,0:T(8,128)(2,1)S(1)}, bf16[128,1024]{1,0:T(8,128)(2,1)S(1)}, u32[]{:S(2)}, u32[]{:S(2)}) collective-permute-start(bf16[128,1024]{1,0:T(8,128)(2,1)S(1)} %constant_dynamic-update-slice_fusion), channel_id=1, source_target_pairs={{0,10},{2,12},{4,14},{6,0},{8,2},{10,4},{12,6},{14,8},{1,11},{3,13... | collective-permute-start | bytes 786440 | tf_op jit(solution)/shard_map/ppermute | solution.py:87
  19.2 1.3 collective-permute-start.5
  20.5 1.0 bitcast_dynamic-update-slice_fusion.6
  21.5 1.5 collective-permute-start.6
  22.9 1.0 bitcast_dynamic-update-slice_fusion.5
  23.9 13.5 %collective-permute-done.2 = bf16[128,1024]{1,0:T(8,128)(2,1)S(1)} collective-permute-done((bf16[128,1024]{1,0:T(8,128)(2,1)S(1)}, bf16[128,1024]{1,0:T(8,128)(2,1)S(1)}, u32[]{:S(2)}, u32[]{:S(2)}) %collective-permute-start.2) | collective-permute-done | bytes 262176 | tf_op jit(solution)/shard_map/ppermute | solution.py:87
  37.9 2.6 %collective-permute-done.6 = bf16[128,1024]{1,0:T(8,128)(2,1)S(1)} collective-permute-done((bf16[128,1024]{1,0:T(8,128)(2,1)S(1)}, bf16[128,1024]{1,0:T(8,128)(2,1)S(1)}, u32[]{:S(2)}, u32[]{:S(2)}) %collective-permute-start.6) | collective-permute-done | bytes 262176 | tf_op jit(solution)/shard_map/ppermute | solution.py:87
  41.2 1.2 fusion.20
  42.3 43.3 %shard_map.93 = (bf16[128,4096]{1,0:T(8,128)(2,1)}, bf16[128,4096]{1,0:T(8,128)(2,1)}, f32[2,320,512]{2,1,0:T(8,128)}, f32[2,320,512]{2,1,0:T(8,128)}) custom-call(s32[128,1]{1,0:T(8,128)} %add.302.refs_0_, s32[128,1]{1,0:T(8,128)} %copy.18.refs_1_, s32[2,1,320]{2,1,0:T(1,128)} %broadcast_add_fusion.refs_2_, bf16[128,4096]{1,0:T(8,128)(2,1)} %refs_3_.1, ...), custom_call_target="tpu_custom_call" | custom-call | tf_op jit(solution)/shard_map/pallas_call | solution.py:121
  85.6 1.9 %pad_maximum_fusion = f32[2,320,1024]{2,1,0:T(8,128)S(1)} fusion(f32[2,320,512]{2,1,0:T(8,128)} %get-tuple-element.11, f32[2,320,512]{2,1,0:T(8,128)} %get-tuple-element.10), kind=kLoop, calls=%fused_computation.4 | loop fusion | flops 655360 | bytes 5242880 | tf_op jit(solution)/shard_map/concatenate | solution.py:124
  87.6 2.5 %broadcast_in_dim.5 = f32[16,64,1024]{2,1,0:T(8,128)} broadcast(f32[]{:T(128)} %constant.116.clone.1), dimensions={} | broadcast | bytes 4194308 | tf_op jit(solution)/shard_map/broadcast_in_dim | solution.py:126
  90.0 8.0 %scatter_fusion = f32[16,64,1024]{2,1,0:T(8,128)} fusion(f32[16,64,1024]{2,1,0:T(8,128)} %broadcast_in_dim.5, s32[10]{0:T(128)S(1)} %fusion.17, f32[10,64,1024]{2,1,0:T(8,128)S(1)} %bitcast.61), kind=kCustom, calls=%fused_computation.3 | custom fusion | flops 655360 | bytes 7864360 | tf_op jit(solution)/shard_map/scatter-add | solution.py:127
  98.0 2.3 %fusion.7 = (bf16[128,1024]{1,0:T(8,128)(2,1)S(1)}, bf16[128,1024]{1,0:T(8,128)(2,1)S(1)}, bf16[128,1024]{1,0:T(8,128)(2,1)S(1)}, bf16[128,1024]{1,0:T(8,128)(2,...) fusion(f32[8,128,1024]{2,1,0:T(8,128)} %bitcast.59, ...), kind=kLoop, calls=%fused_computation.20 | loop fusion | bytes 3670044 | tf_op jit(solution)/shard_map/convert_element_type | solution.py:133
  100.3 16.8 %collective-permute-start.13 = (bf16[128,1024]{1,0:T(8,128)(2,1)S(1)}, bf16[128,1024]{1,0:T(8,128)(2,1)S(1)}, u32[]{:S(2)}, u32[]{:S(2)}) collective-permute-start(bf16[128,1024]{1,0:T(8,128)(2,1)S(1)} %get-tuple-element.13), channel_id=1, source_target_pairs={{0,14},{2,0},{4,2},{6,4},{8,6},{10,8},{12,10},{14,12},{1,15},{3,1}... | collective-permute-start | bytes 786440 | tf_op jit(solution)/shard_map/ppermute | solution.py:132
  117.3 2.8 %collective-permute-start.10 = (bf16[128,1024]{1,0:T(8,128)(2,1)S(1)}, bf16[128,1024]{1,0:T(8,128)(2,1)S(1)}, u32[]{:S(2)}, u32[]{:S(2)}) collective-permute-start(bf16[128,1024]{1,0:T(8,128)(2,1)S(1)} %get-tuple-element.16), channel_id=1, source_target_pairs={{0,8},{2,10},{4,12},{6,14},{8,0},{10,2},{12,4},{14,6},{1,9},{3,11}... | collective-permute-start | bytes 786440 | tf_op jit(solution)/shard_map/ppermute | solution.py:132
  120.2 3.7 %collective-permute-done.13 = bf16[128,1024]{1,0:T(8,128)(2,1)S(1)} collective-permute-done((bf16[128,1024]{1,0:T(8,128)(2,1)S(1)}, bf16[128,1024]{1,0:T(8,128)(2,1)S(1)}, u32[]{:S(2)}, u32[]{:S(2)}) %collective-permute-start.13) | collective-permute-done | bytes 262176 | tf_op jit(solution)/shard_map/ppermute | solution.py:132
  123.9 5.6 %collective-permute-done.12 = bf16[128,1024]{1,0:T(8,128)(2,1)S(1)} collective-permute-done((bf16[128,1024]{1,0:T(8,128)(2,1)S(1)}, bf16[128,1024]{1,0:T(8,128)(2,1)S(1)}, u32[]{:S(2)}, u32[]{:S(2)}) %collective-permute-start.12) | collective-permute-done | bytes 262176 | tf_op jit(solution)/shard_map/ppermute | solution.py:132
  129.5 5.6 %collective-permute-done.11 = bf16[128,1024]{1,0:T(8,128)(2,1)S(1)} collective-permute-done((bf16[128,1024]{1,0:T(8,128)(2,1)S(1)}, bf16[128,1024]{1,0:T(8,128)(2,1)S(1)}, u32[]{:S(2)}, u32[]{:S(2)}) %collective-permute-start.11) | collective-permute-done | bytes 262176 | tf_op jit(solution)/shard_map/ppermute | solution.py:132
  135.1 27.6 %collective-permute-done.10 = bf16[128,1024]{1,0:T(8,128)(2,1)S(1)} collective-permute-done((bf16[128,1024]{1,0:T(8,128)(2,1)S(1)}, bf16[128,1024]{1,0:T(8,128)(2,1)S(1)}, u32[]{:S(2)}, u32[]{:S(2)}) %collective-permute-start.10) | collective-permute-done | bytes 262176 | tf_op jit(solution)/shard_map/ppermute | solution.py:132
  162.8 1.4 fusion.6
  (47 shorter events, 9.5 us)
Async XLA Ops:
  0.6 17.8 %copy-start = (s32[128]{0:T(128)S(1)}, s32[128]{0:T(128)}, u32[]{:S(2)}) copy-start(s32[128]{0:T(128)} %param.10) | copy-start | bytes 1540
  2.5 16.7 %collective-permute-start = (bf16[128,1024]{1,0:T(8,128)(2,1)S(1)}, bf16[128,1024]{1,0:T(8,128)(2,1)}, u32[]{:S(2)}, u32[]{:S(2)}) collective-permute-start(bf16[128,1024]{1,0:T(8,128)(2,1)S(1)} %constant_dynamic-update-slice_fusion), channel_id=1, source_target_pairs={{0,2},{2,4},{4,6},{6,8},{8,10},{10,12},{12,14},{14,0},{1,3},{3,5},... | collective-permute-start | bytes 786440 | tf_op jit(solution)/shard_map/ppermute | solution.py:87
  5.5 16.0 %collective-permute-start.1 = (bf16[128,1024]{1,0:T(8,128)(2,1)S(1)}, bf16[128,1024]{1,0:T(8,128)(2,1)}, u32[]{:S(2)}, u32[]{:S(2)}) collective-permute-start(bf16[128,1024]{1,0:T(8,128)(2,1)S(1)} %constant_dynamic-update-slice_fusion), channel_id=1, source_target_pairs={{0,4},{2,6},{4,8},{6,10},{8,12},{10,14},{12,0},{14,2},{1,5},{3,7},... | collective-permute-start | bytes 786440 | tf_op jit(solution)/shard_map/ppermute | solution.py:87
  7.1 30.4 %collective-permute-start.2 = (bf16[128,1024]{1,0:T(8,128)(2,1)S(1)}, bf16[128,1024]{1,0:T(8,128)(2,1)S(1)}, u32[]{:S(2)}, u32[]{:S(2)}) collective-permute-start(bf16[128,1024]{1,0:T(8,128)(2,1)S(1)} %constant_dynamic-update-slice_fusion), channel_id=1, source_target_pairs={{0,6},{2,8},{4,10},{6,12},{8,14},{10,0},{12,2},{14,4},{1,7},{3,9},... | collective-permute-start | bytes 786440 | tf_op jit(solution)/shard_map/ppermute | solution.py:87
  9.6 28.2 %collective-permute-start.3 = (bf16[128,1024]{1,0:T(8,128)(2,1)S(1)}, bf16[128,1024]{1,0:T(8,128)(2,1)S(1)}, u32[]{:S(2)}, u32[]{:S(2)}) collective-permute-start(bf16[128,1024]{1,0:T(8,128)(2,1)S(1)} %constant_dynamic-update-slice_fusion), channel_id=1, source_target_pairs={{0,8},{2,10},{4,12},{6,14},{8,0},{10,2},{12,4},{14,6},{1,9},{3,11}... | collective-permute-start | bytes 786440 | tf_op jit(solution)/shard_map/ppermute | solution.py:87
  10.8 27.0 %collective-permute-start.4 = (bf16[128,1024]{1,0:T(8,128)(2,1)S(1)}, bf16[128,1024]{1,0:T(8,128)(2,1)S(1)}, u32[]{:S(2)}, u32[]{:S(2)}) collective-permute-start(bf16[128,1024]{1,0:T(8,128)(2,1)S(1)} %constant_dynamic-update-slice_fusion), channel_id=1, source_target_pairs={{0,10},{2,12},{4,14},{6,0},{8,2},{10,4},{12,6},{14,8},{1,11},{3,13... | collective-permute-start | bytes 786440 | tf_op jit(solution)/shard_map/ppermute | solution.py:87
  19.2 18.7 %collective-permute-start.5 = (bf16[128,1024]{1,0:T(8,128)(2,1)S(1)}, bf16[128,1024]{1,0:T(8,128)(2,1)S(1)}, u32[]{:S(2)}, u32[]{:S(2)}) collective-permute-start(bf16[128,1024]{1,0:T(8,128)(2,1)S(1)} %constant_dynamic-update-slice_fusion), channel_id=1, source_target_pairs={{0,12},{2,14},{4,0},{6,2},{8,4},{10,6},{12,8},{14,10},{1,13},{3,15... | collective-permute-start | bytes 786440 | tf_op jit(solution)/shard_map/ppermute | solution.py:87
  21.5 19.0 %collective-permute-start.6 = (bf16[128,1024]{1,0:T(8,128)(2,1)S(1)}, bf16[128,1024]{1,0:T(8,128)(2,1)S(1)}, u32[]{:S(2)}, u32[]{:S(2)}) collective-permute-start(bf16[128,1024]{1,0:T(8,128)(2,1)S(1)} %constant_dynamic-update-slice_fusion), channel_id=1, source_target_pairs={{0,14},{2,0},{4,2},{6,4},{8,6},{10,8},{12,10},{14,12},{1,15},{3,1}... | collective-permute-start | bytes 786440 | tf_op jit(solution)/shard_map/ppermute | solution.py:87
  100.3 23.6 %collective-permute-start.13 = (bf16[128,1024]{1,0:T(8,128)(2,1)S(1)}, bf16[128,1024]{1,0:T(8,128)(2,1)S(1)}, u32[]{:S(2)}, u32[]{:S(2)}) collective-permute-start(bf16[128,1024]{1,0:T(8,128)(2,1)S(1)} %get-tuple-element.13), channel_id=1, source_target_pairs={{0,14},{2,0},{4,2},{6,4},{8,6},{10,8},{12,10},{14,12},{1,15},{3,1}... | collective-permute-start | bytes 786440 | tf_op jit(solution)/shard_map/ppermute | solution.py:132
  117.1 12.4 %collective-permute-start.12 = (bf16[128,1024]{1,0:T(8,128)(2,1)S(1)}, bf16[128,1024]{1,0:T(8,128)(2,1)S(1)}, u32[]{:S(2)}, u32[]{:S(2)}) collective-permute-start(bf16[128,1024]{1,0:T(8,128)(2,1)S(1)} %get-tuple-element.14), channel_id=1, source_target_pairs={{0,12},{2,14},{4,0},{6,2},{8,4},{10,6},{12,8},{14,10},{1,13},{3,15... | collective-permute-start | bytes 786440 | tf_op jit(solution)/shard_map/ppermute | solution.py:132
  117.1 18.0 %collective-permute-start.11 = (bf16[128,1024]{1,0:T(8,128)(2,1)S(1)}, bf16[128,1024]{1,0:T(8,128)(2,1)S(1)}, u32[]{:S(2)}, u32[]{:S(2)}) collective-permute-start(bf16[128,1024]{1,0:T(8,128)(2,1)S(1)} %get-tuple-element.15), channel_id=1, source_target_pairs={{0,10},{2,12},{4,14},{6,0},{8,2},{10,4},{12,6},{14,8},{1,11},{3,13... | collective-permute-start | bytes 786440 | tf_op jit(solution)/shard_map/ppermute | solution.py:132
  117.3 45.5 %collective-permute-start.10 = (bf16[128,1024]{1,0:T(8,128)(2,1)S(1)}, bf16[128,1024]{1,0:T(8,128)(2,1)S(1)}, u32[]{:S(2)}, u32[]{:S(2)}) collective-permute-start(bf16[128,1024]{1,0:T(8,128)(2,1)S(1)} %get-tuple-element.16), channel_id=1, source_target_pairs={{0,8},{2,10},{4,12},{6,14},{8,0},{10,2},{12,4},{14,6},{1,9},{3,11}... | collective-permute-start | bytes 786440 | tf_op jit(solution)/shard_map/ppermute | solution.py:132
  120.1 42.7 %collective-permute-start.9 = (bf16[128,1024]{1,0:T(8,128)(2,1)S(1)}, bf16[128,1024]{1,0:T(8,128)(2,1)S(1)}, u32[]{:S(2)}, u32[]{:S(2)}) collective-permute-start(bf16[128,1024]{1,0:T(8,128)(2,1)S(1)} %get-tuple-element.17), channel_id=1, source_target_pairs={{0,6},{2,8},{4,10},{6,12},{8,14},{10,0},{12,2},{14,4},{1,7},{3,9},... | collective-permute-start | bytes 786440 | tf_op jit(solution)/shard_map/ppermute | solution.py:132
  123.9 38.9 %collective-permute-start.8 = (bf16[128,1024]{1,0:T(8,128)(2,1)S(1)}, bf16[128,1024]{1,0:T(8,128)(2,1)S(1)}, u32[]{:S(2)}, u32[]{:S(2)}) collective-permute-start(bf16[128,1024]{1,0:T(8,128)(2,1)S(1)} %get-tuple-element.18), channel_id=1, source_target_pairs={{0,4},{2,6},{4,8},{6,10},{8,12},{10,14},{12,0},{14,2},{1,5},{3,7},... | collective-permute-start | bytes 786440 | tf_op jit(solution)/shard_map/ppermute | solution.py:132
  129.5 33.3 %collective-permute-start.7 = (bf16[128,1024]{1,0:T(8,128)(2,1)S(1)}, bf16[128,1024]{1,0:T(8,128)(2,1)S(1)}, u32[]{:S(2)}, u32[]{:S(2)}) collective-permute-start(bf16[128,1024]{1,0:T(8,128)(2,1)S(1)} %get-tuple-element.12), channel_id=1, source_target_pairs={{0,2},{2,4},{4,6},{6,8},{8,10},{10,12},{12,14},{14,0},{1,3},{3,5},... | collective-permute-start | bytes 786440 | tf_op jit(solution)/shard_map/ppermute | solution.py:132

commit v3 on v1

v3 whole, which is shorter than its diff:
```python
import math

import jax
import jax.numpy as jnp
from jax import lax
from jax.experimental import pallas as pl
from jax.experimental.pallas import tpu as pltpu
from jax.sharding import PartitionSpec as P

DH = 128
SPAN = 64
CHUNKS = 2


def attention_kernel(index_ref, qpos_ref, qstart_ref, kpos_ref, q_ref, do_ref, k_ref, v_ref,
                     *rest, group_size, window_spans, tiles, score_scale, aliased):
    if aliased:
        rest = rest[2:]
    out_ref, dq_ref, buf_ref = rest
    tile = pl.program_id(1)
    base = tile * window_spans
    key_block = jnp.concatenate(
        [k_ref[index_ref[base + w]] for w in range(window_spans)], axis=0)
    value_block = jnp.concatenate(
        [v_ref[index_ref[base + w]] for w in range(window_spans)], axis=0)
    query_all = jnp.concatenate(
        [q_ref[:, h * DH:(h + 1) * DH] for h in range(group_size)], axis=0)
    grad_all = jnp.concatenate(
        [do_ref[:, h * DH:(h + 1) * DH] for h in range(group_size)], axis=0)
    kpos = kpos_ref[0]
    visible = (kpos >= qstart_ref[0]) & (kpos <= qpos_ref[0])
    contract_last = (((1,), (1,)), ((), ()))
    contract_first = (((0,), (0,)), ((), ()))
    scores = lax.dot_general(query_all, key_block, contract_last,
                             preferred_element_type=jnp.float32) * score_scale
    masked = jnp.where(visible, scores, -jnp.inf)
    row_max = jnp.max(masked, axis=1, keepdims=True)
    shifted = jnp.where(visible, jnp.exp(masked - row_max), 0.0)
    log_totals = row_max + jnp.log(jnp.sum(shifted, axis=1, keepdims=True))
    weights = jnp.where(visible, jnp.exp(masked - log_totals), 0.0)
    weights_low = weights.astype(jnp.bfloat16)
    attended = jnp.dot(weights_low, value_block,
                       preferred_element_type=jnp.float32).astype(jnp.bfloat16)
    row_dots = jnp.sum(attended.astype(jnp.float32) * grad_all.astype(jnp.float32),
                       axis=1, keepdims=True)
    grad_weights = lax.dot_general(grad_all, value_block, contract_last,
                                   preferred_element_type=jnp.float32)
    grad_scores = (weights * (grad_weights - row_dots)).astype(jnp.bfloat16)
    query_grad = (jnp.dot(grad_scores, key_block, preferred_element_type=jnp.float32)
                  * score_scale).astype(jnp.bfloat16)
    for h in range(group_size):
        out_ref[:, h * DH:(h + 1) * DH] = attended[h * SPAN:(h + 1) * SPAN]
        dq_ref[:, h * DH:(h + 1) * DH] = query_grad[h * SPAN:(h + 1) * SPAN]
    key_sum = lax.dot_general(grad_scores, query_all, contract_first,
                              preferred_element_type=jnp.float32) * score_scale
    value_sum = lax.dot_general(weights_low, grad_all, contract_first,
                                preferred_element_type=jnp.float32)

    @pl.when(tile == 0)
    def _():
        buf_ref[...] = jnp.zeros(buf_ref.shape, buf_ref.dtype)

    slot_base = tiles * window_spans + base
    for w in range(window_spans):
        slot = index_ref[slot_base + w]
        rows = slice(w * SPAN, (w + 1) * SPAN)
        buf_ref[0, slot, :, :DH] += key_sum[rows]
        buf_ref[0, slot, :, DH:] += value_sum[rows]


def local(queries, key_rows, value_rows, out_grad, doc_start, span_order):
    local_rows = queries.shape[0]
    tiles = local_rows // SPAN
    head_count = queries.shape[1] // DH
    kv_count = key_rows.shape[1] // DH
    group_size = head_count // kv_count
    group_cols = group_size * DH
    score_scale = 1.0 / math.sqrt(DH)
    ctx_count = lax.axis_size("ctx")
    my_index = lax.axis_index("ctx")
    total_rows = local_rows * ctx_count
    slot_count = total_rows // SPAN
    reach = total_rows // 4 // SPAN
    window_spans = reach + 1
    window = window_spans * SPAN
    chunks = CHUNKS if kv_count % CHUNKS == 0 else 1
    chunk_heads = kv_count // chunks
    chunk_cols = chunk_heads * DH

    slot_of_span = jnp.zeros((slot_count,), jnp.int32).at[span_order].set(
        jnp.arange(slot_count, dtype=jnp.int32))
    my_spans = lax.dynamic_slice_in_dim(span_order, my_index * tiles, tiles)
    window_span = my_spans[:, None] - reach + jnp.arange(window_spans, dtype=jnp.int32)[None, :]
    window_slot = slot_of_span[jnp.clip(window_span, 0, slot_count - 1)]
    window_owner = window_slot // tiles
    window_piece = ((my_index - window_owner) % ctx_count) * tiles + window_slot % tiles
    index_table = jnp.concatenate([window_piece.reshape(-1), window_slot.reshape(-1)])
    row_in_span = jnp.arange(SPAN, dtype=jnp.int32)
    key_pos = (window_span[:, :, None] * SPAN + row_in_span[None, None, :]).reshape(tiles, 1, window)
    query_pos = my_spans[:, None] * SPAN + row_in_span[None, :]
    query_pos = jnp.tile(query_pos[:, None, :], (1, group_size, 1)).reshape(tiles, group_size * SPAN, 1)
    query_start = jnp.tile(doc_start.reshape(tiles, 1, SPAN), (1, group_size, 1)).reshape(
        tiles, group_size * SPAN, 1)

    def shifted_pairs(shift):
        return [(i, (i + shift) % ctx_count) for i in range(ctx_count)]

    attended = None
    query_grad = None
    key_grads = []
    value_grads = []
    for chunk in range(chunks):
        cols = slice(chunk * chunk_cols, (chunk + 1) * chunk_cols)
        pair = jnp.concatenate([key_rows[:, cols], value_rows[:, cols]], axis=1)
        pieces = [pair]
        for shift in range(1, ctx_count):
            pieces.append(lax.ppermute(pair, "ctx", shifted_pairs(shift)))
        pair_all = jnp.stack(pieces).reshape(ctx_count * tiles, SPAN, 2 * chunk_cols)

        aliased = chunk > 0
        head0 = chunk * chunk_heads
        in_specs = [
            pl.BlockSpec((1, group_size * SPAN, 1), lambda j, t, idx: (t, 0, 0)),
            pl.BlockSpec((1, group_size * SPAN, 1), lambda j, t, idx: (t, 0, 0)),
            pl.BlockSpec((1, 1, window), lambda j, t, idx: (t, 0, 0)),
            pl.BlockSpec((SPAN, group_cols), lambda j, t, idx, h=head0: (t, h + j)),
            pl.BlockSpec((SPAN, group_cols), lambda j, t, idx, h=head0: (t, h + j)),
            pl.BlockSpec((ctx_count * tiles, SPAN, DH), lambda j, t, idx: (0, 0, j)),
            pl.BlockSpec((ctx_count * tiles, SPAN, DH),
                         lambda j, t, idx, n=chunk_heads: (0, 0, n + j)),
        ]
        operands = [index_table, query_pos, query_start, key_pos, queries, out_grad,
                    pair_all, pair_all]
        aliases = {}
        if aliased:
            in_specs += [pl.BlockSpec(memory_space=pl.ANY), pl.BlockSpec(memory_space=pl.ANY)]
            operands += [attended, query_grad]
            aliases = {len(operands) - 2: 0, len(operands) - 1: 1}
        kernel = pl.pallas_call(
            lambda *refs, a=aliased: attention_kernel(
                *refs, group_size=group_size, window_spans=window_spans, tiles=tiles,
                score_scale=score_scale, aliased=a),
            grid_spec=pltpu.PrefetchScalarGridSpec(
                num_scalar_prefetch=1,
                grid=(chunk_heads, tiles),
                in_specs=in_specs,
                out_specs=[
                    pl.BlockSpec((SPAN, group_cols), lambda j, t, idx, h=head0: (t, h + j)),
                    pl.BlockSpec((SPAN, group_cols), lambda j, t, idx, h=head0: (t, h + j)),
                    pl.BlockSpec((1, slot_count, SPAN, 2 * DH), lambda j, t, idx: (j, 0, 0, 0)),
                ],
            ),
            out_shape=[
                jax.ShapeDtypeStruct((local_rows, head_count * DH), jnp.bfloat16),
                jax.ShapeDtypeStruct((local_rows, head_count * DH), jnp.bfloat16),
                jax.ShapeDtypeStruct((chunk_heads, slot_count, SPAN, 2 * DH), jnp.float32),
            ],
            input_output_aliases=aliases,
        )
        attended, query_grad, buffer = kernel(*operands)

        blocks = buffer.reshape(chunk_heads, ctx_count, local_rows, 2 * DH)
        summed = lax.dynamic_index_in_dim(blocks, my_index, 1, keepdims=False)
        for shift in range(1, ctx_count):
            send = lax.dynamic_index_in_dim(blocks, (my_index + shift) % ctx_count, 1,
                                            keepdims=False)
            summed = summed + lax.ppermute(
                send.astype(jnp.bfloat16), "ctx", shifted_pairs(shift)).astype(jnp.float32)
        key_grads.append(summed[:, :, :DH])
        value_grads.append(summed[:, :, DH:])

    def heads_to_cols(parts):
        stacked = jnp.concatenate(parts, axis=0)
        return stacked.transpose(1, 0, 2).reshape(local_rows, kv_count * DH).astype(jnp.bfloat16)

    return (attended, query_grad, heads_to_cols(key_grads), heads_to_cols(value_grads))


def solution(mesh):
    in_specs = (
        P(("groups", "ctx"), "head"),
        P(("groups", "ctx"), "head"),
        P(("groups", "ctx"), "head"),
        P(("groups", "ctx"), "head"),
        P(("groups", "ctx")),
        P("groups"),
    )
    out_specs = (
        P(("groups", "ctx"), "head"),
        P(("groups", "ctx"), "head"),
        P(("groups", "ctx"), "head"),
        P(("groups", "ctx"), "head"),
    )
    return jax.shard_map(local, mesh=mesh, in_specs=in_specs, out_specs=out_specs, check_vma=False)
```

time: 248 us -> 108 us (0.44)
  waiting for transfers between devices: 165 us -> 5.59 us
  starting transfers between devices: 0.11 us -> 64.9 us
  Pallas kernels: 43.3 us -> 18.3 us
  between operations: 13.8 us -> 0.92 us
  other arithmetic: 13.2 us -> 6.35 us
    reduce_scatter x1 -> x0, waiting for transfers between devices: 86.9 us -> none  [local(): lax.psum_scatter(buffer.reshape(total_rows, 2 * kv_cols), 'ctx', scatter_...]
    all_gather x2 -> x0, waiting for transfers between devices: 76.5 us -> none  [the longest x1 38.4 us: local(): lax.all_gather(key_rows, 'ctx', axis=0, tiled=True)]
    ppermute x0 -> x28, starting transfers between devices: none -> 64.9 us  [the longest x14 34.2 us: local(): pieces.append(lax.ppermute(pair, 'ctx', shifted_pairs(shift)))]
    pallas_call x1 -> x2, Pallas kernels: 43.3 us -> 18.3 us  [local(): attended, query_grad, buffer = kernel(*operands)]
    scatter-add x1 -> x0, other arithmetic: 7.96 us -> none  [local(): buffer = buffer.at[window_slot.reshape(-1)].add(packed)]
    ppermute x0 -> x28, waiting for transfers between devices: none -> 5.59 us  [the longest x14 5.56 us: local(): lax.ppermute(send.astype(jnp.bfloat16), 'ctx', shifted_pairs(shift))]
    gather x2 -> x0, local copies, waits for them, and re-layouts: 5.38 us -> none  [the longest x1 2.7 us: local(): value_win = value_all[window_slot].reshape(tiles, window, kv_cols)]
    convert_element_type x0 -> x2, local copies, waits for them, and re-layouts: none -> 3.08 us  [local(): send.astype(jnp.bfloat16)]
  transfers between devices with their start and end apart: 3 -> 28, of which waited for: 3 -> 3; matrix products, arithmetic and copies ran while one was open for 4% -> 11% of each run, Pallas kernels for 0% -> 17%
where the time goes in v3:
time: 108 us; the launch traced here: 107 us
  starting transfers between devices  64.9 us (60%)
  Pallas kernels  18.3 us (17%)
  local copies, waits for them, and re-layouts  11.3 us (10%)
  other arithmetic  6.35 us (6%)
  waiting for transfers between devices  5.59 us (5%)
    ppermute x14, starting transfers between devices, local(): pieces.append(lax.ppermute(pair, 'ctx', shifted_pairs(shift)))  34.2 us
    ppermute x14, starting transfers between devices, local(): lax.ppermute(send.astype(jnp.bfloat16), 'ctx', shifted_pairs(shift))  30.7 us
    pallas_call x2, Pallas kernels, local(): attended, query_grad, buffer = kernel(*operands)  18.3 us
    ppermute x14, waiting for transfers between devices, local(): lax.ppermute(send.astype(jnp.bfloat16), 'ctx', shifted_pairs(shift))  5.56 us
    convert_element_type x2, local copies, waits for them, and re-layouts, local(): send.astype(jnp.bfloat16)  3.08 us
  transfers between devices with their start and end apart: 28, of which 3 were waited for; matrix products, arithmetic and copies ran while one was open for 11% of the time, Pallas kernels for 17%

profile of v3, /device:TPU:0, one launch (start us, length us, event | category | flops | bytes accessed | tf_op | source)
XLA Modules:
  0.0 107.4 jit_solution(10424445302064666702)
XLA Ops:
  2.4 3.0 %collective-permute-start.7 = (bf16[128,512]{1,0:T(8,128)(2,1)S(1)}, bf16[128,512]{1,0:T(8,128)(2,1)S(1)}, u32[]{:S(2)}, u32[]{:S(2)}) collective-permute-start(bf16[128,512]{1,0:T(8,128)(2,1)S(1)} %pad_maximum_fusion.1), channel_id=1, source_target_pairs={{0,2},{2,4},{4,6},{6,8},{8,10},{10,12},{12,14},{14,0},{1,3},{3,5},... | collective-permute-start | bytes 393224 | tf_op jit(solution)/shard_map/ppermute | solution.py:117
  5.5 1.6 %collective-permute-start.8 = (bf16[128,512]{1,0:T(8,128)(2,1)S(1)}, bf16[128,512]{1,0:T(8,128)(2,1)S(1)}, u32[]{:S(2)}, u32[]{:S(2)}) collective-permute-start(bf16[128,512]{1,0:T(8,128)(2,1)S(1)} %pad_maximum_fusion.1), channel_id=1, source_target_pairs={{0,4},{2,6},{4,8},{6,10},{8,12},{10,14},{12,0},{14,2},{1,5},{3,7},... | collective-permute-start | bytes 393224 | tf_op jit(solution)/shard_map/ppermute | solution.py:117
  7.0 2.5 %collective-permute-start.9 = (bf16[128,512]{1,0:T(8,128)(2,1)S(1)}, bf16[128,512]{1,0:T(8,128)(2,1)S(1)}, u32[]{:S(2)}, u32[]{:S(2)}) collective-permute-start(bf16[128,512]{1,0:T(8,128)(2,1)S(1)} %pad_maximum_fusion.1), channel_id=1, source_target_pairs={{0,6},{2,8},{4,10},{6,12},{8,14},{10,0},{12,2},{14,4},{1,7},{3,9},... | collective-permute-start | bytes 393224 | tf_op jit(solution)/shard_map/ppermute | solution.py:117
  10.8 2.6 %collective-permute-start.11 = (bf16[128,512]{1,0:T(8,128)(2,1)S(1)}, bf16[128,512]{1,0:T(8,128)(2,1)S(1)}, u32[]{:S(2)}, u32[]{:S(2)}) collective-permute-start(bf16[128,512]{1,0:T(8,128)(2,1)S(1)} %pad_maximum_fusion.1), channel_id=1, source_target_pairs={{0,10},{2,12},{4,14},{6,0},{8,2},{10,4},{12,6},{14,8},{1,11},{3,13... | collective-permute-start | bytes 393224 | tf_op jit(solution)/shard_map/ppermute | solution.py:117
  20.6 1.4 %collective-permute-start.12 = (bf16[128,512]{1,0:T(8,128)(2,1)S(1)}, bf16[128,512]{1,0:T(8,128)(2,1)S(1)}, u32[]{:S(2)}, u32[]{:S(2)}) collective-permute-start(bf16[128,512]{1,0:T(8,128)(2,1)S(1)} %pad_maximum_fusion.1), channel_id=1, source_target_pairs={{0,12},{2,14},{4,0},{6,2},{8,4},{10,6},{12,8},{14,10},{1,13},{3,15... | collective-permute-start | bytes 393224 | tf_op jit(solution)/shard_map/ppermute | solution.py:117
  22.0 1.5 %collective-permute-start.13 = (bf16[128,512]{1,0:T(8,128)(2,1)S(1)}, bf16[128,512]{1,0:T(8,128)(2,1)S(1)}, u32[]{:S(2)}, u32[]{:S(2)}) collective-permute-start(bf16[128,512]{1,0:T(8,128)(2,1)S(1)} %pad_maximum_fusion.1), channel_id=1, source_target_pairs={{0,14},{2,0},{4,2},{6,4},{8,6},{10,8},{12,10},{14,12},{1,15},{3,1}... | collective-permute-start | bytes 393224 | tf_op jit(solution)/shard_map/ppermute | solution.py:117
  24.2 5.2 %collective-permute-start.1 = (bf16[128,512]{1,0:T(8,128)(2,1)S(1)}, bf16[128,512]{1,0:T(8,128)(2,1)S(1)}, u32[]{:S(2)}, u32[]{:S(2)}) collective-permute-start(bf16[128,512]{1,0:T(8,128)(2,1)S(1)} %pad_maximum_fusion), channel_id=1, source_target_pairs={{0,4},{2,6},{4,8},{6,10},{8,12},{10,14},{12,0},{14,2},{1,5},{3,7},... | collective-permute-start | bytes 393224 | tf_op jit(solution)/shard_map/ppermute | solution.py:117
  29.4 4.3 %collective-permute-start.2 = (bf16[128,512]{1,0:T(8,128)(2,1)S(1)}, bf16[128,512]{1,0:T(8,128)(2,1)S(1)}, u32[]{:S(2)}, u32[]{:S(2)}) collective-permute-start(bf16[128,512]{1,0:T(8,128)(2,1)S(1)} %pad_maximum_fusion), channel_id=1, source_target_pairs={{0,6},{2,8},{4,10},{6,12},{8,14},{10,0},{12,2},{14,4},{1,7},{3,9},... | collective-permute-start | bytes 393224 | tf_op jit(solution)/shard_map/ppermute | solution.py:117
  33.8 2.8 %collective-permute-start.3 = (bf16[128,512]{1,0:T(8,128)(2,1)S(1)}, bf16[128,512]{1,0:T(8,128)(2,1)S(1)}, u32[]{:S(2)}, u32[]{:S(2)}) collective-permute-start(bf16[128,512]{1,0:T(8,128)(2,1)S(1)} %pad_maximum_fusion), channel_id=1, source_target_pairs={{0,8},{2,10},{4,12},{6,14},{8,0},{10,2},{12,4},{14,6},{1,9},{3,11}... | collective-permute-start | bytes 393224 | tf_op jit(solution)/shard_map/ppermute | solution.py:117
  36.5 3.7 %collective-permute-start.4 = (bf16[128,512]{1,0:T(8,128)(2,1)S(1)}, bf16[128,512]{1,0:T(8,128)(2,1)S(1)}, u32[]{:S(2)}, u32[]{:S(2)}) collective-permute-start(bf16[128,512]{1,0:T(8,128)(2,1)S(1)} %pad_maximum_fusion), channel_id=1, source_target_pairs={{0,10},{2,12},{4,14},{6,0},{8,2},{10,4},{12,6},{14,8},{1,11},{3,13... | collective-permute-start | bytes 393224 | tf_op jit(solution)/shard_map/ppermute | solution.py:117
  41.3 9.2 %shard_map.93 = (bf16[128,4096]{1,0:T(8,128)(2,1)}, bf16[128,4096]{1,0:T(8,128)(2,1)}, f32[2,16,64,256]{3,2,1,0:T(8,128)}) custom-call(s32[20]{0:T(128)} %pad_add_fusion.refs_0_, s32[2,512,1]{2,1,0:T(8,128)} %tile.21.refs_1_, s32[2,512,1]{2,1,0:T(8,128)} %tile.22.refs_2_, s32[2,1,320]{2,1,0:T(1,128)} %broadcast_add_fusion.refs_3_, ...), custom_call_target="tpu_custom_call" | custom-call | tf_op jit(solution)/shard_map/pallas_call | solution.py:160
  50.5 3.5 %collective-permute-start.5 = (bf16[128,512]{1,0:T(8,128)(2,1)S(1)}, bf16[128,512]{1,0:T(8,128)(2,1)S(1)}, u32[]{:S(2)}, u32[]{:S(2)}) collective-permute-start(bf16[128,512]{1,0:T(8,128)(2,1)S(1)} %pad_maximum_fusion), channel_id=1, source_target_pairs={{0,12},{2,14},{4,0},{6,2},{8,4},{10,6},{12,8},{14,10},{1,13},{3,15... | collective-permute-start | bytes 393224 | tf_op jit(solution)/shard_map/ppermute | solution.py:117
  54.1 1.6 %fusion.15 = (bf16[2,128,256]{2,1,0:T(8,128)(2,1)S(1)}, bf16[2,128,256]{2,1,0:T(8,128)(2,1)S(1)}, bf16[2,128,256]{2,1,0:T(8,128)(2,1)S(1)}, bf16[2,128,256]{2,1,...) fusion(f32[2,8,128,256]{3,2,1,0:T(8,128)} %bitcast.174, ...), kind=kLoop, calls=%fused_computation.33 | loop fusion | bytes 1835036 | tf_op jit(solution)/shard_map/convert_element_type | solution.py:168
  55.6 2.0 %collective-permute-start.14 = (bf16[2,128,256]{2,1,0:T(8,128)(2,1)S(1)}, bf16[2,128,256]{2,1,0:T(8,128)(2,1)S(1)}, u32[]{:S(2)}, u32[]{:S(2)}) collective-permute-start(bf16[2,128,256]{2,1,0:T(8,128)(2,1)S(1)} %get-tuple-element.16), channel_id=1, source_target_pairs={{0,2},{2,4},{4,6},{6,8},{8,10},{10,12},{12,14},{14,0},{1,3},{3,5},... | collective-permute-start | bytes 393224 | tf_op jit(solution)/shard_map/ppermute | solution.py:167
  58.4 1.5 %collective-permute-start.16 = (bf16[2,128,256]{2,1,0:T(8,128)(2,1)S(1)}, bf16[2,128,256]{2,1,0:T(8,128)(2,1)S(1)}, u32[]{:S(2)}, u32[]{:S(2)}) collective-permute-start(bf16[2,128,256]{2,1,0:T(8,128)(2,1)S(1)} %get-tuple-element.20), channel_id=1, source_target_pairs={{0,6},{2,8},{4,10},{6,12},{8,14},{10,0},{12,2},{14,4},{1,7},{3,9},... | collective-permute-start | bytes 393224 | tf_op jit(solution)/shard_map/ppermute | solution.py:167
  59.9 3.3 %collective-permute-start.17 = (bf16[2,128,256]{2,1,0:T(8,128)(2,1)S(1)}, bf16[2,128,256]{2,1,0:T(8,128)(2,1)S(1)}, u32[]{:S(2)}, u32[]{:S(2)}) collective-permute-start(bf16[2,128,256]{2,1,0:T(8,128)(2,1)S(1)} %get-tuple-element.19), channel_id=1, source_target_pairs={{0,8},{2,10},{4,12},{6,14},{8,0},{10,2},{12,4},{14,6},{1,9},{3,11}... | collective-permute-start | bytes 393224 | tf_op jit(solution)/shard_map/ppermute | solution.py:167
  64.9 9.2 %shard_map.94 = (bf16[128,4096]{1,0:T(8,128)(2,1)}, bf16[128,4096]{1,0:T(8,128)(2,1)}, f32[2,16,64,256]{3,2,1,0:T(8,128)}) custom-call(s32[20]{0:T(128)} %pad_add_fusion.refs_0_, s32[2,512,1]{2,1,0:T(8,128)} %tile.21.refs_1_, s32[2,512,1]{2,1,0:T(8,128)} %tile.22.refs_2_, ...), custom_call_target="tpu_custom_call", output_to_operand_aliasing={{0}: (8, {}), {1}: (9, {})} | custom-call | tf_op jit(solution)/shard_map/pallas_call | solution.py:160
  74.1 11.7 %collective-permute-start.19 = (bf16[2,128,256]{2,1,0:T(8,128)(2,1)S(1)}, bf16[2,128,256]{2,1,0:T(8,128)(2,1)S(1)}, u32[]{:S(2)}, u32[]{:S(2)}) collective-permute-start(bf16[2,128,256]{2,1,0:T(8,128)(2,1)S(1)} %get-tuple-element.17), channel_id=1, source_target_pairs={{0,12},{2,14},{4,0},{6,2},{8,4},{10,6},{12,8},{14,10},{1,13},{3,15... | collective-permute-start | bytes 393224 | tf_op jit(solution)/shard_map/ppermute | solution.py:167
  85.8 1.5 %fusion.22 = (bf16[2,128,256]{2,1,0:T(8,128)(2,1)S(1)}, bf16[2,128,256]{2,1,0:T(8,128)(2,1)S(1)}, bf16[2,128,256]{2,1,0:T(8,128)(2,1)S(1)}, bf16[2,128,256]{2,1,...) fusion(f32[2,8,128,256]{3,2,1,0:T(8,128)} %bitcast.176, ...), kind=kLoop, calls=%fused_computation.40 | loop fusion | bytes 1835036 | tf_op jit(solution)/shard_map/convert_element_type | solution.py:168
  87.4 2.1 %collective-permute-start.21 = (bf16[2,128,256]{2,1,0:T(8,128)(2,1)S(1)}, bf16[2,128,256]{2,1,0:T(8,128)(2,1)S(1)}, u32[]{:S(2)}, u32[]{:S(2)}) collective-permute-start(bf16[2,128,256]{2,1,0:T(8,128)(2,1)S(1)} %get-tuple-element.23), channel_id=1, source_target_pairs={{0,2},{2,4},{4,6},{6,8},{8,10},{10,12},{12,14},{14,0},{1,3},{3,5},... | collective-permute-start | bytes 393224 | tf_op jit(solution)/shard_map/ppermute | solution.py:167
  90.0 3.3 %collective-permute-start.24 = (bf16[2,128,256]{2,1,0:T(8,128)(2,1)S(1)}, bf16[2,128,256]{2,1,0:T(8,128)(2,1)S(1)}, u32[]{:S(2)}, u32[]{:S(2)}) collective-permute-start(bf16[2,128,256]{2,1,0:T(8,128)(2,1)S(1)} %get-tuple-element.25), channel_id=1, source_target_pairs={{0,8},{2,10},{4,12},{6,14},{8,0},{10,2},{12,4},{14,6},{1,9},{3,11}... | collective-permute-start | bytes 393224 | tf_op jit(solution)/shard_map/ppermute | solution.py:167
  95.5 2.8 %collective-permute-start.26 = (bf16[2,128,256]{2,1,0:T(8,128)(2,1)S(1)}, bf16[2,128,256]{2,1,0:T(8,128)(2,1)S(1)}, u32[]{:S(2)}, u32[]{:S(2)}) collective-permute-start(bf16[2,128,256]{2,1,0:T(8,128)(2,1)S(1)} %get-tuple-element.29), channel_id=1, source_target_pairs={{0,12},{2,14},{4,0},{6,2},{8,4},{10,6},{12,8},{14,10},{1,13},{3,15... | collective-permute-start | bytes 393224 | tf_op jit(solution)/shard_map/ppermute | solution.py:167
  99.4 2.7 %collective-permute-done.23 = bf16[2,128,256]{2,1,0:T(8,128)(2,1)S(1)} collective-permute-done((bf16[2,128,256]{2,1,0:T(8,128)(2,1)S(1)}, bf16[2,128,256]{2,1,0:T(8,128)(2,1)S(1)}, u32[]{:S(2)}, u32[]{:S(2)}) %collective-permute-start.23) | collective-permute-done | bytes 131104 | tf_op jit(solution)/shard_map/ppermute | solution.py:167
  102.9 2.0 %collective-permute-done.26 = bf16[2,128,256]{2,1,0:T(8,128)(2,1)S(1)} collective-permute-done((bf16[2,128,256]{2,1,0:T(8,128)(2,1)S(1)}, bf16[2,128,256]{2,1,0:T(8,128)(2,1)S(1)}, u32[]{:S(2)}, u32[]{:S(2)}) %collective-permute-start.26) | collective-permute-done | bytes 131104 | tf_op jit(solution)/shard_map/ppermute | solution.py:167
  (89 shorter events, 21.2 us)
Async XLA Ops:
  2.4 18.1 %collective-permute-start.7 = (bf16[128,512]{1,0:T(8,128)(2,1)S(1)}, bf16[128,512]{1,0:T(8,128)(2,1)S(1)}, u32[]{:S(2)}, u32[]{:S(2)}) collective-permute-start(bf16[128,512]{1,0:T(8,128)(2,1)S(1)} %pad_maximum_fusion.1), channel_id=1, source_target_pairs={{0,2},{2,4},{4,6},{6,8},{8,10},{10,12},{12,14},{14,0},{1,3},{3,5},... | collective-permute-start | bytes 393224 | tf_op jit(solution)/shard_map/ppermute | solution.py:117
  5.5 16.5 %collective-permute-start.8 = (bf16[128,512]{1,0:T(8,128)(2,1)S(1)}, bf16[128,512]{1,0:T(8,128)(2,1)S(1)}, u32[]{:S(2)}, u32[]{:S(2)}) collective-permute-start(bf16[128,512]{1,0:T(8,128)(2,1)S(1)} %pad_maximum_fusion.1), channel_id=1, source_target_pairs={{0,4},{2,6},{4,8},{6,10},{8,12},{10,14},{12,0},{14,2},{1,5},{3,7},... | collective-permute-start | bytes 393224 | tf_op jit(solution)/shard_map/ppermute | solution.py:117
  7.0 16.4 %collective-permute-start.9 = (bf16[128,512]{1,0:T(8,128)(2,1)S(1)}, bf16[128,512]{1,0:T(8,128)(2,1)S(1)}, u32[]{:S(2)}, u32[]{:S(2)}) collective-permute-start(bf16[128,512]{1,0:T(8,128)(2,1)S(1)} %pad_maximum_fusion.1), channel_id=1, source_target_pairs={{0,6},{2,8},{4,10},{6,12},{8,14},{10,0},{12,2},{14,4},{1,7},{3,9},... | collective-permute-start | bytes 393224 | tf_op jit(solution)/shard_map/ppermute | solution.py:117
  9.6 14.6 %collective-permute-start.10 = (bf16[128,512]{1,0:T(8,128)(2,1)S(1)}, bf16[128,512]{1,0:T(8,128)(2,1)S(1)}, u32[]{:S(2)}, u32[]{:S(2)}) collective-permute-start(bf16[128,512]{1,0:T(8,128)(2,1)S(1)} %pad_maximum_fusion.1), channel_id=1, source_target_pairs={{0,8},{2,10},{4,12},{6,14},{8,0},{10,2},{12,4},{14,6},{1,9},{3,11}... | collective-permute-start | bytes 393224 | tf_op jit(solution)/shard_map/ppermute | solution.py:117
  10.8 18.6 %collective-permute-start.11 = (bf16[128,512]{1,0:T(8,128)(2,1)S(1)}, bf16[128,512]{1,0:T(8,128)(2,1)S(1)}, u32[]{:S(2)}, u32[]{:S(2)}) collective-permute-start(bf16[128,512]{1,0:T(8,128)(2,1)S(1)} %pad_maximum_fusion.1), channel_id=1, source_target_pairs={{0,10},{2,12},{4,14},{6,0},{8,2},{10,4},{12,6},{14,8},{1,11},{3,13... | collective-permute-start | bytes 393224 | tf_op jit(solution)/shard_map/ppermute | solution.py:117
  20.6 13.2 %collective-permute-start.12 = (bf16[128,512]{1,0:T(8,128)(2,1)S(1)}, bf16[128,512]{1,0:T(8,128)(2,1)S(1)}, u32[]{:S(2)}, u32[]{:S(2)}) collective-permute-start(bf16[128,512]{1,0:T(8,128)(2,1)S(1)} %pad_maximum_fusion.1), channel_id=1, source_target_pairs={{0,12},{2,14},{4,0},{6,2},{8,4},{10,6},{12,8},{14,10},{1,13},{3,15... | collective-permute-start | bytes 393224 | tf_op jit(solution)/shard_map/ppermute | solution.py:117
  22.0 14.6 %collective-permute-start.13 = (bf16[128,512]{1,0:T(8,128)(2,1)S(1)}, bf16[128,512]{1,0:T(8,128)(2,1)S(1)}, u32[]{:S(2)}, u32[]{:S(2)}) collective-permute-start(bf16[128,512]{1,0:T(8,128)(2,1)S(1)} %pad_maximum_fusion.1), channel_id=1, source_target_pairs={{0,14},{2,0},{4,2},{6,4},{8,6},{10,8},{12,10},{14,12},{1,15},{3,1}... | collective-permute-start | bytes 393224 | tf_op jit(solution)/shard_map/ppermute | solution.py:117
  23.5 27.0 %collective-permute-start = (bf16[128,512]{1,0:T(8,128)(2,1)S(1)}, bf16[128,512]{1,0:T(8,128)(2,1)S(1)}, u32[]{:S(2)}, u32[]{:S(2)}) collective-permute-start(bf16[128,512]{1,0:T(8,128)(2,1)S(1)} %pad_maximum_fusion), channel_id=1, source_target_pairs={{0,2},{2,4},{4,6},{6,8},{8,10},{10,12},{12,14},{14,0},{1,3},{3,5},... | collective-permute-start | bytes 393224 | tf_op jit(solution)/shard_map/ppermute | solution.py:117
  24.2 29.8 %collective-permute-start.1 = (bf16[128,512]{1,0:T(8,128)(2,1)S(1)}, bf16[128,512]{1,0:T(8,128)(2,1)S(1)}, u32[]{:S(2)}, u32[]{:S(2)}) collective-permute-start(bf16[128,512]{1,0:T(8,128)(2,1)S(1)} %pad_maximum_fusion), channel_id=1, source_target_pairs={{0,4},{2,6},{4,8},{6,10},{8,12},{10,14},{12,0},{14,2},{1,5},{3,7},... | collective-permute-start | bytes 393224 | tf_op jit(solution)/shard_map/ppermute | solution.py:117
  29.4 26.2 %collective-permute-start.2 = (bf16[128,512]{1,0:T(8,128)(2,1)S(1)}, bf16[128,512]{1,0:T(8,128)(2,1)S(1)}, u32[]{:S(2)}, u32[]{:S(2)}) collective-permute-start(bf16[128,512]{1,0:T(8,128)(2,1)S(1)} %pad_maximum_fusion), channel_id=1, source_target_pairs={{0,6},{2,8},{4,10},{6,12},{8,14},{10,0},{12,2},{14,4},{1,7},{3,9},... | collective-permute-start | bytes 393224 | tf_op jit(solution)/shard_map/ppermute | solution.py:117
  33.8 23.9 %collective-permute-start.3 = (bf16[128,512]{1,0:T(8,128)(2,1)S(1)}, bf16[128,512]{1,0:T(8,128)(2,1)S(1)}, u32[]{:S(2)}, u32[]{:S(2)}) collective-permute-start(bf16[128,512]{1,0:T(8,128)(2,1)S(1)} %pad_maximum_fusion), channel_id=1, source_target_pairs={{0,8},{2,10},{4,12},{6,14},{8,0},{10,2},{12,4},{14,6},{1,9},{3,11}... | collective-permute-start | bytes 393224 | tf_op jit(solution)/shard_map/ppermute | solution.py:117
  36.5 21.8 %collective-permute-start.4 = (bf16[128,512]{1,0:T(8,128)(2,1)S(1)}, bf16[128,512]{1,0:T(8,128)(2,1)S(1)}, u32[]{:S(2)}, u32[]{:S(2)}) collective-permute-start(bf16[128,512]{1,0:T(8,128)(2,1)S(1)} %pad_maximum_fusion), channel_id=1, source_target_pairs={{0,10},{2,12},{4,14},{6,0},{8,2},{10,4},{12,6},{14,8},{1,11},{3,13... | collective-permute-start | bytes 393224 | tf_op jit(solution)/shard_map/ppermute | solution.py:117
  50.5 9.4 %collective-permute-start.5 = (bf16[128,512]{1,0:T(8,128)(2,1)S(1)}, bf16[128,512]{1,0:T(8,128)(2,1)S(1)}, u32[]{:S(2)}, u32[]{:S(2)}) collective-permute-start(bf16[128,512]{1,0:T(8,128)(2,1)S(1)} %pad_maximum_fusion), channel_id=1, source_target_pairs={{0,12},{2,14},{4,0},{6,2},{8,4},{10,6},{12,8},{14,10},{1,13},{3,15... | collective-permute-start | bytes 393224 | tf_op jit(solution)/shard_map/ppermute | solution.py:117
  54.0 9.3 %collective-permute-start.6 = (bf16[128,512]{1,0:T(8,128)(2,1)S(1)}, bf16[128,512]{1,0:T(8,128)(2,1)S(1)}, u32[]{:S(2)}, u32[]{:S(2)}) collective-permute-start(bf16[128,512]{1,0:T(8,128)(2,1)S(1)} %pad_maximum_fusion), channel_id=1, source_target_pairs={{0,14},{2,0},{4,2},{6,4},{8,6},{10,8},{12,10},{14,12},{1,15},{3,1}... | collective-permute-start | bytes 393224 | tf_op jit(solution)/shard_map/ppermute | solution.py:117
  55.6 18.4 %collective-permute-start.14 = (bf16[2,128,256]{2,1,0:T(8,128)(2,1)S(1)}, bf16[2,128,256]{2,1,0:T(8,128)(2,1)S(1)}, u32[]{:S(2)}, u32[]{:S(2)}) collective-permute-start(bf16[2,128,256]{2,1,0:T(8,128)(2,1)S(1)} %get-tuple-element.16), channel_id=1, source_target_pairs={{0,2},{2,4},{4,6},{6,8},{8,10},{10,12},{12,14},{14,0},{1,3},{3,5},... | collective-permute-start | bytes 393224 | tf_op jit(solution)/shard_map/ppermute | solution.py:167
  57.7 28.1 %collective-permute-start.15 = (bf16[2,128,256]{2,1,0:T(8,128)(2,1)S(1)}, bf16[2,128,256]{2,1,0:T(8,128)(2,1)S(1)}, u32[]{:S(2)}, u32[]{:S(2)}) collective-permute-start(bf16[2,128,256]{2,1,0:T(8,128)(2,1)S(1)} %get-tuple-element.21), channel_id=1, source_target_pairs={{0,4},{2,6},{4,8},{6,10},{8,12},{10,14},{12,0},{14,2},{1,5},{3,7},... | collective-permute-start | bytes 393224 | tf_op jit(solution)/shard_map/ppermute | solution.py:167
  58.4 29.0 %collective-permute-start.16 = (bf16[2,128,256]{2,1,0:T(8,128)(2,1)S(1)}, bf16[2,128,256]{2,1,0:T(8,128)(2,1)S(1)}, u32[]{:S(2)}, u32[]{:S(2)}) collective-permute-start(bf16[2,128,256]{2,1,0:T(8,128)(2,1)S(1)} %get-tuple-element.20), channel_id=1, source_target_pairs={{0,6},{2,8},{4,10},{6,12},{8,14},{10,0},{12,2},{14,4},{1,7},{3,9},... | collective-permute-start | bytes 393224 | tf_op jit(solution)/shard_map/ppermute | solution.py:167
  59.9 29.6 %collective-permute-start.17 = (bf16[2,128,256]{2,1,0:T(8,128)(2,1)S(1)}, bf16[2,128,256]{2,1,0:T(8,128)(2,1)S(1)}, u32[]{:S(2)}, u32[]{:S(2)}) collective-permute-start(bf16[2,128,256]{2,1,0:T(8,128)(2,1)S(1)} %get-tuple-element.19), channel_id=1, source_target_pairs={{0,8},{2,10},{4,12},{6,14},{8,0},{10,2},{12,4},{14,6},{1,9},{3,11}... | collective-permute-start | bytes 393224 | tf_op jit(solution)/shard_map/ppermute | solution.py:167
  63.3 26.2 %collective-permute-start.18 = (bf16[2,128,256]{2,1,0:T(8,128)(2,1)S(1)}, bf16[2,128,256]{2,1,0:T(8,128)(2,1)S(1)}, u32[]{:S(2)}, u32[]{:S(2)}) collective-permute-start(bf16[2,128,256]{2,1,0:T(8,128)(2,1)S(1)} %get-tuple-element.18), channel_id=1, source_target_pairs={{0,10},{2,12},{4,14},{6,0},{8,2},{10,4},{12,6},{14,8},{1,11},{3,13... | collective-permute-start | bytes 393224 | tf_op jit(solution)/shard_map/ppermute | solution.py:167
  74.1 15.9 %collective-permute-start.19 = (bf16[2,128,256]{2,1,0:T(8,128)(2,1)S(1)}, bf16[2,128,256]{2,1,0:T(8,128)(2,1)S(1)}, u32[]{:S(2)}, u32[]{:S(2)}) collective-permute-start(bf16[2,128,256]{2,1,0:T(8,128)(2,1)S(1)} %get-tuple-element.17), channel_id=1, source_target_pairs={{0,12},{2,14},{4,0},{6,2},{8,4},{10,6},{12,8},{14,10},{1,13},{3,15... | collective-permute-start | bytes 393224 | tf_op jit(solution)/shard_map/ppermute | solution.py:167
  89.5 12.6 %collective-permute-start.23 = (bf16[2,128,256]{2,1,0:T(8,128)(2,1)S(1)}, bf16[2,128,256]{2,1,0:T(8,128)(2,1)S(1)}, u32[]{:S(2)}, u32[]{:S(2)}) collective-permute-start(bf16[2,128,256]{2,1,0:T(8,128)(2,1)S(1)} %get-tuple-element.26), channel_id=1, source_target_pairs={{0,6},{2,8},{4,10},{6,12},{8,14},{10,0},{12,2},{14,4},{1,7},{3,9},... | collective-permute-start | bytes 393224 | tf_op jit(solution)/shard_map/ppermute | solution.py:167
  90.0 12.8 %collective-permute-start.24 = (bf16[2,128,256]{2,1,0:T(8,128)(2,1)S(1)}, bf16[2,128,256]{2,1,0:T(8,128)(2,1)S(1)}, u32[]{:S(2)}, u32[]{:S(2)}) collective-permute-start(bf16[2,128,256]{2,1,0:T(8,128)(2,1)S(1)} %get-tuple-element.25), channel_id=1, source_target_pairs={{0,8},{2,10},{4,12},{6,14},{8,0},{10,2},{12,4},{14,6},{1,9},{3,11}... | collective-permute-start | bytes 393224 | tf_op jit(solution)/shard_map/ppermute | solution.py:167
  93.4 9.5 %collective-permute-start.25 = (bf16[2,128,256]{2,1,0:T(8,128)(2,1)S(1)}, bf16[2,128,256]{2,1,0:T(8,128)(2,1)S(1)}, u32[]{:S(2)}, u32[]{:S(2)}) collective-permute-start(bf16[2,128,256]{2,1,0:T(8,128)(2,1)S(1)} %get-tuple-element.24), channel_id=1, source_target_pairs={{0,10},{2,12},{4,14},{6,0},{8,2},{10,4},{12,6},{14,8},{1,11},{3,13... | collective-permute-start | bytes 393224 | tf_op jit(solution)/shard_map/ppermute | solution.py:167
  95.5 9.4 %collective-permute-start.26 = (bf16[2,128,256]{2,1,0:T(8,128)(2,1)S(1)}, bf16[2,128,256]{2,1,0:T(8,128)(2,1)S(1)}, u32[]{:S(2)}, u32[]{:S(2)}) collective-permute-start(bf16[2,128,256]{2,1,0:T(8,128)(2,1)S(1)} %get-tuple-element.29), channel_id=1, source_target_pairs={{0,12},{2,14},{4,0},{6,2},{8,4},{10,6},{12,8},{14,10},{1,13},{3,15... | collective-permute-start | bytes 393224 | tf_op jit(solution)/shard_map/ppermute | solution.py:167
  (7 other events, 51.6 us)

commit v4 on v3

--- a/solution.py
+++ b/solution.py
@@ -35,9 +35,9 @@
                              preferred_element_type=jnp.float32) * score_scale
     masked = jnp.where(visible, scores, -jnp.inf)
     row_max = jnp.max(masked, axis=1, keepdims=True)
-    shifted = jnp.where(visible, jnp.exp(masked - row_max), 0.0)
+    shifted = jnp.exp(masked - row_max)
     log_totals = row_max + jnp.log(jnp.sum(shifted, axis=1, keepdims=True))
-    weights = jnp.where(visible, jnp.exp(masked - log_totals), 0.0)
+    weights = jnp.exp(masked - log_totals)
     weights_low = weights.astype(jnp.bfloat16)
     attended = jnp.dot(weights_low, value_block,
                        preferred_element_type=jnp.float32).astype(jnp.bfloat16)
@@ -92,8 +92,13 @@
     my_spans = lax.dynamic_slice_in_dim(span_order, my_index * tiles, tiles)
     window_span = my_spans[:, None] - reach + jnp.arange(window_spans, dtype=jnp.int32)[None, :]
     window_slot = slot_of_span[jnp.clip(window_span, 0, slot_count - 1)]
+    half = ctx_count // 2
+    my_half = my_index // half
+    my_q = my_index % half
     window_owner = window_slot // tiles
-    window_piece = ((my_index - window_owner) % ctx_count) * tiles + window_slot % tiles
+    owner_s = (my_q - window_owner % half) % half
+    owner_k = (window_owner // half != my_half).astype(jnp.int32)
+    window_piece = (owner_s * 2 + owner_k) * tiles + window_slot % tiles
     index_table = jnp.concatenate([window_piece.reshape(-1), window_slot.reshape(-1)])
     row_in_span = jnp.arange(SPAN, dtype=jnp.int32)
     key_pos = (window_span[:, :, None] * SPAN + row_in_span[None, None, :]).reshape(tiles, 1, window)
@@ -102,8 +107,11 @@
     query_start = jnp.tile(doc_start.reshape(tiles, 1, SPAN), (1, group_size, 1)).reshape(
         tiles, group_size * SPAN, 1)
 
-    def shifted_pairs(shift):
-        return [(i, (i + shift) % ctx_count) for i in range(ctx_count)]
+    def cross_pairs():
+        return [(i, i ^ half) for i in range(ctx_count)]
+
+    def half_pairs(shift):
+        return [(i, (i // half) * half + (i % half + shift) % half) for i in range(ctx_count)]
 
     attended = None
     query_grad = None
@@ -112,9 +120,10 @@
     for chunk in range(chunks):
         cols = slice(chunk * chunk_cols, (chunk + 1) * chunk_cols)
         pair = jnp.concatenate([key_rows[:, cols], value_rows[:, cols]], axis=1)
-        pieces = [pair]
-        for shift in range(1, ctx_count):
-            pieces.append(lax.ppermute(pair, "ctx", shifted_pairs(shift)))
+        both = jnp.stack([pair, lax.ppermute(pair, "ctx", cross_pairs())])
+        pieces = [both]
+        for shift in range(1, half):
+            pieces.append(lax.ppermute(both, "ctx", half_pairs(shift)))
         pair_all = jnp.stack(pieces).reshape(ctx_count * tiles, SPAN, 2 * chunk_cols)
 
         aliased = chunk > 0
@@ -160,12 +169,19 @@
         attended, query_grad, buffer = kernel(*operands)
 
         blocks = buffer.reshape(chunk_heads, ctx_count, local_rows, 2 * DH)
-        summed = lax.dynamic_index_in_dim(blocks, my_index, 1, keepdims=False)
-        for shift in range(1, ctx_count):
-            send = lax.dynamic_index_in_dim(blocks, (my_index + shift) % ctx_count, 1,
-                                            keepdims=False)
+        paired = jnp.stack([blocks[:, :half], blocks[:, half:]], axis=1)
+        paired = jnp.concatenate([paired, paired[:, ::-1]], axis=2)
+
+        def pack_for(q):
+            return lax.dynamic_index_in_dim(paired, my_half * half + q, 2, keepdims=False)
+
+        summed = pack_for(my_q)
+        for shift in range(1, half):
+            send = pack_for((my_q + shift) % half)
             summed = summed + lax.ppermute(
-                send.astype(jnp.bfloat16), "ctx", shifted_pairs(shift)).astype(jnp.float32)
+                send.astype(jnp.bfloat16), "ctx", half_pairs(shift)).astype(jnp.float32)
+        summed = summed[:, 0] + lax.ppermute(
+            summed[:, 1].astype(jnp.bfloat16), "ctx", cross_pairs()).astype(jnp.float32)
         key_grads.append(summed[:, :, :DH])
         value_grads.append(summed[:, :, DH:])
 

time: 108 us -> 100 us (0.926)
  starting transfers between devices: 64.9 us -> 27.1 us
  waiting for transfers between devices: 5.59 us -> 19.6 us
  other arithmetic: 6.35 us -> 16 us
  local copies, waits for them, and re-layouts: 11.3 us -> 17.9 us
    ppermute x28 -> x16, starting transfers between devices: 64.9 us -> 27.1 us  [the longest x6 7.85 us: local(): pieces.append(lax.ppermute(both, 'ctx', half_pairs(shift)))]
    ppermute x28 -> x16, waiting for transfers between devices: 5.59 us -> 19.6 us  [the longest x2 6.02 us: local(): both = jnp.stack([pair, lax.ppermute(pair, 'ctx', cross_pairs())])]
    rev x0 -> x2, local copies, waits for them, and re-layouts: none -> 6.25 us  [local(): paired = jnp.concatenate([paired, paired[:, ::-1]], axis=2)]
    another operation x2 -> x10, other arithmetic: 2.16 us -> 6.63 us  [the longest x4 3.39 us: local(): jnp.stack(pieces).reshape(ctx_count * tiles, SPAN, 2 * chunk_cols)]
    concatenate x2, other arithmetic: 0.02 us -> 3.73 us  [local(): paired = jnp.concatenate([paired, paired[:, ::-1]], axis=2)]
    convert_element_type x2, local copies, waits for them, and re-layouts: 3.08 us -> 0.19 us  [local(): send.astype(jnp.bfloat16)]
    another operation x2 -> x1, local copies, waits for them, and re-layouts: 0.02 us -> 1.74 us  [local(): paired = jnp.stack([blocks[:, :half], blocks[:, half:]], axis=1)]
    slice x0 -> x1, local copies, waits for them, and re-layouts: none -> 1.68 us  [local(): paired = jnp.stack([blocks[:, :half], blocks[:, half:]], axis=1)]
  transfers between devices with their start and end apart: 28 -> 16, of which waited for: 3 -> 6; matrix products, arithmetic and copies ran while one was open for 11% -> 30% of each run, Pallas kernels for 17% -> 18%
where the time goes in v4:
time: 100 us; the launch traced here: 99.6 us
  starting transfers between devices  27.1 us (27%)
  waiting for transfers between devices  19.6 us (20%)
  Pallas kernels  18 us (18%)
  local copies, waits for them, and re-layouts  17.9 us (18%)
  other arithmetic  16 us (16%)
    pallas_call x2, Pallas kernels, local(): attended, query_grad, buffer = kernel(*operands)  18 us
    ppermute x6, starting transfers between devices, local(): pieces.append(lax.ppermute(both, 'ctx', half_pairs(shift)))  7.85 us
    ppermute x6, starting transfers between devices, local(): lax.ppermute(send.astype(jnp.bfloat16), 'ctx', half_pairs(shift))  7.55 us
    ppermute x2, starting transfers between devices, local(): lax.ppermute(summed[:, 1].astype(jnp.bfloat16), 'ctx', cross_pairs())  7.54 us
    rev x2, local copies, waits for them, and re-layouts, local(): paired = jnp.concatenate([paired, paired[:, ::-1]], axis=2)  6.25 us
    ppermute x2, waiting for transfers between devices, local(): both = jnp.stack([pair, lax.ppermute(pair, 'ctx', cross_pairs())])  6.02 us
    ppermute x6, waiting for transfers between devices, local(): lax.ppermute(send.astype(jnp.bfloat16), 'ctx', half_pairs(shift))  5.05 us
    ppermute x2, waiting for transfers between devices, local(): lax.ppermute(summed[:, 1].astype(jnp.bfloat16), 'ctx', cross_pairs())  4.57 us
  transfers between devices with their start and end apart: 16, of which 6 were waited for; matrix products, arithmetic and copies ran while one was open for 30% of the time, Pallas kernels for 18%

profile of v4, /device:TPU:0, one launch (start us, length us, event | category | flops | bytes accessed | tf_op | source)
XLA Modules:
  0.0 99.6 jit_solution(5554352350378658441)
XLA Ops:
  1.6 4.1 %collective-permute-start.4 = (bf16[128,512]{1,0:T(8,128)(2,1)S(1)}, bf16[128,512]{1,0:T(8,128)(2,1)S(1)}, u32[]{:S(2)}, u32[]{:S(2)}) collective-permute-start(bf16[128,512]{1,0:T(8,128)(2,1)S(1)} %get-tuple-element.35), channel_id=1, source_target_pairs={{0,8},{2,10},{4,12},{6,14},{8,0},{10,2},{12,4},{14,6},{1,9},{3,11}... | collective-permute-start | bytes 393224 | tf_op jit(solution)/shard_map/ppermute | solution.py:123
  9.6 6.0 %collective-permute-done.4 = bf16[128,512]{1,0:T(8,128)(2,1)S(1)} collective-permute-done((bf16[128,512]{1,0:T(8,128)(2,1)S(1)}, bf16[128,512]{1,0:T(8,128)(2,1)S(1)}, u32[]{:S(2)}, u32[]{:S(2)}) %collective-permute-start.4) | collective-permute-done | bytes 131104 | tf_op jit(solution)/shard_map/ppermute | solution.py:123
  15.7 1.9 %collective-permute-start.5 = (bf16[2,128,512]{2,1,0:T(8,128)(2,1)S(1)}, bf16[2,128,512]{2,1,0:T(8,128)(2,1)S(1)}, u32[]{:S(2)}, u32[]{:S(2)}) collective-permute-start(bf16[2,128,512]{2,1,0:T(8,128)(2,1)S(1)} %get-tuple-element.27), channel_id=1, source_target_pairs={{0,2},{2,4},{4,6},{6,0},{8,10},{10,12},{12,14},{14,8},{1,3},{3,5},... | collective-permute-start | bytes 786440 | tf_op jit(solution)/shard_map/ppermute | solution.py:126
  23.8 2.0 %collective-permute-start.2 = (bf16[2,128,512]{2,1,0:T(8,128)(2,1)S(1)}, bf16[2,128,512]{2,1,0:T(8,128)(2,1)}, u32[]{:S(2)}, u32[]{:S(2)}) collective-permute-start(bf16[2,128,512]{2,1,0:T(8,128)(2,1)S(1)} %get-tuple-element.29), channel_id=1, source_target_pairs={{0,4},{2,6},{4,0},{6,2},{8,12},{10,14},{12,8},{14,10},{1,5},{3,7},... | collective-permute-start | bytes 786440 | tf_op jit(solution)/shard_map/ppermute | solution.py:126
  25.9 1.8 %collective-permute-start.3 = (bf16[2,128,512]{2,1,0:T(8,128)(2,1)S(1)}, bf16[2,128,512]{2,1,0:T(8,128)(2,1)}, u32[]{:S(2)}, u32[]{:S(2)}) collective-permute-start(bf16[2,128,512]{2,1,0:T(8,128)(2,1)S(1)} %get-tuple-element.29), channel_id=1, source_target_pairs={{0,6},{2,0},{4,2},{6,4},{8,14},{10,8},{12,10},{14,12},{1,7},{3,1},... | collective-permute-start | bytes 786440 | tf_op jit(solution)/shard_map/ppermute | solution.py:126
  27.8 3.9 %collective-permute-done.7 = bf16[2,128,512]{2,1,0:T(8,128)(2,1)S(1)} collective-permute-done((bf16[2,128,512]{2,1,0:T(8,128)(2,1)S(1)}, bf16[2,128,512]{2,1,0:T(8,128)(2,1)S(1)}, u32[]{:S(2)}, u32[]{:S(2)}) %collective-permute-start.7) | collective-permute-done | bytes 262176 | tf_op jit(solution)/shard_map/ppermute | solution.py:126
  32.7 9.0 %shard_map.93 = (bf16[128,4096]{1,0:T(8,128)(2,1)}, bf16[128,4096]{1,0:T(8,128)(2,1)}, f32[2,16,64,256]{3,2,1,0:T(8,128)}) custom-call(s32[20]{0:T(128)} %pad_add_fusion.refs_0_, s32[2,512,1]{2,1,0:T(8,128)} %tile.21.refs_1_, s32[2,512,1]{2,1,0:T(8,128)} %tile.22.refs_2_, s32[2,1,320]{2,1,0:T(1,128)} %broadcast_add_fusion.refs_3_, ...), custom_call_target="tpu_custom_call" | custom-call | tf_op jit(solution)/shard_map/pallas_call | solution.py:169
  41.7 1.7 %fusion.27 = (f32[2,4,128,256]{3,2,1,0:T(8,128)S(1)}, f32[2,4,128,256]{3,2,1,0:T(8,128)S(1)}) fusion(f32[2,8,128,256]{3,2,1,0:T(8,128)} %bitcast.109), kind=kLoop, calls=%fused_computation.82 | loop fusion | bytes 4194304 | tf_op jit(solution)/shard_map/slice | solution.py:172
  43.6 1.6 %pad_maximum_fusion.2 = f32[2,2,4,128,256]{4,3,0,1,2:T(8,128)} fusion(f32[2,1,4,128,256]{4,3,0,1,2:T(8,128)S(1)} %bitcast.104, f32[2,1,4,128,256]{4,3,0,1,2:T(8,128)S(1)} %bitcast.106), kind=kLoop, calls=%fused_computation.4 | loop fusion | flops 524288 | bytes 4194304 | tf_op jit(solution)/shard_map/stack | solution.py:172
  45.1 3.1 %rev.6 = f32[2,2,4,128,256]{4,3,0,1,2:T(8,128)} reverse(f32[2,2,4,128,256]{4,3,0,1,2:T(8,128)} %pad_maximum_fusion.2), dimensions={1} | reverse | bytes 4194304 | tf_op jit(solution)/shard_map/rev | solution.py:173
  48.2 1.9 %pad_maximum_fusion = f32[2,2,8,128,256]{4,3,0,1,2:T(8,128)S(1)} fusion(f32[2,2,4,128,256]{4,3,0,1,2:T(8,128)} %rev.6, f32[2,1,4,128,256]{4,3,0,1,2:T(8,128)S(1)} %bitcast.105, f32[2,1,4,128,256]{4,3,0,1,2:T(8,128)S(1)} %bitcast.107), kind=kLoop, calls=%fused_computation.2 | loop fusion | flops 2097152 | bytes 8388608 | tf_op jit(solution)/shard_map/concatenate | solution.py:173
  50.1 1.9 %copy-done = f32[2,2,8,128,256]{4,3,0,1,2:T(8,128)} copy-done((f32[2,2,8,128,256]{4,3,0,1,2:T(8,128)}, f32[2,2,8,128,256]{4,3,0,1,2:T(8,128)S(1)}, u32[]{:S(2)}) %copy-start) | copy-done | bytes 4194328
  52.1 1.9 %collective-permute-start.10 = (bf16[2,2,128,256]{3,2,0,1:T(8,128)(2,1)S(1)}, bf16[2,2,128,256]{3,2,0,1:T(8,128)(2,1)}, u32[]{:S(2)}, u32[]{:S(2)}) collective-permute-start(bf16[2,2,128,256]{3,2,0,1:T(8,128)(2,1)S(1)} %get-tuple-element.17), channel_id=1, source_target_pairs={{0,6},{2,0},{4,2},{6,4},{8,14},{10,8},{12,10},{14,12},{1,7},{3,1},... | collective-permute-start | bytes 786440 | tf_op jit(solution)/shard_map/ppermute | solution.py:181
  56.1 2.2 %pad_maximum_fusion.4 = bf16[4,2,128,512]{3,2,1,0:T(8,128)(2,1)} fusion(bf16[1,2,128,512]{3,2,1,0:T(8,128)(2,1)} %bitcast.5, bf16[1,2,128,512]{3,2,1,0:T(8,128)(2,1)} %bitcast.4, bf16[1,2,128,512]{3,2,1,0:T(8,128)(2,1)} %bitcast.3, bf16[1,2,128,512]{3,2,1,0:T(8,128)(2,1)S(1)} %get-tuple-element.28), kind=kLoop, calls=%fused_computation.8 | loop fusion | flops 1572864 | bytes 2097152 | tf_op jit(solution)/shard_map/stack | solution.py:127
  58.3 9.0 %shard_map.94 = (bf16[128,4096]{1,0:T(8,128)(2,1)}, bf16[128,4096]{1,0:T(8,128)(2,1)}, f32[2,16,64,256]{3,2,1,0:T(8,128)}) custom-call(s32[20]{0:T(128)} %pad_add_fusion.refs_0_, s32[2,512,1]{2,1,0:T(8,128)} %tile.21.refs_1_, s32[2,512,1]{2,1,0:T(8,128)} %tile.22.refs_2_, ...), custom_call_target="tpu_custom_call", output_to_operand_aliasing={{0}: (8, {}), {1}: (9, {})} | custom-call | tf_op jit(solution)/shard_map/pallas_call | solution.py:169
  67.3 1.7 %slice_bitcast_fusion.1 = (f32[2,1,4,128,256]{4,3,2,0,1:T(8,128)S(1)}, f32[2,1,4,128,256]{4,3,2,0,1:T(8,128)S(1)}) fusion(f32[2,8,128,256]{3,2,1,0:T(8,128)} %bitcast.108), kind=kLoop, calls=%fused_computation.7 | loop fusion | bytes 4194304 | tf_op jit(solution)/shard_map/stack | solution.py:172
  69.0 1.6 %pad_maximum_fusion.3 = f32[2,2,4,128,256]{4,3,2,0,1:T(8,128)} fusion(f32[2,1,4,128,256]{4,3,2,0,1:T(8,128)S(1)} %get-tuple-element.25, f32[2,1,4,128,256]{4,3,2,0,1:T(8,128)S(1)} %get-tuple-element.24), kind=kLoop, calls=%fused_computation.5 | loop fusion | flops 524288 | bytes 4194304 | tf_op jit(solution)/shard_map/stack | solution.py:172
  70.6 3.2 %rev.7 = f32[2,2,4,128,256]{4,3,2,0,1:T(8,128)} reverse(f32[2,2,4,128,256]{4,3,2,0,1:T(8,128)} %pad_maximum_fusion.3), dimensions={1} | reverse | bytes 4194304 | tf_op jit(solution)/shard_map/rev | solution.py:173
  73.8 1.9 %pad_maximum_fusion.1 = f32[2,2,8,128,256]{4,3,2,0,1:T(8,128)S(1)} fusion(f32[2,2,4,128,256]{4,3,2,0,1:T(8,128)} %rev.7, f32[2,1,4,128,256]{4,3,2,0,1:T(8,128)S(1)} %get-tuple-element.25, f32[2,1,4,128,256]{4,3,2,0,1:T(8,128)S(1)} %get-tuple-element.24), kind=kLoop, calls=%fused_computation.3 | loop fusion | flops 2097152 | bytes 8388608 | tf_op jit(solution)/shard_map/concatenate | solution.py:173
  77.3 2.0 %collective-permute-start.13 = (bf16[2,2,128,256]{3,2,0,1:T(8,128)(2,1)S(1)}, bf16[2,2,128,256]{3,2,0,1:T(8,128)(2,1)S(1)}, u32[]{:S(2)}, u32[]{:S(2)}) collective-permute-start(bf16[2,2,128,256]{3,2,0,1:T(8,128)(2,1)S(1)} %get-tuple-element.21), channel_id=1, source_target_pairs={{0,4},{2,6},{4,0},{6,2},{8,12},{10,14},{12,8},{14,10},{1,5},{3,7},... | collective-permute-start | bytes 786440 | tf_op jit(solution)/shard_map/ppermute | solution.py:181
  80.8 2.5 %collective-permute-start.11 = (bf16[2,128,256]{2,1,0:T(8,128)(2,1)S(1)}, bf16[2,128,256]{2,1,0:T(8,128)(2,1)S(1)}, u32[]{:S(2)}, u32[]{:S(2)}) collective-permute-start(bf16[2,128,256]{2,1,0:T(8,128)(2,1)S(1)} %fusion.14), channel_id=1, source_target_pairs={{0,8},{2,10},{4,12},{6,14},{8,0},{10,2},{12,4},{14,6},{1,9},{3,11}... | collective-permute-start | bytes 393224 | tf_op jit(solution)/shard_map/ppermute | solution.py:183
  83.3 3.5 %collective-permute-done.12 = bf16[2,2,128,256]{3,2,0,1:T(8,128)(2,1)S(1)} collective-permute-done((bf16[2,2,128,256]{3,2,0,1:T(8,128)(2,1)S(1)}, bf16[2,2,128,256]{3,2,0,1:T(8,128)(2,1)S(1)}, u32[]{:S(2)}, u32[]{:S(2)}) %collective-permute-start.12) | collective-permute-done | bytes 262176 | tf_op jit(solution)/shard_map/ppermute | solution.py:181
  88.5 5.1 %collective-permute-start.15 = (bf16[2,128,256]{2,1,0:T(8,128)(2,1)S(1)}, bf16[2,128,256]{2,1,0:T(8,128)(2,1)S(1)}, u32[]{:S(2)}, u32[]{:S(2)}) collective-permute-start(bf16[2,128,256]{2,1,0:T(8,128)(2,1)S(1)} %fusion.15), channel_id=1, source_target_pairs={{0,8},{2,10},{4,12},{6,14},{8,0},{10,2},{12,4},{14,6},{1,9},{3,11}... | collective-permute-start | bytes 393224 | tf_op jit(solution)/shard_map/ppermute | solution.py:183
  93.6 4.6 %collective-permute-done.15 = bf16[2,128,256]{2,1,0:T(8,128)(2,1)S(1)} collective-permute-done((bf16[2,128,256]{2,1,0:T(8,128)(2,1)S(1)}, bf16[2,128,256]{2,1,0:T(8,128)(2,1)S(1)}, u32[]{:S(2)}, u32[]{:S(2)}) %collective-permute-start.15) | collective-permute-done | bytes 131104 | tf_op jit(solution)/shard_map/ppermute | solution.py:183
  (63 shorter events, 20.8 us)
Async XLA Ops:
  1.6 14.0 %collective-permute-start.4 = (bf16[128,512]{1,0:T(8,128)(2,1)S(1)}, bf16[128,512]{1,0:T(8,128)(2,1)S(1)}, u32[]{:S(2)}, u32[]{:S(2)}) collective-permute-start(bf16[128,512]{1,0:T(8,128)(2,1)S(1)} %get-tuple-element.35), channel_id=1, source_target_pairs={{0,8},{2,10},{4,12},{6,14},{8,0},{10,2},{12,4},{14,6},{1,9},{3,11}... | collective-permute-start | bytes 393224 | tf_op jit(solution)/shard_map/ppermute | solution.py:123
  5.7 17.5 %collective-permute-start = (bf16[128,512]{1,0:T(8,128)(2,1)S(1)}, bf16[128,512]{1,0:T(8,128)(2,1)S(1)}, u32[]{:S(2)}, u32[]{:S(2)}) collective-permute-start(bf16[128,512]{1,0:T(8,128)(2,1)S(1)} %get-tuple-element.41), channel_id=1, source_target_pairs={{0,8},{2,10},{4,12},{6,14},{8,0},{10,2},{12,4},{14,6},{1,9},{3,11}... | collective-permute-start | bytes 393224 | tf_op jit(solution)/shard_map/ppermute | solution.py:123
  15.7 10.2 %collective-permute-start.5 = (bf16[2,128,512]{2,1,0:T(8,128)(2,1)S(1)}, bf16[2,128,512]{2,1,0:T(8,128)(2,1)S(1)}, u32[]{:S(2)}, u32[]{:S(2)}) collective-permute-start(bf16[2,128,512]{2,1,0:T(8,128)(2,1)S(1)} %get-tuple-element.27), channel_id=1, source_target_pairs={{0,2},{2,4},{4,6},{6,0},{8,10},{10,12},{12,14},{14,8},{1,3},{3,5},... | collective-permute-start | bytes 786440 | tf_op jit(solution)/shard_map/ppermute | solution.py:126
  17.6 10.1 %collective-permute-start.6 = (bf16[2,128,512]{2,1,0:T(8,128)(2,1)S(1)}, bf16[2,128,512]{2,1,0:T(8,128)(2,1)S(1)}, u32[]{:S(2)}, u32[]{:S(2)}) collective-permute-start(bf16[2,128,512]{2,1,0:T(8,128)(2,1)S(1)} %get-tuple-element.27), channel_id=1, source_target_pairs={{0,4},{2,6},{4,0},{6,2},{8,12},{10,14},{12,8},{14,10},{1,5},{3,7},... | collective-permute-start | bytes 786440 | tf_op jit(solution)/shard_map/ppermute | solution.py:126
  17.6 14.0 %collective-permute-start.7 = (bf16[2,128,512]{2,1,0:T(8,128)(2,1)S(1)}, bf16[2,128,512]{2,1,0:T(8,128)(2,1)S(1)}, u32[]{:S(2)}, u32[]{:S(2)}) collective-permute-start(bf16[2,128,512]{2,1,0:T(8,128)(2,1)S(1)} %get-tuple-element.27), channel_id=1, source_target_pairs={{0,6},{2,0},{4,2},{6,4},{8,14},{10,8},{12,10},{14,12},{1,7},{3,1},... | collective-permute-start | bytes 786440 | tf_op jit(solution)/shard_map/ppermute | solution.py:126
  23.2 31.4 %collective-permute-start.1 = (bf16[2,128,512]{2,1,0:T(8,128)(2,1)S(1)}, bf16[2,128,512]{2,1,0:T(8,128)(2,1)}, u32[]{:S(2)}, u32[]{:S(2)}) collective-permute-start(bf16[2,128,512]{2,1,0:T(8,128)(2,1)S(1)} %get-tuple-element.29), channel_id=1, source_target_pairs={{0,2},{2,4},{4,6},{6,0},{8,10},{10,12},{12,14},{14,8},{1,3},{3,5},... | collective-permute-start | bytes 786440 | tf_op jit(solution)/shard_map/ppermute | solution.py:126
  23.8 32.3 %collective-permute-start.2 = (bf16[2,128,512]{2,1,0:T(8,128)(2,1)S(1)}, bf16[2,128,512]{2,1,0:T(8,128)(2,1)}, u32[]{:S(2)}, u32[]{:S(2)}) collective-permute-start(bf16[2,128,512]{2,1,0:T(8,128)(2,1)S(1)} %get-tuple-element.29), channel_id=1, source_target_pairs={{0,4},{2,6},{4,0},{6,2},{8,12},{10,14},{12,8},{14,10},{1,5},{3,7},... | collective-permute-start | bytes 786440 | tf_op jit(solution)/shard_map/ppermute | solution.py:126
  25.9 30.1 %collective-permute-start.3 = (bf16[2,128,512]{2,1,0:T(8,128)(2,1)S(1)}, bf16[2,128,512]{2,1,0:T(8,128)(2,1)}, u32[]{:S(2)}, u32[]{:S(2)}) collective-permute-start(bf16[2,128,512]{2,1,0:T(8,128)(2,1)S(1)} %get-tuple-element.29), channel_id=1, source_target_pairs={{0,6},{2,0},{4,2},{6,4},{8,14},{10,8},{12,10},{14,12},{1,7},{3,1},... | collective-permute-start | bytes 786440 | tf_op jit(solution)/shard_map/ppermute | solution.py:126
  50.1 2.0 %copy-start = (f32[2,2,8,128,256]{4,3,0,1,2:T(8,128)}, f32[2,2,8,128,256]{4,3,0,1,2:T(8,128)S(1)}, u32[]{:S(2)}) copy-start(f32[2,2,8,128,256]{4,3,0,1,2:T(8,128)S(1)} %pad_maximum_fusion) | copy-start | bytes 12582916
  52.1 27.2 %collective-permute-start.10 = (bf16[2,2,128,256]{3,2,0,1:T(8,128)(2,1)S(1)}, bf16[2,2,128,256]{3,2,0,1:T(8,128)(2,1)}, u32[]{:S(2)}, u32[]{:S(2)}) collective-permute-start(bf16[2,2,128,256]{3,2,0,1:T(8,128)(2,1)S(1)} %get-tuple-element.17), channel_id=1, source_target_pairs={{0,6},{2,0},{4,2},{6,4},{8,14},{10,8},{12,10},{14,12},{1,7},{3,1},... | collective-permute-start | bytes 786440 | tf_op jit(solution)/shard_map/ppermute | solution.py:181
  54.0 25.4 %collective-permute-start.8 = (bf16[2,2,128,256]{3,2,0,1:T(8,128)(2,1)S(1)}, bf16[2,2,128,256]{3,2,0,1:T(8,128)(2,1)}, u32[]{:S(2)}, u32[]{:S(2)}) collective-permute-start(bf16[2,2,128,256]{3,2,0,1:T(8,128)(2,1)S(1)} %get-tuple-element.16), channel_id=1, source_target_pairs={{0,2},{2,4},{4,6},{6,0},{8,10},{10,12},{12,14},{14,8},{1,3},{3,5},... | collective-permute-start | bytes 786440 | tf_op jit(solution)/shard_map/ppermute | solution.py:181
  54.7 24.7 %collective-permute-start.9 = (bf16[2,2,128,256]{3,2,0,1:T(8,128)(2,1)S(1)}, bf16[2,2,128,256]{3,2,0,1:T(8,128)(2,1)}, u32[]{:S(2)}, u32[]{:S(2)}) collective-permute-start(bf16[2,2,128,256]{3,2,0,1:T(8,128)(2,1)S(1)} %get-tuple-element.18), channel_id=1, source_target_pairs={{0,4},{2,6},{4,0},{6,2},{8,12},{10,14},{12,8},{14,10},{1,5},{3,7},... | collective-permute-start | bytes 786440 | tf_op jit(solution)/shard_map/ppermute | solution.py:181
  75.8 11.0 %collective-permute-start.12 = (bf16[2,2,128,256]{3,2,0,1:T(8,128)(2,1)S(1)}, bf16[2,2,128,256]{3,2,0,1:T(8,128)(2,1)S(1)}, u32[]{:S(2)}, u32[]{:S(2)}) collective-permute-start(bf16[2,2,128,256]{3,2,0,1:T(8,128)(2,1)S(1)} %get-tuple-element.19), channel_id=1, source_target_pairs={{0,2},{2,4},{4,6},{6,0},{8,10},{10,12},{12,14},{14,8},{1,3},{3,5},... | collective-permute-start | bytes 786440 | tf_op jit(solution)/shard_map/ppermute | solution.py:181
  77.3 11.0 %collective-permute-start.13 = (bf16[2,2,128,256]{3,2,0,1:T(8,128)(2,1)S(1)}, bf16[2,2,128,256]{3,2,0,1:T(8,128)(2,1)S(1)}, u32[]{:S(2)}, u32[]{:S(2)}) collective-permute-start(bf16[2,2,128,256]{3,2,0,1:T(8,128)(2,1)S(1)} %get-tuple-element.21), channel_id=1, source_target_pairs={{0,4},{2,6},{4,0},{6,2},{8,12},{10,14},{12,8},{14,10},{1,5},{3,7},... | collective-permute-start | bytes 786440 | tf_op jit(solution)/shard_map/ppermute | solution.py:181
  79.3 9.0 %collective-permute-start.14 = (bf16[2,2,128,256]{3,2,0,1:T(8,128)(2,1)S(1)}, bf16[2,2,128,256]{3,2,0,1:T(8,128)(2,1)S(1)}, u32[]{:S(2)}, u32[]{:S(2)}) collective-permute-start(bf16[2,2,128,256]{3,2,0,1:T(8,128)(2,1)S(1)} %get-tuple-element.20), channel_id=1, source_target_pairs={{0,6},{2,0},{4,2},{6,4},{8,14},{10,8},{12,10},{14,12},{1,7},{3,1},... | collective-permute-start | bytes 786440 | tf_op jit(solution)/shard_map/ppermute | solution.py:181
  80.8 12.7 %collective-permute-start.11 = (bf16[2,128,256]{2,1,0:T(8,128)(2,1)S(1)}, bf16[2,128,256]{2,1,0:T(8,128)(2,1)S(1)}, u32[]{:S(2)}, u32[]{:S(2)}) collective-permute-start(bf16[2,128,256]{2,1,0:T(8,128)(2,1)S(1)} %fusion.14), channel_id=1, source_target_pairs={{0,8},{2,10},{4,12},{6,14},{8,0},{10,2},{12,4},{14,6},{1,9},{3,11}... | collective-permute-start | bytes 393224 | tf_op jit(solution)/shard_map/ppermute | solution.py:183
  88.5 9.7 %collective-permute-start.15 = (bf16[2,128,256]{2,1,0:T(8,128)(2,1)S(1)}, bf16[2,128,256]{2,1,0:T(8,128)(2,1)S(1)}, u32[]{:S(2)}, u32[]{:S(2)}) collective-permute-start(bf16[2,128,256]{2,1,0:T(8,128)(2,1)S(1)} %fusion.15), channel_id=1, source_target_pairs={{0,8},{2,10},{4,12},{6,14},{8,0},{10,2},{12,4},{14,6},{1,9},{3,11}... | collective-permute-start | bytes 393224 | tf_op jit(solution)/shard_map/ppermute | solution.py:183

commit v5 on v4

--- a/solution.py
+++ b/solution.py
@@ -12,7 +12,7 @@
 CHUNKS = 2
 
 
-def attention_kernel(index_ref, qpos_ref, qstart_ref, kpos_ref, q_ref, do_ref, k_ref, v_ref,
+def attention_kernel(index_ref, qstart_ref, q_ref, do_ref, k_ref, v_ref,
                      *rest, group_size, window_spans, tiles, score_scale, aliased):
     if aliased:
         rest = rest[2:]
@@ -27,13 +27,20 @@
         [q_ref[:, h * DH:(h + 1) * DH] for h in range(group_size)], axis=0)
     grad_all = jnp.concatenate(
         [do_ref[:, h * DH:(h + 1) * DH] for h in range(group_size)], axis=0)
-    kpos = kpos_ref[0]
-    visible = (kpos >= qstart_ref[0]) & (kpos <= qpos_ref[0])
+    span = index_ref[2 * tiles * window_spans + tile]
+    window = window_spans * SPAN
+    row_ids = lax.broadcasted_iota(jnp.int32, (SPAN, window), 0)
+    col_ids = lax.broadcasted_iota(jnp.int32, (SPAN, window), 1)
+    query_pos = span * SPAN + row_ids
+    key_pos = (span - (window_spans - 1)) * SPAN + col_ids
+    visible = (key_pos >= qstart_ref[0]) & (key_pos <= query_pos)
+    bias = jnp.where(visible, 0.0, -jnp.inf)
+    bias = jnp.concatenate([bias] * group_size, axis=0)
     contract_last = (((1,), (1,)), ((), ()))
     contract_first = (((0,), (0,)), ((), ()))
     scores = lax.dot_general(query_all, key_block, contract_last,
                              preferred_element_type=jnp.float32) * score_scale
-    masked = jnp.where(visible, scores, -jnp.inf)
+    masked = scores + bias
     row_max = jnp.max(masked, axis=1, keepdims=True)
     shifted = jnp.exp(masked - row_max)
     log_totals = row_max + jnp.log(jnp.sum(shifted, axis=1, keepdims=True))
@@ -87,11 +94,11 @@
     chunk_heads = kv_count // chunks
     chunk_cols = chunk_heads * DH
 
-    slot_of_span = jnp.zeros((slot_count,), jnp.int32).at[span_order].set(
-        jnp.arange(slot_count, dtype=jnp.int32))
     my_spans = lax.dynamic_slice_in_dim(span_order, my_index * tiles, tiles)
     window_span = my_spans[:, None] - reach + jnp.arange(window_spans, dtype=jnp.int32)[None, :]
-    window_slot = slot_of_span[jnp.clip(window_span, 0, slot_count - 1)]
+    window_slot = jnp.sum(
+        jnp.where(span_order[None, None, :] == window_span[:, :, None],
+                  jnp.arange(slot_count, dtype=jnp.int32)[None, None, :], 0), axis=2)
     half = ctx_count // 2
     my_half = my_index // half
     my_q = my_index % half
@@ -99,13 +106,8 @@
     owner_s = (my_q - window_owner % half) % half
     owner_k = (window_owner // half != my_half).astype(jnp.int32)
     window_piece = (owner_s * 2 + owner_k) * tiles + window_slot % tiles
-    index_table = jnp.concatenate([window_piece.reshape(-1), window_slot.reshape(-1)])
-    row_in_span = jnp.arange(SPAN, dtype=jnp.int32)
-    key_pos = (window_span[:, :, None] * SPAN + row_in_span[None, None, :]).reshape(tiles, 1, window)
-    query_pos = my_spans[:, None] * SPAN + row_in_span[None, :]
-    query_pos = jnp.tile(query_pos[:, None, :], (1, group_size, 1)).reshape(tiles, group_size * SPAN, 1)
-    query_start = jnp.tile(doc_start.reshape(tiles, 1, SPAN), (1, group_size, 1)).reshape(
-        tiles, group_size * SPAN, 1)
+    index_table = jnp.concatenate([window_piece.reshape(-1), window_slot.reshape(-1), my_spans])
+    query_start = doc_start.reshape(tiles, SPAN, 1)
 
     def cross_pairs():
         return [(i, i ^ half) for i in range(ctx_count)]
@@ -129,16 +131,14 @@
         aliased = chunk > 0
         head0 = chunk * chunk_heads
         in_specs = [
-            pl.BlockSpec((1, group_size * SPAN, 1), lambda j, t, idx: (t, 0, 0)),
-            pl.BlockSpec((1, group_size * SPAN, 1), lambda j, t, idx: (t, 0, 0)),
-            pl.BlockSpec((1, 1, window), lambda j, t, idx: (t, 0, 0)),
+            pl.BlockSpec((1, SPAN, 1), lambda j, t, idx: (t, 0, 0)),
             pl.BlockSpec((SPAN, group_cols), lambda j, t, idx, h=head0: (t, h + j)),
             pl.BlockSpec((SPAN, group_cols), lambda j, t, idx, h=head0: (t, h + j)),
             pl.BlockSpec((ctx_count * tiles, SPAN, DH), lambda j, t, idx: (0, 0, j)),
             pl.BlockSpec((ctx_count * tiles, SPAN, DH),
                          lambda j, t, idx, n=chunk_heads: (0, 0, n + j)),
         ]
-        operands = [index_table, query_pos, query_start, key_pos, queries, out_grad,
+        operands = [index_table, query_start, queries, out_grad,
                     pair_all, pair_all]
         aliases = {}
         if aliased:
@@ -169,11 +169,12 @@
         attended, query_grad, buffer = kernel(*operands)
 
         blocks = buffer.reshape(chunk_heads, ctx_count, local_rows, 2 * DH)
-        paired = jnp.stack([blocks[:, :half], blocks[:, half:]], axis=1)
-        paired = jnp.concatenate([paired, paired[:, ::-1]], axis=2)
 
         def pack_for(q):
-            return lax.dynamic_index_in_dim(paired, my_half * half + q, 2, keepdims=False)
+            target = my_half * half + q
+            own = lax.dynamic_index_in_dim(blocks, target, 1, keepdims=False)
+            other = lax.dynamic_index_in_dim(blocks, target ^ half, 1, keepdims=False)
+            return jnp.stack([own, other], axis=1)
 
         summed = pack_for(my_q)
         for shift in range(1, half):

time: 100 us -> 81.8 us (0.82)
  local copies, waits for them, and re-layouts: 17.9 us -> 7.08 us
  other arithmetic: 16 us -> 6.41 us
  waiting for transfers between devices: 19.6 us -> 27.5 us
  starting transfers between devices: 27.1 us -> 23.5 us
  Pallas kernels: 18 us -> 16.1 us
    rev x2 -> x0, local copies, waits for them, and re-layouts: 6.25 us -> none  [local(): paired = jnp.concatenate([paired, paired[:, ::-1]], axis=2)]
    concatenate x3 -> x1, other arithmetic: 4.31 us -> 0.59 us  [local(): jnp.concatenate([window_piece.reshape(-1), window_slot.reshape(-1), my_sp...]
    ppermute x6, waiting for transfers between devices: 4 us -> 7.4 us  [local(): pieces.append(lax.ppermute(both, 'ctx', half_pairs(shift)))]
    another operation x4 -> x8, other arithmetic: 3.2 us -> 0.22 us  [the longest x6 0.16 us: pack_for(): return jnp.stack([own, other], axis=1)]
    another operation x6 -> x2, local copies, waits for them, and re-layouts: 5.09 us -> 2.87 us  [the longest x3 2.07 us: local(): jnp.tile(doc_start.reshape(tiles, 1, SPAN), (1, group_size, 1))]
    ppermute x2, starting transfers between devices: 7.54 us -> 5.51 us  [local(): lax.ppermute(summed[:, 1].astype(jnp.bfloat16), 'ctx', cross_pairs())]
    ppermute x2, waiting for transfers between devices: 6.02 us -> 8.02 us  [local(): both = jnp.stack([pair, lax.ppermute(pair, 'ctx', cross_pairs())])]
    pallas_call x2, Pallas kernels: 18 us -> 16.1 us  [local(): attended, query_grad, buffer = kernel(*operands)]
  transfers between devices with their start and end apart: 16 -> 16, of which waited for: 6 -> 7; matrix products, arithmetic and copies ran while one was open for 30% -> 14% of each run, Pallas kernels for 18% -> 20%
where the time goes in v5:
time: 81.8 us; the launch traced here: 81.4 us
  waiting for transfers between devices  27.5 us (34%)
  starting transfers between devices  23.5 us (29%)
  Pallas kernels  16.1 us (20%)
  local copies, waits for them, and re-layouts  7.08 us (9%)
  other arithmetic  6.41 us (8%)
  between operations  0.89 us (1%)
    pallas_call x2, Pallas kernels, local(): attended, query_grad, buffer = kernel(*operands)  16.1 us
    ppermute x2, waiting for transfers between devices, local(): both = jnp.stack([pair, lax.ppermute(pair, 'ctx', cross_pairs())])  8.02 us
    ppermute x6, waiting for transfers between devices, local(): pieces.append(lax.ppermute(both, 'ctx', half_pairs(shift)))  7.4 us
    ppermute x6, starting transfers between devices, local(): pieces.append(lax.ppermute(both, 'ctx', half_pairs(shift)))  7.34 us
    ppermute x6, waiting for transfers between devices, local(): lax.ppermute(send.astype(jnp.bfloat16), 'ctx', half_pairs(shift))  6.85 us
    ppermute x6, starting transfers between devices, local(): lax.ppermute(send.astype(jnp.bfloat16), 'ctx', half_pairs(shift))  6.42 us
    ppermute x2, starting transfers between devices, local(): lax.ppermute(summed[:, 1].astype(jnp.bfloat16), 'ctx', cross_pairs())  5.51 us
    ppermute x2, waiting for transfers between devices, local(): lax.ppermute(summed[:, 1].astype(jnp.bfloat16), 'ctx', cross_pairs())  5.23 us
  transfers between devices with their start and end apart: 16, of which 7 were waited for; matrix products, arithmetic and copies ran while one was open for 14% of the time, Pallas kernels for 20%

profile of v5, /device:TPU:0, one launch (start us, length us, event | category | flops | bytes accessed | tf_op | source)
XLA Modules:
  0.0 81.4 jit_solution(14368737011638974775)
XLA Ops:
  1.6 4.1 %collective-permute-start.4 = (bf16[128,512]{1,0:T(8,128)(2,1)S(1)}, bf16[128,512]{1,0:T(8,128)(2,1)S(1)}, u32[]{:S(2)}, u32[]{:S(2)}) collective-permute-start(bf16[128,512]{1,0:T(8,128)(2,1)S(1)} %get-tuple-element.43), channel_id=1, source_target_pairs={{0,8},{2,10},{4,12},{6,14},{8,0},{10,2},{12,4},{14,6},{1,9},{3,11}... | collective-permute-start | bytes 393224 | tf_op jit(solution)/shard_map/ppermute | solution.py:125
  7.7 8.0 %collective-permute-done.4 = bf16[128,512]{1,0:T(8,128)(2,1)S(1)} collective-permute-done((bf16[128,512]{1,0:T(8,128)(2,1)S(1)}, bf16[128,512]{1,0:T(8,128)(2,1)S(1)}, u32[]{:S(2)}, u32[]{:S(2)}) %collective-permute-start.4) | collective-permute-done | bytes 131104 | tf_op jit(solution)/shard_map/ppermute | solution.py:125
  15.8 1.9 %collective-permute-start.5 = (bf16[2,128,512]{2,1,0:T(8,128)(2,1)S(1)}, bf16[2,128,512]{2,1,0:T(8,128)(2,1)S(1)}, u32[]{:S(2)}, u32[]{:S(2)}) collective-permute-start(bf16[2,128,512]{2,1,0:T(8,128)(2,1)S(1)} %get-tuple-element.35), channel_id=1, source_target_pairs={{0,2},{2,4},{4,6},{6,0},{8,10},{10,12},{12,14},{14,8},{1,3},{3,5},... | collective-permute-start | bytes 786440 | tf_op jit(solution)/shard_map/ppermute | solution.py:128
  17.7 1.4 %collective-permute-start.7 = (bf16[2,128,512]{2,1,0:T(8,128)(2,1)S(1)}, bf16[2,128,512]{2,1,0:T(8,128)(2,1)S(1)}, u32[]{:S(2)}, u32[]{:S(2)}) collective-permute-start(bf16[2,128,512]{2,1,0:T(8,128)(2,1)S(1)} %get-tuple-element.35), channel_id=1, source_target_pairs={{0,6},{2,0},{4,2},{6,4},{8,14},{10,8},{12,10},{14,12},{1,7},{3,1},... | collective-permute-start | bytes 786440 | tf_op jit(solution)/shard_map/ppermute | solution.py:128
  20.7 1.7 %collective-permute-start.2 = (bf16[2,128,512]{2,1,0:T(8,128)(2,1)S(1)}, bf16[2,128,512]{2,1,0:T(8,128)(2,1)S(1)}, u32[]{:S(2)}, u32[]{:S(2)}) collective-permute-start(bf16[2,128,512]{2,1,0:T(8,128)(2,1)S(1)} %get-tuple-element.37), channel_id=1, source_target_pairs={{0,4},{2,6},{4,0},{6,2},{8,12},{10,14},{12,8},{14,10},{1,5},{3,7},... | collective-permute-start | bytes 786440 | tf_op jit(solution)/shard_map/ppermute | solution.py:128
  22.4 1.0 %collective-permute-start.1 = (bf16[2,128,512]{2,1,0:T(8,128)(2,1)S(1)}, bf16[2,128,512]{2,1,0:T(8,128)(2,1)S(1)}, u32[]{:S(2)}, u32[]{:S(2)}) collective-permute-start(bf16[2,128,512]{2,1,0:T(8,128)(2,1)S(1)} %get-tuple-element.37), channel_id=1, source_target_pairs={{0,2},{2,4},{4,6},{6,0},{8,10},{10,12},{12,14},{14,8},{1,3},{3,5},... | collective-permute-start | bytes 786440 | tf_op jit(solution)/shard_map/ppermute | solution.py:128
  23.3 1.7 %collective-permute-done.6 = bf16[2,128,512]{2,1,0:T(8,128)(2,1)S(1)} collective-permute-done((bf16[2,128,512]{2,1,0:T(8,128)(2,1)S(1)}, bf16[2,128,512]{2,1,0:T(8,128)(2,1)S(1)}, u32[]{:S(2)}, u32[]{:S(2)}) %collective-permute-start.6) | collective-permute-done | bytes 262176 | tf_op jit(solution)/shard_map/ppermute | solution.py:128
  25.0 1.3 %collective-permute-start.3 = (bf16[2,128,512]{2,1,0:T(8,128)(2,1)S(1)}, bf16[2,128,512]{2,1,0:T(8,128)(2,1)S(1)}, u32[]{:S(2)}, u32[]{:S(2)}) collective-permute-start(bf16[2,128,512]{2,1,0:T(8,128)(2,1)S(1)} %get-tuple-element.37), channel_id=1, source_target_pairs={{0,6},{2,0},{4,2},{6,4},{8,14},{10,8},{12,10},{14,12},{1,7},{3,1},... | collective-permute-start | bytes 786440 | tf_op jit(solution)/shard_map/ppermute | solution.py:128
  26.3 5.7 %collective-permute-done.5 = bf16[2,128,512]{2,1,0:T(8,128)(2,1)S(1)} collective-permute-done((bf16[2,128,512]{2,1,0:T(8,128)(2,1)S(1)}, bf16[2,128,512]{2,1,0:T(8,128)(2,1)S(1)}, u32[]{:S(2)}, u32[]{:S(2)}) %collective-permute-start.5) | collective-permute-done | bytes 262176 | tf_op jit(solution)/shard_map/ppermute | solution.py:128
  32.0 1.1 %pad_maximum_fusion.1 = bf16[4,2,128,512]{3,2,1,0:T(8,128)(2,1)} fusion(bf16[1,2,128,512]{3,2,1,0:T(8,128)(2,1)S(1)} %bitcast.76, bf16[1,2,128,512]{3,2,1,0:T(8,128)(2,1)S(1)} %bitcast.74, bf16[1,2,128,512]{3,2,1,0:T(8,128)(2,1)S(1)} %bitcast.75, bf16[1,2,128,512]{3,2,1,0:T(8,128)(2,1)S(1)} %get-tuple-element.34), kind=kLoop, calls=%fused_computation.1 | loop fusion | flops 1572864 | bytes 2097152 | tf_op jit(solution)/shard_map/stack | solution.py:129
  33.2 8.0 %shard_map.93 = (bf16[128,4096]{1,0:T(8,128)(2,1)}, bf16[128,4096]{1,0:T(8,128)(2,1)}, f32[2,16,64,256]{3,2,1,0:T(8,128)}) custom-call(s32[22]{0:T(128)} %pad_add_fusion.refs_0_, s32[2,64,1]{2,1,0:T(8,128)} %reshape.60.refs_1_, bf16[128,4096]{1,0:T(8,128)(2,1)} %refs_2_.3, bf16[128,4096]{1,0:T(8,128)(2,1)} %refs_3_.3, bf16[16,64,512]{2,1,0:T(8,128)(2,1)} %bitcast.68, ...), custom_call_target="tpu_custom_call" | custom-call | tf_op jit(solution)/shard_map/pallas_call | solution.py:169
  41.2 1.4 %bitcast_convert_fusion.5 = (bf16[2,1,128,256]{3,2,0,1:T(8,128)(2,1)S(1)}, bf16[2,1,128,256]{3,2,0,1:T(8,128)(2,1)S(1)}, bf16[2,1,128,256]{3,2,0,1:T(8,128)(2,1)...) fusion(f32[2,8,128,256]{3,2,1,0:T(8,128)} %bitcast.70, ...), kind=kLoop, calls=%fused_computation.29 | loop fusion | bytes 1572888 | tf_op jit(solution)/shard_map/convert.20
  42.7 1.2 %collective-permute-start.9 = (bf16[2,2,128,256]{3,2,0,1:T(8,128)(2,1)S(1)}, bf16[2,2,128,256]{3,2,0,1:T(8,128)(2,1)S(1)}, u32[]{:S(2)}, u32[]{:S(2)}) collective-permute-start(bf16[2,2,128,256]{3,2,0,1:T(8,128)(2,1)S(1)} %pad_maximum_fusion.5), channel_id=1, source_target_pairs={{0,4},{2,6},{4,0},{6,2},{8,12},{10,14},{12,8},{14,10},{1,5},{3,7},... | collective-permute-start | bytes 786440 | tf_op jit(solution)/shard_map/ppermute | solution.py:182
  44.9 1.2 %collective-permute-start.8 = (bf16[2,2,128,256]{3,2,0,1:T(8,128)(2,1)S(1)}, bf16[2,2,128,256]{3,2,0,1:T(8,128)(2,1)S(1)}, u32[]{:S(2)}, u32[]{:S(2)}) collective-permute-start(bf16[2,2,128,256]{3,2,0,1:T(8,128)(2,1)S(1)} %pad_maximum_fusion.4), channel_id=1, source_target_pairs={{0,2},{2,4},{4,6},{6,0},{8,10},{10,12},{12,14},{14,8},{1,3},{3,5},... | collective-permute-start | bytes 786440 | tf_op jit(solution)/shard_map/ppermute | solution.py:182
  46.1 1.1 %pad_maximum_fusion = bf16[4,2,128,512]{3,2,1,0:T(8,128)(2,1)} fusion(bf16[1,2,128,512]{3,2,1,0:T(8,128)(2,1)S(1)} %bitcast.79, bf16[1,2,128,512]{3,2,1,0:T(8,128)(2,1)S(1)} %bitcast.77, bf16[1,2,128,512]{3,2,1,0:T(8,128)(2,1)S(1)} %bitcast.78, bf16[1,2,128,512]{3,2,1,0:T(8,128)(2,1)S(1)} %get-tuple-element.36), kind=kLoop, calls=%fused_computation | loop fusion | flops 1572864 | bytes 2097152 | tf_op jit(solution)/shard_map/stack | solution.py:129
  47.2 8.1 %shard_map.94 = (bf16[128,4096]{1,0:T(8,128)(2,1)}, bf16[128,4096]{1,0:T(8,128)(2,1)}, f32[2,16,64,256]{3,2,1,0:T(8,128)}) custom-call(s32[22]{0:T(128)} %pad_add_fusion.refs_0_, s32[2,64,1]{2,1,0:T(8,128)} %reshape.60.refs_1_, bf16[128,4096]{1,0:T(8,128)(2,1)} %refs_2_.3, bf16[128,4096]{1,0:T(8,128)(2,1)} %refs_3_.3, ...), custom_call_target="tpu_custom_call", output_to_operand_aliasing={{0}: (6, {}), {1}: (7, {})} | custom-call | tf_op jit(solution)/shard_map/pallas_call | solution.py:169
  55.3 1.4 %dynamic-slice_convert_fusion.5 = (bf16[2,1,128,256]{3,2,1,0:T(8,128)(2,1)S(1)}, bf16[2,1,128,256]{3,2,1,0:T(8,128)(2,1)S(1)}, bf16[2,1,128,256]{3,2,1,0:T(8,128...) fusion(f32[2,8,128,256]{3,2,1,0:T(8,128)} %bitcast.72, ...), kind=kLoop, calls=%fused_computation.35 | loop fusion | bytes 1572888 | tf_op jit(solution)/shard_map/convert.13
  57.8 1.7 %collective-permute-start.14 = (bf16[2,2,128,256]{3,2,1,0:T(8,128)(2,1)S(1)}, bf16[2,2,128,256]{3,2,1,0:T(8,128)(2,1)S(1)}, u32[]{:S(2)}, u32[]{:S(2)}) collective-permute-start(bf16[2,2,128,256]{3,2,1,0:T(8,128)(2,1)S(1)} %pad_maximum_fusion.9), channel_id=1, source_target_pairs={{0,6},{2,0},{4,2},{6,4},{8,14},{10,8},{12,10},{14,12},{1,7},{3,1},... | collective-permute-start | bytes 786440 | tf_op jit(solution)/shard_map/ppermute | solution.py:182
  59.5 1.1 %dynamic-slice_bitcast_fusion.1 = (f32[2,1,128,256]{3,2,0,1:T(8,128)S(1)}, f32[2,1,128,256]{3,2,0,1:T(8,128)S(1)}) fusion(f32[2,8,128,256]{3,2,1,0:T(8,128)} %bitcast.71, s32[]{:T(128)S(6)} %select_n.105, s32[]{:T(128)S(6)} %select_n.106), kind=kLoop, calls=%fused_computation.37 | loop fusion | bytes 1048584
  60.6 1.1 %constant_dynamic-slice_fusion.1 = (f32[2,1,128,256]{3,2,1,0:T(8,128)S(1)}, f32[2,1,128,256]{3,2,1,0:T(8,128)S(1)}) fusion(f32[2,8,128,256]{3,2,1,0:T(8,128)} %bitcast.73, s32[]{:T(128)S(6)} %select_n.105, s32[]{:T(128)S(6)} %select_n.106), kind=kLoop, calls=%fused_computation.50 | loop fusion | bytes 1048584 | tf_op jit(solution)/shard_map/jit(dynamic_index_in_dim)/dynamic_slice | solution.py:175
  62.2 3.5 %collective-permute-start.11 = (bf16[2,128,256]{2,1,0:T(8,128)(2,1)S(1)}, bf16[2,128,256]{2,1,0:T(8,128)(2,1)S(1)}, u32[]{:S(2)}, u32[]{:S(2)}) collective-permute-start(bf16[2,128,256]{2,1,0:T(8,128)(2,1)S(1)} %fusion.8), channel_id=1, source_target_pairs={{0,8},{2,10},{4,12},{6,14},{8,0},{10,2},{12,4},{14,6},{1,9},{3,11}... | collective-permute-start | bytes 393224 | tf_op jit(solution)/shard_map/ppermute | solution.py:184
  65.9 6.7 %collective-permute-done.12 = bf16[2,2,128,256]{3,2,1,0:T(8,128)(2,1)S(1)} collective-permute-done((bf16[2,2,128,256]{3,2,1,0:T(8,128)(2,1)S(1)}, bf16[2,2,128,256]{3,2,1,0:T(8,128)(2,1)S(1)}, u32[]{:S(2)}, u32[]{:S(2)}) %collective-permute-start.12) | collective-permute-done | bytes 262176 | tf_op jit(solution)/shard_map/ppermute | solution.py:182
  72.7 2.0 %collective-permute-start.15 = (bf16[2,128,256]{2,1,0:T(8,128)(2,1)S(1)}, bf16[2,128,256]{2,1,0:T(8,128)(2,1)S(1)}, u32[]{:S(2)}, u32[]{:S(2)}) collective-permute-start(bf16[2,128,256]{2,1,0:T(8,128)(2,1)S(1)} %fusion.9), channel_id=1, source_target_pairs={{0,8},{2,10},{4,12},{6,14},{8,0},{10,2},{12,4},{14,6},{1,9},{3,11}... | collective-permute-start | bytes 393224 | tf_op jit(solution)/shard_map/ppermute | solution.py:184
  74.8 5.2 %collective-permute-done.15 = bf16[2,128,256]{2,1,0:T(8,128)(2,1)S(1)} collective-permute-done((bf16[2,128,256]{2,1,0:T(8,128)(2,1)S(1)}, bf16[2,128,256]{2,1,0:T(8,128)(2,1)S(1)}, u32[]{:S(2)}, u32[]{:S(2)}) %collective-permute-start.15) | collective-permute-done | bytes 131104 | tf_op jit(solution)/shard_map/ppermute | solution.py:184
  (47 shorter events, 8.9 us)
Async XLA Ops:
  0.6 18.6 %copy-start = (s32[128]{0:T(128)S(1)}, s32[128]{0:T(128)}, u32[]{:S(2)}) copy-start(s32[128]{0:T(128)} %param.10) | copy-start | bytes 1540
  1.6 14.0 %collective-permute-start.4 = (bf16[128,512]{1,0:T(8,128)(2,1)S(1)}, bf16[128,512]{1,0:T(8,128)(2,1)S(1)}, u32[]{:S(2)}, u32[]{:S(2)}) collective-permute-start(bf16[128,512]{1,0:T(8,128)(2,1)S(1)} %get-tuple-element.43), channel_id=1, source_target_pairs={{0,8},{2,10},{4,12},{6,14},{8,0},{10,2},{12,4},{14,6},{1,9},{3,11}... | collective-permute-start | bytes 393224 | tf_op jit(solution)/shard_map/ppermute | solution.py:125
  5.8 14.9 %collective-permute-start = (bf16[128,512]{1,0:T(8,128)(2,1)S(1)}, bf16[128,512]{1,0:T(8,128)(2,1)S(1)}, u32[]{:S(2)}, u32[]{:S(2)}) collective-permute-start(bf16[128,512]{1,0:T(8,128)(2,1)S(1)} %get-tuple-element.49), channel_id=1, source_target_pairs={{0,8},{2,10},{4,12},{6,14},{8,0},{10,2},{12,4},{14,6},{1,9},{3,11}... | collective-permute-start | bytes 393224 | tf_op jit(solution)/shard_map/ppermute | solution.py:125
  15.7 9.3 %collective-permute-start.6 = (bf16[2,128,512]{2,1,0:T(8,128)(2,1)S(1)}, bf16[2,128,512]{2,1,0:T(8,128)(2,1)S(1)}, u32[]{:S(2)}, u32[]{:S(2)}) collective-permute-start(bf16[2,128,512]{2,1,0:T(8,128)(2,1)S(1)} %get-tuple-element.35), channel_id=1, source_target_pairs={{0,4},{2,6},{4,0},{6,2},{8,12},{10,14},{12,8},{14,10},{1,5},{3,7},... | collective-permute-start | bytes 786440 | tf_op jit(solution)/shard_map/ppermute | solution.py:128
  15.8 16.2 %collective-permute-start.5 = (bf16[2,128,512]{2,1,0:T(8,128)(2,1)S(1)}, bf16[2,128,512]{2,1,0:T(8,128)(2,1)S(1)}, u32[]{:S(2)}, u32[]{:S(2)}) collective-permute-start(bf16[2,128,512]{2,1,0:T(8,128)(2,1)S(1)} %get-tuple-element.35), channel_id=1, source_target_pairs={{0,2},{2,4},{4,6},{6,0},{8,10},{10,12},{12,14},{14,8},{1,3},{3,5},... | collective-permute-start | bytes 786440 | tf_op jit(solution)/shard_map/ppermute | solution.py:128
  17.7 14.3 %collective-permute-start.7 = (bf16[2,128,512]{2,1,0:T(8,128)(2,1)S(1)}, bf16[2,128,512]{2,1,0:T(8,128)(2,1)S(1)}, u32[]{:S(2)}, u32[]{:S(2)}) collective-permute-start(bf16[2,128,512]{2,1,0:T(8,128)(2,1)S(1)} %get-tuple-element.35), channel_id=1, source_target_pairs={{0,6},{2,0},{4,2},{6,4},{8,14},{10,8},{12,10},{14,12},{1,7},{3,1},... | collective-permute-start | bytes 786440 | tf_op jit(solution)/shard_map/ppermute | solution.py:128
  20.7 24.2 %collective-permute-start.2 = (bf16[2,128,512]{2,1,0:T(8,128)(2,1)S(1)}, bf16[2,128,512]{2,1,0:T(8,128)(2,1)S(1)}, u32[]{:S(2)}, u32[]{:S(2)}) collective-permute-start(bf16[2,128,512]{2,1,0:T(8,128)(2,1)S(1)} %get-tuple-element.37), channel_id=1, source_target_pairs={{0,4},{2,6},{4,0},{6,2},{8,12},{10,14},{12,8},{14,10},{1,5},{3,7},... | collective-permute-start | bytes 786440 | tf_op jit(solution)/shard_map/ppermute | solution.py:128
  22.4 23.7 %collective-permute-start.1 = (bf16[2,128,512]{2,1,0:T(8,128)(2,1)S(1)}, bf16[2,128,512]{2,1,0:T(8,128)(2,1)S(1)}, u32[]{:S(2)}, u32[]{:S(2)}) collective-permute-start(bf16[2,128,512]{2,1,0:T(8,128)(2,1)S(1)} %get-tuple-element.37), channel_id=1, source_target_pairs={{0,2},{2,4},{4,6},{6,0},{8,10},{10,12},{12,14},{14,8},{1,3},{3,5},... | collective-permute-start | bytes 786440 | tf_op jit(solution)/shard_map/ppermute | solution.py:128
  25.0 21.1 %collective-permute-start.3 = (bf16[2,128,512]{2,1,0:T(8,128)(2,1)S(1)}, bf16[2,128,512]{2,1,0:T(8,128)(2,1)S(1)}, u32[]{:S(2)}, u32[]{:S(2)}) collective-permute-start(bf16[2,128,512]{2,1,0:T(8,128)(2,1)S(1)} %get-tuple-element.37), channel_id=1, source_target_pairs={{0,6},{2,0},{4,2},{6,4},{8,14},{10,8},{12,10},{14,12},{1,7},{3,1},... | collective-permute-start | bytes 786440 | tf_op jit(solution)/shard_map/ppermute | solution.py:128
  42.7 19.0 %collective-permute-start.9 = (bf16[2,2,128,256]{3,2,0,1:T(8,128)(2,1)S(1)}, bf16[2,2,128,256]{3,2,0,1:T(8,128)(2,1)S(1)}, u32[]{:S(2)}, u32[]{:S(2)}) collective-permute-start(bf16[2,2,128,256]{3,2,0,1:T(8,128)(2,1)S(1)} %pad_maximum_fusion.5), channel_id=1, source_target_pairs={{0,4},{2,6},{4,0},{6,2},{8,12},{10,14},{12,8},{14,10},{1,5},{3,7},... | collective-permute-start | bytes 786440 | tf_op jit(solution)/shard_map/ppermute | solution.py:182
  43.9 18.2 %collective-permute-start.10 = (bf16[2,2,128,256]{3,2,0,1:T(8,128)(2,1)S(1)}, bf16[2,2,128,256]{3,2,0,1:T(8,128)(2,1)S(1)}, u32[]{:S(2)}, u32[]{:S(2)}) collective-permute-start(bf16[2,2,128,256]{3,2,0,1:T(8,128)(2,1)S(1)} %pad_maximum_fusion.6), channel_id=1, source_target_pairs={{0,6},{2,0},{4,2},{6,4},{8,14},{10,8},{12,10},{14,12},{1,7},{3,1},... | collective-permute-start | bytes 786440 | tf_op jit(solution)/shard_map/ppermute | solution.py:182
  44.9 17.2 %collective-permute-start.8 = (bf16[2,2,128,256]{3,2,0,1:T(8,128)(2,1)S(1)}, bf16[2,2,128,256]{3,2,0,1:T(8,128)(2,1)S(1)}, u32[]{:S(2)}, u32[]{:S(2)}) collective-permute-start(bf16[2,2,128,256]{3,2,0,1:T(8,128)(2,1)S(1)} %pad_maximum_fusion.4), channel_id=1, source_target_pairs={{0,2},{2,4},{4,6},{6,0},{8,10},{10,12},{12,14},{14,8},{1,3},{3,5},... | collective-permute-start | bytes 786440 | tf_op jit(solution)/shard_map/ppermute | solution.py:182
  56.8 8.9 %collective-permute-start.13 = (bf16[2,2,128,256]{3,2,1,0:T(8,128)(2,1)S(1)}, bf16[2,2,128,256]{3,2,1,0:T(8,128)(2,1)S(1)}, u32[]{:S(2)}, u32[]{:S(2)}) collective-permute-start(bf16[2,2,128,256]{3,2,1,0:T(8,128)(2,1)S(1)} %pad_maximum_fusion.8), channel_id=1, source_target_pairs={{0,4},{2,6},{4,0},{6,2},{8,12},{10,14},{12,8},{14,10},{1,5},{3,7},... | collective-permute-start | bytes 786440 | tf_op jit(solution)/shard_map/ppermute | solution.py:182
  57.8 8.1 %collective-permute-start.14 = (bf16[2,2,128,256]{3,2,1,0:T(8,128)(2,1)S(1)}, bf16[2,2,128,256]{3,2,1,0:T(8,128)(2,1)S(1)}, u32[]{:S(2)}, u32[]{:S(2)}) collective-permute-start(bf16[2,2,128,256]{3,2,1,0:T(8,128)(2,1)S(1)} %pad_maximum_fusion.9), channel_id=1, source_target_pairs={{0,6},{2,0},{4,2},{6,4},{8,14},{10,8},{12,10},{14,12},{1,7},{3,1},... | collective-permute-start | bytes 786440 | tf_op jit(solution)/shard_map/ppermute | solution.py:182
  61.7 10.9 %collective-permute-start.12 = (bf16[2,2,128,256]{3,2,1,0:T(8,128)(2,1)S(1)}, bf16[2,2,128,256]{3,2,1,0:T(8,128)(2,1)S(1)}, u32[]{:S(2)}, u32[]{:S(2)}) collective-permute-start(bf16[2,2,128,256]{3,2,1,0:T(8,128)(2,1)S(1)} %pad_maximum_fusion.7), channel_id=1, source_target_pairs={{0,2},{2,4},{4,6},{6,0},{8,10},{10,12},{12,14},{14,8},{1,3},{3,5},... | collective-permute-start | bytes 786440 | tf_op jit(solution)/shard_map/ppermute | solution.py:182
  62.2 12.5 %collective-permute-start.11 = (bf16[2,128,256]{2,1,0:T(8,128)(2,1)S(1)}, bf16[2,128,256]{2,1,0:T(8,128)(2,1)S(1)}, u32[]{:S(2)}, u32[]{:S(2)}) collective-permute-start(bf16[2,128,256]{2,1,0:T(8,128)(2,1)S(1)} %fusion.8), channel_id=1, source_target_pairs={{0,8},{2,10},{4,12},{6,14},{8,0},{10,2},{12,4},{14,6},{1,9},{3,11}... | collective-permute-start | bytes 393224 | tf_op jit(solution)/shard_map/ppermute | solution.py:184
  72.7 7.3 %collective-permute-start.15 = (bf16[2,128,256]{2,1,0:T(8,128)(2,1)S(1)}, bf16[2,128,256]{2,1,0:T(8,128)(2,1)S(1)}, u32[]{:S(2)}, u32[]{:S(2)}) collective-permute-start(bf16[2,128,256]{2,1,0:T(8,128)(2,1)S(1)} %fusion.9), channel_id=1, source_target_pairs={{0,8},{2,10},{4,12},{6,14},{8,0},{10,2},{12,4},{14,6},{1,9},{3,11}... | collective-permute-start | bytes 393224 | tf_op jit(solution)/shard_map/ppermute | solution.py:184

commit v6 on v5

--- a/solution.py
+++ b/solution.py
@@ -43,8 +43,7 @@
     masked = scores + bias
     row_max = jnp.max(masked, axis=1, keepdims=True)
     shifted = jnp.exp(masked - row_max)
-    log_totals = row_max + jnp.log(jnp.sum(shifted, axis=1, keepdims=True))
-    weights = jnp.exp(masked - log_totals)
+    weights = shifted * (1.0 / jnp.sum(shifted, axis=1, keepdims=True))
     weights_low = weights.astype(jnp.bfloat16)
     attended = jnp.dot(weights_low, value_block,
                        preferred_element_type=jnp.float32).astype(jnp.bfloat16)
@@ -119,24 +118,23 @@
     query_grad = None
     key_grads = []
     value_grads = []
+    own = jnp.concatenate([key_rows, value_rows], axis=1)
+    partner = lax.ppermute(own, "ctx", cross_pairs())
+    own_pieces = [own] + [lax.ppermute(own, "ctx", half_pairs(shift)) for shift in range(1, half)]
+    partner_pieces = [partner] + [
+        lax.ppermute(partner, "ctx", half_pairs(shift)) for shift in range(1, half)]
+    pair_all = jnp.stack([jnp.stack([a, b]) for a, b in zip(own_pieces, partner_pieces)]).reshape(
+        ctx_count * tiles, SPAN, 2 * kv_count * DH)
     for chunk in range(chunks):
-        cols = slice(chunk * chunk_cols, (chunk + 1) * chunk_cols)
-        pair = jnp.concatenate([key_rows[:, cols], value_rows[:, cols]], axis=1)
-        both = jnp.stack([pair, lax.ppermute(pair, "ctx", cross_pairs())])
-        pieces = [both]
-        for shift in range(1, half):
-            pieces.append(lax.ppermute(both, "ctx", half_pairs(shift)))
-        pair_all = jnp.stack(pieces).reshape(ctx_count * tiles, SPAN, 2 * chunk_cols)
-
         aliased = chunk > 0
         head0 = chunk * chunk_heads
         in_specs = [
             pl.BlockSpec((1, SPAN, 1), lambda j, t, idx: (t, 0, 0)),
             pl.BlockSpec((SPAN, group_cols), lambda j, t, idx, h=head0: (t, h + j)),
             pl.BlockSpec((SPAN, group_cols), lambda j, t, idx, h=head0: (t, h + j)),
-            pl.BlockSpec((ctx_count * tiles, SPAN, DH), lambda j, t, idx: (0, 0, j)),
+            pl.BlockSpec((ctx_count * tiles, SPAN, DH), lambda j, t, idx, h=head0: (0, 0, h + j)),
             pl.BlockSpec((ctx_count * tiles, SPAN, DH),
-                         lambda j, t, idx, n=chunk_heads: (0, 0, n + j)),
+                         lambda j, t, idx, h=kv_count + head0: (0, 0, h + j)),
         ]
         operands = [index_table, query_start, queries, out_grad,
                     pair_all, pair_all]

time: 81.8 us -> 86.2 us (1.054)
  local copies, waits for them, and re-layouts: 7.08 us -> 9.96 us
  starting transfers between devices: 23.5 us -> 25.9 us
  other arithmetic: 6.41 us -> 4.49 us
  waiting for transfers between devices: 27.5 us -> 28.6 us
    ppermute x6, waiting for transfers between devices: 6.85 us -> 5.01 us  [local(): lax.ppermute(send.astype(jnp.bfloat16), 'ctx', half_pairs(shift))]
    ppermute x6, starting transfers between devices: 6.42 us -> 8.21 us  [local(): lax.ppermute(send.astype(jnp.bfloat16), 'ctx', half_pairs(shift))]
    ppermute x2, waiting for transfers between devices: 5.23 us -> 6.7 us  [local(): lax.ppermute(summed[:, 1].astype(jnp.bfloat16), 'ctx', cross_pairs())]
    ppermute x8 -> x7, waiting for transfers between devices: 15.4 us -> 16.9 us  [the longest x3 11.2 us: local(): lax.ppermute(partner, 'ctx', half_pairs(shift))]
    convert_element_type x0 -> x2, local copies, waits for them, and re-layouts: none -> 1.36 us  [heads_to_cols(): stacked.transpose(1, 0, 2).reshape(local_rows, kv_count * DH)]
    convert_element_type x2 -> x0, other arithmetic: 1.34 us -> none  [heads_to_cols(): stacked.transpose(1, 0, 2).reshape(local_rows, kv_count * DH)]
    slice x1 -> x0, local copies, waits for them, and re-layouts: 0.96 us -> none  [local(): pair = jnp.concatenate([key_rows[:, cols], value_rows[:, cols]], axis=1)]
    concatenate x0 -> x1, local copies, waits for them, and re-layouts: none -> 0.92 us  [local(): own = jnp.concatenate([key_rows, value_rows], axis=1)]
  transfers between devices with their start and end apart: 16 -> 15, of which waited for: 7 -> 8; matrix products, arithmetic and copies ran while one was open for 14% -> 9% of each run, Pallas kernels for 20% -> 9%
where the time goes in v6:
time: 86.2 us; the launch traced here: 85.8 us
  waiting for transfers between devices  28.6 us (33%)
  starting transfers between devices  25.9 us (30%)
  Pallas kernels  16.1 us (19%)
  local copies, waits for them, and re-layouts  9.96 us (12%)
  other arithmetic  4.49 us (5%)
    pallas_call x2, Pallas kernels, local(): attended, query_grad, buffer = kernel(*operands)  16.1 us
    ppermute x3, waiting for transfers between devices, local(): lax.ppermute(partner, 'ctx', half_pairs(shift))  11.2 us
    ppermute x6, starting transfers between devices, local(): lax.ppermute(send.astype(jnp.bfloat16), 'ctx', half_pairs(shift))  8.21 us
    ppermute x2, waiting for transfers between devices, local(): lax.ppermute(summed[:, 1].astype(jnp.bfloat16), 'ctx', cross_pairs())  6.7 us
    ppermute x1, waiting for transfers between devices, local(): partner = lax.ppermute(own, 'ctx', cross_pairs())  5.71 us
    ppermute x2, starting transfers between devices, local(): lax.ppermute(summed[:, 1].astype(jnp.bfloat16), 'ctx', cross_pairs())  5.41 us
    ppermute x6, waiting for transfers between devices, local(): lax.ppermute(send.astype(jnp.bfloat16), 'ctx', half_pairs(shift))  5.01 us
    ppermute x3, starting transfers between devices, local(): lax.ppermute(own, 'ctx', half_pairs(shift))  4.5 us
  transfers between devices with their start and end apart: 15, of which 8 were waited for; matrix products, arithmetic and copies ran while one was open for 9% of the time, Pallas kernels for 9%

profile of v6, /device:TPU:0, one launch (start us, length us, event | category | flops | bytes accessed | tf_op | source)
XLA Modules:
  0.0 85.8 jit_solution(5900501220953490043)
XLA Ops:
  2.5 4.1 %collective-permute-start = (bf16[128,1024]{1,0:T(8,128)(2,1)S(1)}, bf16[128,1024]{1,0:T(8,128)(2,1)S(1)}, u32[]{:S(2)}, u32[]{:S(2)}) collective-permute-start(bf16[128,1024]{1,0:T(8,128)(2,1)S(1)} %constant_dynamic-update-slice_fusion), channel_id=1, source_target_pairs={{0,8},{2,10},{4,12},{6,14},{8,0},{10,2},{12,4},{14,6},{1,9},{3,11}... | collective-permute-start | bytes 786440 | tf_op jit(solution)/shard_map/ppermute | solution.py:122
  6.6 1.5 %collective-permute-start.1 = (bf16[128,1024]{1,0:T(8,128)(2,1)S(1)}, bf16[128,1024]{1,0:T(8,128)(2,1)S(1)}, u32[]{:S(2)}, u32[]{:S(2)}) collective-permute-start(bf16[128,1024]{1,0:T(8,128)(2,1)S(1)} %constant_dynamic-update-slice_fusion), channel_id=1, source_target_pairs={{0,2},{2,4},{4,6},{6,0},{8,10},{10,12},{12,14},{14,8},{1,3},{3,5},... | collective-permute-start | bytes 786440 | tf_op jit(solution)/shard_map/ppermute | solution.py:123
  8.1 1.6 %collective-permute-start.3 = (bf16[128,1024]{1,0:T(8,128)(2,1)S(1)}, bf16[128,1024]{1,0:T(8,128)(2,1)S(1)}, u32[]{:S(2)}, u32[]{:S(2)}) collective-permute-start(bf16[128,1024]{1,0:T(8,128)(2,1)S(1)} %constant_dynamic-update-slice_fusion), channel_id=1, source_target_pairs={{0,4},{2,6},{4,0},{6,2},{8,12},{10,14},{12,8},{14,10},{1,5},{3,7},... | collective-permute-start | bytes 786440 | tf_op jit(solution)/shard_map/ppermute | solution.py:123
  9.7 1.4 %collective-permute-start.5 = (bf16[128,1024]{1,0:T(8,128)(2,1)S(1)}, bf16[128,1024]{1,0:T(8,128)(2,1)S(1)}, u32[]{:S(2)}, u32[]{:S(2)}) collective-permute-start(bf16[128,1024]{1,0:T(8,128)(2,1)S(1)} %constant_dynamic-update-slice_fusion), channel_id=1, source_target_pairs={{0,6},{2,0},{4,2},{6,4},{8,14},{10,8},{12,10},{14,12},{1,7},{3,1},... | collective-permute-start | bytes 786440 | tf_op jit(solution)/shard_map/ppermute | solution.py:123
  12.9 5.7 %collective-permute-done = bf16[128,1024]{1,0:T(8,128)(2,1)S(1)} collective-permute-done((bf16[128,1024]{1,0:T(8,128)(2,1)S(1)}, bf16[128,1024]{1,0:T(8,128)(2,1)S(1)}, u32[]{:S(2)}, u32[]{:S(2)}) %collective-permute-start) | collective-permute-done | bytes 262176 | tf_op jit(solution)/shard_map/ppermute | solution.py:122
  18.6 1.6 %collective-permute-start.2 = (bf16[128,1024]{1,0:T(8,128)(2,1)S(1)}, bf16[128,1024]{1,0:T(8,128)(2,1)S(1)}, u32[]{:S(2)}, u32[]{:S(2)}) collective-permute-start(bf16[128,1024]{1,0:T(8,128)(2,1)S(1)} %collective-permute-done), channel_id=1, source_target_pairs={{0,2},{2,4},{4,6},{6,0},{8,10},{10,12},{12,14},{14,8},{1,3},{3,5},... | collective-permute-start | bytes 786440 | tf_op jit(solution)/shard_map/ppermute | solution.py:125
  21.5 1.5 %reshape.56.refs_1_ = s32[2,64,1]{2,1,0:T(8,128)} reshape(s32[128]{0:T(128)} %param.10) | data formatting | bytes 1024 | tf_op jit(solution)/shard_map/reshape | solution.py:109
  23.0 1.4 %collective-permute-start.6 = (bf16[128,1024]{1,0:T(8,128)(2,1)S(1)}, bf16[128,1024]{1,0:T(8,128)(2,1)S(1)}, u32[]{:S(2)}, u32[]{:S(2)}) collective-permute-start(bf16[128,1024]{1,0:T(8,128)(2,1)S(1)} %collective-permute-done), channel_id=1, source_target_pairs={{0,6},{2,0},{4,2},{6,4},{8,14},{10,8},{12,10},{14,12},{1,7},{3,1},... | collective-permute-start | bytes 786440 | tf_op jit(solution)/shard_map/ppermute | solution.py:125
  24.4 8.1 %collective-permute-done.2 = bf16[128,1024]{1,0:T(8,128)(2,1)S(1)} collective-permute-done((bf16[128,1024]{1,0:T(8,128)(2,1)S(1)}, bf16[128,1024]{1,0:T(8,128)(2,1)S(1)}, u32[]{:S(2)}, u32[]{:S(2)}) %collective-permute-start.2) | collective-permute-done | bytes 262176 | tf_op jit(solution)/shard_map/ppermute | solution.py:125
  33.1 2.6 %collective-permute-done.6 = bf16[128,1024]{1,0:T(8,128)(2,1)S(1)} collective-permute-done((bf16[128,1024]{1,0:T(8,128)(2,1)S(1)}, bf16[128,1024]{1,0:T(8,128)(2,1)S(1)}, u32[]{:S(2)}, u32[]{:S(2)}) %collective-permute-start.6) | collective-permute-done | bytes 262176 | tf_op jit(solution)/shard_map/ppermute | solution.py:125
  35.8 1.6 %pad_maximum_fusion = bf16[4,2,128,1024]{3,2,1,0:T(8,128)(2,1)} fusion(bf16[1,2,128,1024]{3,2,1,0:T(8,128)(2,1)S(1)} %maximum_bitcast_fusion.3, bf16[1,2,128,1024]{3,2,1,0:T(8,128)(2,1)S(1)} %maximum_bitcast_fusion.2, bf16[1,2,128,1024]{3,2,1,0:T(8,128)(2,1)S(1)} %maximum_bitcast_fusion.1, bf16[1,2,128,1024]{3,2,1,0:T(8,128)(2,1)S(1)} %maximum_bitcast_fusion), kind=kLoop, calls=%fused_computation | loop fusion | flops 3145728 | bytes 4194304 | tf_op jit(solution)/shard_map/stack | solution.py:126
  37.3 8.0 %shard_map.93 = (bf16[128,4096]{1,0:T(8,128)(2,1)}, bf16[128,4096]{1,0:T(8,128)(2,1)}, f32[2,16,64,256]{3,2,1,0:T(8,128)}) custom-call(s32[22]{0:T(128)} %pad_add_fusion.refs_0_, s32[2,64,1]{2,1,0:T(8,128)} %reshape.56.refs_1_, bf16[128,4096]{1,0:T(8,128)(2,1)} %refs_2_.3, bf16[128,4096]{1,0:T(8,128)(2,1)} %refs_3_.3, bf16[16,64,1024]{2,1,0:T(8,128)(2,1)} %bitcast.65, ...), custom_call_target="tpu_custom_call" | custom-call | tf_op jit(solution)/shard_map/pallas_call | solution.py:167
  45.4 1.4 %bitcast_convert_fusion.5 = (bf16[2,1,128,256]{3,2,0,1:T(8,128)(2,1)S(1)}, bf16[2,1,128,256]{3,2,0,1:T(8,128)(2,1)S(1)}, bf16[2,1,128,256]{3,2,0,1:T(8,128)(2,1)...) fusion(f32[2,8,128,256]{3,2,1,0:T(8,128)} %bitcast.69, ...), kind=kLoop, calls=%fused_computation.30 | loop fusion | bytes 1572888 | tf_op jit(solution)/shard_map/convert.20
  46.8 2.7 %collective-permute-start.7 = (bf16[2,2,128,256]{3,2,0,1:T(8,128)(2,1)S(1)}, bf16[2,2,128,256]{3,2,0,1:T(8,128)(2,1)S(1)}, u32[]{:S(2)}, u32[]{:S(2)}) collective-permute-start(bf16[2,2,128,256]{3,2,0,1:T(8,128)(2,1)S(1)} %pad_maximum_fusion.1), channel_id=1, source_target_pairs={{0,2},{2,4},{4,6},{6,0},{8,10},{10,12},{12,14},{14,8},{1,3},{3,5},... | collective-permute-start | bytes 786440 | tf_op jit(solution)/shard_map/ppermute | solution.py:180
  50.1 1.1 %collective-permute-start.9 = (bf16[2,2,128,256]{3,2,0,1:T(8,128)(2,1)S(1)}, bf16[2,2,128,256]{3,2,0,1:T(8,128)(2,1)S(1)}, u32[]{:S(2)}, u32[]{:S(2)}) collective-permute-start(bf16[2,2,128,256]{3,2,0,1:T(8,128)(2,1)S(1)} %pad_maximum_fusion.3), channel_id=1, source_target_pairs={{0,6},{2,0},{4,2},{6,4},{8,14},{10,8},{12,10},{14,12},{1,7},{3,1},... | collective-permute-start | bytes 786440 | tf_op jit(solution)/shard_map/ppermute | solution.py:180
  51.2 8.1 %shard_map.94 = (bf16[128,4096]{1,0:T(8,128)(2,1)}, bf16[128,4096]{1,0:T(8,128)(2,1)}, f32[2,16,64,256]{3,2,1,0:T(8,128)}) custom-call(s32[22]{0:T(128)} %pad_add_fusion.refs_0_, s32[2,64,1]{2,1,0:T(8,128)} %reshape.56.refs_1_, bf16[128,4096]{1,0:T(8,128)(2,1)} %refs_2_.3, bf16[128,4096]{1,0:T(8,128)(2,1)} %refs_3_.3, ...), custom_call_target="tpu_custom_call", output_to_operand_aliasing={{0}: (6, {}), {1}: (7, {})} | custom-call | tf_op jit(solution)/shard_map/pallas_call | solution.py:167
  59.3 1.4 %dynamic-slice_convert_fusion.5 = (bf16[2,1,128,256]{3,2,1,0:T(8,128)(2,1)S(1)}, bf16[2,1,128,256]{3,2,1,0:T(8,128)(2,1)S(1)}, bf16[2,1,128,256]{3,2,1,0:T(8,128...) fusion(f32[2,8,128,256]{3,2,1,0:T(8,128)} %bitcast.71, ...), kind=kLoop, calls=%fused_computation.36 | loop fusion | bytes 1572888 | tf_op jit(solution)/shard_map/convert.13
  61.8 1.7 %collective-permute-start.12 = (bf16[2,2,128,256]{3,2,1,0:T(8,128)(2,1)S(1)}, bf16[2,2,128,256]{3,2,1,0:T(8,128)(2,1)S(1)}, u32[]{:S(2)}, u32[]{:S(2)}) collective-permute-start(bf16[2,2,128,256]{3,2,1,0:T(8,128)(2,1)S(1)} %pad_maximum_fusion.5), channel_id=1, source_target_pairs={{0,4},{2,6},{4,0},{6,2},{8,12},{10,14},{12,8},{14,10},{1,5},{3,7},... | collective-permute-start | bytes 786440 | tf_op jit(solution)/shard_map/ppermute | solution.py:180
  65.7 1.2 %collective-permute-start.13 = (bf16[2,2,128,256]{3,2,1,0:T(8,128)(2,1)S(1)}, bf16[2,2,128,256]{3,2,1,0:T(8,128)(2,1)S(1)}, u32[]{:S(2)}, u32[]{:S(2)}) collective-permute-start(bf16[2,2,128,256]{3,2,1,0:T(8,128)(2,1)S(1)} %pad_maximum_fusion.6), channel_id=1, source_target_pairs={{0,6},{2,0},{4,2},{6,4},{8,14},{10,8},{12,10},{14,12},{1,7},{3,1},... | collective-permute-start | bytes 786440 | tf_op jit(solution)/shard_map/ppermute | solution.py:180
  67.0 2.4 %collective-permute-start.10 = (bf16[2,128,256]{2,1,0:T(8,128)(2,1)S(1)}, bf16[2,128,256]{2,1,0:T(8,128)(2,1)S(1)}, u32[]{:S(2)}, u32[]{:S(2)}) collective-permute-start(bf16[2,128,256]{2,1,0:T(8,128)(2,1)S(1)} %fusion.8), channel_id=1, source_target_pairs={{0,8},{2,10},{4,12},{6,14},{8,0},{10,2},{12,4},{14,6},{1,9},{3,11}... | collective-permute-start | bytes 393224 | tf_op jit(solution)/shard_map/ppermute | solution.py:182
  69.4 2.6 %collective-permute-done.11 = bf16[2,2,128,256]{3,2,1,0:T(8,128)(2,1)S(1)} collective-permute-done((bf16[2,2,128,256]{3,2,1,0:T(8,128)(2,1)S(1)}, bf16[2,2,128,256]{3,2,1,0:T(8,128)(2,1)S(1)}, u32[]{:S(2)}, u32[]{:S(2)}) %collective-permute-start.11) | collective-permute-done | bytes 262176 | tf_op jit(solution)/shard_map/ppermute | solution.py:180
  72.1 1.4 %collective-permute-done.12 = bf16[2,2,128,256]{3,2,1,0:T(8,128)(2,1)S(1)} collective-permute-done((bf16[2,2,128,256]{3,2,1,0:T(8,128)(2,1)S(1)}, bf16[2,2,128,256]{3,2,1,0:T(8,128)(2,1)S(1)}, u32[]{:S(2)}, u32[]{:S(2)}) %collective-permute-start.12) | collective-permute-done | bytes 262176 | tf_op jit(solution)/shard_map/ppermute | solution.py:180
  74.5 3.0 %collective-permute-start.14 = (bf16[2,128,256]{2,1,0:T(8,128)(2,1)S(1)}, bf16[2,128,256]{2,1,0:T(8,128)(2,1)S(1)}, u32[]{:S(2)}, u32[]{:S(2)}) collective-permute-start(bf16[2,128,256]{2,1,0:T(8,128)(2,1)S(1)} %fusion.9), channel_id=1, source_target_pairs={{0,8},{2,10},{4,12},{6,14},{8,0},{10,2},{12,4},{14,6},{1,9},{3,11}... | collective-permute-start | bytes 393224 | tf_op jit(solution)/shard_map/ppermute | solution.py:182
  77.6 6.7 %collective-permute-done.14 = bf16[2,128,256]{2,1,0:T(8,128)(2,1)S(1)} collective-permute-done((bf16[2,128,256]{2,1,0:T(8,128)(2,1)S(1)}, bf16[2,128,256]{2,1,0:T(8,128)(2,1)S(1)}, u32[]{:S(2)}, u32[]{:S(2)}) %collective-permute-start.14) | collective-permute-done | bytes 131104 | tf_op jit(solution)/shard_map/ppermute | solution.py:182
  (44 shorter events, 12.1 us)
Async XLA Ops:
  2.5 16.1 %collective-permute-start = (bf16[128,1024]{1,0:T(8,128)(2,1)S(1)}, bf16[128,1024]{1,0:T(8,128)(2,1)S(1)}, u32[]{:S(2)}, u32[]{:S(2)}) collective-permute-start(bf16[128,1024]{1,0:T(8,128)(2,1)S(1)} %constant_dynamic-update-slice_fusion), channel_id=1, source_target_pairs={{0,8},{2,10},{4,12},{6,14},{8,0},{10,2},{12,4},{14,6},{1,9},{3,11}... | collective-permute-start | bytes 786440 | tf_op jit(solution)/shard_map/ppermute | solution.py:122
  6.6 16.4 %collective-permute-start.1 = (bf16[128,1024]{1,0:T(8,128)(2,1)S(1)}, bf16[128,1024]{1,0:T(8,128)(2,1)S(1)}, u32[]{:S(2)}, u32[]{:S(2)}) collective-permute-start(bf16[128,1024]{1,0:T(8,128)(2,1)S(1)} %constant_dynamic-update-slice_fusion), channel_id=1, source_target_pairs={{0,2},{2,4},{4,6},{6,0},{8,10},{10,12},{12,14},{14,8},{1,3},{3,5},... | collective-permute-start | bytes 786440 | tf_op jit(solution)/shard_map/ppermute | solution.py:123
  8.1 24.5 %collective-permute-start.3 = (bf16[128,1024]{1,0:T(8,128)(2,1)S(1)}, bf16[128,1024]{1,0:T(8,128)(2,1)S(1)}, u32[]{:S(2)}, u32[]{:S(2)}) collective-permute-start(bf16[128,1024]{1,0:T(8,128)(2,1)S(1)} %constant_dynamic-update-slice_fusion), channel_id=1, source_target_pairs={{0,4},{2,6},{4,0},{6,2},{8,12},{10,14},{12,8},{14,10},{1,5},{3,7},... | collective-permute-start | bytes 786440 | tf_op jit(solution)/shard_map/ppermute | solution.py:123
  9.7 23.5 %collective-permute-start.5 = (bf16[128,1024]{1,0:T(8,128)(2,1)S(1)}, bf16[128,1024]{1,0:T(8,128)(2,1)S(1)}, u32[]{:S(2)}, u32[]{:S(2)}) collective-permute-start(bf16[128,1024]{1,0:T(8,128)(2,1)S(1)} %constant_dynamic-update-slice_fusion), channel_id=1, source_target_pairs={{0,6},{2,0},{4,2},{6,4},{8,14},{10,8},{12,10},{14,12},{1,7},{3,1},... | collective-permute-start | bytes 786440 | tf_op jit(solution)/shard_map/ppermute | solution.py:123
  18.6 13.9 %collective-permute-start.2 = (bf16[128,1024]{1,0:T(8,128)(2,1)S(1)}, bf16[128,1024]{1,0:T(8,128)(2,1)S(1)}, u32[]{:S(2)}, u32[]{:S(2)}) collective-permute-start(bf16[128,1024]{1,0:T(8,128)(2,1)S(1)} %collective-permute-done), channel_id=1, source_target_pairs={{0,2},{2,4},{4,6},{6,0},{8,10},{10,12},{12,14},{14,8},{1,3},{3,5},... | collective-permute-start | bytes 786440 | tf_op jit(solution)/shard_map/ppermute | solution.py:125
  20.2 12.9 %collective-permute-start.4 = (bf16[128,1024]{1,0:T(8,128)(2,1)S(1)}, bf16[128,1024]{1,0:T(8,128)(2,1)S(1)}, u32[]{:S(2)}, u32[]{:S(2)}) collective-permute-start(bf16[128,1024]{1,0:T(8,128)(2,1)S(1)} %collective-permute-done), channel_id=1, source_target_pairs={{0,4},{2,6},{4,0},{6,2},{8,12},{10,14},{12,8},{14,10},{1,5},{3,7},... | collective-permute-start | bytes 786440 | tf_op jit(solution)/shard_map/ppermute | solution.py:125
  23.0 12.7 %collective-permute-start.6 = (bf16[128,1024]{1,0:T(8,128)(2,1)S(1)}, bf16[128,1024]{1,0:T(8,128)(2,1)S(1)}, u32[]{:S(2)}, u32[]{:S(2)}) collective-permute-start(bf16[128,1024]{1,0:T(8,128)(2,1)S(1)} %collective-permute-done), channel_id=1, source_target_pairs={{0,6},{2,0},{4,2},{6,4},{8,14},{10,8},{12,10},{14,12},{1,7},{3,1},... | collective-permute-start | bytes 786440 | tf_op jit(solution)/shard_map/ppermute | solution.py:125
  46.8 18.9 %collective-permute-start.7 = (bf16[2,2,128,256]{3,2,0,1:T(8,128)(2,1)S(1)}, bf16[2,2,128,256]{3,2,0,1:T(8,128)(2,1)S(1)}, u32[]{:S(2)}, u32[]{:S(2)}) collective-permute-start(bf16[2,2,128,256]{3,2,0,1:T(8,128)(2,1)S(1)} %pad_maximum_fusion.1), channel_id=1, source_target_pairs={{0,2},{2,4},{4,6},{6,0},{8,10},{10,12},{12,14},{14,8},{1,3},{3,5},... | collective-permute-start | bytes 786440 | tf_op jit(solution)/shard_map/ppermute | solution.py:180
  49.6 17.3 %collective-permute-start.8 = (bf16[2,2,128,256]{3,2,0,1:T(8,128)(2,1)S(1)}, bf16[2,2,128,256]{3,2,0,1:T(8,128)(2,1)S(1)}, u32[]{:S(2)}, u32[]{:S(2)}) collective-permute-start(bf16[2,2,128,256]{3,2,0,1:T(8,128)(2,1)S(1)} %pad_maximum_fusion.2), channel_id=1, source_target_pairs={{0,4},{2,6},{4,0},{6,2},{8,12},{10,14},{12,8},{14,10},{1,5},{3,7},... | collective-permute-start | bytes 786440 | tf_op jit(solution)/shard_map/ppermute | solution.py:180
  50.1 16.8 %collective-permute-start.9 = (bf16[2,2,128,256]{3,2,0,1:T(8,128)(2,1)S(1)}, bf16[2,2,128,256]{3,2,0,1:T(8,128)(2,1)S(1)}, u32[]{:S(2)}, u32[]{:S(2)}) collective-permute-start(bf16[2,2,128,256]{3,2,0,1:T(8,128)(2,1)S(1)} %pad_maximum_fusion.3), channel_id=1, source_target_pairs={{0,6},{2,0},{4,2},{6,4},{8,14},{10,8},{12,10},{14,12},{1,7},{3,1},... | collective-permute-start | bytes 786440 | tf_op jit(solution)/shard_map/ppermute | solution.py:180
  60.8 11.3 %collective-permute-start.11 = (bf16[2,2,128,256]{3,2,1,0:T(8,128)(2,1)S(1)}, bf16[2,2,128,256]{3,2,1,0:T(8,128)(2,1)S(1)}, u32[]{:S(2)}, u32[]{:S(2)}) collective-permute-start(bf16[2,2,128,256]{3,2,1,0:T(8,128)(2,1)S(1)} %pad_maximum_fusion.4), channel_id=1, source_target_pairs={{0,2},{2,4},{4,6},{6,0},{8,10},{10,12},{12,14},{14,8},{1,3},{3,5},... | collective-permute-start | bytes 786440 | tf_op jit(solution)/shard_map/ppermute | solution.py:180
  61.8 11.7 %collective-permute-start.12 = (bf16[2,2,128,256]{3,2,1,0:T(8,128)(2,1)S(1)}, bf16[2,2,128,256]{3,2,1,0:T(8,128)(2,1)S(1)}, u32[]{:S(2)}, u32[]{:S(2)}) collective-permute-start(bf16[2,2,128,256]{3,2,1,0:T(8,128)(2,1)S(1)} %pad_maximum_fusion.5), channel_id=1, source_target_pairs={{0,4},{2,6},{4,0},{6,2},{8,12},{10,14},{12,8},{14,10},{1,5},{3,7},... | collective-permute-start | bytes 786440 | tf_op jit(solution)/shard_map/ppermute | solution.py:180
  65.7 8.7 %collective-permute-start.13 = (bf16[2,2,128,256]{3,2,1,0:T(8,128)(2,1)S(1)}, bf16[2,2,128,256]{3,2,1,0:T(8,128)(2,1)S(1)}, u32[]{:S(2)}, u32[]{:S(2)}) collective-permute-start(bf16[2,2,128,256]{3,2,1,0:T(8,128)(2,1)S(1)} %pad_maximum_fusion.6), channel_id=1, source_target_pairs={{0,6},{2,0},{4,2},{6,4},{8,14},{10,8},{12,10},{14,12},{1,7},{3,1},... | collective-permute-start | bytes 786440 | tf_op jit(solution)/shard_map/ppermute | solution.py:180
  67.0 10.6 %collective-permute-start.10 = (bf16[2,128,256]{2,1,0:T(8,128)(2,1)S(1)}, bf16[2,128,256]{2,1,0:T(8,128)(2,1)S(1)}, u32[]{:S(2)}, u32[]{:S(2)}) collective-permute-start(bf16[2,128,256]{2,1,0:T(8,128)(2,1)S(1)} %fusion.8), channel_id=1, source_target_pairs={{0,8},{2,10},{4,12},{6,14},{8,0},{10,2},{12,4},{14,6},{1,9},{3,11}... | collective-permute-start | bytes 393224 | tf_op jit(solution)/shard_map/ppermute | solution.py:182
  74.5 9.8 %collective-permute-start.14 = (bf16[2,128,256]{2,1,0:T(8,128)(2,1)S(1)}, bf16[2,128,256]{2,1,0:T(8,128)(2,1)S(1)}, u32[]{:S(2)}, u32[]{:S(2)}) collective-permute-start(bf16[2,128,256]{2,1,0:T(8,128)(2,1)S(1)} %fusion.9), channel_id=1, source_target_pairs={{0,8},{2,10},{4,12},{6,14},{8,0},{10,2},{12,4},{14,6},{1,9},{3,11}... | collective-permute-start | bytes 393224 | tf_op jit(solution)/shard_map/ppermute | solution.py:182

commit v7 on v5

--- a/solution.py
+++ b/solution.py
@@ -13,10 +13,12 @@
 
 
 def attention_kernel(index_ref, qstart_ref, q_ref, do_ref, k_ref, v_ref,
-                     *rest, group_size, window_spans, tiles, score_scale, aliased):
+                     *rest, group_size, window_spans, tiles, half, score_scale, aliased):
     if aliased:
         rest = rest[2:]
-    out_ref, dq_ref, buf_ref = rest
+    out_ref, dq_ref, own_ref = rest[:3]
+    send_refs = rest[3:-1]
+    buf_ref = rest[-1]
     tile = pl.program_id(1)
     base = tile * window_spans
     key_block = jnp.concatenate(
@@ -71,8 +73,20 @@
     for w in range(window_spans):
         slot = index_ref[slot_base + w]
         rows = slice(w * SPAN, (w + 1) * SPAN)
-        buf_ref[0, slot, :, :DH] += key_sum[rows]
-        buf_ref[0, slot, :, DH:] += value_sum[rows]
+        buf_ref[slot, :, :DH] += key_sum[rows]
+        buf_ref[slot, :, DH:] += value_sum[rows]
+
+    @pl.when(tile == tiles - 1)
+    def _():
+        info = 2 * tiles * window_spans + tiles
+        my_half = index_ref[info]
+        my_q = index_ref[info + 1]
+        for shift, ref in enumerate((own_ref,) + tuple(send_refs)):
+            target = my_half * half + (my_q + shift) % half
+            other = (target + half) % (2 * half)
+            for k, device in enumerate((target, other)):
+                block = buf_ref[pl.ds(device * tiles, tiles)]
+                ref[0, k] = block.astype(ref.dtype)
 
 
 def local(queries, key_rows, value_rows, out_grad, doc_start, span_order):
@@ -106,7 +120,8 @@
     owner_s = (my_q - window_owner % half) % half
     owner_k = (window_owner // half != my_half).astype(jnp.int32)
     window_piece = (owner_s * 2 + owner_k) * tiles + window_slot % tiles
-    index_table = jnp.concatenate([window_piece.reshape(-1), window_slot.reshape(-1), my_spans])
+    index_table = jnp.concatenate([window_piece.reshape(-1), window_slot.reshape(-1), my_spans,
+                                   jnp.stack([my_half, my_q]).astype(jnp.int32)])
     query_start = doc_start.reshape(tiles, SPAN, 1)
 
     def cross_pairs():
@@ -148,7 +163,7 @@
         kernel = pl.pallas_call(
             lambda *refs, a=aliased: attention_kernel(
                 *refs, group_size=group_size, window_spans=window_spans, tiles=tiles,
-                score_scale=score_scale, aliased=a),
+                half=half, score_scale=score_scale, aliased=a),
             grid_spec=pltpu.PrefetchScalarGridSpec(
                 num_scalar_prefetch=1,
                 grid=(chunk_heads, tiles),
@@ -156,31 +171,24 @@
                 out_specs=[
                     pl.BlockSpec((SPAN, group_cols), lambda j, t, idx, h=head0: (t, h + j)),
                     pl.BlockSpec((SPAN, group_cols), lambda j, t, idx, h=head0: (t, h + j)),
-                    pl.BlockSpec((1, slot_count, SPAN, 2 * DH), lambda j, t, idx: (j, 0, 0, 0)),
-                ],
+                ] + [pl.BlockSpec((1, 2, tiles, SPAN, 2 * DH), lambda j, t, idx: (j, 0, 0, 0, 0))] * half,
+                scratch_shapes=[pltpu.VMEM((slot_count, SPAN, 2 * DH), jnp.float32)],
             ),
             out_shape=[
                 jax.ShapeDtypeStruct((local_rows, head_count * DH), jnp.bfloat16),
                 jax.ShapeDtypeStruct((local_rows, head_count * DH), jnp.bfloat16),
-                jax.ShapeDtypeStruct((chunk_heads, slot_count, SPAN, 2 * DH), jnp.float32),
-            ],
+                jax.ShapeDtypeStruct((chunk_heads, 2, tiles, SPAN, 2 * DH), jnp.float32),
+            ] + [jax.ShapeDtypeStruct((chunk_heads, 2, tiles, SPAN, 2 * DH), jnp.bfloat16)] * (half - 1),
             input_output_aliases=aliases,
         )
-        attended, query_grad, buffer = kernel(*operands)
-
-        blocks = buffer.reshape(chunk_heads, ctx_count, local_rows, 2 * DH)
-
-        def pack_for(q):
-            target = my_half * half + q
-            own = lax.dynamic_index_in_dim(blocks, target, 1, keepdims=False)
-            other = lax.dynamic_index_in_dim(blocks, target ^ half, 1, keepdims=False)
-            return jnp.stack([own, other], axis=1)
-
-        summed = pack_for(my_q)
+        attended, query_grad, own_pack, *send_packs = kernel(*operands)
+
+        pack_shape = (chunk_heads, 2, local_rows, 2 * DH)
+        summed = own_pack.reshape(pack_shape)
         for shift in range(1, half):
-            send = pack_for((my_q + shift) % half)
             summed = summed + lax.ppermute(
-                send.astype(jnp.bfloat16), "ctx", half_pairs(shift)).astype(jnp.float32)
+                send_packs[shift - 1].reshape(pack_shape), "ctx",
+                half_pairs(shift)).astype(jnp.float32)
         summed = summed[:, 0] + lax.ppermute(
             summed[:, 1].astype(jnp.bfloat16), "ctx", cross_pairs()).astype(jnp.float32)
         key_grads.append(summed[:, :, :DH])

time: 81.8 us -> 80.1 us (0.979)
  other arithmetic: 6.41 us -> 4.33 us
  local copies, waits for them, and re-layouts: 7.08 us -> 5.17 us
  starting transfers between devices: 23.5 us -> 25 us
    another operation x2 -> x0, local copies, waits for them, and re-layouts: 2.87 us -> none
    ppermute x6, waiting for transfers between devices: 7.4 us -> 9.2 us  [local(): pieces.append(lax.ppermute(both, 'ctx', half_pairs(shift)))]
    ppermute x2, starting transfers between devices: 5.51 us -> 7.13 us  [local(): lax.ppermute(summed[:, 1].astype(jnp.bfloat16), 'ctx', cross_pairs())]
    ppermute x6, starting transfers between devices: 7.34 us -> 6.03 us  [local(): pieces.append(lax.ppermute(both, 'ctx', half_pairs(shift)))]
    ppermute x6, starting transfers between devices: 6.42 us -> 7.69 us  [local(): lax.ppermute(send_packs[shift - 1].reshape(pack_shape), 'ctx', half_pairs...]
    dynamic_slice x1 -> x0, local copies, waits for them, and re-layouts: 1.08 us -> none  [pack_for(): own = lax.dynamic_index_in_dim(blocks, target, 1, keepdims=False)]
    reshape x0 -> x3, local copies, waits for them, and re-layouts: none -> 1.05 us  [local(): send_packs[shift - 1].reshape(pack_shape)]
  transfers between devices with their start and end apart: 16 -> 16, of which waited for: 7 -> 7; matrix products, arithmetic and copies ran while one was open for 14% -> 7% of each run, Pallas kernels for 20% -> 21%
where the time goes in v7:
time: 80.1 us; the launch traced here: 79.8 us
  waiting for transfers between devices  28.1 us (35%)
  starting transfers between devices  25 us (31%)
  Pallas kernels  16.4 us (20%)
  local copies, waits for them, and re-layouts  5.17 us (6%)
  other arithmetic  4.33 us (5%)
    pallas_call x2, Pallas kernels, local(): attended, query_grad, own_pack, *send_packs = kernel(*operands)  16.4 us
    ppermute x6, waiting for transfers between devices, local(): pieces.append(lax.ppermute(both, 'ctx', half_pairs(shift)))  9.2 us
    ppermute x6, starting transfers between devices, local(): lax.ppermute(send_packs[shift - 1].reshape(pack_shape), 'ctx', half_pairs...  7.69 us
    ppermute x2, waiting for transfers between devices, local(): both = jnp.stack([pair, lax.ppermute(pair, 'ctx', cross_pairs())])  7.25 us
    ppermute x2, starting transfers between devices, local(): lax.ppermute(summed[:, 1].astype(jnp.bfloat16), 'ctx', cross_pairs())  7.13 us
    ppermute x6, waiting for transfers between devices, local(): lax.ppermute(send_packs[shift - 1].reshape(pack_shape), 'ctx', half_pairs...  6.07 us
    ppermute x6, starting transfers between devices, local(): pieces.append(lax.ppermute(both, 'ctx', half_pairs(shift)))  6.03 us
    ppermute x2, waiting for transfers between devices, local(): lax.ppermute(summed[:, 1].astype(jnp.bfloat16), 'ctx', cross_pairs())  5.61 us
  transfers between devices with their start and end apart: 16, of which 7 were waited for; matrix products, arithmetic and copies ran while one was open for 7% of the time, Pallas kernels for 21%

profile of v7, /device:TPU:0, one launch (start us, length us, event | category | flops | bytes accessed | tf_op | source)
XLA Modules:
  0.0 79.8 jit_solution(10451722156075730285)
XLA Ops:
  0.6 1.0 %fusion.22 = (bf16[128,256]{1,0:T(8,128)(2,1)S(1)}, bf16[128,256]{1,0:T(8,128)(2,1)S(1)}, bf16[128,256]{1,0:T(8,128)(2,1)S(1)}, bf16[128,256]{1,0:T(8,128)(2,1)S(1)}) fusion(bf16[128,512]{1,0:T(8,128)(2,1)} %param.7, bf16[128,512]{1,0:T(8,128)(2,1)} %param.8), kind=kLoop, calls=%fused_computation.55 | loop fusion | bytes 524288 | tf_op jit(solution)/shard_map/slice | solution.py:139
  1.6 4.1 %collective-permute-start.4 = (bf16[128,512]{1,0:T(8,128)(2,1)S(1)}, bf16[128,512]{1,0:T(8,128)(2,1)S(1)}, u32[]{:S(2)}, u32[]{:S(2)}) collective-permute-start(bf16[128,512]{1,0:T(8,128)(2,1)S(1)} %get-tuple-element.39), channel_id=1, source_target_pairs={{0,8},{2,10},{4,12},{6,14},{8,0},{10,2},{12,4},{14,6},{1,9},{3,11}... | collective-permute-start | bytes 393224 | tf_op jit(solution)/shard_map/ppermute | solution.py:140
  7.6 0.8 %reshape.84.refs_1_ = s32[2,64,1]{2,1,0:T(8,128)} reshape(s32[128]{0:T(128)S(1)} %copy-done.5) | data formatting | bytes 1024 | tf_op jit(solution)/shard_map/reshape | solution.py:125
  8.4 7.2 %collective-permute-done.4 = bf16[128,512]{1,0:T(8,128)(2,1)S(1)} collective-permute-done((bf16[128,512]{1,0:T(8,128)(2,1)S(1)}, bf16[128,512]{1,0:T(8,128)(2,1)S(1)}, u32[]{:S(2)}, u32[]{:S(2)}) %collective-permute-start.4) | collective-permute-done | bytes 131104 | tf_op jit(solution)/shard_map/ppermute | solution.py:140
  15.7 1.9 %collective-permute-start.5 = (bf16[2,128,512]{2,1,0:T(8,128)(2,1)S(1)}, bf16[2,128,512]{2,1,0:T(8,128)(2,1)S(1)}, u32[]{:S(2)}, u32[]{:S(2)}) collective-permute-start(bf16[2,128,512]{2,1,0:T(8,128)(2,1)S(1)} %get-tuple-element.31), channel_id=1, source_target_pairs={{0,2},{2,4},{4,6},{6,0},{8,10},{10,12},{12,14},{14,8},{1,3},{3,5},... | collective-permute-start | bytes 786440 | tf_op jit(solution)/shard_map/ppermute | solution.py:143
  17.6 1.5 %collective-permute-start.7 = (bf16[2,128,512]{2,1,0:T(8,128)(2,1)S(1)}, bf16[2,128,512]{2,1,0:T(8,128)(2,1)S(1)}, u32[]{:S(2)}, u32[]{:S(2)}) collective-permute-start(bf16[2,128,512]{2,1,0:T(8,128)(2,1)S(1)} %get-tuple-element.31), channel_id=1, source_target_pairs={{0,6},{2,0},{4,2},{6,4},{8,14},{10,8},{12,10},{14,12},{1,7},{3,1},... | collective-permute-start | bytes 786440 | tf_op jit(solution)/shard_map/ppermute | solution.py:143
  20.4 2.0 %collective-permute-start.2 = (bf16[2,128,512]{2,1,0:T(8,128)(2,1)S(1)}, bf16[2,128,512]{2,1,0:T(8,128)(2,1)S(1)}, u32[]{:S(2)}, u32[]{:S(2)}) collective-permute-start(bf16[2,128,512]{2,1,0:T(8,128)(2,1)S(1)} %get-tuple-element.33), channel_id=1, source_target_pairs={{0,4},{2,6},{4,0},{6,2},{8,12},{10,14},{12,8},{14,10},{1,5},{3,7},... | collective-permute-start | bytes 786440 | tf_op jit(solution)/shard_map/ppermute | solution.py:143
  22.4 5.6 %collective-permute-done.5 = bf16[2,128,512]{2,1,0:T(8,128)(2,1)S(1)} collective-permute-done((bf16[2,128,512]{2,1,0:T(8,128)(2,1)S(1)}, bf16[2,128,512]{2,1,0:T(8,128)(2,1)S(1)}, u32[]{:S(2)}, u32[]{:S(2)}) %collective-permute-start.5) | collective-permute-done | bytes 262176 | tf_op jit(solution)/shard_map/ppermute | solution.py:143
  28.0 3.6 %collective-permute-done.7 = bf16[2,128,512]{2,1,0:T(8,128)(2,1)S(1)} collective-permute-done((bf16[2,128,512]{2,1,0:T(8,128)(2,1)S(1)}, bf16[2,128,512]{2,1,0:T(8,128)(2,1)S(1)}, u32[]{:S(2)}, u32[]{:S(2)}) %collective-permute-start.7) | collective-permute-done | bytes 262176 | tf_op jit(solution)/shard_map/ppermute | solution.py:143
  31.6 1.1 %pad_maximum_fusion.1 = bf16[4,2,128,512]{3,2,1,0:T(8,128)(2,1)} fusion(bf16[1,2,128,512]{3,2,1,0:T(8,128)(2,1)S(1)} %bitcast.77, bf16[1,2,128,512]{3,2,1,0:T(8,128)(2,1)S(1)} %bitcast.76, bf16[1,2,128,512]{3,2,1,0:T(8,128)(2,1)S(1)} %bitcast.75, bf16[1,2,128,512]{3,2,1,0:T(8,128)(2,1)S(1)} %get-tuple-element.30), kind=kLoop, calls=%fused_computation.1 | loop fusion | flops 1572864 | bytes 2097152 | tf_op jit(solution)/shard_map/stack | solution.py:144
  32.7 8.1 %shard_map.93 = (bf16[128,4096]{1,0:T(8,128)(2,1)}, bf16[128,4096]{1,0:T(8,128)(2,1)}, f32[2,2,2,64,256]{4,3,2,1,0:T(8,128)}, bf16[2,2,2,64,256]{4,3,2,1,0:T(8,1...) custom-call(s32[24]{0:T(128)} %concatenate.17.refs_0_, s32[2,64,1]{2,1,0:T(8,128)} %reshape.84.refs_1_, ...), custom_call_target="tpu_custom_call" | custom-call | tf_op jit(solution)/shard_map/pallas_call | solution.py:184
  40.9 1.0 %copy.27 = bf16[2,2,128,256]{3,2,0,1:T(8,128)(2,1)S(1)} copy(bf16[2,2,128,256]{3,2,1,0:T(8,128)(2,1)} %bitcast.71) | data formatting | bytes 524288 | tf_op jit(solution)/shard_map/reshape | solution.py:190
  41.9 1.9 %collective-permute-start.10 = (bf16[2,2,128,256]{3,2,0,1:T(8,128)(2,1)S(1)}, bf16[2,2,128,256]{3,2,0,1:T(8,128)(2,1)S(1)}, u32[]{:S(2)}, u32[]{:S(2)}) collective-permute-start(bf16[2,2,128,256]{3,2,0,1:T(8,128)(2,1)S(1)} %copy.27), channel_id=1, source_target_pairs={{0,6},{2,0},{4,2},{6,4},{8,14},{10,8},{12,10},{14,12},{1,7},{3,1},... | collective-permute-start | bytes 786440 | tf_op jit(solution)/shard_map/ppermute | solution.py:189
  43.8 0.7 collective-permute-start.8
  44.7 2.1 %collective-permute-start.9 = (bf16[2,2,128,256]{3,2,0,1:T(8,128)(2,1)S(1)}, bf16[2,2,128,256]{3,2,0,1:T(8,128)(2,1)S(1)}, u32[]{:S(2)}, u32[]{:S(2)}) collective-permute-start(bf16[2,2,128,256]{3,2,0,1:T(8,128)(2,1)S(1)} %copy.26), channel_id=1, source_target_pairs={{0,4},{2,6},{4,0},{6,2},{8,12},{10,14},{12,8},{14,10},{1,5},{3,7},... | collective-permute-start | bytes 786440 | tf_op jit(solution)/shard_map/ppermute | solution.py:189
  46.9 1.1 %pad_maximum_fusion = bf16[4,2,128,512]{3,2,1,0:T(8,128)(2,1)} fusion(bf16[1,2,128,512]{3,2,1,0:T(8,128)(2,1)S(1)} %bitcast.74, bf16[1,2,128,512]{3,2,1,0:T(8,128)(2,1)S(1)} %bitcast.73, bf16[1,2,128,512]{3,2,1,0:T(8,128)(2,1)S(1)} %bitcast.72, bf16[1,2,128,512]{3,2,1,0:T(8,128)(2,1)S(1)} %get-tuple-element.32), kind=kLoop, calls=%fused_computation | loop fusion | flops 1572864 | bytes 2097152 | tf_op jit(solution)/shard_map/stack | solution.py:144
  48.0 8.3 %shard_map.94 = (bf16[128,4096]{1,0:T(8,128)(2,1)}, bf16[128,4096]{1,0:T(8,128)(2,1)}, f32[2,2,2,64,256]{4,3,2,1,0:T(8,128)}, bf16[2,2,2,64,256]{4,3,2,1,0:T(8,1...) custom-call(s32[24]{0:T(128)} %concatenate.17.refs_0_, ...), custom_call_target="tpu_custom_call", output_to_operand_aliasing={{0}: (6, {}), {1}: (7, {})} | custom-call | tf_op jit(solution)/shard_map/pallas_call | solution.py:184
  56.9 2.0 %collective-permute-start.13 = (bf16[2,2,128,256]{3,2,1,0:T(8,128)(2,1)}, bf16[2,2,128,256]{3,2,1,0:T(8,128)(2,1)S(1)}, u32[]{:S(2)}, u32[]{:S(2)}) collective-permute-start(bf16[2,2,128,256]{3,2,1,0:T(8,128)(2,1)} %bitcast.81), channel_id=1, source_target_pairs={{0,4},{2,6},{4,0},{6,2},{8,12},{10,14},{12,8},{14,10},{1,5},{3,7},... | collective-permute-start | bytes 786440 | tf_op jit(solution)/shard_map/ppermute | solution.py:189
  59.4 3.0 %collective-permute-start.11 = (bf16[2,128,256]{2,1,0:T(8,128)(2,1)S(1)}, bf16[2,128,256]{2,1,0:T(8,128)(2,1)S(1)}, u32[]{:S(2)}, u32[]{:S(2)}) collective-permute-start(bf16[2,128,256]{2,1,0:T(8,128)(2,1)S(1)} %fusion.8), channel_id=1, source_target_pairs={{0,8},{2,10},{4,12},{6,14},{8,0},{10,2},{12,4},{14,6},{1,9},{3,11}... | collective-permute-start | bytes 393224 | tf_op jit(solution)/shard_map/ppermute | solution.py:192
  62.4 5.4 %collective-permute-done.12 = bf16[2,2,128,256]{3,2,1,0:T(8,128)(2,1)S(1)} collective-permute-done((bf16[2,2,128,256]{3,2,1,0:T(8,128)(2,1)}, bf16[2,2,128,256]{3,2,1,0:T(8,128)(2,1)S(1)}, u32[]{:S(2)}, u32[]{:S(2)}) %collective-permute-start.12) | collective-permute-done | bytes 262176 | tf_op jit(solution)/shard_map/ppermute | solution.py:189
  68.6 4.1 %collective-permute-start.15 = (bf16[2,128,256]{2,1,0:T(8,128)(2,1)S(1)}, bf16[2,128,256]{2,1,0:T(8,128)(2,1)S(1)}, u32[]{:S(2)}, u32[]{:S(2)}) collective-permute-start(bf16[2,128,256]{2,1,0:T(8,128)(2,1)S(1)} %fusion.9), channel_id=1, source_target_pairs={{0,8},{2,10},{4,12},{6,14},{8,0},{10,2},{12,4},{14,6},{1,9},{3,11}... | collective-permute-start | bytes 393224 | tf_op jit(solution)/shard_map/ppermute | solution.py:192
  72.8 5.6 %collective-permute-done.15 = bf16[2,128,256]{2,1,0:T(8,128)(2,1)S(1)} collective-permute-done((bf16[2,128,256]{2,1,0:T(8,128)(2,1)S(1)}, bf16[2,128,256]{2,1,0:T(8,128)(2,1)S(1)}, u32[]{:S(2)}, u32[]{:S(2)}) %collective-permute-start.15) | collective-permute-done | bytes 131104 | tf_op jit(solution)/shard_map/ppermute | solution.py:192
  78.5 0.7 copy_bitcast_fusion
  79.2 0.7 copy_bitcast_fusion.1
  (50 shorter events, 5.4 us)
Async XLA Ops:
  1.6 14.0 %collective-permute-start.4 = (bf16[128,512]{1,0:T(8,128)(2,1)S(1)}, bf16[128,512]{1,0:T(8,128)(2,1)S(1)}, u32[]{:S(2)}, u32[]{:S(2)}) collective-permute-start(bf16[128,512]{1,0:T(8,128)(2,1)S(1)} %get-tuple-element.39), channel_id=1, source_target_pairs={{0,8},{2,10},{4,12},{6,14},{8,0},{10,2},{12,4},{14,6},{1,9},{3,11}... | collective-permute-start | bytes 393224 | tf_op jit(solution)/shard_map/ppermute | solution.py:140
  5.7 13.4 %collective-permute-start = (bf16[128,512]{1,0:T(8,128)(2,1)S(1)}, bf16[128,512]{1,0:T(8,128)(2,1)S(1)}, u32[]{:S(2)}, u32[]{:S(2)}) collective-permute-start(bf16[128,512]{1,0:T(8,128)(2,1)S(1)} %get-tuple-element.45), channel_id=1, source_target_pairs={{0,8},{2,10},{4,12},{6,14},{8,0},{10,2},{12,4},{14,6},{1,9},{3,11}... | collective-permute-start | bytes 393224 | tf_op jit(solution)/shard_map/ppermute | solution.py:140
  5.8 0.7 copy-start.4
  6.9 0.7 copy-start.5
  15.7 12.3 %collective-permute-start.5 = (bf16[2,128,512]{2,1,0:T(8,128)(2,1)S(1)}, bf16[2,128,512]{2,1,0:T(8,128)(2,1)S(1)}, u32[]{:S(2)}, u32[]{:S(2)}) collective-permute-start(bf16[2,128,512]{2,1,0:T(8,128)(2,1)S(1)} %get-tuple-element.31), channel_id=1, source_target_pairs={{0,2},{2,4},{4,6},{6,0},{8,10},{10,12},{12,14},{14,8},{1,3},{3,5},... | collective-permute-start | bytes 786440 | tf_op jit(solution)/shard_map/ppermute | solution.py:143
  17.6 10.4 %collective-permute-start.6 = (bf16[2,128,512]{2,1,0:T(8,128)(2,1)S(1)}, bf16[2,128,512]{2,1,0:T(8,128)(2,1)S(1)}, u32[]{:S(2)}, u32[]{:S(2)}) collective-permute-start(bf16[2,128,512]{2,1,0:T(8,128)(2,1)S(1)} %get-tuple-element.31), channel_id=1, source_target_pairs={{0,4},{2,6},{4,0},{6,2},{8,12},{10,14},{12,8},{14,10},{1,5},{3,7},... | collective-permute-start | bytes 786440 | tf_op jit(solution)/shard_map/ppermute | solution.py:143
  17.6 14.0 %collective-permute-start.7 = (bf16[2,128,512]{2,1,0:T(8,128)(2,1)S(1)}, bf16[2,128,512]{2,1,0:T(8,128)(2,1)S(1)}, u32[]{:S(2)}, u32[]{:S(2)}) collective-permute-start(bf16[2,128,512]{2,1,0:T(8,128)(2,1)S(1)} %get-tuple-element.31), channel_id=1, source_target_pairs={{0,6},{2,0},{4,2},{6,4},{8,14},{10,8},{12,10},{14,12},{1,7},{3,1},... | collective-permute-start | bytes 786440 | tf_op jit(solution)/shard_map/ppermute | solution.py:143
  19.2 25.5 %collective-permute-start.1 = (bf16[2,128,512]{2,1,0:T(8,128)(2,1)S(1)}, bf16[2,128,512]{2,1,0:T(8,128)(2,1)S(1)}, u32[]{:S(2)}, u32[]{:S(2)}) collective-permute-start(bf16[2,128,512]{2,1,0:T(8,128)(2,1)S(1)} %get-tuple-element.33), channel_id=1, source_target_pairs={{0,2},{2,4},{4,6},{6,0},{8,10},{10,12},{12,14},{14,8},{1,3},{3,5},... | collective-permute-start | bytes 786440 | tf_op jit(solution)/shard_map/ppermute | solution.py:143
  20.4 26.5 %collective-permute-start.2 = (bf16[2,128,512]{2,1,0:T(8,128)(2,1)S(1)}, bf16[2,128,512]{2,1,0:T(8,128)(2,1)S(1)}, u32[]{:S(2)}, u32[]{:S(2)}) collective-permute-start(bf16[2,128,512]{2,1,0:T(8,128)(2,1)S(1)} %get-tuple-element.33), channel_id=1, source_target_pairs={{0,4},{2,6},{4,0},{6,2},{8,12},{10,14},{12,8},{14,10},{1,5},{3,7},... | collective-permute-start | bytes 786440 | tf_op jit(solution)/shard_map/ppermute | solution.py:143
  28.0 18.9 %collective-permute-start.3 = (bf16[2,128,512]{2,1,0:T(8,128)(2,1)S(1)}, bf16[2,128,512]{2,1,0:T(8,128)(2,1)S(1)}, u32[]{:S(2)}, u32[]{:S(2)}) collective-permute-start(bf16[2,128,512]{2,1,0:T(8,128)(2,1)S(1)} %get-tuple-element.33), channel_id=1, source_target_pairs={{0,6},{2,0},{4,2},{6,4},{8,14},{10,8},{12,10},{14,12},{1,7},{3,1},... | collective-permute-start | bytes 786440 | tf_op jit(solution)/shard_map/ppermute | solution.py:143
  40.9 2.9 %copy-start.3 = (bf16[2,2,2,64,256]{4,3,2,1,0:T(8,128)(2,1)S(1)}, bf16[2,2,2,64,256]{4,3,2,1,0:T(8,128)(2,1)}, u32[]{:S(2)}) copy-start(bf16[2,2,2,64,256]{4,3,2,1,0:T(8,128)(2,1)} %get-tuple-element.21) | copy-start | bytes 786436
  41.9 17.0 %collective-permute-start.10 = (bf16[2,2,128,256]{3,2,0,1:T(8,128)(2,1)S(1)}, bf16[2,2,128,256]{3,2,0,1:T(8,128)(2,1)S(1)}, u32[]{:S(2)}, u32[]{:S(2)}) collective-permute-start(bf16[2,2,128,256]{3,2,0,1:T(8,128)(2,1)S(1)} %copy.27), channel_id=1, source_target_pairs={{0,6},{2,0},{4,2},{6,4},{8,14},{10,8},{12,10},{14,12},{1,7},{3,1},... | collective-permute-start | bytes 786440 | tf_op jit(solution)/shard_map/ppermute | solution.py:189
  43.8 1.0 %copy-start.2 = (bf16[2,2,2,64,256]{4,3,2,1,0:T(8,128)(2,1)S(1)}, bf16[2,2,2,64,256]{4,3,2,1,0:T(8,128)(2,1)}, u32[]{:S(2)}) copy-start(bf16[2,2,2,64,256]{4,3,2,1,0:T(8,128)(2,1)} %get-tuple-element.22) | copy-start | bytes 786436
  43.8 15.5 %collective-permute-start.8 = (bf16[2,2,128,256]{3,2,0,1:T(8,128)(2,1)S(1)}, bf16[2,2,128,256]{3,2,0,1:T(8,128)(2,1)S(1)}, u32[]{:S(2)}, u32[]{:S(2)}) collective-permute-start(bf16[2,2,128,256]{3,2,0,1:T(8,128)(2,1)S(1)} %copy.24), channel_id=1, source_target_pairs={{0,2},{2,4},{4,6},{6,0},{8,10},{10,12},{12,14},{14,8},{1,3},{3,5},... | collective-permute-start | bytes 786440 | tf_op jit(solution)/shard_map/ppermute | solution.py:189
  44.7 14.5 %collective-permute-start.9 = (bf16[2,2,128,256]{3,2,0,1:T(8,128)(2,1)S(1)}, bf16[2,2,128,256]{3,2,0,1:T(8,128)(2,1)S(1)}, u32[]{:S(2)}, u32[]{:S(2)}) collective-permute-start(bf16[2,2,128,256]{3,2,0,1:T(8,128)(2,1)S(1)} %copy.26), channel_id=1, source_target_pairs={{0,4},{2,6},{4,0},{6,2},{8,12},{10,14},{12,8},{14,10},{1,5},{3,7},... | collective-permute-start | bytes 786440 | tf_op jit(solution)/shard_map/ppermute | solution.py:189
  48.0 11.3 %copy-start = (f32[2,2,2,64,256]{4,3,2,1,0:T(8,128)S(1)}, f32[2,2,2,64,256]{4,3,2,1,0:T(8,128)}, u32[]{:S(2)}) copy-start(f32[2,2,2,64,256]{4,3,2,1,0:T(8,128)} %get-tuple-element.20) | copy-start | bytes 1572868
  56.3 11.6 %collective-permute-start.12 = (bf16[2,2,128,256]{3,2,1,0:T(8,128)(2,1)}, bf16[2,2,128,256]{3,2,1,0:T(8,128)(2,1)S(1)}, u32[]{:S(2)}, u32[]{:S(2)}) collective-permute-start(bf16[2,2,128,256]{3,2,1,0:T(8,128)(2,1)} %bitcast.82), channel_id=1, source_target_pairs={{0,2},{2,4},{4,6},{6,0},{8,10},{10,12},{12,14},{14,8},{1,3},{3,5},... | collective-permute-start | bytes 786440 | tf_op jit(solution)/shard_map/ppermute | solution.py:189
  56.9 11.1 %collective-permute-start.13 = (bf16[2,2,128,256]{3,2,1,0:T(8,128)(2,1)}, bf16[2,2,128,256]{3,2,1,0:T(8,128)(2,1)S(1)}, u32[]{:S(2)}, u32[]{:S(2)}) collective-permute-start(bf16[2,2,128,256]{3,2,1,0:T(8,128)(2,1)} %bitcast.81), channel_id=1, source_target_pairs={{0,4},{2,6},{4,0},{6,2},{8,12},{10,14},{12,8},{14,10},{1,5},{3,7},... | collective-permute-start | bytes 786440 | tf_op jit(solution)/shard_map/ppermute | solution.py:189
  58.9 9.5 %collective-permute-start.14 = (bf16[2,2,128,256]{3,2,1,0:T(8,128)(2,1)}, bf16[2,2,128,256]{3,2,1,0:T(8,128)(2,1)S(1)}, u32[]{:S(2)}, u32[]{:S(2)}) collective-permute-start(bf16[2,2,128,256]{3,2,1,0:T(8,128)(2,1)} %bitcast.80), channel_id=1, source_target_pairs={{0,6},{2,0},{4,2},{6,4},{8,14},{10,8},{12,10},{14,12},{1,7},{3,1},... | collective-permute-start | bytes 786440 | tf_op jit(solution)/shard_map/ppermute | solution.py:189
  59.3 9.2 %copy-start.1 = (f32[2,2,2,64,256]{4,3,2,1,0:T(8,128)S(1)}, f32[2,2,2,64,256]{4,3,2,1,0:T(8,128)}, u32[]{:S(2)}) copy-start(f32[2,2,2,64,256]{4,3,2,1,0:T(8,128)} %get-tuple-element.24) | copy-start | bytes 1572868
  59.4 13.3 %collective-permute-start.11 = (bf16[2,128,256]{2,1,0:T(8,128)(2,1)S(1)}, bf16[2,128,256]{2,1,0:T(8,128)(2,1)S(1)}, u32[]{:S(2)}, u32[]{:S(2)}) collective-permute-start(bf16[2,128,256]{2,1,0:T(8,128)(2,1)S(1)} %fusion.8), channel_id=1, source_target_pairs={{0,8},{2,10},{4,12},{6,14},{8,0},{10,2},{12,4},{14,6},{1,9},{3,11}... | collective-permute-start | bytes 393224 | tf_op jit(solution)/shard_map/ppermute | solution.py:192
  68.6 9.8 %collective-permute-start.15 = (bf16[2,128,256]{2,1,0:T(8,128)(2,1)S(1)}, bf16[2,128,256]{2,1,0:T(8,128)(2,1)S(1)}, u32[]{:S(2)}, u32[]{:S(2)}) collective-permute-start(bf16[2,128,256]{2,1,0:T(8,128)(2,1)S(1)} %fusion.9), channel_id=1, source_target_pairs={{0,8},{2,10},{4,12},{6,14},{8,0},{10,2},{12,4},{14,6},{1,9},{3,11}... | collective-permute-start | bytes 393224 | tf_op jit(solution)/shard_map/ppermute | solution.py:192

commit v8 on v7

--- a/solution.py
+++ b/solution.py
@@ -12,8 +12,11 @@
 CHUNKS = 2
 
 
-def attention_kernel(index_ref, qstart_ref, q_ref, do_ref, k_ref, v_ref,
+def attention_kernel(index_ref, qstart_ref, q_ref, do_ref,
                      *rest, group_size, window_spans, tiles, half, score_scale, aliased):
+    key_refs = rest[:half]
+    value_refs = rest[half:2 * half]
+    rest = rest[2 * half:]
     if aliased:
         rest = rest[2:]
     out_ref, dq_ref, own_ref = rest[:3]
@@ -21,10 +24,21 @@
     buf_ref = rest[-1]
     tile = pl.program_id(1)
     base = tile * window_spans
-    key_block = jnp.concatenate(
-        [k_ref[index_ref[base + w]] for w in range(window_spans)], axis=0)
-    value_block = jnp.concatenate(
-        [v_ref[index_ref[base + w]] for w in range(window_spans)], axis=0)
+    info = 2 * tiles * window_spans + tiles
+
+    def window_rows(refs):
+        parts = []
+        for w in range(window_spans):
+            piece = index_ref[base + w]
+            row = index_ref[info + 2 + base + w]
+            part = refs[0][row]
+            for other in range(1, half):
+                part = jnp.where(piece == other, refs[other][row], part)
+            parts.append(part)
+        return jnp.concatenate(parts, axis=0)
+
+    key_block = window_rows(key_refs)
+    value_block = window_rows(value_refs)
     query_all = jnp.concatenate(
         [q_ref[:, h * DH:(h + 1) * DH] for h in range(group_size)], axis=0)
     grad_all = jnp.concatenate(
@@ -78,7 +92,6 @@
 
     @pl.when(tile == tiles - 1)
     def _():
-        info = 2 * tiles * window_spans + tiles
         my_half = index_ref[info]
         my_q = index_ref[info + 1]
         for shift, ref in enumerate((own_ref,) + tuple(send_refs)):
@@ -86,7 +99,7 @@
             other = (target + half) % (2 * half)
             for k, device in enumerate((target, other)):
                 block = buf_ref[pl.ds(device * tiles, tiles)]
-                ref[0, k] = block.astype(ref.dtype)
+                ref[k, 0] = block.astype(ref.dtype)
 
 
 def local(queries, key_rows, value_rows, out_grad, doc_start, span_order):
@@ -119,9 +132,10 @@
     window_owner = window_slot // tiles
     owner_s = (my_q - window_owner % half) % half
     owner_k = (window_owner // half != my_half).astype(jnp.int32)
-    window_piece = (owner_s * 2 + owner_k) * tiles + window_slot % tiles
-    index_table = jnp.concatenate([window_piece.reshape(-1), window_slot.reshape(-1), my_spans,
-                                   jnp.stack([my_half, my_q]).astype(jnp.int32)])
+    window_row = owner_k * tiles + window_slot % tiles
+    index_table = jnp.concatenate([owner_s.reshape(-1), window_slot.reshape(-1), my_spans,
+                                   jnp.stack([my_half, my_q]).astype(jnp.int32),
+                                   window_row.reshape(-1)])
     query_start = doc_start.reshape(tiles, SPAN, 1)
 
     def cross_pairs():
@@ -141,7 +155,7 @@
         pieces = [both]
         for shift in range(1, half):
             pieces.append(lax.ppermute(both, "ctx", half_pairs(shift)))
-        pair_all = jnp.stack(pieces).reshape(ctx_count * tiles, SPAN, 2 * chunk_cols)
+        pieces = [piece.reshape(2 * tiles, SPAN, 2 * chunk_cols) for piece in pieces]
 
         aliased = chunk > 0
         head0 = chunk * chunk_heads
@@ -149,12 +163,10 @@
             pl.BlockSpec((1, SPAN, 1), lambda j, t, idx: (t, 0, 0)),
             pl.BlockSpec((SPAN, group_cols), lambda j, t, idx, h=head0: (t, h + j)),
             pl.BlockSpec((SPAN, group_cols), lambda j, t, idx, h=head0: (t, h + j)),
-            pl.BlockSpec((ctx_count * tiles, SPAN, DH), lambda j, t, idx: (0, 0, j)),
-            pl.BlockSpec((ctx_count * tiles, SPAN, DH),
-                         lambda j, t, idx, n=chunk_heads: (0, 0, n + j)),
-        ]
-        operands = [index_table, query_start, queries, out_grad,
-                    pair_all, pair_all]
+        ] + [pl.BlockSpec((2 * tiles, SPAN, DH), lambda j, t, idx: (0, 0, j))] * half + [
+            pl.BlockSpec((2 * tiles, SPAN, DH), lambda j, t, idx, n=chunk_heads: (0, 0, n + j))
+        ] * half
+        operands = [index_table, query_start, queries, out_grad] + pieces + pieces
         aliases = {}
         if aliased:
             in_specs += [pl.BlockSpec(memory_space=pl.ANY), pl.BlockSpec(memory_space=pl.ANY)]
@@ -171,26 +183,26 @@
                 out_specs=[
                     pl.BlockSpec((SPAN, group_cols), lambda j, t, idx, h=head0: (t, h + j)),
                     pl.BlockSpec((SPAN, group_cols), lambda j, t, idx, h=head0: (t, h + j)),
-                ] + [pl.BlockSpec((1, 2, tiles, SPAN, 2 * DH), lambda j, t, idx: (j, 0, 0, 0, 0))] * half,
+                ] + [pl.BlockSpec((2, 1, tiles, SPAN, 2 * DH), lambda j, t, idx: (0, j, 0, 0, 0))] * half,
                 scratch_shapes=[pltpu.VMEM((slot_count, SPAN, 2 * DH), jnp.float32)],
             ),
             out_shape=[
                 jax.ShapeDtypeStruct((local_rows, head_count * DH), jnp.bfloat16),
                 jax.ShapeDtypeStruct((local_rows, head_count * DH), jnp.bfloat16),
-                jax.ShapeDtypeStruct((chunk_heads, 2, tiles, SPAN, 2 * DH), jnp.float32),
-            ] + [jax.ShapeDtypeStruct((chunk_heads, 2, tiles, SPAN, 2 * DH), jnp.bfloat16)] * (half - 1),
+                jax.ShapeDtypeStruct((2, chunk_heads, tiles, SPAN, 2 * DH), jnp.float32),
+            ] + [jax.ShapeDtypeStruct((2, chunk_heads, tiles, SPAN, 2 * DH), jnp.bfloat16)] * (half - 1),
             input_output_aliases=aliases,
         )
         attended, query_grad, own_pack, *send_packs = kernel(*operands)
 
-        pack_shape = (chunk_heads, 2, local_rows, 2 * DH)
+        pack_shape = (2, chunk_heads, local_rows, 2 * DH)
         summed = own_pack.reshape(pack_shape)
         for shift in range(1, half):
             summed = summed + lax.ppermute(
                 send_packs[shift - 1].reshape(pack_shape), "ctx",
                 half_pairs(shift)).astype(jnp.float32)
-        summed = summed[:, 0] + lax.ppermute(
-            summed[:, 1].astype(jnp.bfloat16), "ctx", cross_pairs()).astype(jnp.float32)
+        summed = summed[0] + lax.ppermute(
+            summed[1].astype(jnp.bfloat16), "ctx", cross_pairs()).astype(jnp.float32)
         key_grads.append(summed[:, :, :DH])
         value_grads.append(summed[:, :, DH:])
 

time: 80.1 us -> 78.3 us (0.978)
  other arithmetic: 4.33 us -> 2.07 us
    another operation x6 -> x2, other arithmetic: 2.37 us -> 0.06 us  [the longest x4 2.32 us: local(): jnp.stack(pieces).reshape(ctx_count * tiles, SPAN, 2 * chunk_cols)]
    ppermute x6, waiting for transfers between devices: 9.2 us -> 7.7 us  [local(): pieces.append(lax.ppermute(both, 'ctx', half_pairs(shift)))]
    ppermute x2, waiting for transfers between devices: 7.25 us -> 8.66 us  [local(): both = jnp.stack([pair, lax.ppermute(pair, 'ctx', cross_pairs())])]
    unnamed x12 -> x24, local copies, waits for them, and re-layouts: 1.45 us -> 2.82 us
    ppermute x2, waiting for transfers between devices: 5.61 us -> 4.49 us  [local(): lax.ppermute(summed[1].astype(jnp.bfloat16), 'ctx', cross_pairs())]
    reshape x3 -> x0, local copies, waits for them, and re-layouts: 1.05 us -> none  [local(): send_packs[shift - 1].reshape(pack_shape)]
  transfers between devices with their start and end apart: 16 -> 16, of which waited for: 7 -> 5; matrix products, arithmetic and copies ran while one was open for 7% -> 3% of each run, Pallas kernels for 21% -> 22%
where the time goes in v8:
time: 78.3 us; the launch traced here: 78 us
  waiting for transfers between devices  27.5 us (35%)
  starting transfers between devices  25.2 us (32%)
  Pallas kernels  16.9 us (22%)
  local copies, waits for them, and re-layouts  5.46 us (7%)
  other arithmetic  2.07 us (3%)
  between operations  0.85 us (1%)
    pallas_call x2, Pallas kernels, local(): attended, query_grad, own_pack, *send_packs = kernel(*operands)  16.9 us
    ppermute x2, waiting for transfers between devices, local(): both = jnp.stack([pair, lax.ppermute(pair, 'ctx', cross_pairs())])  8.66 us
    ppermute x6, waiting for transfers between devices, local(): pieces.append(lax.ppermute(both, 'ctx', half_pairs(shift)))  7.7 us
    ppermute x6, starting transfers between devices, local(): lax.ppermute(send_packs[shift - 1].reshape(pack_shape), 'ctx', half_pairs...  7.55 us
    ppermute x2, starting transfers between devices, local(): lax.ppermute(summed[1].astype(jnp.bfloat16), 'ctx', cross_pairs())  7.45 us
    ppermute x6, waiting for transfers between devices, local(): lax.ppermute(send_packs[shift - 1].reshape(pack_shape), 'ctx', half_pairs...  6.69 us
    ppermute x6, starting transfers between devices, local(): pieces.append(lax.ppermute(both, 'ctx', half_pairs(shift)))  6.03 us
    ppermute x2, waiting for transfers between devices, local(): lax.ppermute(summed[1].astype(jnp.bfloat16), 'ctx', cross_pairs())  4.49 us
  transfers between devices with their start and end apart: 16, of which 5 were waited for; matrix products, arithmetic and copies ran while one was open for 3% of the time, Pallas kernels for 22%

profile of v8, /device:TPU:0, one launch (start us, length us, event | category | flops | bytes accessed | tf_op | source)
XLA Modules:
  0.0 78.0 jit_solution(11126343651910543618)
XLA Ops:
  0.6 1.0 %fusion.18 = (bf16[128,256]{1,0:T(8,128)(2,1)S(1)}, bf16[128,256]{1,0:T(8,128)(2,1)S(1)}, bf16[128,256]{1,0:T(8,128)(2,1)S(1)}, bf16[128,256]{1,0:T(8,128)(2,1)S(1)}) fusion(bf16[128,512]{1,0:T(8,128)(2,1)} %param.7, bf16[128,512]{1,0:T(8,128)(2,1)} %param.8), kind=kLoop, calls=%fused_computation.49 | loop fusion | bytes 524288 | tf_op jit(solution)/shard_map/slice | solution.py:153
  1.6 4.1 %collective-permute-start.4 = (bf16[128,512]{1,0:T(8,128)(2,1)S(1)}, bf16[128,512]{1,0:T(8,128)(2,1)S(1)}, u32[]{:S(2)}, u32[]{:S(2)}) collective-permute-start(bf16[128,512]{1,0:T(8,128)(2,1)S(1)} %get-tuple-element.37), channel_id=1, source_target_pairs={{0,8},{2,10},{4,12},{6,14},{8,0},{10,2},{12,4},{14,6},{1,9},{3,11}... | collective-permute-start | bytes 393224 | tf_op jit(solution)/shard_map/ppermute | solution.py:154
  7.0 8.7 %collective-permute-done.4 = bf16[128,512]{1,0:T(8,128)(2,1)S(1)} collective-permute-done((bf16[128,512]{1,0:T(8,128)(2,1)S(1)}, bf16[128,512]{1,0:T(8,128)(2,1)S(1)}, u32[]{:S(2)}, u32[]{:S(2)}) %collective-permute-start.4) | collective-permute-done | bytes 131104 | tf_op jit(solution)/shard_map/ppermute | solution.py:154
  15.7 1.9 %collective-permute-start.5 = (bf16[2,128,512]{2,1,0:T(8,128)(2,1)S(1)}, bf16[2,128,512]{2,1,0:T(8,128)(2,1)S(1)}, u32[]{:S(2)}, u32[]{:S(2)}) collective-permute-start(bf16[2,128,512]{2,1,0:T(8,128)(2,1)S(1)} %pad_maximum_fusion.1), channel_id=1, source_target_pairs={{0,2},{2,4},{4,6},{6,0},{8,10},{10,12},{12,14},{14,8},{1,3},{3,5},... | collective-permute-start | bytes 786440 | tf_op jit(solution)/shard_map/ppermute | solution.py:157
  17.6 1.5 %collective-permute-start.7 = (bf16[2,128,512]{2,1,0:T(8,128)(2,1)S(1)}, bf16[2,128,512]{2,1,0:T(8,128)(2,1)S(1)}, u32[]{:S(2)}, u32[]{:S(2)}) collective-permute-start(bf16[2,128,512]{2,1,0:T(8,128)(2,1)S(1)} %pad_maximum_fusion.1), channel_id=1, source_target_pairs={{0,6},{2,0},{4,2},{6,4},{8,14},{10,8},{12,10},{14,12},{1,7},{3,1},... | collective-permute-start | bytes 786440 | tf_op jit(solution)/shard_map/ppermute | solution.py:157
  20.4 0.8 %reshape.110.refs_1_ = s32[2,64,1]{2,1,0:T(8,128)} reshape(s32[128]{0:T(128)S(1)} %copy-done.11) | data formatting | bytes 1024 | tf_op jit(solution)/shard_map/reshape | solution.py:139
  21.9 2.0 %collective-permute-start.2 = (bf16[2,128,512]{2,1,0:T(8,128)(2,1)S(1)}, bf16[2,128,512]{2,1,0:T(8,128)(2,1)S(1)}, u32[]{:S(2)}, u32[]{:S(2)}) collective-permute-start(bf16[2,128,512]{2,1,0:T(8,128)(2,1)S(1)} %pad_maximum_fusion), channel_id=1, source_target_pairs={{0,4},{2,6},{4,0},{6,2},{8,12},{10,14},{12,8},{14,10},{1,5},{3,7},... | collective-permute-start | bytes 786440 | tf_op jit(solution)/shard_map/ppermute | solution.py:157
  23.9 4.1 %collective-permute-done.5 = bf16[2,128,512]{2,1,0:T(8,128)(2,1)S(1)} collective-permute-done((bf16[2,128,512]{2,1,0:T(8,128)(2,1)S(1)}, bf16[2,128,512]{2,1,0:T(8,128)(2,1)S(1)}, u32[]{:S(2)}, u32[]{:S(2)}) %collective-permute-start.5) | collective-permute-done | bytes 262176 | tf_op jit(solution)/shard_map/ppermute | solution.py:157
  28.1 3.6 %collective-permute-done.7 = bf16[2,128,512]{2,1,0:T(8,128)(2,1)S(1)} collective-permute-done((bf16[2,128,512]{2,1,0:T(8,128)(2,1)S(1)}, bf16[2,128,512]{2,1,0:T(8,128)(2,1)S(1)}, u32[]{:S(2)}, u32[]{:S(2)}) %collective-permute-start.7) | collective-permute-done | bytes 262176 | tf_op jit(solution)/shard_map/ppermute | solution.py:157
  31.6 0.7 copy-done.5
  32.3 8.4 %shard_map.93 = (bf16[128,4096]{1,0:T(8,128)(2,1)}, bf16[128,4096]{1,0:T(8,128)(2,1)}, f32[2,2,2,64,256]{4,3,2,1,0:T(8,128)}, bf16[2,2,2,64,256]{4,3,2,1,0:T(8,1...) custom-call(s32[34]{0:T(128)} %concatenate.17.refs_0_, s32[2,64,1]{2,1,0:T(8,128)} %reshape.110.refs_1_, ...), custom_call_target="tpu_custom_call" | custom-call | tf_op jit(solution)/shard_map/pallas_call | solution.py:196
  40.7 1.9 %collective-permute-start.10 = (bf16[2,2,128,256]{3,2,1,0:T(8,128)(2,1)}, bf16[2,2,128,256]{3,2,1,0:T(8,128)(2,1)S(1)}, u32[]{:S(2)}, u32[]{:S(2)}) collective-permute-start(bf16[2,2,128,256]{3,2,1,0:T(8,128)(2,1)} %bitcast.83), channel_id=1, source_target_pairs={{0,6},{2,0},{4,2},{6,4},{8,14},{10,8},{12,10},{14,12},{1,7},{3,1},... | collective-permute-start | bytes 786440 | tf_op jit(solution)/shard_map/ppermute | solution.py:201
  42.6 0.7 collective-permute-start.8
  43.3 1.5 %collective-permute-start.9 = (bf16[2,2,128,256]{3,2,1,0:T(8,128)(2,1)}, bf16[2,2,128,256]{3,2,1,0:T(8,128)(2,1)S(1)}, u32[]{:S(2)}, u32[]{:S(2)}) collective-permute-start(bf16[2,2,128,256]{3,2,1,0:T(8,128)(2,1)} %bitcast.80), channel_id=1, source_target_pairs={{0,4},{2,6},{4,0},{6,2},{8,12},{10,14},{12,8},{14,10},{1,5},{3,7},... | collective-permute-start | bytes 786440 | tf_op jit(solution)/shard_map/ppermute | solution.py:201
  44.8 0.7 copy-done.6
  45.5 8.5 %shard_map.94 = (bf16[128,4096]{1,0:T(8,128)(2,1)}, bf16[128,4096]{1,0:T(8,128)(2,1)}, f32[2,2,2,64,256]{4,3,2,1,0:T(8,128)}, bf16[2,2,2,64,256]{4,3,2,1,0:T(8,1...) custom-call(s32[34]{0:T(128)} %concatenate.17.refs_0_, ...), custom_call_target="tpu_custom_call", output_to_operand_aliasing={{0}: (12, {}), {1}: (13, {})} | custom-call | tf_op jit(solution)/shard_map/pallas_call | solution.py:196
  54.0 1.5 %collective-permute-start.12 = (bf16[2,2,128,256]{3,2,1,0:T(8,128)(2,1)}, bf16[2,2,128,256]{3,2,1,0:T(8,128)(2,1)S(1)}, u32[]{:S(2)}, u32[]{:S(2)}) collective-permute-start(bf16[2,2,128,256]{3,2,1,0:T(8,128)(2,1)} %bitcast.85), channel_id=1, source_target_pairs={{0,2},{2,4},{4,6},{6,0},{8,10},{10,12},{12,14},{14,8},{1,3},{3,5},... | collective-permute-start | bytes 786440 | tf_op jit(solution)/shard_map/ppermute | solution.py:201
  55.6 1.9 %collective-permute-start.13 = (bf16[2,2,128,256]{3,2,1,0:T(8,128)(2,1)}, bf16[2,2,128,256]{3,2,1,0:T(8,128)(2,1)S(1)}, u32[]{:S(2)}, u32[]{:S(2)}) collective-permute-start(bf16[2,2,128,256]{3,2,1,0:T(8,128)(2,1)} %bitcast.84), channel_id=1, source_target_pairs={{0,4},{2,6},{4,0},{6,2},{8,12},{10,14},{12,8},{14,10},{1,5},{3,7},... | collective-permute-start | bytes 786440 | tf_op jit(solution)/shard_map/ppermute | solution.py:201
  57.7 2.4 %collective-permute-start.11 = (bf16[2,128,256]{2,1,0:T(8,128)(2,1)S(1)}, bf16[2,128,256]{2,1,0:T(8,128)(2,1)S(1)}, u32[]{:S(2)}, u32[]{:S(2)}) collective-permute-start(bf16[2,128,256]{2,1,0:T(8,128)(2,1)S(1)} %fusion.8), channel_id=1, source_target_pairs={{0,8},{2,10},{4,12},{6,14},{8,0},{10,2},{12,4},{14,6},{1,9},{3,11}... | collective-permute-start | bytes 393224 | tf_op jit(solution)/shard_map/ppermute | solution.py:204
  60.2 6.7 %collective-permute-done.12 = bf16[2,2,128,256]{3,2,1,0:T(8,128)(2,1)S(1)} collective-permute-done((bf16[2,2,128,256]{3,2,1,0:T(8,128)(2,1)}, bf16[2,2,128,256]{3,2,1,0:T(8,128)(2,1)S(1)}, u32[]{:S(2)}, u32[]{:S(2)}) %collective-permute-start.12) | collective-permute-done | bytes 262176 | tf_op jit(solution)/shard_map/ppermute | solution.py:201
  67.0 5.0 %collective-permute-start.15 = (bf16[2,128,256]{2,1,0:T(8,128)(2,1)S(1)}, bf16[2,128,256]{2,1,0:T(8,128)(2,1)S(1)}, u32[]{:S(2)}, u32[]{:S(2)}) collective-permute-start(bf16[2,128,256]{2,1,0:T(8,128)(2,1)S(1)} %fusion.9), channel_id=1, source_target_pairs={{0,8},{2,10},{4,12},{6,14},{8,0},{10,2},{12,4},{14,6},{1,9},{3,11}... | collective-permute-start | bytes 393224 | tf_op jit(solution)/shard_map/ppermute | solution.py:204
  72.1 4.5 %collective-permute-done.15 = bf16[2,128,256]{2,1,0:T(8,128)(2,1)S(1)} collective-permute-done((bf16[2,128,256]{2,1,0:T(8,128)(2,1)S(1)}, bf16[2,128,256]{2,1,0:T(8,128)(2,1)S(1)}, u32[]{:S(2)}, u32[]{:S(2)}) %collective-permute-start.15) | collective-permute-done | bytes 131104 | tf_op jit(solution)/shard_map/ppermute | solution.py:204
  76.7 0.7 copy_bitcast_fusion
  77.3 0.7 copy_bitcast_fusion.1
  (58 shorter events, 3.7 us)
Async XLA Ops:
  1.6 14.0 %collective-permute-start.4 = (bf16[128,512]{1,0:T(8,128)(2,1)S(1)}, bf16[128,512]{1,0:T(8,128)(2,1)S(1)}, u32[]{:S(2)}, u32[]{:S(2)}) collective-permute-start(bf16[128,512]{1,0:T(8,128)(2,1)S(1)} %get-tuple-element.37), channel_id=1, source_target_pairs={{0,8},{2,10},{4,12},{6,14},{8,0},{10,2},{12,4},{14,6},{1,9},{3,11}... | collective-permute-start | bytes 393224 | tf_op jit(solution)/shard_map/ppermute | solution.py:154
  5.7 13.4 %collective-permute-start = (bf16[128,512]{1,0:T(8,128)(2,1)S(1)}, bf16[128,512]{1,0:T(8,128)(2,1)S(1)}, u32[]{:S(2)}, u32[]{:S(2)}) collective-permute-start(bf16[128,512]{1,0:T(8,128)(2,1)S(1)} %get-tuple-element.43), channel_id=1, source_target_pairs={{0,8},{2,10},{4,12},{6,14},{8,0},{10,2},{12,4},{14,6},{1,9},{3,11}... | collective-permute-start | bytes 393224 | tf_op jit(solution)/shard_map/ppermute | solution.py:154
  15.7 3.5 %copy-start.1 = (bf16[2,128,512]{2,1,0:T(8,128)(2,1)}, bf16[2,128,512]{2,1,0:T(8,128)(2,1)S(1)}, u32[]{:S(2)}) copy-start(bf16[2,128,512]{2,1,0:T(8,128)(2,1)S(1)} %pad_maximum_fusion.1) | copy-start | bytes 786436
  15.7 12.3 %collective-permute-start.5 = (bf16[2,128,512]{2,1,0:T(8,128)(2,1)S(1)}, bf16[2,128,512]{2,1,0:T(8,128)(2,1)S(1)}, u32[]{:S(2)}, u32[]{:S(2)}) collective-permute-start(bf16[2,128,512]{2,1,0:T(8,128)(2,1)S(1)} %pad_maximum_fusion.1), channel_id=1, source_target_pairs={{0,2},{2,4},{4,6},{6,0},{8,10},{10,12},{12,14},{14,8},{1,3},{3,5},... | collective-permute-start | bytes 786440 | tf_op jit(solution)/shard_map/ppermute | solution.py:157
  17.6 10.4 %collective-permute-start.6 = (bf16[2,128,512]{2,1,0:T(8,128)(2,1)S(1)}, bf16[2,128,512]{2,1,0:T(8,128)(2,1)S(1)}, u32[]{:S(2)}, u32[]{:S(2)}) collective-permute-start(bf16[2,128,512]{2,1,0:T(8,128)(2,1)S(1)} %pad_maximum_fusion.1), channel_id=1, source_target_pairs={{0,4},{2,6},{4,0},{6,2},{8,12},{10,14},{12,8},{14,10},{1,5},{3,7},... | collective-permute-start | bytes 786440 | tf_op jit(solution)/shard_map/ppermute | solution.py:157
  17.6 14.0 %collective-permute-start.7 = (bf16[2,128,512]{2,1,0:T(8,128)(2,1)S(1)}, bf16[2,128,512]{2,1,0:T(8,128)(2,1)S(1)}, u32[]{:S(2)}, u32[]{:S(2)}) collective-permute-start(bf16[2,128,512]{2,1,0:T(8,128)(2,1)S(1)} %pad_maximum_fusion.1), channel_id=1, source_target_pairs={{0,6},{2,0},{4,2},{6,4},{8,14},{10,8},{12,10},{14,12},{1,7},{3,1},... | collective-permute-start | bytes 786440 | tf_op jit(solution)/shard_map/ppermute | solution.py:157
  19.2 21.5 %copy-start = (bf16[2,128,512]{2,1,0:T(8,128)(2,1)}, bf16[2,128,512]{2,1,0:T(8,128)(2,1)S(1)}, u32[]{:S(2)}) copy-start(bf16[2,128,512]{2,1,0:T(8,128)(2,1)S(1)} %pad_maximum_fusion) | copy-start | bytes 786436
  19.2 24.1 %collective-permute-start.1 = (bf16[2,128,512]{2,1,0:T(8,128)(2,1)S(1)}, bf16[2,128,512]{2,1,0:T(8,128)(2,1)S(1)}, u32[]{:S(2)}, u32[]{:S(2)}) collective-permute-start(bf16[2,128,512]{2,1,0:T(8,128)(2,1)S(1)} %pad_maximum_fusion), channel_id=1, source_target_pairs={{0,2},{2,4},{4,6},{6,0},{8,10},{10,12},{12,14},{14,8},{1,3},{3,5},... | collective-permute-start | bytes 786440 | tf_op jit(solution)/shard_map/ppermute | solution.py:157
  21.9 22.9 %collective-permute-start.2 = (bf16[2,128,512]{2,1,0:T(8,128)(2,1)S(1)}, bf16[2,128,512]{2,1,0:T(8,128)(2,1)S(1)}, u32[]{:S(2)}, u32[]{:S(2)}) collective-permute-start(bf16[2,128,512]{2,1,0:T(8,128)(2,1)S(1)} %pad_maximum_fusion), channel_id=1, source_target_pairs={{0,4},{2,6},{4,0},{6,2},{8,12},{10,14},{12,8},{14,10},{1,5},{3,7},... | collective-permute-start | bytes 786440 | tf_op jit(solution)/shard_map/ppermute | solution.py:157
  28.0 3.6 %copy-start.3 = (bf16[2,128,512]{2,1,0:T(8,128)(2,1)}, bf16[2,128,512]{2,1,0:T(8,128)(2,1)S(1)}, u32[]{:S(2)}) copy-start(bf16[2,128,512]{2,1,0:T(8,128)(2,1)S(1)} %collective-permute-done.5) | copy-start | bytes 786436
  28.0 16.7 %collective-permute-start.3 = (bf16[2,128,512]{2,1,0:T(8,128)(2,1)S(1)}, bf16[2,128,512]{2,1,0:T(8,128)(2,1)S(1)}, u32[]{:S(2)}, u32[]{:S(2)}) collective-permute-start(bf16[2,128,512]{2,1,0:T(8,128)(2,1)S(1)} %pad_maximum_fusion), channel_id=1, source_target_pairs={{0,6},{2,0},{4,2},{6,4},{8,14},{10,8},{12,10},{14,12},{1,7},{3,1},... | collective-permute-start | bytes 786440 | tf_op jit(solution)/shard_map/ppermute | solution.py:157
  28.0 3.6 %copy-start.4 = (bf16[2,128,512]{2,1,0:T(8,128)(2,1)}, bf16[2,128,512]{2,1,0:T(8,128)(2,1)S(1)}, u32[]{:S(2)}) copy-start(bf16[2,128,512]{2,1,0:T(8,128)(2,1)S(1)} %collective-permute-done.6) | copy-start | bytes 786436
  40.7 16.8 %collective-permute-start.10 = (bf16[2,2,128,256]{3,2,1,0:T(8,128)(2,1)}, bf16[2,2,128,256]{3,2,1,0:T(8,128)(2,1)S(1)}, u32[]{:S(2)}, u32[]{:S(2)}) collective-permute-start(bf16[2,2,128,256]{3,2,1,0:T(8,128)(2,1)} %bitcast.83), channel_id=1, source_target_pairs={{0,6},{2,0},{4,2},{6,4},{8,14},{10,8},{12,10},{14,12},{1,7},{3,1},... | collective-permute-start | bytes 786440 | tf_op jit(solution)/shard_map/ppermute | solution.py:201
  42.6 15.0 %collective-permute-start.8 = (bf16[2,2,128,256]{3,2,1,0:T(8,128)(2,1)}, bf16[2,2,128,256]{3,2,1,0:T(8,128)(2,1)S(1)}, u32[]{:S(2)}, u32[]{:S(2)}) collective-permute-start(bf16[2,2,128,256]{3,2,1,0:T(8,128)(2,1)} %bitcast.81), channel_id=1, source_target_pairs={{0,2},{2,4},{4,6},{6,0},{8,10},{10,12},{12,14},{14,8},{1,3},{3,5},... | collective-permute-start | bytes 786440 | tf_op jit(solution)/shard_map/ppermute | solution.py:201
  43.3 1.5 %copy-start.2 = (bf16[2,128,512]{2,1,0:T(8,128)(2,1)}, bf16[2,128,512]{2,1,0:T(8,128)(2,1)S(1)}, u32[]{:S(2)}) copy-start(bf16[2,128,512]{2,1,0:T(8,128)(2,1)S(1)} %collective-permute-done.1) | copy-start | bytes 786436
  43.3 14.3 %collective-permute-start.9 = (bf16[2,2,128,256]{3,2,1,0:T(8,128)(2,1)}, bf16[2,2,128,256]{3,2,1,0:T(8,128)(2,1)S(1)}, u32[]{:S(2)}, u32[]{:S(2)}) collective-permute-start(bf16[2,2,128,256]{3,2,1,0:T(8,128)(2,1)} %bitcast.80), channel_id=1, source_target_pairs={{0,4},{2,6},{4,0},{6,2},{8,12},{10,14},{12,8},{14,10},{1,5},{3,7},... | collective-permute-start | bytes 786440 | tf_op jit(solution)/shard_map/ppermute | solution.py:201
  44.8 0.8 %copy-start.7 = (bf16[2,128,512]{2,1,0:T(8,128)(2,1)}, bf16[2,128,512]{2,1,0:T(8,128)(2,1)S(1)}, u32[]{:S(2)}) copy-start(bf16[2,128,512]{2,1,0:T(8,128)(2,1)S(1)} %collective-permute-done.3) | copy-start | bytes 786436
  45.5 12.1 %copy-start.8 = (f32[2,2,2,64,256]{4,3,2,1,0:T(8,128)S(1)}, f32[2,2,2,64,256]{4,3,2,1,0:T(8,128)}, u32[]{:S(2)}) copy-start(f32[2,2,2,64,256]{4,3,2,1,0:T(8,128)} %get-tuple-element.20) | copy-start | bytes 1572868
  54.0 12.8 %collective-permute-start.12 = (bf16[2,2,128,256]{3,2,1,0:T(8,128)(2,1)}, bf16[2,2,128,256]{3,2,1,0:T(8,128)(2,1)S(1)}, u32[]{:S(2)}, u32[]{:S(2)}) collective-permute-start(bf16[2,2,128,256]{3,2,1,0:T(8,128)(2,1)} %bitcast.85), channel_id=1, source_target_pairs={{0,2},{2,4},{4,6},{6,0},{8,10},{10,12},{12,14},{14,8},{1,3},{3,5},... | collective-permute-start | bytes 786440 | tf_op jit(solution)/shard_map/ppermute | solution.py:201
  55.6 11.3 %collective-permute-start.13 = (bf16[2,2,128,256]{3,2,1,0:T(8,128)(2,1)}, bf16[2,2,128,256]{3,2,1,0:T(8,128)(2,1)S(1)}, u32[]{:S(2)}, u32[]{:S(2)}) collective-permute-start(bf16[2,2,128,256]{3,2,1,0:T(8,128)(2,1)} %bitcast.84), channel_id=1, source_target_pairs={{0,4},{2,6},{4,0},{6,2},{8,12},{10,14},{12,8},{14,10},{1,5},{3,7},... | collective-permute-start | bytes 786440 | tf_op jit(solution)/shard_map/ppermute | solution.py:201
  57.5 9.4 %collective-permute-start.14 = (bf16[2,2,128,256]{3,2,1,0:T(8,128)(2,1)}, bf16[2,2,128,256]{3,2,1,0:T(8,128)(2,1)S(1)}, u32[]{:S(2)}, u32[]{:S(2)}) collective-permute-start(bf16[2,2,128,256]{3,2,1,0:T(8,128)(2,1)} %bitcast.82), channel_id=1, source_target_pairs={{0,6},{2,0},{4,2},{6,4},{8,14},{10,8},{12,10},{14,12},{1,7},{3,1},... | collective-permute-start | bytes 786440 | tf_op jit(solution)/shard_map/ppermute | solution.py:201
  57.6 9.3 %copy-start.9 = (f32[2,2,2,64,256]{4,3,2,1,0:T(8,128)S(1)}, f32[2,2,2,64,256]{4,3,2,1,0:T(8,128)}, u32[]{:S(2)}) copy-start(f32[2,2,2,64,256]{4,3,2,1,0:T(8,128)} %get-tuple-element.24) | copy-start | bytes 1572868
  57.7 14.3 %collective-permute-start.11 = (bf16[2,128,256]{2,1,0:T(8,128)(2,1)S(1)}, bf16[2,128,256]{2,1,0:T(8,128)(2,1)S(1)}, u32[]{:S(2)}, u32[]{:S(2)}) collective-permute-start(bf16[2,128,256]{2,1,0:T(8,128)(2,1)S(1)} %fusion.8), channel_id=1, source_target_pairs={{0,8},{2,10},{4,12},{6,14},{8,0},{10,2},{12,4},{14,6},{1,9},{3,11}... | collective-permute-start | bytes 393224 | tf_op jit(solution)/shard_map/ppermute | solution.py:204
  67.0 9.6 %collective-permute-start.15 = (bf16[2,128,256]{2,1,0:T(8,128)(2,1)S(1)}, bf16[2,128,256]{2,1,0:T(8,128)(2,1)S(1)}, u32[]{:S(2)}, u32[]{:S(2)}) collective-permute-start(bf16[2,128,256]{2,1,0:T(8,128)(2,1)S(1)} %fusion.9), channel_id=1, source_target_pairs={{0,8},{2,10},{4,12},{6,14},{8,0},{10,2},{12,4},{14,6},{1,9},{3,11}... | collective-permute-start | bytes 393224 | tf_op jit(solution)/shard_map/ppermute | solution.py:204
  (4 other events, 2.7 us)

commit v9 on v8

--- a/solution.py
+++ b/solution.py
@@ -9,7 +9,6 @@
 
 DH = 128
 SPAN = 64
-CHUNKS = 2
 
 
 def attention_kernel(index_ref, qstart_ref, q_ref, do_ref,
@@ -117,9 +116,11 @@
     reach = total_rows // 4 // SPAN
     window_spans = reach + 1
     window = window_spans * SPAN
-    chunks = CHUNKS if kv_count % CHUNKS == 0 else 1
-    chunk_heads = kv_count // chunks
-    chunk_cols = chunk_heads * DH
+    if kv_count >= 4:
+        chunk_sizes = [1, kv_count - 2, 1]
+    else:
+        chunk_sizes = [kv_count]
+    chunk_starts = [sum(chunk_sizes[:c]) for c in range(len(chunk_sizes))]
 
     my_spans = lax.dynamic_slice_in_dim(span_order, my_index * tiles, tiles)
     window_span = my_spans[:, None] - reach + jnp.arange(window_spans, dtype=jnp.int32)[None, :]
@@ -148,8 +149,9 @@
     query_grad = None
     key_grads = []
     value_grads = []
-    for chunk in range(chunks):
-        cols = slice(chunk * chunk_cols, (chunk + 1) * chunk_cols)
+    for chunk, (head0, chunk_heads) in enumerate(zip(chunk_starts, chunk_sizes)):
+        chunk_cols = chunk_heads * DH
+        cols = slice(head0 * DH, (head0 + chunk_heads) * DH)
         pair = jnp.concatenate([key_rows[:, cols], value_rows[:, cols]], axis=1)
         both = jnp.stack([pair, lax.ppermute(pair, "ctx", cross_pairs())])
         pieces = [both]
@@ -158,7 +160,6 @@
         pieces = [piece.reshape(2 * tiles, SPAN, 2 * chunk_cols) for piece in pieces]
 
         aliased = chunk > 0
-        head0 = chunk * chunk_heads
         in_specs = [
             pl.BlockSpec((1, SPAN, 1), lambda j, t, idx: (t, 0, 0)),
             pl.BlockSpec((SPAN, group_cols), lambda j, t, idx, h=head0: (t, h + j)),

time: 78.3 us -> 101 us (1.29)
  starting transfers between devices: 25.2 us -> 41.9 us
  Pallas kernels: 16.9 us -> 19.4 us
  local copies, waits for them, and re-layouts: 5.46 us -> 6.82 us
  waiting for transfers between devices: 27.5 us -> 28.6 us
    ppermute x2 -> x3, waiting for transfers between devices: 8.66 us -> 0.01 us  [local(): both = jnp.stack([pair, lax.ppermute(pair, 'ctx', cross_pairs())])]
    ppermute x6 -> x9, starting transfers between devices: 6.03 us -> 13.2 us  [local(): pieces.append(lax.ppermute(both, 'ctx', half_pairs(shift)))]
    ppermute x6 -> x9, starting transfers between devices: 7.55 us -> 13.2 us  [local(): lax.ppermute(send_packs[shift - 1].reshape(pack_shape), 'ctx', half_pairs...]
    ppermute x6 -> x9, waiting for transfers between devices: 6.69 us -> 10.5 us  [local(): lax.ppermute(send_packs[shift - 1].reshape(pack_shape), 'ctx', half_pairs...]
    ppermute x6 -> x9, waiting for transfers between devices: 7.7 us -> 11.4 us  [local(): pieces.append(lax.ppermute(both, 'ctx', half_pairs(shift)))]
    ppermute x2 -> x3, starting transfers between devices: 4.19 us -> 7.16 us  [local(): both = jnp.stack([pair, lax.ppermute(pair, 'ctx', cross_pairs())])]
    pallas_call x2 -> x3, Pallas kernels: 16.9 us -> 19.4 us  [local(): attended, query_grad, own_pack, *send_packs = kernel(*operands)]
    ppermute x2 -> x3, waiting for transfers between devices: 4.49 us -> 6.67 us  [local(): lax.ppermute(summed[1].astype(jnp.bfloat16), 'ctx', cross_pairs())]
  transfers between devices with their start and end apart: 16 -> 24, of which waited for: 5 -> 11; matrix products, arithmetic and copies ran while one was open for 3% -> 2% of each run, Pallas kernels for 22% -> 19%
where the time goes in v9:
time: 101 us; the launch traced here: 99.8 us
  starting transfers between devices  41.9 us (41%)
  waiting for transfers between devices  28.6 us (28%)
  Pallas kernels  19.4 us (19%)
  local copies, waits for them, and re-layouts  6.82 us (7%)
  other arithmetic  2.11 us (2%)
    pallas_call x3, Pallas kernels, local(): attended, query_grad, own_pack, *send_packs = kernel(*operands)  19.4 us
    ppermute x9, starting transfers between devices, local(): lax.ppermute(send_packs[shift - 1].reshape(pack_shape), 'ctx', half_pairs...  13.2 us
    ppermute x9, starting transfers between devices, local(): pieces.append(lax.ppermute(both, 'ctx', half_pairs(shift)))  13.2 us
    ppermute x9, waiting for transfers between devices, local(): pieces.append(lax.ppermute(both, 'ctx', half_pairs(shift)))  11.4 us
    ppermute x9, waiting for transfers between devices, local(): lax.ppermute(send_packs[shift - 1].reshape(pack_shape), 'ctx', half_pairs...  10.5 us
    ppermute x3, starting transfers between devices, local(): lax.ppermute(summed[1].astype(jnp.bfloat16), 'ctx', cross_pairs())  8.31 us
    ppermute x3, starting transfers between devices, local(): both = jnp.stack([pair, lax.ppermute(pair, 'ctx', cross_pairs())])  7.16 us
    ppermute x3, waiting for transfers between devices, local(): lax.ppermute(summed[1].astype(jnp.bfloat16), 'ctx', cross_pairs())  6.67 us
  transfers between devices with their start and end apart: 24, of which 11 were waited for; matrix products, arithmetic and copies ran while one was open for 2% of the time, Pallas kernels for 19%

profile of v9, /device:TPU:0, one launch (start us, length us, event | category | flops | bytes accessed | tf_op | source)
XLA Modules:
  0.0 99.8 jit_solution(13904242606409232655)
XLA Ops:
  1.5 4.1 %collective-permute-start.8 = (bf16[128,256]{1,0:T(8,128)(2,1)S(1)}, bf16[128,256]{1,0:T(8,128)(2,1)S(1)}, u32[]{:S(2)}, u32[]{:S(2)}) collective-permute-start(bf16[128,256]{1,0:T(8,128)(2,1)S(1)} %get-tuple-element.57), channel_id=1, source_target_pairs={{0,8},{2,10},{4,12},{6,14},{8,0},{10,2},{12,4},{14,6},{1,9},{3,11}... | collective-permute-start | bytes 196616 | tf_op jit(solution)/shard_map/ppermute | solution.py:156
  6.6 3.0 %collective-permute-start = (bf16[128,256]{1,0:T(8,128)(2,1)S(1)}, bf16[128,256]{1,0:T(8,128)(2,1)S(1)}, u32[]{:S(2)}, u32[]{:S(2)}) collective-permute-start(bf16[128,256]{1,0:T(8,128)(2,1)S(1)} %get-tuple-element.59), channel_id=1, source_target_pairs={{0,8},{2,10},{4,12},{6,14},{8,0},{10,2},{12,4},{14,6},{1,9},{3,11}... | collective-permute-start | bytes 196616 | tf_op jit(solution)/shard_map/ppermute | solution.py:156
  12.3 1.6 %collective-permute-start.9 = (bf16[2,128,256]{2,1,0:T(8,128)(2,1)S(1)}, bf16[2,128,256]{2,1,0:T(8,128)(2,1)S(1)}, u32[]{:S(2)}, u32[]{:S(2)}) collective-permute-start(bf16[2,128,256]{2,1,0:T(8,128)(2,1)S(1)} %pad_maximum_fusion.3), channel_id=1, source_target_pairs={{0,2},{2,4},{4,6},{6,0},{8,10},{10,12},{12,14},{14,8},{1,3},{3,5},... | collective-permute-start | bytes 393224 | tf_op jit(solution)/shard_map/ppermute | solution.py:159
  13.8 2.1 %collective-permute-start.10 = (bf16[2,128,256]{2,1,0:T(8,128)(2,1)S(1)}, bf16[2,128,256]{2,1,0:T(8,128)(2,1)S(1)}, u32[]{:S(2)}, u32[]{:S(2)}) collective-permute-start(bf16[2,128,256]{2,1,0:T(8,128)(2,1)S(1)} %pad_maximum_fusion.3), channel_id=1, source_target_pairs={{0,4},{2,6},{4,0},{6,2},{8,12},{10,14},{12,8},{14,10},{1,5},{3,7},... | collective-permute-start | bytes 393224 | tf_op jit(solution)/shard_map/ppermute | solution.py:159
  18.0 3.9 %collective-permute-done.9 = bf16[2,128,256]{2,1,0:T(8,128)(2,1)S(1)} collective-permute-done((bf16[2,128,256]{2,1,0:T(8,128)(2,1)S(1)}, bf16[2,128,256]{2,1,0:T(8,128)(2,1)S(1)}, u32[]{:S(2)}, u32[]{:S(2)}) %collective-permute-start.9) | collective-permute-done | bytes 131104 | tf_op jit(solution)/shard_map/ppermute | solution.py:159
  23.5 5.5 %shard_map.93 = (bf16[128,4096]{1,0:T(8,128)(2,1)}, bf16[128,4096]{1,0:T(8,128)(2,1)}, f32[2,1,2,64,256]{4,3,2,1,0:T(8,128)}, bf16[2,1,2,64,256]{4,3,2,1,0:T(8,1...) custom-call(s32[34]{0:T(128)} %concatenate.20.refs_0_, s32[2,64,1]{2,1,0:T(8,128)} %reshape.167.refs_1_, ...), custom_call_target="tpu_custom_call" | custom-call | tf_op jit(solution)/shard_map/pallas_call | solution.py:197
  29.0 2.3 %collective-permute-start.12 = (bf16[2,1,128,256]{3,2,1,0:T(8,128)(2,1)}, bf16[2,1,128,256]{3,2,1,0:T(8,128)(2,1)S(1)}, u32[]{:S(2)}, u32[]{:S(2)}) collective-permute-start(bf16[2,1,128,256]{3,2,1,0:T(8,128)(2,1)} %bitcast.124), channel_id=1, source_target_pairs={{0,2},{2,4},{4,6},{6,0},{8,10},{10,12},{12,14},{14,8},{1,3},{3,5},... | collective-permute-start | bytes 393224 | tf_op jit(solution)/shard_map/ppermute | solution.py:202
  33.4 2.2 %collective-permute-start.1 = (bf16[2,128,256]{2,1,0:T(8,128)(2,1)S(1)}, bf16[2,128,256]{2,1,0:T(8,128)(2,1)S(1)}, u32[]{:S(2)}, u32[]{:S(2)}) collective-permute-start(bf16[2,128,256]{2,1,0:T(8,128)(2,1)S(1)} %pad_maximum_fusion.1), channel_id=1, source_target_pairs={{0,2},{2,4},{4,6},{6,0},{8,10},{10,12},{12,14},{14,8},{1,3},{3,5},... | collective-permute-start | bytes 393224 | tf_op jit(solution)/shard_map/ppermute | solution.py:159
  37.9 2.4 %collective-permute-start.3 = (bf16[2,128,256]{2,1,0:T(8,128)(2,1)S(1)}, bf16[2,128,256]{2,1,0:T(8,128)(2,1)S(1)}, u32[]{:S(2)}, u32[]{:S(2)}) collective-permute-start(bf16[2,128,256]{2,1,0:T(8,128)(2,1)S(1)} %pad_maximum_fusion.1), channel_id=1, source_target_pairs={{0,6},{2,0},{4,2},{6,4},{8,14},{10,8},{12,10},{14,12},{1,7},{3,1},... | collective-permute-start | bytes 393224 | tf_op jit(solution)/shard_map/ppermute | solution.py:159
  40.3 5.8 %collective-permute-done.14 = bf16[2,1,128,256]{3,2,1,0:T(8,128)(2,1)S(1)} collective-permute-done((bf16[2,1,128,256]{3,2,1,0:T(8,128)(2,1)}, bf16[2,1,128,256]{3,2,1,0:T(8,128)(2,1)S(1)}, u32[]{:S(2)}, u32[]{:S(2)}) %collective-permute-start.14) | collective-permute-done | bytes 131104 | tf_op jit(solution)/shard_map/ppermute | solution.py:202
  46.6 2.3 %collective-permute-start.7 = (bf16[2,128,512]{2,1,0:T(8,128)(2,1)S(1)}, bf16[2,128,512]{2,1,0:T(8,128)(2,1)S(1)}, u32[]{:S(2)}, u32[]{:S(2)}) collective-permute-start(bf16[2,128,512]{2,1,0:T(8,128)(2,1)S(1)} %pad_maximum_fusion), channel_id=1, source_target_pairs={{0,6},{2,0},{4,2},{6,4},{8,14},{10,8},{12,10},{14,12},{1,7},{3,1},... | collective-permute-start | bytes 786440 | tf_op jit(solution)/shard_map/ppermute | solution.py:159
  49.0 6.2 %collective-permute-done.6 = bf16[2,128,512]{2,1,0:T(8,128)(2,1)S(1)} collective-permute-done((bf16[2,128,512]{2,1,0:T(8,128)(2,1)S(1)}, bf16[2,128,512]{2,1,0:T(8,128)(2,1)S(1)}, u32[]{:S(2)}, u32[]{:S(2)}) %collective-permute-start.6) | collective-permute-done | bytes 262176 | tf_op jit(solution)/shard_map/ppermute | solution.py:159
  55.1 1.6 %collective-permute-start.15 = (bf16[1,128,256]{2,1,0:T(8,128)(2,1)S(1)}, bf16[1,128,256]{2,1,0:T(8,128)(2,1)S(1)}, u32[]{:S(2)}, u32[]{:S(2)}) collective-permute-start(bf16[1,128,256]{2,1,0:T(8,128)(2,1)S(1)} %fusion.11), channel_id=1, source_target_pairs={{0,8},{2,10},{4,12},{6,14},{8,0},{10,2},{12,4},{14,6},{1,9},{3,11}... | collective-permute-start | bytes 196616 | tf_op jit(solution)/shard_map/ppermute | solution.py:205
  57.4 8.4 %shard_map.94 = (bf16[128,4096]{1,0:T(8,128)(2,1)}, bf16[128,4096]{1,0:T(8,128)(2,1)}, f32[2,2,2,64,256]{4,3,2,1,0:T(8,128)}, bf16[2,2,2,64,256]{4,3,2,1,0:T(8,1...) custom-call(s32[34]{0:T(128)} %concatenate.20.refs_0_, ...), custom_call_target="tpu_custom_call", output_to_operand_aliasing={{0}: (12, {}), {1}: (13, {})} | custom-call | tf_op jit(solution)/shard_map/pallas_call | solution.py:197
  65.8 2.7 %collective-permute-start.16 = (bf16[2,2,128,256]{3,2,1,0:T(8,128)(2,1)}, bf16[2,2,128,256]{3,2,1,0:T(8,128)(2,1)S(1)}, u32[]{:S(2)}, u32[]{:S(2)}) collective-permute-start(bf16[2,2,128,256]{3,2,1,0:T(8,128)(2,1)} %bitcast.121), channel_id=1, source_target_pairs={{0,2},{2,4},{4,6},{6,0},{8,10},{10,12},{12,14},{14,8},{1,3},{3,5},... | collective-permute-start | bytes 786440 | tf_op jit(solution)/shard_map/ppermute | solution.py:202
  69.3 5.6 %shard_map.95 = (bf16[128,4096]{1,0:T(8,128)(2,1)}, bf16[128,4096]{1,0:T(8,128)(2,1)}, f32[2,1,2,64,256]{4,3,2,1,0:T(8,128)}, bf16[2,1,2,64,256]{4,3,2,1,0:T(8,1...) custom-call(s32[34]{0:T(128)} %concatenate.20.refs_0_, ...), custom_call_target="tpu_custom_call", output_to_operand_aliasing={{0}: (12, {}), {1}: (13, {})} | custom-call | tf_op jit(solution)/shard_map/pallas_call | solution.py:197
  75.9 2.0 %collective-permute-start.21 = (bf16[2,1,128,256]{3,2,0,1:T(8,128)(2,1)}, bf16[2,1,128,256]{3,2,0,1:T(8,128)(2,1)S(1)}, u32[]{:S(2)}, u32[]{:S(2)}) collective-permute-start(bf16[2,1,128,256]{3,2,0,1:T(8,128)(2,1)} %bitcast.126), channel_id=1, source_target_pairs={{0,4},{2,6},{4,0},{6,2},{8,12},{10,14},{12,8},{14,10},{1,5},{3,7},... | collective-permute-start | bytes 393224 | tf_op jit(solution)/shard_map/ppermute | solution.py:202
  77.9 2.0 %collective-permute-start.22 = (bf16[2,1,128,256]{3,2,0,1:T(8,128)(2,1)}, bf16[2,1,128,256]{3,2,0,1:T(8,128)(2,1)S(1)}, u32[]{:S(2)}, u32[]{:S(2)}) collective-permute-start(bf16[2,1,128,256]{3,2,0,1:T(8,128)(2,1)} %bitcast.125), channel_id=1, source_target_pairs={{0,6},{2,0},{4,2},{6,4},{8,14},{10,8},{12,10},{14,12},{1,7},{3,1},... | collective-permute-start | bytes 393224 | tf_op jit(solution)/shard_map/ppermute | solution.py:202
  79.9 2.6 %collective-permute-done.20 = bf16[2,1,128,256]{3,2,0,1:T(8,128)(2,1)S(1)} collective-permute-done((bf16[2,1,128,256]{3,2,0,1:T(8,128)(2,1)}, bf16[2,1,128,256]{3,2,0,1:T(8,128)(2,1)S(1)}, u32[]{:S(2)}, u32[]{:S(2)}) %collective-permute-start.20) | collective-permute-done | bytes 131104 | tf_op jit(solution)/shard_map/ppermute | solution.py:202
  82.5 1.7 %collective-permute-start.18 = (bf16[2,2,128,256]{3,2,1,0:T(8,128)(2,1)S(1)}, bf16[2,2,128,256]{3,2,1,0:T(8,128)(2,1)S(1)}, u32[]{:S(2)}, u32[]{:S(2)}) collective-permute-start(bf16[2,2,128,256]{3,2,1,0:T(8,128)(2,1)S(1)} %bitcast.119), channel_id=1, source_target_pairs={{0,6},{2,0},{4,2},{6,4},{8,14},{10,8},{12,10},{14,12},{1,7},{3,1},... | collective-permute-start | bytes 786440 | tf_op jit(solution)/shard_map/ppermute | solution.py:202
  84.7 3.2 %collective-permute-start.23 = (bf16[1,128,256]{2,1,0:T(8,128)(2,1)S(1)}, bf16[1,128,256]{2,1,0:T(8,128)(2,1)S(1)}, u32[]{:S(2)}, u32[]{:S(2)}) collective-permute-start(bf16[1,128,256]{2,1,0:T(8,128)(2,1)S(1)} %fusion.12), channel_id=1, source_target_pairs={{0,8},{2,10},{4,12},{6,14},{8,0},{10,2},{12,4},{14,6},{1,9},{3,11}... | collective-permute-start | bytes 196616 | tf_op jit(solution)/shard_map/ppermute | solution.py:205
  88.0 2.3 %collective-permute-done.23 = bf16[1,128,256]{2,1,0:T(8,128)(2,1)S(1)} collective-permute-done((bf16[1,128,256]{2,1,0:T(8,128)(2,1)S(1)}, bf16[1,128,256]{2,1,0:T(8,128)(2,1)S(1)}, u32[]{:S(2)}, u32[]{:S(2)}) %collective-permute-start.23) | collective-permute-done | bytes 65568 | tf_op jit(solution)/shard_map/ppermute | solution.py:205
  90.5 3.5 %collective-permute-start.19 = (bf16[2,128,256]{2,1,0:T(8,128)(2,1)S(1)}, bf16[2,128,256]{2,1,0:T(8,128)(2,1)S(1)}, u32[]{:S(2)}, u32[]{:S(2)}) collective-permute-start(bf16[2,128,256]{2,1,0:T(8,128)(2,1)S(1)} %fusion.6), channel_id=1, source_target_pairs={{0,8},{2,10},{4,12},{6,14},{8,0},{10,2},{12,4},{14,6},{1,9},{3,11}... | collective-permute-start | bytes 393224 | tf_op jit(solution)/shard_map/ppermute | solution.py:205
  94.0 4.3 %collective-permute-done.19 = bf16[2,128,256]{2,1,0:T(8,128)(2,1)S(1)} collective-permute-done((bf16[2,128,256]{2,1,0:T(8,128)(2,1)S(1)}, bf16[2,128,256]{2,1,0:T(8,128)(2,1)S(1)}, u32[]{:S(2)}, u32[]{:S(2)}) %collective-permute-start.19) | collective-permute-done | bytes 131104 | tf_op jit(solution)/shard_map/ppermute | solution.py:205
  (97 shorter events, 17.5 us)
Async XLA Ops:
  1.5 10.8 %collective-permute-start.8 = (bf16[128,256]{1,0:T(8,128)(2,1)S(1)}, bf16[128,256]{1,0:T(8,128)(2,1)S(1)}, u32[]{:S(2)}, u32[]{:S(2)}) collective-permute-start(bf16[128,256]{1,0:T(8,128)(2,1)S(1)} %get-tuple-element.57), channel_id=1, source_target_pairs={{0,8},{2,10},{4,12},{6,14},{8,0},{10,2},{12,4},{14,6},{1,9},{3,11}... | collective-permute-start | bytes 196616 | tf_op jit(solution)/shard_map/ppermute | solution.py:156
  6.5 26.3 %collective-permute-start.4 = (bf16[128,512]{1,0:T(8,128)(2,1)S(1)}, bf16[128,512]{1,0:T(8,128)(2,1)S(1)}, u32[]{:S(2)}, u32[]{:S(2)}) collective-permute-start(bf16[128,512]{1,0:T(8,128)(2,1)S(1)} %get-tuple-element.51), channel_id=1, source_target_pairs={{0,8},{2,10},{4,12},{6,14},{8,0},{10,2},{12,4},{14,6},{1,9},{3,11}... | collective-permute-start | bytes 393224 | tf_op jit(solution)/shard_map/ppermute | solution.py:156
  6.6 26.8 %collective-permute-start = (bf16[128,256]{1,0:T(8,128)(2,1)S(1)}, bf16[128,256]{1,0:T(8,128)(2,1)S(1)}, u32[]{:S(2)}, u32[]{:S(2)}) collective-permute-start(bf16[128,256]{1,0:T(8,128)(2,1)S(1)} %get-tuple-element.59), channel_id=1, source_target_pairs={{0,8},{2,10},{4,12},{6,14},{8,0},{10,2},{12,4},{14,6},{1,9},{3,11}... | collective-permute-start | bytes 196616 | tf_op jit(solution)/shard_map/ppermute | solution.py:156
  12.3 9.7 %collective-permute-start.9 = (bf16[2,128,256]{2,1,0:T(8,128)(2,1)S(1)}, bf16[2,128,256]{2,1,0:T(8,128)(2,1)S(1)}, u32[]{:S(2)}, u32[]{:S(2)}) collective-permute-start(bf16[2,128,256]{2,1,0:T(8,128)(2,1)S(1)} %pad_maximum_fusion.3), channel_id=1, source_target_pairs={{0,2},{2,4},{4,6},{6,0},{8,10},{10,12},{12,14},{14,8},{1,3},{3,5},... | collective-permute-start | bytes 393224 | tf_op jit(solution)/shard_map/ppermute | solution.py:159
  13.8 8.1 %collective-permute-start.10 = (bf16[2,128,256]{2,1,0:T(8,128)(2,1)S(1)}, bf16[2,128,256]{2,1,0:T(8,128)(2,1)S(1)}, u32[]{:S(2)}, u32[]{:S(2)}) collective-permute-start(bf16[2,128,256]{2,1,0:T(8,128)(2,1)S(1)} %pad_maximum_fusion.3), channel_id=1, source_target_pairs={{0,4},{2,6},{4,0},{6,2},{8,12},{10,14},{12,8},{14,10},{1,5},{3,7},... | collective-permute-start | bytes 393224 | tf_op jit(solution)/shard_map/ppermute | solution.py:159
  15.9 7.0 %collective-permute-start.11 = (bf16[2,128,256]{2,1,0:T(8,128)(2,1)S(1)}, bf16[2,128,256]{2,1,0:T(8,128)(2,1)S(1)}, u32[]{:S(2)}, u32[]{:S(2)}) collective-permute-start(bf16[2,128,256]{2,1,0:T(8,128)(2,1)S(1)} %pad_maximum_fusion.3), channel_id=1, source_target_pairs={{0,6},{2,0},{4,2},{6,4},{8,14},{10,8},{12,10},{14,12},{1,7},{3,1},... | collective-permute-start | bytes 393224 | tf_op jit(solution)/shard_map/ppermute | solution.py:159
  29.0 7.6 %collective-permute-start.12 = (bf16[2,1,128,256]{3,2,1,0:T(8,128)(2,1)}, bf16[2,1,128,256]{3,2,1,0:T(8,128)(2,1)S(1)}, u32[]{:S(2)}, u32[]{:S(2)}) collective-permute-start(bf16[2,1,128,256]{3,2,1,0:T(8,128)(2,1)} %bitcast.124), channel_id=1, source_target_pairs={{0,2},{2,4},{4,6},{6,0},{8,10},{10,12},{12,14},{14,8},{1,3},{3,5},... | collective-permute-start | bytes 393224 | tf_op jit(solution)/shard_map/ppermute | solution.py:202
  31.3 6.6 %collective-permute-start.13 = (bf16[2,1,128,256]{3,2,1,0:T(8,128)(2,1)}, bf16[2,1,128,256]{3,2,1,0:T(8,128)(2,1)S(1)}, u32[]{:S(2)}, u32[]{:S(2)}) collective-permute-start(bf16[2,1,128,256]{3,2,1,0:T(8,128)(2,1)} %bitcast.123), channel_id=1, source_target_pairs={{0,4},{2,6},{4,0},{6,2},{8,12},{10,14},{12,8},{14,10},{1,5},{3,7},... | collective-permute-start | bytes 393224 | tf_op jit(solution)/shard_map/ppermute | solution.py:202
  31.3 14.9 %collective-permute-start.14 = (bf16[2,1,128,256]{3,2,1,0:T(8,128)(2,1)}, bf16[2,1,128,256]{3,2,1,0:T(8,128)(2,1)S(1)}, u32[]{:S(2)}, u32[]{:S(2)}) collective-permute-start(bf16[2,1,128,256]{3,2,1,0:T(8,128)(2,1)} %bitcast.122), channel_id=1, source_target_pairs={{0,6},{2,0},{4,2},{6,4},{8,14},{10,8},{12,10},{14,12},{1,7},{3,1},... | collective-permute-start | bytes 393224 | tf_op jit(solution)/shard_map/ppermute | solution.py:202
  32.9 13.7 %collective-permute-start.5 = (bf16[2,128,512]{2,1,0:T(8,128)(2,1)S(1)}, bf16[2,128,512]{2,1,0:T(8,128)(2,1)S(1)}, u32[]{:S(2)}, u32[]{:S(2)}) collective-permute-start(bf16[2,128,512]{2,1,0:T(8,128)(2,1)S(1)} %pad_maximum_fusion), channel_id=1, source_target_pairs={{0,2},{2,4},{4,6},{6,0},{8,10},{10,12},{12,14},{14,8},{1,3},{3,5},... | collective-permute-start | bytes 786440 | tf_op jit(solution)/shard_map/ppermute | solution.py:159
  33.4 35.1 %collective-permute-start.1 = (bf16[2,128,256]{2,1,0:T(8,128)(2,1)S(1)}, bf16[2,128,256]{2,1,0:T(8,128)(2,1)S(1)}, u32[]{:S(2)}, u32[]{:S(2)}) collective-permute-start(bf16[2,128,256]{2,1,0:T(8,128)(2,1)S(1)} %pad_maximum_fusion.1), channel_id=1, source_target_pairs={{0,2},{2,4},{4,6},{6,0},{8,10},{10,12},{12,14},{14,8},{1,3},{3,5},... | collective-permute-start | bytes 393224 | tf_op jit(solution)/shard_map/ppermute | solution.py:159
  36.6 31.9 %collective-permute-start.2 = (bf16[2,128,256]{2,1,0:T(8,128)(2,1)S(1)}, bf16[2,128,256]{2,1,0:T(8,128)(2,1)S(1)}, u32[]{:S(2)}, u32[]{:S(2)}) collective-permute-start(bf16[2,128,256]{2,1,0:T(8,128)(2,1)S(1)} %pad_maximum_fusion.1), channel_id=1, source_target_pairs={{0,4},{2,6},{4,0},{6,2},{8,12},{10,14},{12,8},{14,10},{1,5},{3,7},... | collective-permute-start | bytes 393224 | tf_op jit(solution)/shard_map/ppermute | solution.py:159
  37.9 30.7 %collective-permute-start.3 = (bf16[2,128,256]{2,1,0:T(8,128)(2,1)S(1)}, bf16[2,128,256]{2,1,0:T(8,128)(2,1)S(1)}, u32[]{:S(2)}, u32[]{:S(2)}) collective-permute-start(bf16[2,128,256]{2,1,0:T(8,128)(2,1)S(1)} %pad_maximum_fusion.1), channel_id=1, source_target_pairs={{0,6},{2,0},{4,2},{6,4},{8,14},{10,8},{12,10},{14,12},{1,7},{3,1},... | collective-permute-start | bytes 393224 | tf_op jit(solution)/shard_map/ppermute | solution.py:159
  46.2 9.0 %collective-permute-start.6 = (bf16[2,128,512]{2,1,0:T(8,128)(2,1)S(1)}, bf16[2,128,512]{2,1,0:T(8,128)(2,1)S(1)}, u32[]{:S(2)}, u32[]{:S(2)}) collective-permute-start(bf16[2,128,512]{2,1,0:T(8,128)(2,1)S(1)} %pad_maximum_fusion), channel_id=1, source_target_pairs={{0,4},{2,6},{4,0},{6,2},{8,12},{10,14},{12,8},{14,10},{1,5},{3,7},... | collective-permute-start | bytes 786440 | tf_op jit(solution)/shard_map/ppermute | solution.py:159
  46.6 10.1 %collective-permute-start.7 = (bf16[2,128,512]{2,1,0:T(8,128)(2,1)S(1)}, bf16[2,128,512]{2,1,0:T(8,128)(2,1)S(1)}, u32[]{:S(2)}, u32[]{:S(2)}) collective-permute-start(bf16[2,128,512]{2,1,0:T(8,128)(2,1)S(1)} %pad_maximum_fusion), channel_id=1, source_target_pairs={{0,6},{2,0},{4,2},{6,4},{8,14},{10,8},{12,10},{14,12},{1,7},{3,1},... | collective-permute-start | bytes 786440 | tf_op jit(solution)/shard_map/ppermute | solution.py:159
  55.1 22.8 %collective-permute-start.15 = (bf16[1,128,256]{2,1,0:T(8,128)(2,1)S(1)}, bf16[1,128,256]{2,1,0:T(8,128)(2,1)S(1)}, u32[]{:S(2)}, u32[]{:S(2)}) collective-permute-start(bf16[1,128,256]{2,1,0:T(8,128)(2,1)S(1)} %fusion.11), channel_id=1, source_target_pairs={{0,8},{2,10},{4,12},{6,14},{8,0},{10,2},{12,4},{14,6},{1,9},{3,11}... | collective-permute-start | bytes 196616 | tf_op jit(solution)/shard_map/ppermute | solution.py:205
  65.8 24.5 %collective-permute-start.16 = (bf16[2,2,128,256]{3,2,1,0:T(8,128)(2,1)}, bf16[2,2,128,256]{3,2,1,0:T(8,128)(2,1)S(1)}, u32[]{:S(2)}, u32[]{:S(2)}) collective-permute-start(bf16[2,2,128,256]{3,2,1,0:T(8,128)(2,1)} %bitcast.121), channel_id=1, source_target_pairs={{0,2},{2,4},{4,6},{6,0},{8,10},{10,12},{12,14},{14,8},{1,3},{3,5},... | collective-permute-start | bytes 786440 | tf_op jit(solution)/shard_map/ppermute | solution.py:202
  68.5 21.8 %collective-permute-start.17 = (bf16[2,2,128,256]{3,2,1,0:T(8,128)(2,1)}, bf16[2,2,128,256]{3,2,1,0:T(8,128)(2,1)S(1)}, u32[]{:S(2)}, u32[]{:S(2)}) collective-permute-start(bf16[2,2,128,256]{3,2,1,0:T(8,128)(2,1)} %bitcast.120), channel_id=1, source_target_pairs={{0,4},{2,6},{4,0},{6,2},{8,12},{10,14},{12,8},{14,10},{1,5},{3,7},... | collective-permute-start | bytes 786440 | tf_op jit(solution)/shard_map/ppermute | solution.py:202
  74.9 7.6 %collective-permute-start.20 = (bf16[2,1,128,256]{3,2,0,1:T(8,128)(2,1)}, bf16[2,1,128,256]{3,2,0,1:T(8,128)(2,1)S(1)}, u32[]{:S(2)}, u32[]{:S(2)}) collective-permute-start(bf16[2,1,128,256]{3,2,0,1:T(8,128)(2,1)} %bitcast.127), channel_id=1, source_target_pairs={{0,2},{2,4},{4,6},{6,0},{8,10},{10,12},{12,14},{14,8},{1,3},{3,5},... | collective-permute-start | bytes 393224 | tf_op jit(solution)/shard_map/ppermute | solution.py:202
  75.9 8.3 %collective-permute-start.21 = (bf16[2,1,128,256]{3,2,0,1:T(8,128)(2,1)}, bf16[2,1,128,256]{3,2,0,1:T(8,128)(2,1)S(1)}, u32[]{:S(2)}, u32[]{:S(2)}) collective-permute-start(bf16[2,1,128,256]{3,2,0,1:T(8,128)(2,1)} %bitcast.126), channel_id=1, source_target_pairs={{0,4},{2,6},{4,0},{6,2},{8,12},{10,14},{12,8},{14,10},{1,5},{3,7},... | collective-permute-start | bytes 393224 | tf_op jit(solution)/shard_map/ppermute | solution.py:202
  77.9 6.8 %collective-permute-start.22 = (bf16[2,1,128,256]{3,2,0,1:T(8,128)(2,1)}, bf16[2,1,128,256]{3,2,0,1:T(8,128)(2,1)S(1)}, u32[]{:S(2)}, u32[]{:S(2)}) collective-permute-start(bf16[2,1,128,256]{3,2,0,1:T(8,128)(2,1)} %bitcast.125), channel_id=1, source_target_pairs={{0,6},{2,0},{4,2},{6,4},{8,14},{10,8},{12,10},{14,12},{1,7},{3,1},... | collective-permute-start | bytes 393224 | tf_op jit(solution)/shard_map/ppermute | solution.py:202
  82.5 7.9 %collective-permute-start.18 = (bf16[2,2,128,256]{3,2,1,0:T(8,128)(2,1)S(1)}, bf16[2,2,128,256]{3,2,1,0:T(8,128)(2,1)S(1)}, u32[]{:S(2)}, u32[]{:S(2)}) collective-permute-start(bf16[2,2,128,256]{3,2,1,0:T(8,128)(2,1)S(1)} %bitcast.119), channel_id=1, source_target_pairs={{0,6},{2,0},{4,2},{6,4},{8,14},{10,8},{12,10},{14,12},{1,7},{3,1},... | collective-permute-start | bytes 786440 | tf_op jit(solution)/shard_map/ppermute | solution.py:202
  84.7 5.5 %collective-permute-start.23 = (bf16[1,128,256]{2,1,0:T(8,128)(2,1)S(1)}, bf16[1,128,256]{2,1,0:T(8,128)(2,1)S(1)}, u32[]{:S(2)}, u32[]{:S(2)}) collective-permute-start(bf16[1,128,256]{2,1,0:T(8,128)(2,1)S(1)} %fusion.12), channel_id=1, source_target_pairs={{0,8},{2,10},{4,12},{6,14},{8,0},{10,2},{12,4},{14,6},{1,9},{3,11}... | collective-permute-start | bytes 196616 | tf_op jit(solution)/shard_map/ppermute | solution.py:205
  90.5 7.9 %collective-permute-start.19 = (bf16[2,128,256]{2,1,0:T(8,128)(2,1)S(1)}, bf16[2,128,256]{2,1,0:T(8,128)(2,1)S(1)}, u32[]{:S(2)}, u32[]{:S(2)}) collective-permute-start(bf16[2,128,256]{2,1,0:T(8,128)(2,1)S(1)} %fusion.6), channel_id=1, source_target_pairs={{0,8},{2,10},{4,12},{6,14},{8,0},{10,2},{12,4},{14,6},{1,9},{3,11}... | collective-permute-start | bytes 393224 | tf_op jit(solution)/shard_map/ppermute | solution.py:205
  (20 other events, 99.2 us)

commit v10 on v8

--- a/solution.py
+++ b/solution.py
@@ -148,15 +148,24 @@
     query_grad = None
     key_grads = []
     value_grads = []
+    chunk_boths = []
     for chunk in range(chunks):
         cols = slice(chunk * chunk_cols, (chunk + 1) * chunk_cols)
         pair = jnp.concatenate([key_rows[:, cols], value_rows[:, cols]], axis=1)
-        both = jnp.stack([pair, lax.ppermute(pair, "ctx", cross_pairs())])
+        chunk_boths.append(jnp.stack([pair, lax.ppermute(pair, "ctx", cross_pairs())]))
+    gathered = []
+    for chunk in range(chunks):
+        both = chunk_boths[chunk]
         pieces = [both]
         for shift in range(1, half):
             pieces.append(lax.ppermute(both, "ctx", half_pairs(shift)))
-        pieces = [piece.reshape(2 * tiles, SPAN, 2 * chunk_cols) for piece in pieces]
-
+        gathered.append([piece.reshape(2 * tiles, SPAN, 2 * chunk_cols) for piece in pieces])
+        if chunk + 1 < chunks:
+            gathered[chunk], chunk_boths[chunk + 1] = lax.optimization_barrier(
+                (gathered[chunk], chunk_boths[chunk + 1]))
+
+    for chunk in range(chunks):
+        pieces = gathered[chunk]
         aliased = chunk > 0
         head0 = chunk * chunk_heads
         in_specs = [

time: 78.3 us -> 98.7 us (1.26)
  waiting for transfers between devices: 27.5 us -> 46.4 us
  other arithmetic: 2.07 us -> 3.11 us
    ppermute x6, waiting for transfers between devices: 6.69 us -> 17.8 us  [local(): lax.ppermute(send_packs[shift - 1].reshape(pack_shape), 'ctx', half_pairs...]
    ppermute x6, waiting for transfers between devices: 7.7 us -> 16.4 us  [local(): pieces.append(lax.ppermute(both, 'ctx', half_pairs(shift)))]
    ppermute x2, waiting for transfers between devices: 8.66 us -> 7.22 us  [local(): lax.ppermute(pair, 'ctx', cross_pairs())]
    add x2, other arithmetic: 0.22 us -> 1.26 us  [local(): summed + lax.ppermute(send_packs[shift - 1].reshape(pack_shape), 'ctx', h...]
    unnamed x24 -> x22, local copies, waits for them, and re-layouts: 2.82 us -> 2.89 us
  transfers between devices with their start and end apart: 16 -> 16, of which waited for: 5 -> 10; matrix products, arithmetic and copies ran while one was open for 3% -> 3% of each run, Pallas kernels for 22% -> 9%
where the time goes in v10:
time: 98.7 us; the launch traced here: 98.4 us
  waiting for transfers between devices  46.4 us (47%)
  starting transfers between devices  25.7 us (26%)
  Pallas kernels  16.7 us (17%)
  local copies, waits for them, and re-layouts  5.62 us (6%)
  other arithmetic  3.11 us (3%)
    ppermute x6, waiting for transfers between devices, local(): lax.ppermute(send_packs[shift - 1].reshape(pack_shape), 'ctx', half_pairs...  17.8 us
    pallas_call x2, Pallas kernels, local(): attended, query_grad, own_pack, *send_packs = kernel(*operands)  16.7 us
    ppermute x6, waiting for transfers between devices, local(): pieces.append(lax.ppermute(both, 'ctx', half_pairs(shift)))  16.4 us
    ppermute x6, starting transfers between devices, local(): lax.ppermute(send_packs[shift - 1].reshape(pack_shape), 'ctx', half_pairs...  7.57 us
    ppermute x2, starting transfers between devices, local(): lax.ppermute(summed[1].astype(jnp.bfloat16), 'ctx', cross_pairs())  7.36 us
    ppermute x2, waiting for transfers between devices, local(): lax.ppermute(pair, 'ctx', cross_pairs())  7.22 us
    ppermute x6, starting transfers between devices, local(): pieces.append(lax.ppermute(both, 'ctx', half_pairs(shift)))  6.57 us
    ppermute x2, waiting for transfers between devices, local(): lax.ppermute(summed[1].astype(jnp.bfloat16), 'ctx', cross_pairs())  5 us
  transfers between devices with their start and end apart: 16, of which 10 were waited for; matrix products, arithmetic and copies ran while one was open for 3% of the time, Pallas kernels for 9%

profile of v10, /device:TPU:0, one launch (start us, length us, event | category | flops | bytes accessed | tf_op | source)
XLA Modules:
  0.0 98.4 jit_solution(10653023434516758357)
XLA Ops:
  0.6 1.0 fusion.18
  1.6 4.1 %collective-permute-start = (bf16[128,512]{1,0:T(8,128)(2,1)S(1)}, bf16[128,512]{1,0:T(8,128)(2,1)S(1)}, u32[]{:S(2)}, u32[]{:S(2)}) collective-permute-start(bf16[128,512]{1,0:T(8,128)(2,1)S(1)} %get-tuple-element.53), channel_id=1, source_target_pairs={{0,8},{2,10},{4,12},{6,14},{8,0},{10,2},{12,4},{14,6},{1,9},{3,11}... | collective-permute-start | bytes 393224 | tf_op jit(solution)/shard_map/ppermute | solution.py:155
  7.6 0.8 reshape.110.refs_1_
  8.4 7.2 %collective-permute-done = bf16[128,512]{1,0:T(8,128)(2,1)S(1)} collective-permute-done((bf16[128,512]{1,0:T(8,128)(2,1)S(1)}, bf16[128,512]{1,0:T(8,128)(2,1)S(1)}, u32[]{:S(2)}, u32[]{:S(2)}) %collective-permute-start) | collective-permute-done | bytes 131104 | tf_op jit(solution)/shard_map/ppermute | solution.py:155
  15.7 1.9 %collective-permute-start.1 = (bf16[2,128,512]{2,1,0:T(8,128)(2,1)S(1)}, bf16[2,128,512]{2,1,0:T(8,128)(2,1)S(1)}, u32[]{:S(2)}, u32[]{:S(2)}) collective-permute-start(bf16[2,128,512]{2,1,0:T(8,128)(2,1)S(1)} %pad_maximum_fusion), channel_id=1, source_target_pairs={{0,2},{2,4},{4,6},{6,0},{8,10},{10,12},{12,14},{14,8},{1,3},{3,5},... | collective-permute-start | bytes 786440 | tf_op jit(solution)/shard_map/ppermute | solution.py:161
  17.6 1.5 %collective-permute-start.3 = (bf16[2,128,512]{2,1,0:T(8,128)(2,1)S(1)}, bf16[2,128,512]{2,1,0:T(8,128)(2,1)S(1)}, u32[]{:S(2)}, u32[]{:S(2)}) collective-permute-start(bf16[2,128,512]{2,1,0:T(8,128)(2,1)S(1)} %pad_maximum_fusion), channel_id=1, source_target_pairs={{0,6},{2,0},{4,2},{6,4},{8,14},{10,8},{12,10},{14,12},{1,7},{3,1},... | collective-permute-start | bytes 786440 | tf_op jit(solution)/shard_map/ppermute | solution.py:161
  19.9 6.0 %collective-permute-done.1 = bf16[2,128,512]{2,1,0:T(8,128)(2,1)S(1)} collective-permute-done((bf16[2,128,512]{2,1,0:T(8,128)(2,1)S(1)}, bf16[2,128,512]{2,1,0:T(8,128)(2,1)S(1)}, u32[]{:S(2)}, u32[]{:S(2)}) %collective-permute-start.1) | collective-permute-done | bytes 262176 | tf_op jit(solution)/shard_map/ppermute | solution.py:161
  26.2 3.7 %collective-permute-done.3 = bf16[2,128,512]{2,1,0:T(8,128)(2,1)S(1)} collective-permute-done((bf16[2,128,512]{2,1,0:T(8,128)(2,1)S(1)}, bf16[2,128,512]{2,1,0:T(8,128)(2,1)S(1)}, u32[]{:S(2)}, u32[]{:S(2)}) %collective-permute-start.3) | collective-permute-done | bytes 262176 | tf_op jit(solution)/shard_map/ppermute | solution.py:161
  29.9 0.7 copy-done.7
  30.6 8.4 %shard_map.93 = (bf16[128,4096]{1,0:T(8,128)(2,1)}, bf16[128,4096]{1,0:T(8,128)(2,1)}, f32[2,2,2,64,256]{4,3,2,1,0:T(8,128)}, bf16[2,2,2,64,256]{4,3,2,1,0:T(8,1...) custom-call(s32[34]{0:T(128)} %concatenate.17.refs_0_, s32[2,64,1]{2,1,0:T(8,128)} %reshape.110.refs_1_, ...), custom_call_target="tpu_custom_call" | custom-call | tf_op jit(solution)/shard_map/pallas_call | solution.py:205
  39.0 1.8 %collective-permute-start.10 = (bf16[2,2,128,256]{3,2,1,0:T(8,128)(2,1)}, bf16[2,2,128,256]{3,2,1,0:T(8,128)(2,1)S(1)}, u32[]{:S(2)}, u32[]{:S(2)}) collective-permute-start(bf16[2,2,128,256]{3,2,1,0:T(8,128)(2,1)} %bitcast.85), channel_id=1, source_target_pairs={{0,6},{2,0},{4,2},{6,4},{8,14},{10,8},{12,10},{14,12},{1,7},{3,1},... | collective-permute-start | bytes 786440 | tf_op jit(solution)/shard_map/ppermute | solution.py:210
  41.6 2.7 %collective-permute-start.5 = (bf16[2,128,512]{2,1,0:T(8,128)(2,1)S(1)}, bf16[2,128,512]{2,1,0:T(8,128)(2,1)S(1)}, u32[]{:S(2)}, u32[]{:S(2)}) collective-permute-start(bf16[2,128,512]{2,1,0:T(8,128)(2,1)S(1)} %pad_maximum_fusion.1), channel_id=1, source_target_pairs={{0,2},{2,4},{4,6},{6,0},{8,10},{10,12},{12,14},{14,8},{1,3},{3,5},... | collective-permute-start | bytes 786440 | tf_op jit(solution)/shard_map/ppermute | solution.py:161
  44.7 10.1 %collective-permute-done.10 = bf16[2,2,128,256]{3,2,1,0:T(8,128)(2,1)S(1)} collective-permute-done((bf16[2,2,128,256]{3,2,1,0:T(8,128)(2,1)}, bf16[2,2,128,256]{3,2,1,0:T(8,128)(2,1)S(1)}, u32[]{:S(2)}, u32[]{:S(2)}) %collective-permute-start.10) | collective-permute-done | bytes 262176 | tf_op jit(solution)/shard_map/ppermute | solution.py:210
  54.8 1.1 %fusion.3 = f32[2,2,128,256]{3,2,1,0:T(8,128)S(1)} fusion(f32[2,2,2,64,256]{4,3,2,1,0:T(8,128)} %get-tuple-element.30, bf16[2,2,128,256]{3,2,1,0:T(8,128)(2,1)S(1)} %collective-permute-done.10, bf16[2,2,128,256]{3,2,1,0:T(8,128)(2,1)S(1)} %collective-permute-done.9, bf16[2,2,128,256]{3,2,1,0:T(8,128)(2,1)S(1)} %collective-permute-done.8), kind=kLoop, calls=%fused_computation.5 | loop fusion | flops 786432 | bytes 1835008 | tf_op jit(solution)/shard_map/add | solution.py:210
  55.9 2.8 %collective-permute-start.11 = (bf16[2,128,256]{2,1,0:T(8,128)(2,1)S(1)}, bf16[2,128,256]{2,1,0:T(8,128)(2,1)S(1)}, u32[]{:S(2)}, u32[]{:S(2)}) collective-permute-start(bf16[2,128,256]{2,1,0:T(8,128)(2,1)S(1)} %fusion.8), channel_id=1, source_target_pairs={{0,8},{2,10},{4,12},{6,14},{8,0},{10,2},{12,4},{14,6},{1,9},{3,11}... | collective-permute-start | bytes 393224 | tf_op jit(solution)/shard_map/ppermute | solution.py:213
  58.8 6.4 %collective-permute-done.5 = bf16[2,128,512]{2,1,0:T(8,128)(2,1)S(1)} collective-permute-done((bf16[2,128,512]{2,1,0:T(8,128)(2,1)S(1)}, bf16[2,128,512]{2,1,0:T(8,128)(2,1)S(1)}, u32[]{:S(2)}, u32[]{:S(2)}) %collective-permute-start.5) | collective-permute-done | bytes 262176 | tf_op jit(solution)/shard_map/ppermute | solution.py:161
  66.1 8.4 %shard_map.94 = (bf16[128,4096]{1,0:T(8,128)(2,1)}, bf16[128,4096]{1,0:T(8,128)(2,1)}, f32[2,2,2,64,256]{4,3,2,1,0:T(8,128)}, bf16[2,2,2,64,256]{4,3,2,1,0:T(8,1...) custom-call(s32[34]{0:T(128)} %concatenate.17.refs_0_, ...), custom_call_target="tpu_custom_call", output_to_operand_aliasing={{0}: (12, {}), {1}: (13, {})} | custom-call | tf_op jit(solution)/shard_map/pallas_call | solution.py:205
  74.5 3.4 %collective-permute-start.12 = (bf16[2,2,128,256]{3,2,1,0:T(8,128)(2,1)}, bf16[2,2,128,256]{3,2,1,0:T(8,128)(2,1)S(1)}, u32[]{:S(2)}, u32[]{:S(2)}) collective-permute-start(bf16[2,2,128,256]{3,2,1,0:T(8,128)(2,1)} %bitcast.84), channel_id=1, source_target_pairs={{0,2},{2,4},{4,6},{6,0},{8,10},{10,12},{12,14},{14,8},{1,3},{3,5},... | collective-permute-start | bytes 786440 | tf_op jit(solution)/shard_map/ppermute | solution.py:210
  78.0 1.5 %collective-permute-start.14 = (bf16[2,2,128,256]{3,2,1,0:T(8,128)(2,1)}, bf16[2,2,128,256]{3,2,1,0:T(8,128)(2,1)S(1)}, u32[]{:S(2)}, u32[]{:S(2)}) collective-permute-start(bf16[2,2,128,256]{3,2,1,0:T(8,128)(2,1)} %bitcast.81), channel_id=1, source_target_pairs={{0,6},{2,0},{4,2},{6,4},{8,14},{10,8},{12,10},{14,12},{1,7},{3,1},... | collective-permute-start | bytes 786440 | tf_op jit(solution)/shard_map/ppermute | solution.py:210
  79.5 5.5 %collective-permute-done.12 = bf16[2,2,128,256]{3,2,1,0:T(8,128)(2,1)S(1)} collective-permute-done((bf16[2,2,128,256]{3,2,1,0:T(8,128)(2,1)}, bf16[2,2,128,256]{3,2,1,0:T(8,128)(2,1)S(1)}, u32[]{:S(2)}, u32[]{:S(2)}) %collective-permute-start.12) | collective-permute-done | bytes 262176 | tf_op jit(solution)/shard_map/ppermute | solution.py:210
  85.0 1.4 %collective-permute-done.13 = bf16[2,2,128,256]{3,2,1,0:T(8,128)(2,1)S(1)} collective-permute-done((bf16[2,2,128,256]{3,2,1,0:T(8,128)(2,1)}, bf16[2,2,128,256]{3,2,1,0:T(8,128)(2,1)S(1)}, u32[]{:S(2)}, u32[]{:S(2)}) %collective-permute-start.13) | collective-permute-done | bytes 262176 | tf_op jit(solution)/shard_map/ppermute | solution.py:210
  86.4 0.9 collective-permute-done.14
  87.4 4.6 %collective-permute-start.15 = (bf16[2,128,256]{2,1,0:T(8,128)(2,1)S(1)}, bf16[2,128,256]{2,1,0:T(8,128)(2,1)S(1)}, u32[]{:S(2)}, u32[]{:S(2)}) collective-permute-start(bf16[2,128,256]{2,1,0:T(8,128)(2,1)S(1)} %fusion.9), channel_id=1, source_target_pairs={{0,8},{2,10},{4,12},{6,14},{8,0},{10,2},{12,4},{14,6},{1,9},{3,11}... | collective-permute-start | bytes 393224 | tf_op jit(solution)/shard_map/ppermute | solution.py:213
  92.0 5.0 %collective-permute-done.15 = bf16[2,128,256]{2,1,0:T(8,128)(2,1)S(1)} collective-permute-done((bf16[2,128,256]{2,1,0:T(8,128)(2,1)S(1)}, bf16[2,128,256]{2,1,0:T(8,128)(2,1)S(1)}, u32[]{:S(2)}, u32[]{:S(2)}) %collective-permute-start.15) | collective-permute-done | bytes 131104 | tf_op jit(solution)/shard_map/ppermute | solution.py:213
  (56 shorter events, 6.6 us)
Async XLA Ops:
  1.6 14.0 %collective-permute-start = (bf16[128,512]{1,0:T(8,128)(2,1)S(1)}, bf16[128,512]{1,0:T(8,128)(2,1)S(1)}, u32[]{:S(2)}, u32[]{:S(2)}) collective-permute-start(bf16[128,512]{1,0:T(8,128)(2,1)S(1)} %get-tuple-element.53), channel_id=1, source_target_pairs={{0,8},{2,10},{4,12},{6,14},{8,0},{10,2},{12,4},{14,6},{1,9},{3,11}... | collective-permute-start | bytes 393224 | tf_op jit(solution)/shard_map/ppermute | solution.py:155
  5.7 14.1 %collective-permute-start.4 = (bf16[128,512]{1,0:T(8,128)(2,1)S(1)}, bf16[128,512]{1,0:T(8,128)(2,1)S(1)}, u32[]{:S(2)}, u32[]{:S(2)}) collective-permute-start(bf16[128,512]{1,0:T(8,128)(2,1)S(1)} %get-tuple-element.47), channel_id=1, source_target_pairs={{0,8},{2,10},{4,12},{6,14},{8,0},{10,2},{12,4},{14,6},{1,9},{3,11}... | collective-permute-start | bytes 393224 | tf_op jit(solution)/shard_map/ppermute | solution.py:155
  15.7 4.2 %copy-start.1 = (bf16[2,128,512]{2,1,0:T(8,128)(2,1)}, bf16[2,128,512]{2,1,0:T(8,128)(2,1)S(1)}, u32[]{:S(2)}) copy-start(bf16[2,128,512]{2,1,0:T(8,128)(2,1)S(1)} %pad_maximum_fusion) | copy-start | bytes 786436
  15.7 10.2 %collective-permute-start.1 = (bf16[2,128,512]{2,1,0:T(8,128)(2,1)S(1)}, bf16[2,128,512]{2,1,0:T(8,128)(2,1)S(1)}, u32[]{:S(2)}, u32[]{:S(2)}) collective-permute-start(bf16[2,128,512]{2,1,0:T(8,128)(2,1)S(1)} %pad_maximum_fusion), channel_id=1, source_target_pairs={{0,2},{2,4},{4,6},{6,0},{8,10},{10,12},{12,14},{14,8},{1,3},{3,5},... | collective-permute-start | bytes 786440 | tf_op jit(solution)/shard_map/ppermute | solution.py:161
  17.6 8.6 %collective-permute-start.2 = (bf16[2,128,512]{2,1,0:T(8,128)(2,1)S(1)}, bf16[2,128,512]{2,1,0:T(8,128)(2,1)S(1)}, u32[]{:S(2)}, u32[]{:S(2)}) collective-permute-start(bf16[2,128,512]{2,1,0:T(8,128)(2,1)S(1)} %pad_maximum_fusion), channel_id=1, source_target_pairs={{0,4},{2,6},{4,0},{6,2},{8,12},{10,14},{12,8},{14,10},{1,5},{3,7},... | collective-permute-start | bytes 786440 | tf_op jit(solution)/shard_map/ppermute | solution.py:161
  17.6 12.3 %collective-permute-start.3 = (bf16[2,128,512]{2,1,0:T(8,128)(2,1)S(1)}, bf16[2,128,512]{2,1,0:T(8,128)(2,1)S(1)}, u32[]{:S(2)}, u32[]{:S(2)}) collective-permute-start(bf16[2,128,512]{2,1,0:T(8,128)(2,1)S(1)} %pad_maximum_fusion), channel_id=1, source_target_pairs={{0,6},{2,0},{4,2},{6,4},{8,14},{10,8},{12,10},{14,12},{1,7},{3,1},... | collective-permute-start | bytes 786440 | tf_op jit(solution)/shard_map/ppermute | solution.py:161
  19.9 34.8 %copy-start = (bf16[2,128,512]{2,1,0:T(8,128)(2,1)}, bf16[2,128,512]{2,1,0:T(8,128)(2,1)S(1)}, u32[]{:S(2)}) copy-start(bf16[2,128,512]{2,1,0:T(8,128)(2,1)S(1)} %pad_maximum_fusion.1) | copy-start | bytes 786436
  25.9 3.9 %copy-start.4 = (bf16[2,128,512]{2,1,0:T(8,128)(2,1)}, bf16[2,128,512]{2,1,0:T(8,128)(2,1)S(1)}, u32[]{:S(2)}) copy-start(bf16[2,128,512]{2,1,0:T(8,128)(2,1)S(1)} %collective-permute-done.1) | copy-start | bytes 786436
  26.2 3.7 %copy-start.6 = (bf16[2,128,512]{2,1,0:T(8,128)(2,1)}, bf16[2,128,512]{2,1,0:T(8,128)(2,1)S(1)}, u32[]{:S(2)}) copy-start(bf16[2,128,512]{2,1,0:T(8,128)(2,1)S(1)} %collective-permute-done.2) | copy-start | bytes 786436
  29.9 0.7 copy-start.7
  39.0 15.8 %collective-permute-start.10 = (bf16[2,2,128,256]{3,2,1,0:T(8,128)(2,1)}, bf16[2,2,128,256]{3,2,1,0:T(8,128)(2,1)S(1)}, u32[]{:S(2)}, u32[]{:S(2)}) collective-permute-start(bf16[2,2,128,256]{3,2,1,0:T(8,128)(2,1)} %bitcast.85), channel_id=1, source_target_pairs={{0,6},{2,0},{4,2},{6,4},{8,14},{10,8},{12,10},{14,12},{1,7},{3,1},... | collective-permute-start | bytes 786440 | tf_op jit(solution)/shard_map/ppermute | solution.py:210
  40.8 14.0 %collective-permute-start.8 = (bf16[2,2,128,256]{3,2,1,0:T(8,128)(2,1)}, bf16[2,2,128,256]{3,2,1,0:T(8,128)(2,1)S(1)}, u32[]{:S(2)}, u32[]{:S(2)}) collective-permute-start(bf16[2,2,128,256]{3,2,1,0:T(8,128)(2,1)} %bitcast.82), channel_id=1, source_target_pairs={{0,2},{2,4},{4,6},{6,0},{8,10},{10,12},{12,14},{14,8},{1,3},{3,5},... | collective-permute-start | bytes 786440 | tf_op jit(solution)/shard_map/ppermute | solution.py:210
  41.1 13.7 %collective-permute-start.9 = (bf16[2,2,128,256]{3,2,1,0:T(8,128)(2,1)}, bf16[2,2,128,256]{3,2,1,0:T(8,128)(2,1)S(1)}, u32[]{:S(2)}, u32[]{:S(2)}) collective-permute-start(bf16[2,2,128,256]{3,2,1,0:T(8,128)(2,1)} %bitcast.80), channel_id=1, source_target_pairs={{0,4},{2,6},{4,0},{6,2},{8,12},{10,14},{12,8},{14,10},{1,5},{3,7},... | collective-permute-start | bytes 786440 | tf_op jit(solution)/shard_map/ppermute | solution.py:210
  41.6 23.6 %collective-permute-start.5 = (bf16[2,128,512]{2,1,0:T(8,128)(2,1)S(1)}, bf16[2,128,512]{2,1,0:T(8,128)(2,1)S(1)}, u32[]{:S(2)}, u32[]{:S(2)}) collective-permute-start(bf16[2,128,512]{2,1,0:T(8,128)(2,1)S(1)} %pad_maximum_fusion.1), channel_id=1, source_target_pairs={{0,2},{2,4},{4,6},{6,0},{8,10},{10,12},{12,14},{14,8},{1,3},{3,5},... | collective-permute-start | bytes 786440 | tf_op jit(solution)/shard_map/ppermute | solution.py:161
  44.3 20.9 %collective-permute-start.6 = (bf16[2,128,512]{2,1,0:T(8,128)(2,1)S(1)}, bf16[2,128,512]{2,1,0:T(8,128)(2,1)S(1)}, u32[]{:S(2)}, u32[]{:S(2)}) collective-permute-start(bf16[2,128,512]{2,1,0:T(8,128)(2,1)S(1)} %pad_maximum_fusion.1), channel_id=1, source_target_pairs={{0,4},{2,6},{4,0},{6,2},{8,12},{10,14},{12,8},{14,10},{1,5},{3,7},... | collective-permute-start | bytes 786440 | tf_op jit(solution)/shard_map/ppermute | solution.py:161
  54.7 10.5 %collective-permute-start.7 = (bf16[2,128,512]{2,1,0:T(8,128)(2,1)S(1)}, bf16[2,128,512]{2,1,0:T(8,128)(2,1)S(1)}, u32[]{:S(2)}, u32[]{:S(2)}) collective-permute-start(bf16[2,128,512]{2,1,0:T(8,128)(2,1)S(1)} %pad_maximum_fusion.1), channel_id=1, source_target_pairs={{0,6},{2,0},{4,2},{6,4},{8,14},{10,8},{12,10},{14,12},{1,7},{3,1},... | collective-permute-start | bytes 786440 | tf_op jit(solution)/shard_map/ppermute | solution.py:161
  55.9 23.5 %collective-permute-start.11 = (bf16[2,128,256]{2,1,0:T(8,128)(2,1)S(1)}, bf16[2,128,256]{2,1,0:T(8,128)(2,1)S(1)}, u32[]{:S(2)}, u32[]{:S(2)}) collective-permute-start(bf16[2,128,256]{2,1,0:T(8,128)(2,1)S(1)} %fusion.8), channel_id=1, source_target_pairs={{0,8},{2,10},{4,12},{6,14},{8,0},{10,2},{12,4},{14,6},{1,9},{3,11}... | collective-permute-start | bytes 393224 | tf_op jit(solution)/shard_map/ppermute | solution.py:213
  65.2 0.8 copy-start.3
  65.2 0.9 copy-start.5
  74.5 12.8 %copy-start.8 = (f32[2,2,2,64,256]{4,3,2,1,0:T(8,128)S(1)}, f32[2,2,2,64,256]{4,3,2,1,0:T(8,128)}, u32[]{:S(2)}) copy-start(f32[2,2,2,64,256]{4,3,2,1,0:T(8,128)} %get-tuple-element.34) | copy-start | bytes 1572868
  74.5 10.5 %collective-permute-start.12 = (bf16[2,2,128,256]{3,2,1,0:T(8,128)(2,1)}, bf16[2,2,128,256]{3,2,1,0:T(8,128)(2,1)S(1)}, u32[]{:S(2)}, u32[]{:S(2)}) collective-permute-start(bf16[2,2,128,256]{3,2,1,0:T(8,128)(2,1)} %bitcast.84), channel_id=1, source_target_pairs={{0,2},{2,4},{4,6},{6,0},{8,10},{10,12},{12,14},{14,8},{1,3},{3,5},... | collective-permute-start | bytes 786440 | tf_op jit(solution)/shard_map/ppermute | solution.py:210
  77.9 8.4 %collective-permute-start.13 = (bf16[2,2,128,256]{3,2,1,0:T(8,128)(2,1)}, bf16[2,2,128,256]{3,2,1,0:T(8,128)(2,1)S(1)}, u32[]{:S(2)}, u32[]{:S(2)}) collective-permute-start(bf16[2,2,128,256]{3,2,1,0:T(8,128)(2,1)} %bitcast.83), channel_id=1, source_target_pairs={{0,4},{2,6},{4,0},{6,2},{8,12},{10,14},{12,8},{14,10},{1,5},{3,7},... | collective-permute-start | bytes 786440 | tf_op jit(solution)/shard_map/ppermute | solution.py:210
  78.0 9.3 %collective-permute-start.14 = (bf16[2,2,128,256]{3,2,1,0:T(8,128)(2,1)}, bf16[2,2,128,256]{3,2,1,0:T(8,128)(2,1)S(1)}, u32[]{:S(2)}, u32[]{:S(2)}) collective-permute-start(bf16[2,2,128,256]{3,2,1,0:T(8,128)(2,1)} %bitcast.81), channel_id=1, source_target_pairs={{0,6},{2,0},{4,2},{6,4},{8,14},{10,8},{12,10},{14,12},{1,7},{3,1},... | collective-permute-start | bytes 786440 | tf_op jit(solution)/shard_map/ppermute | solution.py:210
  87.4 9.6 %collective-permute-start.15 = (bf16[2,128,256]{2,1,0:T(8,128)(2,1)S(1)}, bf16[2,128,256]{2,1,0:T(8,128)(2,1)S(1)}, u32[]{:S(2)}, u32[]{:S(2)}) collective-permute-start(bf16[2,128,256]{2,1,0:T(8,128)(2,1)S(1)} %fusion.9), channel_id=1, source_target_pairs={{0,8},{2,10},{4,12},{6,14},{8,0},{10,2},{12,4},{14,6},{1,9},{3,11}... | collective-permute-start | bytes 393224 | tf_op jit(solution)/shard_map/ppermute | solution.py:213
  (3 other events, 2.0 us)

commit v11 on v8

--- a/solution.py
+++ b/solution.py
@@ -22,84 +22,80 @@
     out_ref, dq_ref, own_ref = rest[:3]
     send_refs = rest[3:-1]
     buf_ref = rest[-1]
-    tile = pl.program_id(1)
-    base = tile * window_spans
     info = 2 * tiles * window_spans + tiles
-
-    def window_rows(refs):
-        parts = []
+    buf_ref[...] = jnp.zeros(buf_ref.shape, buf_ref.dtype)
+    for tile in range(tiles):
+        rows = slice(tile * SPAN, (tile + 1) * SPAN)
+        base = tile * window_spans
+
+        def window_rows(refs):
+            parts = []
+            for w in range(window_spans):
+                piece = index_ref[base + w]
+                row = index_ref[info + 2 + base + w]
+                part = refs[0][row]
+                for other in range(1, half):
+                    part = jnp.where(piece == other, refs[other][row], part)
+                parts.append(part)
+            return jnp.concatenate(parts, axis=0)
+
+        key_block = window_rows(key_refs)
+        value_block = window_rows(value_refs)
+        query_all = jnp.concatenate(
+            [q_ref[rows, h * DH:(h + 1) * DH] for h in range(group_size)], axis=0)
+        grad_all = jnp.concatenate(
+            [do_ref[rows, h * DH:(h + 1) * DH] for h in range(group_size)], axis=0)
+        span = index_ref[2 * tiles * window_spans + tile]
+        window = window_spans * SPAN
+        row_ids = lax.broadcasted_iota(jnp.int32, (SPAN, window), 0)
+        col_ids = lax.broadcasted_iota(jnp.int32, (SPAN, window), 1)
+        query_pos = span * SPAN + row_ids
+        key_pos = (span - (window_spans - 1)) * SPAN + col_ids
+        visible = (key_pos >= qstart_ref[tile]) & (key_pos <= query_pos)
+        bias = jnp.where(visible, 0.0, -jnp.inf)
+        bias = jnp.concatenate([bias] * group_size, axis=0)
+        contract_last = (((1,), (1,)), ((), ()))
+        contract_first = (((0,), (0,)), ((), ()))
+        scores = lax.dot_general(query_all, key_block, contract_last,
+                                 preferred_element_type=jnp.float32) * score_scale
+        masked = scores + bias
+        row_max = jnp.max(masked, axis=1, keepdims=True)
+        shifted = jnp.exp(masked - row_max)
+        log_totals = row_max + jnp.log(jnp.sum(shifted, axis=1, keepdims=True))
+        weights = jnp.exp(masked - log_totals)
+        weights_low = weights.astype(jnp.bfloat16)
+        attended = jnp.dot(weights_low, value_block,
+                           preferred_element_type=jnp.float32).astype(jnp.bfloat16)
+        row_dots = jnp.sum(attended.astype(jnp.float32) * grad_all.astype(jnp.float32),
+                           axis=1, keepdims=True)
+        grad_weights = lax.dot_general(grad_all, value_block, contract_last,
+                                       preferred_element_type=jnp.float32)
+        grad_scores = (weights * (grad_weights - row_dots)).astype(jnp.bfloat16)
+        query_grad = (jnp.dot(grad_scores, key_block, preferred_element_type=jnp.float32)
+                      * score_scale).astype(jnp.bfloat16)
+        for h in range(group_size):
+            out_ref[rows, h * DH:(h + 1) * DH] = attended[h * SPAN:(h + 1) * SPAN]
+            dq_ref[rows, h * DH:(h + 1) * DH] = query_grad[h * SPAN:(h + 1) * SPAN]
+        key_sum = lax.dot_general(grad_scores, query_all, contract_first,
+                                  preferred_element_type=jnp.float32) * score_scale
+        value_sum = lax.dot_general(weights_low, grad_all, contract_first,
+                                    preferred_element_type=jnp.float32)
+
+        slot_base = tiles * window_spans + base
         for w in range(window_spans):
-            piece = index_ref[base + w]
-            row = index_ref[info + 2 + base + w]
-            part = refs[0][row]
-            for other in range(1, half):
-                part = jnp.where(piece == other, refs[other][row], part)
-            parts.append(part)
-        return jnp.concatenate(parts, axis=0)
-
-    key_block = window_rows(key_refs)
-    value_block = window_rows(value_refs)
-    query_all = jnp.concatenate(
-        [q_ref[:, h * DH:(h + 1) * DH] for h in range(group_size)], axis=0)
-    grad_all = jnp.concatenate(
-        [do_ref[:, h * DH:(h + 1) * DH] for h in range(group_size)], axis=0)
-    span = index_ref[2 * tiles * window_spans + tile]
-    window = window_spans * SPAN
-    row_ids = lax.broadcasted_iota(jnp.int32, (SPAN, window), 0)
-    col_ids = lax.broadcasted_iota(jnp.int32, (SPAN, window), 1)
-    query_pos = span * SPAN + row_ids
-    key_pos = (span - (window_spans - 1)) * SPAN + col_ids
-    visible = (key_pos >= qstart_ref[0]) & (key_pos <= query_pos)
-    bias = jnp.where(visible, 0.0, -jnp.inf)
-    bias = jnp.concatenate([bias] * group_size, axis=0)
-    contract_last = (((1,), (1,)), ((), ()))
-    contract_first = (((0,), (0,)), ((), ()))
-    scores = lax.dot_general(query_all, key_block, contract_last,
-                             preferred_element_type=jnp.float32) * score_scale
-    masked = scores + bias
-    row_max = jnp.max(masked, axis=1, keepdims=True)
-    shifted = jnp.exp(masked - row_max)
-    log_totals = row_max + jnp.log(jnp.sum(shifted, axis=1, keepdims=True))
-    weights = jnp.exp(masked - log_totals)
-    weights_low = weights.astype(jnp.bfloat16)
-    attended = jnp.dot(weights_low, value_block,
-                       preferred_element_type=jnp.float32).astype(jnp.bfloat16)
-    row_dots = jnp.sum(attended.astype(jnp.float32) * grad_all.astype(jnp.float32),
-                       axis=1, keepdims=True)
-    grad_weights = lax.dot_general(grad_all, value_block, contract_last,
-                                   preferred_element_type=jnp.float32)
-    grad_scores = (weights * (grad_weights - row_dots)).astype(jnp.bfloat16)
-    query_grad = (jnp.dot(grad_scores, key_block, preferred_element_type=jnp.float32)
-                  * score_scale).astype(jnp.bfloat16)
-    for h in range(group_size):
-        out_ref[:, h * DH:(h + 1) * DH] = attended[h * SPAN:(h + 1) * SPAN]
-        dq_ref[:, h * DH:(h + 1) * DH] = query_grad[h * SPAN:(h + 1) * SPAN]
-    key_sum = lax.dot_general(grad_scores, query_all, contract_first,
-                              preferred_element_type=jnp.float32) * score_scale
-    value_sum = lax.dot_general(weights_low, grad_all, contract_first,
-                                preferred_element_type=jnp.float32)
-
-    @pl.when(tile == 0)
-    def _():
-        buf_ref[...] = jnp.zeros(buf_ref.shape, buf_ref.dtype)
-
-    slot_base = tiles * window_spans + base
-    for w in range(window_spans):
-        slot = index_ref[slot_base + w]
-        rows = slice(w * SPAN, (w + 1) * SPAN)
-        buf_ref[slot, :, :DH] += key_sum[rows]
-        buf_ref[slot, :, DH:] += value_sum[rows]
-
-    @pl.when(tile == tiles - 1)
-    def _():
-        my_half = index_ref[info]
-        my_q = index_ref[info + 1]
-        for shift, ref in enumerate((own_ref,) + tuple(send_refs)):
-            target = my_half * half + (my_q + shift) % half
-            other = (target + half) % (2 * half)
-            for k, device in enumerate((target, other)):
-                block = buf_ref[pl.ds(device * tiles, tiles)]
-                ref[k, 0] = block.astype(ref.dtype)
+            slot = index_ref[slot_base + w]
+            part = slice(w * SPAN, (w + 1) * SPAN)
+            buf_ref[slot, :, :DH] += key_sum[part]
+            buf_ref[slot, :, DH:] += value_sum[part]
+
+    my_half = index_ref[info]
+    my_q = index_ref[info + 1]
+    for shift, ref in enumerate((own_ref,) + tuple(send_refs)):
+        target = my_half * half + (my_q + shift) % half
+        other = (target + half) % (2 * half)
+        for k, device in enumerate((target, other)):
+            block = buf_ref[pl.ds(device * tiles, tiles)]
+            ref[k, 0] = block.astype(ref.dtype)
 
 
 def local(queries, key_rows, value_rows, out_grad, doc_start, span_order):
@@ -160,11 +156,11 @@
         aliased = chunk > 0
         head0 = chunk * chunk_heads
         in_specs = [
-            pl.BlockSpec((1, SPAN, 1), lambda j, t, idx: (t, 0, 0)),
-            pl.BlockSpec((SPAN, group_cols), lambda j, t, idx, h=head0: (t, h + j)),
-            pl.BlockSpec((SPAN, group_cols), lambda j, t, idx, h=head0: (t, h + j)),
-        ] + [pl.BlockSpec((2 * tiles, SPAN, DH), lambda j, t, idx: (0, 0, j))] * half + [
-            pl.BlockSpec((2 * tiles, SPAN, DH), lambda j, t, idx, n=chunk_heads: (0, 0, n + j))
+            pl.BlockSpec((tiles, SPAN, 1), lambda j, idx: (0, 0, 0)),
+            pl.BlockSpec((local_rows, group_cols), lambda j, idx, h=head0: (0, h + j)),
+            pl.BlockSpec((local_rows, group_cols), lambda j, idx, h=head0: (0, h + j)),
+        ] + [pl.BlockSpec((2 * tiles, SPAN, DH), lambda j, idx: (0, 0, j))] * half + [
+            pl.BlockSpec((2 * tiles, SPAN, DH), lambda j, idx, n=chunk_heads: (0, 0, n + j))
         ] * half
         operands = [index_table, query_start, queries, out_grad] + pieces + pieces
         aliases = {}
@@ -178,12 +174,12 @@
                 half=half, score_scale=score_scale, aliased=a),
             grid_spec=pltpu.PrefetchScalarGridSpec(
                 num_scalar_prefetch=1,
-                grid=(chunk_heads, tiles),
+                grid=(chunk_heads,),
                 in_specs=in_specs,
                 out_specs=[
-                    pl.BlockSpec((SPAN, group_cols), lambda j, t, idx, h=head0: (t, h + j)),
-                    pl.BlockSpec((SPAN, group_cols), lambda j, t, idx, h=head0: (t, h + j)),
-                ] + [pl.BlockSpec((2, 1, tiles, SPAN, 2 * DH), lambda j, t, idx: (0, j, 0, 0, 0))] * half,
+                    pl.BlockSpec((local_rows, group_cols), lambda j, idx, h=head0: (0, h + j)),
+                    pl.BlockSpec((local_rows, group_cols), lambda j, idx, h=head0: (0, h + j)),
+                ] + [pl.BlockSpec((2, 1, tiles, SPAN, 2 * DH), lambda j, idx: (0, j, 0, 0, 0))] * half,
                 scratch_shapes=[pltpu.VMEM((slot_count, SPAN, 2 * DH), jnp.float32)],
             ),
             out_shape=[

time: 78.3 us -> 76.8 us (0.981)
  Pallas kernels: 16.9 us -> 15.4 us
    pallas_call x2, Pallas kernels: 16.9 us -> 15.4 us  [local(): attended, query_grad, own_pack, *send_packs = kernel(*operands)]
  transfers between devices with their start and end apart: 16 -> 16, of which waited for: 5 -> 6; matrix products, arithmetic and copies ran while one was open for 3% -> 3% of each run, Pallas kernels for 22% -> 20%
where the time goes in v11:
time: 76.8 us; the launch traced here: 76.5 us
  waiting for transfers between devices  28.1 us (37%)
  starting transfers between devices  24.7 us (32%)
  Pallas kernels  15.4 us (20%)
  local copies, waits for them, and re-layouts  5.46 us (7%)
  other arithmetic  2.07 us (3%)
  between operations  0.84 us (1%)
    pallas_call x2, Pallas kernels, local(): attended, query_grad, own_pack, *send_packs = kernel(*operands)  15.4 us
    ppermute x2, waiting for transfers between devices, local(): both = jnp.stack([pair, lax.ppermute(pair, 'ctx', cross_pairs())])  8.66 us
    ppermute x6, waiting for transfers between devices, local(): pieces.append(lax.ppermute(both, 'ctx', half_pairs(shift)))  7.7 us
    ppermute x6, starting transfers between devices, local(): lax.ppermute(send_packs[shift - 1].reshape(pack_shape), 'ctx', half_pairs...  7.55 us
    ppermute x6, waiting for transfers between devices, local(): lax.ppermute(send_packs[shift - 1].reshape(pack_shape), 'ctx', half_pairs...  7.22 us
    ppermute x2, starting transfers between devices, local(): lax.ppermute(summed[1].astype(jnp.bfloat16), 'ctx', cross_pairs())  6.95 us
    ppermute x6, starting transfers between devices, local(): pieces.append(lax.ppermute(both, 'ctx', half_pairs(shift)))  6.03 us
    ppermute x2, waiting for transfers between devices, local(): lax.ppermute(summed[1].astype(jnp.bfloat16), 'ctx', cross_pairs())  4.49 us
  transfers between devices with their start and end apart: 16, of which 6 were waited for; matrix products, arithmetic and copies ran while one was open for 3% of the time, Pallas kernels for 20%

profile of v11, /device:TPU:0, one launch (start us, length us, event | category | flops | bytes accessed | tf_op | source)
XLA Modules:
  0.0 76.5 jit_solution(5527758557805100828)
XLA Ops:
  0.6 1.0 %fusion.18 = (bf16[128,256]{1,0:T(8,128)(2,1)S(1)}, bf16[128,256]{1,0:T(8,128)(2,1)S(1)}, bf16[128,256]{1,0:T(8,128)(2,1)S(1)}, bf16[128,256]{1,0:T(8,128)(2,1)S(1)}) fusion(bf16[128,512]{1,0:T(8,128)(2,1)} %param.7, bf16[128,512]{1,0:T(8,128)(2,1)} %param.8), kind=kLoop, calls=%fused_computation.49 | loop fusion | bytes 524288 | tf_op jit(solution)/shard_map/slice | solution.py:149
  1.6 4.1 %collective-permute-start.4 = (bf16[128,512]{1,0:T(8,128)(2,1)S(1)}, bf16[128,512]{1,0:T(8,128)(2,1)S(1)}, u32[]{:S(2)}, u32[]{:S(2)}) collective-permute-start(bf16[128,512]{1,0:T(8,128)(2,1)S(1)} %get-tuple-element.37), channel_id=1, source_target_pairs={{0,8},{2,10},{4,12},{6,14},{8,0},{10,2},{12,4},{14,6},{1,9},{3,11}... | collective-permute-start | bytes 393224 | tf_op jit(solution)/shard_map/ppermute | solution.py:150
  7.0 8.7 %collective-permute-done.4 = bf16[128,512]{1,0:T(8,128)(2,1)S(1)} collective-permute-done((bf16[128,512]{1,0:T(8,128)(2,1)S(1)}, bf16[128,512]{1,0:T(8,128)(2,1)S(1)}, u32[]{:S(2)}, u32[]{:S(2)}) %collective-permute-start.4) | collective-permute-done | bytes 131104 | tf_op jit(solution)/shard_map/ppermute | solution.py:150
  15.7 1.9 %collective-permute-start.5 = (bf16[2,128,512]{2,1,0:T(8,128)(2,1)S(1)}, bf16[2,128,512]{2,1,0:T(8,128)(2,1)S(1)}, u32[]{:S(2)}, u32[]{:S(2)}) collective-permute-start(bf16[2,128,512]{2,1,0:T(8,128)(2,1)S(1)} %pad_maximum_fusion.1), channel_id=1, source_target_pairs={{0,2},{2,4},{4,6},{6,0},{8,10},{10,12},{12,14},{14,8},{1,3},{3,5},... | collective-permute-start | bytes 786440 | tf_op jit(solution)/shard_map/ppermute | solution.py:153
  17.6 1.5 %collective-permute-start.7 = (bf16[2,128,512]{2,1,0:T(8,128)(2,1)S(1)}, bf16[2,128,512]{2,1,0:T(8,128)(2,1)S(1)}, u32[]{:S(2)}, u32[]{:S(2)}) collective-permute-start(bf16[2,128,512]{2,1,0:T(8,128)(2,1)S(1)} %pad_maximum_fusion.1), channel_id=1, source_target_pairs={{0,6},{2,0},{4,2},{6,4},{8,14},{10,8},{12,10},{14,12},{1,7},{3,1},... | collective-permute-start | bytes 786440 | tf_op jit(solution)/shard_map/ppermute | solution.py:153
  20.4 0.8 %reshape.110.refs_1_ = s32[2,64,1]{2,1,0:T(8,128)} reshape(s32[128]{0:T(128)S(1)} %copy-done.11) | data formatting | bytes 1024 | tf_op jit(solution)/shard_map/reshape | solution.py:135
  21.9 2.0 %collective-permute-start.2 = (bf16[2,128,512]{2,1,0:T(8,128)(2,1)S(1)}, bf16[2,128,512]{2,1,0:T(8,128)(2,1)S(1)}, u32[]{:S(2)}, u32[]{:S(2)}) collective-permute-start(bf16[2,128,512]{2,1,0:T(8,128)(2,1)S(1)} %pad_maximum_fusion), channel_id=1, source_target_pairs={{0,4},{2,6},{4,0},{6,2},{8,12},{10,14},{12,8},{14,10},{1,5},{3,7},... | collective-permute-start | bytes 786440 | tf_op jit(solution)/shard_map/ppermute | solution.py:153
  23.9 4.1 %collective-permute-done.5 = bf16[2,128,512]{2,1,0:T(8,128)(2,1)S(1)} collective-permute-done((bf16[2,128,512]{2,1,0:T(8,128)(2,1)S(1)}, bf16[2,128,512]{2,1,0:T(8,128)(2,1)S(1)}, u32[]{:S(2)}, u32[]{:S(2)}) %collective-permute-start.5) | collective-permute-done | bytes 262176 | tf_op jit(solution)/shard_map/ppermute | solution.py:153
  28.1 3.6 %collective-permute-done.7 = bf16[2,128,512]{2,1,0:T(8,128)(2,1)S(1)} collective-permute-done((bf16[2,128,512]{2,1,0:T(8,128)(2,1)S(1)}, bf16[2,128,512]{2,1,0:T(8,128)(2,1)S(1)}, u32[]{:S(2)}, u32[]{:S(2)}) %collective-permute-start.7) | collective-permute-done | bytes 262176 | tf_op jit(solution)/shard_map/ppermute | solution.py:153
  31.6 0.7 copy-done.5
  32.3 7.6 %shard_map.93 = (bf16[128,4096]{1,0:T(8,128)(2,1)}, bf16[128,4096]{1,0:T(8,128)(2,1)}, f32[2,2,2,64,256]{4,3,2,1,0:T(8,128)}, bf16[2,2,2,64,256]{4,3,2,1,0:T(8,1...) custom-call(s32[34]{0:T(128)} %concatenate.17.refs_0_, s32[2,64,1]{2,1,0:T(8,128)} %reshape.110.refs_1_, ...), custom_call_target="tpu_custom_call" | custom-call | tf_op jit(solution)/shard_map/pallas_call | solution.py:192
  40.0 1.9 %collective-permute-start.10 = (bf16[2,2,128,256]{3,2,1,0:T(8,128)(2,1)}, bf16[2,2,128,256]{3,2,1,0:T(8,128)(2,1)S(1)}, u32[]{:S(2)}, u32[]{:S(2)}) collective-permute-start(bf16[2,2,128,256]{3,2,1,0:T(8,128)(2,1)} %bitcast.83), channel_id=1, source_target_pairs={{0,6},{2,0},{4,2},{6,4},{8,14},{10,8},{12,10},{14,12},{1,7},{3,1},... | collective-permute-start | bytes 786440 | tf_op jit(solution)/shard_map/ppermute | solution.py:197
  41.8 0.7 collective-permute-start.8
  42.5 1.5 %collective-permute-start.9 = (bf16[2,2,128,256]{3,2,1,0:T(8,128)(2,1)}, bf16[2,2,128,256]{3,2,1,0:T(8,128)(2,1)S(1)}, u32[]{:S(2)}, u32[]{:S(2)}) collective-permute-start(bf16[2,2,128,256]{3,2,1,0:T(8,128)(2,1)} %bitcast.80), channel_id=1, source_target_pairs={{0,4},{2,6},{4,0},{6,2},{8,12},{10,14},{12,8},{14,10},{1,5},{3,7},... | collective-permute-start | bytes 786440 | tf_op jit(solution)/shard_map/ppermute | solution.py:197
  44.0 0.7 copy-done.6
  44.8 7.8 %shard_map.94 = (bf16[128,4096]{1,0:T(8,128)(2,1)}, bf16[128,4096]{1,0:T(8,128)(2,1)}, f32[2,2,2,64,256]{4,3,2,1,0:T(8,128)}, bf16[2,2,2,64,256]{4,3,2,1,0:T(8,1...) custom-call(s32[34]{0:T(128)} %concatenate.17.refs_0_, ...), custom_call_target="tpu_custom_call", output_to_operand_aliasing={{0}: (12, {}), {1}: (13, {})} | custom-call | tf_op jit(solution)/shard_map/pallas_call | solution.py:192
  52.6 1.5 %collective-permute-start.12 = (bf16[2,2,128,256]{3,2,1,0:T(8,128)(2,1)}, bf16[2,2,128,256]{3,2,1,0:T(8,128)(2,1)S(1)}, u32[]{:S(2)}, u32[]{:S(2)}) collective-permute-start(bf16[2,2,128,256]{3,2,1,0:T(8,128)(2,1)} %bitcast.85), channel_id=1, source_target_pairs={{0,2},{2,4},{4,6},{6,0},{8,10},{10,12},{12,14},{14,8},{1,3},{3,5},... | collective-permute-start | bytes 786440 | tf_op jit(solution)/shard_map/ppermute | solution.py:197
  54.1 1.9 %collective-permute-start.13 = (bf16[2,2,128,256]{3,2,1,0:T(8,128)(2,1)}, bf16[2,2,128,256]{3,2,1,0:T(8,128)(2,1)S(1)}, u32[]{:S(2)}, u32[]{:S(2)}) collective-permute-start(bf16[2,2,128,256]{3,2,1,0:T(8,128)(2,1)} %bitcast.84), channel_id=1, source_target_pairs={{0,4},{2,6},{4,0},{6,2},{8,12},{10,14},{12,8},{14,10},{1,5},{3,7},... | collective-permute-start | bytes 786440 | tf_op jit(solution)/shard_map/ppermute | solution.py:197
  56.3 2.5 %collective-permute-start.11 = (bf16[2,128,256]{2,1,0:T(8,128)(2,1)S(1)}, bf16[2,128,256]{2,1,0:T(8,128)(2,1)S(1)}, u32[]{:S(2)}, u32[]{:S(2)}) collective-permute-start(bf16[2,128,256]{2,1,0:T(8,128)(2,1)S(1)} %fusion.8), channel_id=1, source_target_pairs={{0,8},{2,10},{4,12},{6,14},{8,0},{10,2},{12,4},{14,6},{1,9},{3,11}... | collective-permute-start | bytes 393224 | tf_op jit(solution)/shard_map/ppermute | solution.py:200
  58.7 7.0 %collective-permute-done.12 = bf16[2,2,128,256]{3,2,1,0:T(8,128)(2,1)S(1)} collective-permute-done((bf16[2,2,128,256]{3,2,1,0:T(8,128)(2,1)}, bf16[2,2,128,256]{3,2,1,0:T(8,128)(2,1)S(1)}, u32[]{:S(2)}, u32[]{:S(2)}) %collective-permute-start.12) | collective-permute-done | bytes 262176 | tf_op jit(solution)/shard_map/ppermute | solution.py:197
  66.1 4.5 %collective-permute-start.15 = (bf16[2,128,256]{2,1,0:T(8,128)(2,1)S(1)}, bf16[2,128,256]{2,1,0:T(8,128)(2,1)S(1)}, u32[]{:S(2)}, u32[]{:S(2)}) collective-permute-start(bf16[2,128,256]{2,1,0:T(8,128)(2,1)S(1)} %fusion.9), channel_id=1, source_target_pairs={{0,8},{2,10},{4,12},{6,14},{8,0},{10,2},{12,4},{14,6},{1,9},{3,11}... | collective-permute-start | bytes 393224 | tf_op jit(solution)/shard_map/ppermute | solution.py:200
  70.6 4.5 %collective-permute-done.15 = bf16[2,128,256]{2,1,0:T(8,128)(2,1)S(1)} collective-permute-done((bf16[2,128,256]{2,1,0:T(8,128)(2,1)S(1)}, bf16[2,128,256]{2,1,0:T(8,128)(2,1)S(1)}, u32[]{:S(2)}, u32[]{:S(2)}) %collective-permute-start.15) | collective-permute-done | bytes 131104 | tf_op jit(solution)/shard_map/ppermute | solution.py:200
  75.2 0.7 copy_bitcast_fusion
  75.8 0.7 copy_bitcast_fusion.1
  (58 shorter events, 3.9 us)
Async XLA Ops:
  1.6 14.0 %collective-permute-start.4 = (bf16[128,512]{1,0:T(8,128)(2,1)S(1)}, bf16[128,512]{1,0:T(8,128)(2,1)S(1)}, u32[]{:S(2)}, u32[]{:S(2)}) collective-permute-start(bf16[128,512]{1,0:T(8,128)(2,1)S(1)} %get-tuple-element.37), channel_id=1, source_target_pairs={{0,8},{2,10},{4,12},{6,14},{8,0},{10,2},{12,4},{14,6},{1,9},{3,11}... | collective-permute-start | bytes 393224 | tf_op jit(solution)/shard_map/ppermute | solution.py:150
  5.7 13.4 %collective-permute-start = (bf16[128,512]{1,0:T(8,128)(2,1)S(1)}, bf16[128,512]{1,0:T(8,128)(2,1)S(1)}, u32[]{:S(2)}, u32[]{:S(2)}) collective-permute-start(bf16[128,512]{1,0:T(8,128)(2,1)S(1)} %get-tuple-element.43), channel_id=1, source_target_pairs={{0,8},{2,10},{4,12},{6,14},{8,0},{10,2},{12,4},{14,6},{1,9},{3,11}... | collective-permute-start | bytes 393224 | tf_op jit(solution)/shard_map/ppermute | solution.py:150
  15.7 3.5 %copy-start.1 = (bf16[2,128,512]{2,1,0:T(8,128)(2,1)}, bf16[2,128,512]{2,1,0:T(8,128)(2,1)S(1)}, u32[]{:S(2)}) copy-start(bf16[2,128,512]{2,1,0:T(8,128)(2,1)S(1)} %pad_maximum_fusion.1) | copy-start | bytes 786436
  15.7 12.3 %collective-permute-start.5 = (bf16[2,128,512]{2,1,0:T(8,128)(2,1)S(1)}, bf16[2,128,512]{2,1,0:T(8,128)(2,1)S(1)}, u32[]{:S(2)}, u32[]{:S(2)}) collective-permute-start(bf16[2,128,512]{2,1,0:T(8,128)(2,1)S(1)} %pad_maximum_fusion.1), channel_id=1, source_target_pairs={{0,2},{2,4},{4,6},{6,0},{8,10},{10,12},{12,14},{14,8},{1,3},{3,5},... | collective-permute-start | bytes 786440 | tf_op jit(solution)/shard_map/ppermute | solution.py:153
  17.6 10.4 %collective-permute-start.6 = (bf16[2,128,512]{2,1,0:T(8,128)(2,1)S(1)}, bf16[2,128,512]{2,1,0:T(8,128)(2,1)S(1)}, u32[]{:S(2)}, u32[]{:S(2)}) collective-permute-start(bf16[2,128,512]{2,1,0:T(8,128)(2,1)S(1)} %pad_maximum_fusion.1), channel_id=1, source_target_pairs={{0,4},{2,6},{4,0},{6,2},{8,12},{10,14},{12,8},{14,10},{1,5},{3,7},... | collective-permute-start | bytes 786440 | tf_op jit(solution)/shard_map/ppermute | solution.py:153
  17.6 14.0 %collective-permute-start.7 = (bf16[2,128,512]{2,1,0:T(8,128)(2,1)S(1)}, bf16[2,128,512]{2,1,0:T(8,128)(2,1)S(1)}, u32[]{:S(2)}, u32[]{:S(2)}) collective-permute-start(bf16[2,128,512]{2,1,0:T(8,128)(2,1)S(1)} %pad_maximum_fusion.1), channel_id=1, source_target_pairs={{0,6},{2,0},{4,2},{6,4},{8,14},{10,8},{12,10},{14,12},{1,7},{3,1},... | collective-permute-start | bytes 786440 | tf_op jit(solution)/shard_map/ppermute | solution.py:153
  19.2 20.8 %copy-start = (bf16[2,128,512]{2,1,0:T(8,128)(2,1)}, bf16[2,128,512]{2,1,0:T(8,128)(2,1)S(1)}, u32[]{:S(2)}) copy-start(bf16[2,128,512]{2,1,0:T(8,128)(2,1)S(1)} %pad_maximum_fusion) | copy-start | bytes 786436
  19.2 23.3 %collective-permute-start.1 = (bf16[2,128,512]{2,1,0:T(8,128)(2,1)S(1)}, bf16[2,128,512]{2,1,0:T(8,128)(2,1)S(1)}, u32[]{:S(2)}, u32[]{:S(2)}) collective-permute-start(bf16[2,128,512]{2,1,0:T(8,128)(2,1)S(1)} %pad_maximum_fusion), channel_id=1, source_target_pairs={{0,2},{2,4},{4,6},{6,0},{8,10},{10,12},{12,14},{14,8},{1,3},{3,5},... | collective-permute-start | bytes 786440 | tf_op jit(solution)/shard_map/ppermute | solution.py:153
  21.9 22.1 %collective-permute-start.2 = (bf16[2,128,512]{2,1,0:T(8,128)(2,1)S(1)}, bf16[2,128,512]{2,1,0:T(8,128)(2,1)S(1)}, u32[]{:S(2)}, u32[]{:S(2)}) collective-permute-start(bf16[2,128,512]{2,1,0:T(8,128)(2,1)S(1)} %pad_maximum_fusion), channel_id=1, source_target_pairs={{0,4},{2,6},{4,0},{6,2},{8,12},{10,14},{12,8},{14,10},{1,5},{3,7},... | collective-permute-start | bytes 786440 | tf_op jit(solution)/shard_map/ppermute | solution.py:153
  28.0 3.6 %copy-start.3 = (bf16[2,128,512]{2,1,0:T(8,128)(2,1)}, bf16[2,128,512]{2,1,0:T(8,128)(2,1)S(1)}, u32[]{:S(2)}) copy-start(bf16[2,128,512]{2,1,0:T(8,128)(2,1)S(1)} %collective-permute-done.5) | copy-start | bytes 786436
  28.0 16.0 %collective-permute-start.3 = (bf16[2,128,512]{2,1,0:T(8,128)(2,1)S(1)}, bf16[2,128,512]{2,1,0:T(8,128)(2,1)S(1)}, u32[]{:S(2)}, u32[]{:S(2)}) collective-permute-start(bf16[2,128,512]{2,1,0:T(8,128)(2,1)S(1)} %pad_maximum_fusion), channel_id=1, source_target_pairs={{0,6},{2,0},{4,2},{6,4},{8,14},{10,8},{12,10},{14,12},{1,7},{3,1},... | collective-permute-start | bytes 786440 | tf_op jit(solution)/shard_map/ppermute | solution.py:153
  28.0 3.6 %copy-start.4 = (bf16[2,128,512]{2,1,0:T(8,128)(2,1)}, bf16[2,128,512]{2,1,0:T(8,128)(2,1)S(1)}, u32[]{:S(2)}) copy-start(bf16[2,128,512]{2,1,0:T(8,128)(2,1)S(1)} %collective-permute-done.6) | copy-start | bytes 786436
  40.0 16.1 %collective-permute-start.10 = (bf16[2,2,128,256]{3,2,1,0:T(8,128)(2,1)}, bf16[2,2,128,256]{3,2,1,0:T(8,128)(2,1)S(1)}, u32[]{:S(2)}, u32[]{:S(2)}) collective-permute-start(bf16[2,2,128,256]{3,2,1,0:T(8,128)(2,1)} %bitcast.83), channel_id=1, source_target_pairs={{0,6},{2,0},{4,2},{6,4},{8,14},{10,8},{12,10},{14,12},{1,7},{3,1},... | collective-permute-start | bytes 786440 | tf_op jit(solution)/shard_map/ppermute | solution.py:197
  41.8 14.3 %collective-permute-start.8 = (bf16[2,2,128,256]{3,2,1,0:T(8,128)(2,1)}, bf16[2,2,128,256]{3,2,1,0:T(8,128)(2,1)S(1)}, u32[]{:S(2)}, u32[]{:S(2)}) collective-permute-start(bf16[2,2,128,256]{3,2,1,0:T(8,128)(2,1)} %bitcast.81), channel_id=1, source_target_pairs={{0,2},{2,4},{4,6},{6,0},{8,10},{10,12},{12,14},{14,8},{1,3},{3,5},... | collective-permute-start | bytes 786440 | tf_op jit(solution)/shard_map/ppermute | solution.py:197
  42.5 1.5 %copy-start.2 = (bf16[2,128,512]{2,1,0:T(8,128)(2,1)}, bf16[2,128,512]{2,1,0:T(8,128)(2,1)S(1)}, u32[]{:S(2)}) copy-start(bf16[2,128,512]{2,1,0:T(8,128)(2,1)S(1)} %collective-permute-done.1) | copy-start | bytes 786436
  42.5 13.6 %collective-permute-start.9 = (bf16[2,2,128,256]{3,2,1,0:T(8,128)(2,1)}, bf16[2,2,128,256]{3,2,1,0:T(8,128)(2,1)S(1)}, u32[]{:S(2)}, u32[]{:S(2)}) collective-permute-start(bf16[2,2,128,256]{3,2,1,0:T(8,128)(2,1)} %bitcast.80), channel_id=1, source_target_pairs={{0,4},{2,6},{4,0},{6,2},{8,12},{10,14},{12,8},{14,10},{1,5},{3,7},... | collective-permute-start | bytes 786440 | tf_op jit(solution)/shard_map/ppermute | solution.py:197
  44.0 0.8 %copy-start.7 = (bf16[2,128,512]{2,1,0:T(8,128)(2,1)}, bf16[2,128,512]{2,1,0:T(8,128)(2,1)S(1)}, u32[]{:S(2)}) copy-start(bf16[2,128,512]{2,1,0:T(8,128)(2,1)S(1)} %collective-permute-done.3) | copy-start | bytes 786436
  44.8 11.3 %copy-start.8 = (f32[2,2,2,64,256]{4,3,2,1,0:T(8,128)S(1)}, f32[2,2,2,64,256]{4,3,2,1,0:T(8,128)}, u32[]{:S(2)}) copy-start(f32[2,2,2,64,256]{4,3,2,1,0:T(8,128)} %get-tuple-element.20) | copy-start | bytes 1572868
  52.6 13.2 %collective-permute-start.12 = (bf16[2,2,128,256]{3,2,1,0:T(8,128)(2,1)}, bf16[2,2,128,256]{3,2,1,0:T(8,128)(2,1)S(1)}, u32[]{:S(2)}, u32[]{:S(2)}) collective-permute-start(bf16[2,2,128,256]{3,2,1,0:T(8,128)(2,1)} %bitcast.85), channel_id=1, source_target_pairs={{0,2},{2,4},{4,6},{6,0},{8,10},{10,12},{12,14},{14,8},{1,3},{3,5},... | collective-permute-start | bytes 786440 | tf_op jit(solution)/shard_map/ppermute | solution.py:197
  54.1 11.7 %collective-permute-start.13 = (bf16[2,2,128,256]{3,2,1,0:T(8,128)(2,1)}, bf16[2,2,128,256]{3,2,1,0:T(8,128)(2,1)S(1)}, u32[]{:S(2)}, u32[]{:S(2)}) collective-permute-start(bf16[2,2,128,256]{3,2,1,0:T(8,128)(2,1)} %bitcast.84), channel_id=1, source_target_pairs={{0,4},{2,6},{4,0},{6,2},{8,12},{10,14},{12,8},{14,10},{1,5},{3,7},... | collective-permute-start | bytes 786440 | tf_op jit(solution)/shard_map/ppermute | solution.py:197
  56.0 9.9 %collective-permute-start.14 = (bf16[2,2,128,256]{3,2,1,0:T(8,128)(2,1)}, bf16[2,2,128,256]{3,2,1,0:T(8,128)(2,1)S(1)}, u32[]{:S(2)}, u32[]{:S(2)}) collective-permute-start(bf16[2,2,128,256]{3,2,1,0:T(8,128)(2,1)} %bitcast.82), channel_id=1, source_target_pairs={{0,6},{2,0},{4,2},{6,4},{8,14},{10,8},{12,10},{14,12},{1,7},{3,1},... | collective-permute-start | bytes 786440 | tf_op jit(solution)/shard_map/ppermute | solution.py:197
  56.1 9.8 %copy-start.9 = (f32[2,2,2,64,256]{4,3,2,1,0:T(8,128)S(1)}, f32[2,2,2,64,256]{4,3,2,1,0:T(8,128)}, u32[]{:S(2)}) copy-start(f32[2,2,2,64,256]{4,3,2,1,0:T(8,128)} %get-tuple-element.24) | copy-start | bytes 1572868
  56.3 14.3 %collective-permute-start.11 = (bf16[2,128,256]{2,1,0:T(8,128)(2,1)S(1)}, bf16[2,128,256]{2,1,0:T(8,128)(2,1)S(1)}, u32[]{:S(2)}, u32[]{:S(2)}) collective-permute-start(bf16[2,128,256]{2,1,0:T(8,128)(2,1)S(1)} %fusion.8), channel_id=1, source_target_pairs={{0,8},{2,10},{4,12},{6,14},{8,0},{10,2},{12,4},{14,6},{1,9},{3,11}... | collective-permute-start | bytes 393224 | tf_op jit(solution)/shard_map/ppermute | solution.py:200
  66.1 9.0 %collective-permute-start.15 = (bf16[2,128,256]{2,1,0:T(8,128)(2,1)S(1)}, bf16[2,128,256]{2,1,0:T(8,128)(2,1)S(1)}, u32[]{:S(2)}, u32[]{:S(2)}) collective-permute-start(bf16[2,128,256]{2,1,0:T(8,128)(2,1)S(1)} %fusion.9), channel_id=1, source_target_pairs={{0,8},{2,10},{4,12},{6,14},{8,0},{10,2},{12,4},{14,6},{1,9},{3,11}... | collective-permute-start | bytes 393224 | tf_op jit(solution)/shard_map/ppermute | solution.py:200
  (4 other events, 2.7 us)

commit v12 on v11

--- a/solution.py
+++ b/solution.py
@@ -14,9 +14,9 @@
 
 def attention_kernel(index_ref, qstart_ref, q_ref, do_ref,
                      *rest, group_size, window_spans, tiles, half, score_scale, aliased):
-    key_refs = rest[:half]
-    value_refs = rest[half:2 * half]
-    rest = rest[2 * half:]
+    key_refs = rest[:2 * half]
+    value_refs = rest[2 * half:4 * half]
+    rest = rest[4 * half:]
     if aliased:
         rest = rest[2:]
     out_ref, dq_ref, own_ref = rest[:3]
@@ -34,7 +34,7 @@
                 piece = index_ref[base + w]
                 row = index_ref[info + 2 + base + w]
                 part = refs[0][row]
-                for other in range(1, half):
+                for other in range(1, len(refs)):
                     part = jnp.where(piece == other, refs[other][row], part)
                 parts.append(part)
             return jnp.concatenate(parts, axis=0)
@@ -128,8 +128,8 @@
     window_owner = window_slot // tiles
     owner_s = (my_q - window_owner % half) % half
     owner_k = (window_owner // half != my_half).astype(jnp.int32)
-    window_row = owner_k * tiles + window_slot % tiles
-    index_table = jnp.concatenate([owner_s.reshape(-1), window_slot.reshape(-1), my_spans,
+    window_row = window_slot % tiles
+    index_table = jnp.concatenate([(owner_s * 2 + owner_k).reshape(-1), window_slot.reshape(-1), my_spans,
                                    jnp.stack([my_half, my_q]).astype(jnp.int32),
                                    window_row.reshape(-1)])
     query_start = doc_start.reshape(tiles, SPAN, 1)
@@ -147,21 +147,22 @@
     for chunk in range(chunks):
         cols = slice(chunk * chunk_cols, (chunk + 1) * chunk_cols)
         pair = jnp.concatenate([key_rows[:, cols], value_rows[:, cols]], axis=1)
-        both = jnp.stack([pair, lax.ppermute(pair, "ctx", cross_pairs())])
-        pieces = [both]
-        for shift in range(1, half):
-            pieces.append(lax.ppermute(both, "ctx", half_pairs(shift)))
-        pieces = [piece.reshape(2 * tiles, SPAN, 2 * chunk_cols) for piece in pieces]
-
+        partner = lax.ppermute(pair, "ctx", cross_pairs())
+        pieces = []
+        for shift in range(half):
+            for data in (pair, partner):
+                piece = data if shift == 0 else lax.ppermute(data, "ctx", half_pairs(shift))
+                pieces.append(piece.reshape(tiles, SPAN, 2 * chunk_cols))
+        head0 = chunk * chunk_heads
         aliased = chunk > 0
         head0 = chunk * chunk_heads
         in_specs = [
             pl.BlockSpec((tiles, SPAN, 1), lambda j, idx: (0, 0, 0)),
             pl.BlockSpec((local_rows, group_cols), lambda j, idx, h=head0: (0, h + j)),
             pl.BlockSpec((local_rows, group_cols), lambda j, idx, h=head0: (0, h + j)),
-        ] + [pl.BlockSpec((2 * tiles, SPAN, DH), lambda j, idx: (0, 0, j))] * half + [
-            pl.BlockSpec((2 * tiles, SPAN, DH), lambda j, idx, n=chunk_heads: (0, 0, n + j))
-        ] * half
+        ] + [pl.BlockSpec((tiles, SPAN, DH), lambda j, idx: (0, 0, j))] * (2 * half) + [
+            pl.BlockSpec((tiles, SPAN, DH), lambda j, idx, n=chunk_heads: (0, 0, n + j))
+        ] * (2 * half)
         operands = [index_table, query_start, queries, out_grad] + pieces + pieces
         aliases = {}
         if aliased:

time: 76.8 us -> 90.2 us (1.17)
  waiting for transfers between devices: 28.1 us -> 35.8 us
  starting transfers between devices: 24.7 us -> 30.5 us
    ppermute x8 -> x14, starting transfers between devices: 10.2 us -> 18.1 us  [the longest x12 13.6 us: local(): piece = data if shift == 0 else lax.ppermute(data, 'ctx', half_pairs(shift))]
    ppermute x8 -> x14, waiting for transfers between devices: 16.4 us -> 21.3 us  [the longest x12 21.3 us: local(): piece = data if shift == 0 else lax.ppermute(data, 'ctx', half_pairs(shift))]
    ppermute x2, starting transfers between devices: 6.95 us -> 3.85 us  [local(): lax.ppermute(summed[1].astype(jnp.bfloat16), 'ctx', cross_pairs())]
    ppermute x2, waiting for transfers between devices: 4.49 us -> 6.03 us  [local(): lax.ppermute(summed[1].astype(jnp.bfloat16), 'ctx', cross_pairs())]
    ppermute x6, waiting for transfers between devices: 7.22 us -> 8.5 us  [local(): lax.ppermute(send_packs[shift - 1].reshape(pack_shape), 'ctx', half_pairs...]
    ppermute x6, starting transfers between devices: 7.55 us -> 8.48 us  [local(): lax.ppermute(send_packs[shift - 1].reshape(pack_shape), 'ctx', half_pairs...]
    unnamed x24 -> x40, local copies, waits for them, and re-layouts: 2.82 us -> 2.55 us
  transfers between devices with their start and end apart: 16 -> 22, of which waited for: 6 -> 8; matrix products, arithmetic and copies ran while one was open for 3% -> 3% of each run, Pallas kernels for 20% -> 17%
where the time goes in v12:
time: 90.2 us; the launch traced here: 90 us
  waiting for transfers between devices  35.8 us (40%)
  starting transfers between devices  30.5 us (34%)
  Pallas kernels  15.6 us (17%)
  local copies, waits for them, and re-layouts  5.19 us (6%)
  other arithmetic  1.99 us (2%)
    ppermute x12, waiting for transfers between devices, local(): piece = data if shift == 0 else lax.ppermute(data, 'ctx', half_pairs(shift))  21.3 us
    pallas_call x2, Pallas kernels, local(): attended, query_grad, own_pack, *send_packs = kernel(*operands)  15.6 us
    ppermute x12, starting transfers between devices, local(): piece = data if shift == 0 else lax.ppermute(data, 'ctx', half_pairs(shift))  13.6 us
    ppermute x6, waiting for transfers between devices, local(): lax.ppermute(send_packs[shift - 1].reshape(pack_shape), 'ctx', half_pairs...  8.5 us
    ppermute x6, starting transfers between devices, local(): lax.ppermute(send_packs[shift - 1].reshape(pack_shape), 'ctx', half_pairs...  8.48 us
    ppermute x2, waiting for transfers between devices, local(): lax.ppermute(summed[1].astype(jnp.bfloat16), 'ctx', cross_pairs())  6.03 us
    ppermute x2, starting transfers between devices, local(): partner = lax.ppermute(pair, 'ctx', cross_pairs())  4.5 us
    ppermute x2, starting transfers between devices, local(): lax.ppermute(summed[1].astype(jnp.bfloat16), 'ctx', cross_pairs())  3.85 us
  transfers between devices with their start and end apart: 22, of which 8 were waited for; matrix products, arithmetic and copies ran while one was open for 3% of the time, Pallas kernels for 17%

profile of v12, /device:TPU:0, one launch (start us, length us, event | category | flops | bytes accessed | tf_op | source)
XLA Modules:
  0.0 90.0 jit_solution(9837576953226633221)
XLA Ops:
  0.6 1.0 %fusion.17 = (bf16[128,256]{1,0:T(8,128)(2,1)S(1)}, bf16[128,256]{1,0:T(8,128)(2,1)S(1)}, bf16[128,256]{1,0:T(8,128)(2,1)S(1)}, bf16[128,256]{1,0:T(8,128)(2,1)S(1)}) fusion(bf16[128,512]{1,0:T(8,128)(2,1)} %param.7, bf16[128,512]{1,0:T(8,128)(2,1)} %param.8), kind=kLoop, calls=%fused_computation.46 | loop fusion | bytes 524288 | tf_op jit(solution)/shard_map/slice | solution.py:149
  1.6 4.1 %collective-permute-start.7 = (bf16[128,512]{1,0:T(8,128)(2,1)S(1)}, bf16[128,512]{1,0:T(8,128)(2,1)S(1)}, u32[]{:S(2)}, u32[]{:S(2)}) collective-permute-start(bf16[128,512]{1,0:T(8,128)(2,1)S(1)} %pad_maximum_fusion.1), channel_id=1, source_target_pairs={{0,8},{2,10},{4,12},{6,14},{8,0},{10,2},{12,4},{14,6},{1,9},{3,11}... | collective-permute-start | bytes 393224 | tf_op jit(solution)/shard_map/ppermute | solution.py:150
  5.7 1.5 %collective-permute-start.8 = (bf16[128,512]{1,0:T(8,128)(2,1)S(1)}, bf16[128,512]{1,0:T(8,128)(2,1)S(1)}, u32[]{:S(2)}, u32[]{:S(2)}) collective-permute-start(bf16[128,512]{1,0:T(8,128)(2,1)S(1)} %pad_maximum_fusion.1), channel_id=1, source_target_pairs={{0,2},{2,4},{4,6},{6,0},{8,10},{10,12},{12,14},{14,8},{1,3},{3,5},... | collective-permute-start | bytes 393224 | tf_op jit(solution)/shard_map/ppermute | solution.py:154
  7.2 1.6 %collective-permute-start.10 = (bf16[128,512]{1,0:T(8,128)(2,1)S(1)}, bf16[128,512]{1,0:T(8,128)(2,1)S(1)}, u32[]{:S(2)}, u32[]{:S(2)}) collective-permute-start(bf16[128,512]{1,0:T(8,128)(2,1)S(1)} %pad_maximum_fusion.1), channel_id=1, source_target_pairs={{0,4},{2,6},{4,0},{6,2},{8,12},{10,14},{12,8},{14,10},{1,5},{3,7},... | collective-permute-start | bytes 393224 | tf_op jit(solution)/shard_map/ppermute | solution.py:154
  8.8 1.4 %collective-permute-start.12 = (bf16[128,512]{1,0:T(8,128)(2,1)S(1)}, bf16[128,512]{1,0:T(8,128)(2,1)S(1)}, u32[]{:S(2)}, u32[]{:S(2)}) collective-permute-start(bf16[128,512]{1,0:T(8,128)(2,1)S(1)} %pad_maximum_fusion.1), channel_id=1, source_target_pairs={{0,6},{2,0},{4,2},{6,4},{8,14},{10,8},{12,10},{14,12},{1,7},{3,1},... | collective-permute-start | bytes 393224 | tf_op jit(solution)/shard_map/ppermute | solution.py:154
  12.4 0.8 reshape.142.refs_1_
  13.3 0.8 collective-permute-start.1
  14.1 3.5 %collective-permute-done.8 = bf16[128,512]{1,0:T(8,128)(2,1)S(1)} collective-permute-done((bf16[128,512]{1,0:T(8,128)(2,1)S(1)}, bf16[128,512]{1,0:T(8,128)(2,1)S(1)}, u32[]{:S(2)}, u32[]{:S(2)}) %collective-permute-start.8) | collective-permute-done | bytes 131104 | tf_op jit(solution)/shard_map/ppermute | solution.py:154
  17.6 3.4 %collective-permute-start.9 = (bf16[128,512]{1,0:T(8,128)(2,1)S(1)}, bf16[128,512]{1,0:T(8,128)(2,1)S(1)}, u32[]{:S(2)}, u32[]{:S(2)}) collective-permute-start(bf16[128,512]{1,0:T(8,128)(2,1)S(1)} %collective-permute-done.7), channel_id=1, source_target_pairs={{0,2},{2,4},{4,6},{6,0},{8,10},{10,12},{12,14},{14,8},{1,3},{3,5},... | collective-permute-start | bytes 393224 | tf_op jit(solution)/shard_map/ppermute | solution.py:154
  21.0 2.2 %collective-permute-start.13 = (bf16[128,512]{1,0:T(8,128)(2,1)S(1)}, bf16[128,512]{1,0:T(8,128)(2,1)S(1)}, u32[]{:S(2)}, u32[]{:S(2)}) collective-permute-start(bf16[128,512]{1,0:T(8,128)(2,1)S(1)} %collective-permute-done.7), channel_id=1, source_target_pairs={{0,6},{2,0},{4,2},{6,4},{8,14},{10,8},{12,10},{14,12},{1,7},{3,1},... | collective-permute-start | bytes 393224 | tf_op jit(solution)/shard_map/ppermute | solution.py:154
  23.2 5.6 %collective-permute-done.9 = bf16[128,512]{1,0:T(8,128)(2,1)S(1)} collective-permute-done((bf16[128,512]{1,0:T(8,128)(2,1)S(1)}, bf16[128,512]{1,0:T(8,128)(2,1)S(1)}, u32[]{:S(2)}, u32[]{:S(2)}) %collective-permute-start.9) | collective-permute-done | bytes 131104 | tf_op jit(solution)/shard_map/ppermute | solution.py:154
  28.7 2.0 %collective-permute-start.2 = (bf16[128,512]{1,0:T(8,128)(2,1)S(1)}, bf16[128,512]{1,0:T(8,128)(2,1)S(1)}, u32[]{:S(2)}, u32[]{:S(2)}) collective-permute-start(bf16[128,512]{1,0:T(8,128)(2,1)S(1)} %collective-permute-done), channel_id=1, source_target_pairs={{0,2},{2,4},{4,6},{6,0},{8,10},{10,12},{12,14},{14,8},{1,3},{3,5},... | collective-permute-start | bytes 393224 | tf_op jit(solution)/shard_map/ppermute | solution.py:154
  32.0 7.7 %shard_map.93 = (bf16[128,4096]{1,0:T(8,128)(2,1)}, bf16[128,4096]{1,0:T(8,128)(2,1)}, f32[2,2,2,64,256]{4,3,2,1,0:T(8,128)}, bf16[2,2,2,64,256]{4,3,2,1,0:T(8,1...) custom-call(s32[34]{0:T(128)} %concatenate.17.refs_0_, s32[2,64,1]{2,1,0:T(8,128)} %reshape.142.refs_1_, ...), custom_call_target="tpu_custom_call" | custom-call | tf_op jit(solution)/shard_map/pallas_call | solution.py:193
  40.5 0.8 collective-permute-start.15
  41.4 2.8 %collective-permute-start.16 = (bf16[2,2,128,256]{3,2,1,0:T(8,128)(2,1)}, bf16[2,2,128,256]{3,2,1,0:T(8,128)(2,1)S(1)}, u32[]{:S(2)}, u32[]{:S(2)}) collective-permute-start(bf16[2,2,128,256]{3,2,1,0:T(8,128)(2,1)} %bitcast.96), channel_id=1, source_target_pairs={{0,6},{2,0},{4,2},{6,4},{8,14},{10,8},{12,10},{14,12},{1,7},{3,1},... | collective-permute-start | bytes 786440 | tf_op jit(solution)/shard_map/ppermute | solution.py:198
  44.9 11.6 %collective-permute-done.4 = bf16[128,512]{1,0:T(8,128)(2,1)S(1)} collective-permute-done((bf16[128,512]{1,0:T(8,128)(2,1)S(1)}, bf16[128,512]{1,0:T(8,128)(2,1)S(1)}, u32[]{:S(2)}, u32[]{:S(2)}) %collective-permute-start.4) | collective-permute-done | bytes 131104 | tf_op jit(solution)/shard_map/ppermute | solution.py:154
  57.8 7.9 %shard_map.94 = (bf16[128,4096]{1,0:T(8,128)(2,1)}, bf16[128,4096]{1,0:T(8,128)(2,1)}, f32[2,2,2,64,256]{4,3,2,1,0:T(8,128)}, bf16[2,2,2,64,256]{4,3,2,1,0:T(8,1...) custom-call(s32[34]{0:T(128)} %concatenate.17.refs_0_, ...), custom_call_target="tpu_custom_call", output_to_operand_aliasing={{0}: (20, {}), {1}: (21, {})} | custom-call | tf_op jit(solution)/shard_map/pallas_call | solution.py:193
  65.7 2.3 %collective-permute-start.18 = (bf16[2,2,128,256]{3,2,1,0:T(8,128)(2,1)}, bf16[2,2,128,256]{3,2,1,0:T(8,128)(2,1)S(1)}, u32[]{:S(2)}, u32[]{:S(2)}) collective-permute-start(bf16[2,2,128,256]{3,2,1,0:T(8,128)(2,1)} %bitcast.101), channel_id=1, source_target_pairs={{0,2},{2,4},{4,6},{6,0},{8,10},{10,12},{12,14},{14,8},{1,3},{3,5},... | collective-permute-start | bytes 786440 | tf_op jit(solution)/shard_map/ppermute | solution.py:198
  68.0 1.7 %collective-permute-start.19 = (bf16[2,2,128,256]{3,2,1,0:T(8,128)(2,1)}, bf16[2,2,128,256]{3,2,1,0:T(8,128)(2,1)S(1)}, u32[]{:S(2)}, u32[]{:S(2)}) collective-permute-start(bf16[2,2,128,256]{3,2,1,0:T(8,128)(2,1)} %bitcast.100), channel_id=1, source_target_pairs={{0,4},{2,6},{4,0},{6,2},{8,12},{10,14},{12,8},{14,10},{1,5},{3,7},... | collective-permute-start | bytes 786440 | tf_op jit(solution)/shard_map/ppermute | solution.py:198
  70.0 1.5 %collective-permute-start.17 = (bf16[2,128,256]{2,1,0:T(8,128)(2,1)S(1)}, bf16[2,128,256]{2,1,0:T(8,128)(2,1)S(1)}, u32[]{:S(2)}, u32[]{:S(2)}) collective-permute-start(bf16[2,128,256]{2,1,0:T(8,128)(2,1)S(1)} %fusion.8), channel_id=1, source_target_pairs={{0,8},{2,10},{4,12},{6,14},{8,0},{10,2},{12,4},{14,6},{1,9},{3,11}... | collective-permute-start | bytes 393224 | tf_op jit(solution)/shard_map/ppermute | solution.py:201
  71.4 7.5 %collective-permute-done.18 = bf16[2,2,128,256]{3,2,1,0:T(8,128)(2,1)S(1)} collective-permute-done((bf16[2,2,128,256]{3,2,1,0:T(8,128)(2,1)}, bf16[2,2,128,256]{3,2,1,0:T(8,128)(2,1)S(1)}, u32[]{:S(2)}, u32[]{:S(2)}) %collective-permute-start.18) | collective-permute-done | bytes 262176 | tf_op jit(solution)/shard_map/ppermute | solution.py:198
  79.2 0.8 collective-permute-done.20
  80.1 2.4 %collective-permute-start.21 = (bf16[2,128,256]{2,1,0:T(8,128)(2,1)S(1)}, bf16[2,128,256]{2,1,0:T(8,128)(2,1)S(1)}, u32[]{:S(2)}, u32[]{:S(2)}) collective-permute-start(bf16[2,128,256]{2,1,0:T(8,128)(2,1)S(1)} %fusion.9), channel_id=1, source_target_pairs={{0,8},{2,10},{4,12},{6,14},{8,0},{10,2},{12,4},{14,6},{1,9},{3,11}... | collective-permute-start | bytes 393224 | tf_op jit(solution)/shard_map/ppermute | solution.py:201
  82.5 6.0 %collective-permute-done.21 = bf16[2,128,256]{2,1,0:T(8,128)(2,1)S(1)} collective-permute-done((bf16[2,128,256]{2,1,0:T(8,128)(2,1)S(1)}, bf16[2,128,256]{2,1,0:T(8,128)(2,1)S(1)}, u32[]{:S(2)}, u32[]{:S(2)}) %collective-permute-start.21) | collective-permute-done | bytes 131104 | tf_op jit(solution)/shard_map/ppermute | solution.py:201
  (83 shorter events, 8.3 us)
Async XLA Ops:
  1.6 11.6 %collective-permute-start.7 = (bf16[128,512]{1,0:T(8,128)(2,1)S(1)}, bf16[128,512]{1,0:T(8,128)(2,1)S(1)}, u32[]{:S(2)}, u32[]{:S(2)}) collective-permute-start(bf16[128,512]{1,0:T(8,128)(2,1)S(1)} %pad_maximum_fusion.1), channel_id=1, source_target_pairs={{0,8},{2,10},{4,12},{6,14},{8,0},{10,2},{12,4},{14,6},{1,9},{3,11}... | collective-permute-start | bytes 393224 | tf_op jit(solution)/shard_map/ppermute | solution.py:150
  5.7 11.8 %collective-permute-start.8 = (bf16[128,512]{1,0:T(8,128)(2,1)S(1)}, bf16[128,512]{1,0:T(8,128)(2,1)S(1)}, u32[]{:S(2)}, u32[]{:S(2)}) collective-permute-start(bf16[128,512]{1,0:T(8,128)(2,1)S(1)} %pad_maximum_fusion.1), channel_id=1, source_target_pairs={{0,2},{2,4},{4,6},{6,0},{8,10},{10,12},{12,14},{14,8},{1,3},{3,5},... | collective-permute-start | bytes 393224 | tf_op jit(solution)/shard_map/ppermute | solution.py:154
  7.2 10.3 %collective-permute-start.10 = (bf16[128,512]{1,0:T(8,128)(2,1)S(1)}, bf16[128,512]{1,0:T(8,128)(2,1)S(1)}, u32[]{:S(2)}, u32[]{:S(2)}) collective-permute-start(bf16[128,512]{1,0:T(8,128)(2,1)S(1)} %pad_maximum_fusion.1), channel_id=1, source_target_pairs={{0,4},{2,6},{4,0},{6,2},{8,12},{10,14},{12,8},{14,10},{1,5},{3,7},... | collective-permute-start | bytes 393224 | tf_op jit(solution)/shard_map/ppermute | solution.py:154
  8.8 12.1 %collective-permute-start.12 = (bf16[128,512]{1,0:T(8,128)(2,1)S(1)}, bf16[128,512]{1,0:T(8,128)(2,1)S(1)}, u32[]{:S(2)}, u32[]{:S(2)}) collective-permute-start(bf16[128,512]{1,0:T(8,128)(2,1)S(1)} %pad_maximum_fusion.1), channel_id=1, source_target_pairs={{0,6},{2,0},{4,2},{6,4},{8,14},{10,8},{12,10},{14,12},{1,7},{3,1},... | collective-permute-start | bytes 393224 | tf_op jit(solution)/shard_map/ppermute | solution.py:154
  10.2 29.5 %copy-start = (bf16[128,512]{1,0:T(8,128)(2,1)}, bf16[128,512]{1,0:T(8,128)(2,1)S(1)}, u32[]{:S(2)}) copy-start(bf16[128,512]{1,0:T(8,128)(2,1)S(1)} %pad_maximum_fusion) | copy-start | bytes 393220
  10.3 10.7 %collective-permute-start = (bf16[128,512]{1,0:T(8,128)(2,1)S(1)}, bf16[128,512]{1,0:T(8,128)(2,1)S(1)}, u32[]{:S(2)}, u32[]{:S(2)}) collective-permute-start(bf16[128,512]{1,0:T(8,128)(2,1)S(1)} %pad_maximum_fusion), channel_id=1, source_target_pairs={{0,8},{2,10},{4,12},{6,14},{8,0},{10,2},{12,4},{14,6},{1,9},{3,11}... | collective-permute-start | bytes 393224 | tf_op jit(solution)/shard_map/ppermute | solution.py:150
  13.3 27.3 %collective-permute-start.1 = (bf16[128,512]{1,0:T(8,128)(2,1)S(1)}, bf16[128,512]{1,0:T(8,128)(2,1)S(1)}, u32[]{:S(2)}, u32[]{:S(2)}) collective-permute-start(bf16[128,512]{1,0:T(8,128)(2,1)S(1)} %pad_maximum_fusion), channel_id=1, source_target_pairs={{0,2},{2,4},{4,6},{6,0},{8,10},{10,12},{12,14},{14,8},{1,3},{3,5},... | collective-permute-start | bytes 393224 | tf_op jit(solution)/shard_map/ppermute | solution.py:154
  17.5 23.8 %collective-permute-start.3 = (bf16[128,512]{1,0:T(8,128)(2,1)S(1)}, bf16[128,512]{1,0:T(8,128)(2,1)S(1)}, u32[]{:S(2)}, u32[]{:S(2)}) collective-permute-start(bf16[128,512]{1,0:T(8,128)(2,1)S(1)} %pad_maximum_fusion), channel_id=1, source_target_pairs={{0,4},{2,6},{4,0},{6,2},{8,12},{10,14},{12,8},{14,10},{1,5},{3,7},... | collective-permute-start | bytes 393224 | tf_op jit(solution)/shard_map/ppermute | solution.py:154
  17.6 11.2 %collective-permute-start.9 = (bf16[128,512]{1,0:T(8,128)(2,1)S(1)}, bf16[128,512]{1,0:T(8,128)(2,1)S(1)}, u32[]{:S(2)}, u32[]{:S(2)}) collective-permute-start(bf16[128,512]{1,0:T(8,128)(2,1)S(1)} %collective-permute-done.7), channel_id=1, source_target_pairs={{0,2},{2,4},{4,6},{6,0},{8,10},{10,12},{12,14},{14,8},{1,3},{3,5},... | collective-permute-start | bytes 393224 | tf_op jit(solution)/shard_map/ppermute | solution.py:154
  20.9 7.8 %collective-permute-start.11 = (bf16[128,512]{1,0:T(8,128)(2,1)S(1)}, bf16[128,512]{1,0:T(8,128)(2,1)S(1)}, u32[]{:S(2)}, u32[]{:S(2)}) collective-permute-start(bf16[128,512]{1,0:T(8,128)(2,1)S(1)} %collective-permute-done.7), channel_id=1, source_target_pairs={{0,4},{2,6},{4,0},{6,2},{8,12},{10,14},{12,8},{14,10},{1,5},{3,7},... | collective-permute-start | bytes 393224 | tf_op jit(solution)/shard_map/ppermute | solution.py:154
  20.9 23.8 %copy-start.4 = (bf16[128,512]{1,0:T(8,128)(2,1)}, bf16[128,512]{1,0:T(8,128)(2,1)S(1)}, u32[]{:S(2)}) copy-start(bf16[128,512]{1,0:T(8,128)(2,1)S(1)} %collective-permute-done) | copy-start | bytes 393220
  21.0 10.4 %collective-permute-start.13 = (bf16[128,512]{1,0:T(8,128)(2,1)S(1)}, bf16[128,512]{1,0:T(8,128)(2,1)S(1)}, u32[]{:S(2)}, u32[]{:S(2)}) collective-permute-start(bf16[128,512]{1,0:T(8,128)(2,1)S(1)} %collective-permute-done.7), channel_id=1, source_target_pairs={{0,6},{2,0},{4,2},{6,4},{8,14},{10,8},{12,10},{14,12},{1,7},{3,1},... | collective-permute-start | bytes 393224 | tf_op jit(solution)/shard_map/ppermute | solution.py:154
  28.7 15.4 %collective-permute-start.5 = (bf16[128,512]{1,0:T(8,128)(2,1)S(1)}, bf16[128,512]{1,0:T(8,128)(2,1)S(1)}, u32[]{:S(2)}, u32[]{:S(2)}) collective-permute-start(bf16[128,512]{1,0:T(8,128)(2,1)S(1)} %pad_maximum_fusion), channel_id=1, source_target_pairs={{0,6},{2,0},{4,2},{6,4},{8,14},{10,8},{12,10},{14,12},{1,7},{3,1},... | collective-permute-start | bytes 393224 | tf_op jit(solution)/shard_map/ppermute | solution.py:154
  28.7 16.0 %collective-permute-start.2 = (bf16[128,512]{1,0:T(8,128)(2,1)S(1)}, bf16[128,512]{1,0:T(8,128)(2,1)S(1)}, u32[]{:S(2)}, u32[]{:S(2)}) collective-permute-start(bf16[128,512]{1,0:T(8,128)(2,1)S(1)} %collective-permute-done), channel_id=1, source_target_pairs={{0,2},{2,4},{4,6},{6,0},{8,10},{10,12},{12,14},{14,8},{1,3},{3,5},... | collective-permute-start | bytes 393224 | tf_op jit(solution)/shard_map/ppermute | solution.py:154
  39.8 29.9 %collective-permute-start.14 = (bf16[2,2,128,256]{3,2,1,0:T(8,128)(2,1)}, bf16[2,2,128,256]{3,2,1,0:T(8,128)(2,1)S(1)}, u32[]{:S(2)}, u32[]{:S(2)}) collective-permute-start(bf16[2,2,128,256]{3,2,1,0:T(8,128)(2,1)} %bitcast.98), channel_id=1, source_target_pairs={{0,2},{2,4},{4,6},{6,0},{8,10},{10,12},{12,14},{14,8},{1,3},{3,5},... | collective-permute-start | bytes 786440 | tf_op jit(solution)/shard_map/ppermute | solution.py:198
  40.5 29.3 %collective-permute-start.15 = (bf16[2,2,128,256]{3,2,1,0:T(8,128)(2,1)}, bf16[2,2,128,256]{3,2,1,0:T(8,128)(2,1)S(1)}, u32[]{:S(2)}, u32[]{:S(2)}) collective-permute-start(bf16[2,2,128,256]{3,2,1,0:T(8,128)(2,1)} %bitcast.97), channel_id=1, source_target_pairs={{0,4},{2,6},{4,0},{6,2},{8,12},{10,14},{12,8},{14,10},{1,5},{3,7},... | collective-permute-start | bytes 786440 | tf_op jit(solution)/shard_map/ppermute | solution.py:198
  41.4 28.5 %collective-permute-start.16 = (bf16[2,2,128,256]{3,2,1,0:T(8,128)(2,1)}, bf16[2,2,128,256]{3,2,1,0:T(8,128)(2,1)S(1)}, u32[]{:S(2)}, u32[]{:S(2)}) collective-permute-start(bf16[2,2,128,256]{3,2,1,0:T(8,128)(2,1)} %bitcast.96), channel_id=1, source_target_pairs={{0,6},{2,0},{4,2},{6,4},{8,14},{10,8},{12,10},{14,12},{1,7},{3,1},... | collective-permute-start | bytes 786440 | tf_op jit(solution)/shard_map/ppermute | solution.py:198
  44.2 12.3 %collective-permute-start.4 = (bf16[128,512]{1,0:T(8,128)(2,1)S(1)}, bf16[128,512]{1,0:T(8,128)(2,1)S(1)}, u32[]{:S(2)}, u32[]{:S(2)}) collective-permute-start(bf16[128,512]{1,0:T(8,128)(2,1)S(1)} %collective-permute-done), channel_id=1, source_target_pairs={{0,4},{2,6},{4,0},{6,2},{8,12},{10,14},{12,8},{14,10},{1,5},{3,7},... | collective-permute-start | bytes 393224 | tf_op jit(solution)/shard_map/ppermute | solution.py:154
  44.8 12.4 %collective-permute-start.6 = (bf16[128,512]{1,0:T(8,128)(2,1)S(1)}, bf16[128,512]{1,0:T(8,128)(2,1)S(1)}, u32[]{:S(2)}, u32[]{:S(2)}) collective-permute-start(bf16[128,512]{1,0:T(8,128)(2,1)S(1)} %collective-permute-done), channel_id=1, source_target_pairs={{0,6},{2,0},{4,2},{6,4},{8,14},{10,8},{12,10},{14,12},{1,7},{3,1},... | collective-permute-start | bytes 393224 | tf_op jit(solution)/shard_map/ppermute | solution.py:154
  65.7 13.2 %collective-permute-start.18 = (bf16[2,2,128,256]{3,2,1,0:T(8,128)(2,1)}, bf16[2,2,128,256]{3,2,1,0:T(8,128)(2,1)S(1)}, u32[]{:S(2)}, u32[]{:S(2)}) collective-permute-start(bf16[2,2,128,256]{3,2,1,0:T(8,128)(2,1)} %bitcast.101), channel_id=1, source_target_pairs={{0,2},{2,4},{4,6},{6,0},{8,10},{10,12},{12,14},{14,8},{1,3},{3,5},... | collective-permute-start | bytes 786440 | tf_op jit(solution)/shard_map/ppermute | solution.py:198
  68.0 11.2 %collective-permute-start.19 = (bf16[2,2,128,256]{3,2,1,0:T(8,128)(2,1)}, bf16[2,2,128,256]{3,2,1,0:T(8,128)(2,1)S(1)}, u32[]{:S(2)}, u32[]{:S(2)}) collective-permute-start(bf16[2,2,128,256]{3,2,1,0:T(8,128)(2,1)} %bitcast.100), channel_id=1, source_target_pairs={{0,4},{2,6},{4,0},{6,2},{8,12},{10,14},{12,8},{14,10},{1,5},{3,7},... | collective-permute-start | bytes 786440 | tf_op jit(solution)/shard_map/ppermute | solution.py:198
  69.7 10.2 %collective-permute-start.20 = (bf16[2,2,128,256]{3,2,1,0:T(8,128)(2,1)}, bf16[2,2,128,256]{3,2,1,0:T(8,128)(2,1)S(1)}, u32[]{:S(2)}, u32[]{:S(2)}) collective-permute-start(bf16[2,2,128,256]{3,2,1,0:T(8,128)(2,1)} %bitcast.99), channel_id=1, source_target_pairs={{0,6},{2,0},{4,2},{6,4},{8,14},{10,8},{12,10},{14,12},{1,7},{3,1},... | collective-permute-start | bytes 786440 | tf_op jit(solution)/shard_map/ppermute | solution.py:198
  70.0 12.5 %collective-permute-start.17 = (bf16[2,128,256]{2,1,0:T(8,128)(2,1)S(1)}, bf16[2,128,256]{2,1,0:T(8,128)(2,1)S(1)}, u32[]{:S(2)}, u32[]{:S(2)}) collective-permute-start(bf16[2,128,256]{2,1,0:T(8,128)(2,1)S(1)} %fusion.8), channel_id=1, source_target_pairs={{0,8},{2,10},{4,12},{6,14},{8,0},{10,2},{12,4},{14,6},{1,9},{3,11}... | collective-permute-start | bytes 393224 | tf_op jit(solution)/shard_map/ppermute | solution.py:201
  80.1 8.5 %collective-permute-start.21 = (bf16[2,128,256]{2,1,0:T(8,128)(2,1)S(1)}, bf16[2,128,256]{2,1,0:T(8,128)(2,1)S(1)}, u32[]{:S(2)}, u32[]{:S(2)}) collective-permute-start(bf16[2,128,256]{2,1,0:T(8,128)(2,1)S(1)} %fusion.9), channel_id=1, source_target_pairs={{0,8},{2,10},{4,12},{6,14},{8,0},{10,2},{12,4},{14,6},{1,9},{3,11}... | collective-permute-start | bytes 393224 | tf_op jit(solution)/shard_map/ppermute | solution.py:201
  (18 other events, 153.4 us)

commit v13 on v11

--- a/solution.py
+++ b/solution.py
@@ -144,10 +144,18 @@
     query_grad = None
     key_grads = []
     value_grads = []
+    pairs = [jnp.concatenate([key_rows[:, c * chunk_cols:(c + 1) * chunk_cols],
+                              value_rows[:, c * chunk_cols:(c + 1) * chunk_cols]], axis=1)
+             for c in range(chunks)]
+    partners = []
     for chunk in range(chunks):
-        cols = slice(chunk * chunk_cols, (chunk + 1) * chunk_cols)
-        pair = jnp.concatenate([key_rows[:, cols], value_rows[:, cols]], axis=1)
-        both = jnp.stack([pair, lax.ppermute(pair, "ctx", cross_pairs())])
+        partners.append(lax.ppermute(pairs[chunk], "ctx", cross_pairs()))
+        if chunk + 1 < chunks:
+            partners[chunk], pairs[chunk + 1] = lax.optimization_barrier(
+                (partners[chunk], pairs[chunk + 1]))
+    for chunk in range(chunks):
+        pair = pairs[chunk]
+        both = jnp.stack([pair, partners[chunk]])
         pieces = [both]
         for shift in range(1, half):
             pieces.append(lax.ppermute(both, "ctx", half_pairs(shift)))

time: 76.8 us -> 76.7 us (level)
  the two profiles are of different devices: /device:TPU:0 before, /device:TPU:6 now
where the time goes in v13:
time: 76.7 us; the launch traced here: 76.4 us
  waiting for transfers between devices  29.3 us (38%)
  starting transfers between devices  23.3 us (30%)
  Pallas kernels  15.4 us (20%)
  local copies, waits for them, and re-layouts  5.56 us (7%)
  other arithmetic  2.06 us (3%)
  between operations  0.84 us (1%)
    pallas_call x2, Pallas kernels, local(): attended, query_grad, own_pack, *send_packs = kernel(*operands)  15.4 us
    ppermute x6, waiting for transfers between devices, local(): lax.ppermute(send_packs[shift - 1].reshape(pack_shape), 'ctx', half_pairs...  10.3 us
    ppermute x6, starting transfers between devices, local(): pieces.append(lax.ppermute(both, 'ctx', half_pairs(shift)))  9.71 us
    ppermute x2, waiting for transfers between devices, local(): partners.append(lax.ppermute(pairs[chunk], 'ctx', cross_pairs()))  7.67 us
    ppermute x6, starting transfers between devices, local(): lax.ppermute(send_packs[shift - 1].reshape(pack_shape), 'ctx', half_pairs...  7.08 us
    ppermute x2, waiting for transfers between devices, local(): lax.ppermute(summed[1].astype(jnp.bfloat16), 'ctx', cross_pairs())  6.17 us
    ppermute x6, waiting for transfers between devices, local(): pieces.append(lax.ppermute(both, 'ctx', half_pairs(shift)))  5.19 us
    ppermute x2, starting transfers between devices, local(): lax.ppermute(summed[1].astype(jnp.bfloat16), 'ctx', cross_pairs())  3.81 us
  transfers between devices with their start and end apart: 16, of which 8 were waited for; matrix products, arithmetic and copies ran while one was open for 3% of the time, Pallas kernels for 20%

profile of v13, /device:TPU:6, one launch (start us, length us, event | category | flops | bytes accessed | tf_op | source)
XLA Modules:
  0.0 76.4 jit_solution(17475857031892381472)
XLA Ops:
  0.6 1.0 %fusion.17 = (bf16[128,256]{1,0:T(8,128)(2,1)S(1)}, bf16[128,256]{1,0:T(8,128)(2,1)S(1)}, bf16[128,256]{1,0:T(8,128)(2,1)S(1)}, bf16[128,256]{1,0:T(8,128)(2,1)S(1)}) fusion(bf16[128,512]{1,0:T(8,128)(2,1)} %param.7, bf16[128,512]{1,0:T(8,128)(2,1)} %param.8), kind=kLoop, calls=%fused_computation.48 | loop fusion | bytes 524288 | tf_op jit(solution)/shard_map/slice | solution.py:147
  1.6 2.7 %collective-permute-start = (bf16[128,512]{1,0:T(8,128)(2,1)S(1)}, bf16[128,512]{1,0:T(8,128)(2,1)S(1)}, u32[]{:S(2)}, u32[]{:S(2)}) collective-permute-start(bf16[128,512]{1,0:T(8,128)(2,1)S(1)} %get-tuple-element.41), channel_id=1, source_target_pairs={{0,8},{2,10},{4,12},{6,14},{8,0},{10,2},{12,4},{14,6},{1,9},{3,11}... | collective-permute-start | bytes 393224 | tf_op jit(solution)/shard_map/ppermute | solution.py:152
  5.0 5.6 %collective-permute-done = bf16[128,512]{1,0:T(8,128)(2,1)S(1)} collective-permute-done((bf16[128,512]{1,0:T(8,128)(2,1)S(1)}, bf16[128,512]{1,0:T(8,128)(2,1)S(1)}, u32[]{:S(2)}, u32[]{:S(2)}) %collective-permute-start) | collective-permute-done | bytes 131104 | tf_op jit(solution)/shard_map/ppermute | solution.py:152
  11.1 4.0 %collective-permute-start.5 = (bf16[2,128,512]{2,1,0:T(8,128)(2,1)S(1)}, bf16[2,128,512]{2,1,0:T(8,128)(2,1)S(1)}, u32[]{:S(2)}, u32[]{:S(2)}) collective-permute-start(bf16[2,128,512]{2,1,0:T(8,128)(2,1)S(1)} %pad_maximum_fusion.1), channel_id=1, source_target_pairs={{0,2},{2,4},{4,6},{6,0},{8,10},{10,12},{12,14},{14,8},{1,3},{3,5},... | collective-permute-start | bytes 786440 | tf_op jit(solution)/shard_map/ppermute | solution.py:161
  15.3 1.9 %collective-permute-start.7 = (bf16[2,128,512]{2,1,0:T(8,128)(2,1)S(1)}, bf16[2,128,512]{2,1,0:T(8,128)(2,1)S(1)}, u32[]{:S(2)}, u32[]{:S(2)}) collective-permute-start(bf16[2,128,512]{2,1,0:T(8,128)(2,1)S(1)} %pad_maximum_fusion.1), channel_id=1, source_target_pairs={{0,6},{2,0},{4,2},{6,4},{8,14},{10,8},{12,10},{14,12},{1,7},{3,1},... | collective-permute-start | bytes 786440 | tf_op jit(solution)/shard_map/ppermute | solution.py:161
  17.2 2.1 %collective-permute-done.1 = bf16[128,512]{1,0:T(8,128)(2,1)S(1)} collective-permute-done((bf16[128,512]{1,0:T(8,128)(2,1)S(1)}, bf16[128,512]{1,0:T(8,128)(2,1)S(1)}, u32[]{:S(2)}, u32[]{:S(2)}) %collective-permute-start.1) | collective-permute-done | bytes 131104 | tf_op jit(solution)/shard_map/ppermute | solution.py:152
  20.1 0.8 %reshape.110.refs_1_ = s32[2,64,1]{2,1,0:T(8,128)} reshape(s32[128]{0:T(128)S(1)} %copy-done.11) | data formatting | bytes 1024 | tf_op jit(solution)/shard_map/reshape | solution.py:135
  21.0 0.7 concatenate.17.refs_0_
  21.6 2.0 %collective-permute-start.3 = (bf16[2,128,512]{2,1,0:T(8,128)(2,1)S(1)}, bf16[2,128,512]{2,1,0:T(8,128)(2,1)S(1)}, u32[]{:S(2)}, u32[]{:S(2)}) collective-permute-start(bf16[2,128,512]{2,1,0:T(8,128)(2,1)S(1)} %pad_maximum_fusion), channel_id=1, source_target_pairs={{0,4},{2,6},{4,0},{6,2},{8,12},{10,14},{12,8},{14,10},{1,5},{3,7},... | collective-permute-start | bytes 786440 | tf_op jit(solution)/shard_map/ppermute | solution.py:161
  23.6 1.6 %collective-permute-start.4 = (bf16[2,128,512]{2,1,0:T(8,128)(2,1)S(1)}, bf16[2,128,512]{2,1,0:T(8,128)(2,1)S(1)}, u32[]{:S(2)}, u32[]{:S(2)}) collective-permute-start(bf16[2,128,512]{2,1,0:T(8,128)(2,1)S(1)} %pad_maximum_fusion), channel_id=1, source_target_pairs={{0,6},{2,0},{4,2},{6,4},{8,14},{10,8},{12,10},{14,12},{1,7},{3,1},... | collective-permute-start | bytes 786440 | tf_op jit(solution)/shard_map/ppermute | solution.py:161
  25.2 4.2 %collective-permute-done.6 = bf16[2,128,512]{2,1,0:T(8,128)(2,1)S(1)} collective-permute-done((bf16[2,128,512]{2,1,0:T(8,128)(2,1)S(1)}, bf16[2,128,512]{2,1,0:T(8,128)(2,1)S(1)}, u32[]{:S(2)}, u32[]{:S(2)}) %collective-permute-start.6) | collective-permute-done | bytes 262176 | tf_op jit(solution)/shard_map/ppermute | solution.py:161
  29.3 1.0 %collective-permute-done.7 = bf16[2,128,512]{2,1,0:T(8,128)(2,1)S(1)} collective-permute-done((bf16[2,128,512]{2,1,0:T(8,128)(2,1)S(1)}, bf16[2,128,512]{2,1,0:T(8,128)(2,1)S(1)}, u32[]{:S(2)}, u32[]{:S(2)}) %collective-permute-start.7) | collective-permute-done | bytes 262176 | tf_op jit(solution)/shard_map/ppermute | solution.py:161
  30.4 0.7 copy-done.5
  31.1 7.6 %shard_map.93 = (bf16[128,4096]{1,0:T(8,128)(2,1)}, bf16[128,4096]{1,0:T(8,128)(2,1)}, f32[2,2,2,64,256]{4,3,2,1,0:T(8,128)}, bf16[2,2,2,64,256]{4,3,2,1,0:T(8,1...) custom-call(s32[34]{0:T(128)} %concatenate.17.refs_0_, s32[2,64,1]{2,1,0:T(8,128)} %reshape.110.refs_1_, ...), custom_call_target="tpu_custom_call" | custom-call | tf_op jit(solution)/shard_map/pallas_call | solution.py:200
  39.2 2.4 %collective-permute-start.8 = (bf16[2,2,128,256]{3,2,1,0:T(8,128)(2,1)}, bf16[2,2,128,256]{3,2,1,0:T(8,128)(2,1)S(1)}, u32[]{:S(2)}, u32[]{:S(2)}) collective-permute-start(bf16[2,2,128,256]{3,2,1,0:T(8,128)(2,1)} %bitcast.81), channel_id=1, source_target_pairs={{0,2},{2,4},{4,6},{6,0},{8,10},{10,12},{12,14},{14,8},{1,3},{3,5},... | collective-permute-start | bytes 786440 | tf_op jit(solution)/shard_map/ppermute | solution.py:205
  41.7 1.2 %collective-permute-start.9 = (bf16[2,2,128,256]{3,2,1,0:T(8,128)(2,1)}, bf16[2,2,128,256]{3,2,1,0:T(8,128)(2,1)S(1)}, u32[]{:S(2)}, u32[]{:S(2)}) collective-permute-start(bf16[2,2,128,256]{3,2,1,0:T(8,128)(2,1)} %bitcast.80), channel_id=1, source_target_pairs={{0,4},{2,6},{4,0},{6,2},{8,12},{10,14},{12,8},{14,10},{1,5},{3,7},... | collective-permute-start | bytes 786440 | tf_op jit(solution)/shard_map/ppermute | solution.py:205
  43.7 7.8 %shard_map.94 = (bf16[128,4096]{1,0:T(8,128)(2,1)}, bf16[128,4096]{1,0:T(8,128)(2,1)}, f32[2,2,2,64,256]{4,3,2,1,0:T(8,128)}, bf16[2,2,2,64,256]{4,3,2,1,0:T(8,1...) custom-call(s32[34]{0:T(128)} %concatenate.17.refs_0_, ...), custom_call_target="tpu_custom_call", output_to_operand_aliasing={{0}: (12, {}), {1}: (13, {})} | custom-call | tf_op jit(solution)/shard_map/pallas_call | solution.py:200
  51.6 0.8 %collective-permute-start.13 = (bf16[2,2,128,256]{3,2,1,0:T(8,128)(2,1)}, bf16[2,2,128,256]{3,2,1,0:T(8,128)(2,1)S(1)}, u32[]{:S(2)}, u32[]{:S(2)}) collective-permute-start(bf16[2,2,128,256]{3,2,1,0:T(8,128)(2,1)} %bitcast.84), channel_id=1, source_target_pairs={{0,4},{2,6},{4,0},{6,2},{8,12},{10,14},{12,8},{14,10},{1,5},{3,7},... | collective-permute-start | bytes 786440 | tf_op jit(solution)/shard_map/ppermute | solution.py:205
  52.4 1.9 %collective-permute-start.14 = (bf16[2,2,128,256]{3,2,1,0:T(8,128)(2,1)}, bf16[2,2,128,256]{3,2,1,0:T(8,128)(2,1)S(1)}, u32[]{:S(2)}, u32[]{:S(2)}) collective-permute-start(bf16[2,2,128,256]{3,2,1,0:T(8,128)(2,1)} %bitcast.82), channel_id=1, source_target_pairs={{0,6},{2,0},{4,2},{6,4},{8,14},{10,8},{12,10},{14,12},{1,7},{3,1},... | collective-permute-start | bytes 786440 | tf_op jit(solution)/shard_map/ppermute | solution.py:205
  54.5 3.2 %collective-permute-start.11 = (bf16[2,128,256]{2,1,0:T(8,128)(2,1)S(1)}, bf16[2,128,256]{2,1,0:T(8,128)(2,1)S(1)}, u32[]{:S(2)}, u32[]{:S(2)}) collective-permute-start(bf16[2,128,256]{2,1,0:T(8,128)(2,1)S(1)} %fusion.8), channel_id=1, source_target_pairs={{0,8},{2,10},{4,12},{6,14},{8,0},{10,2},{12,4},{14,6},{1,9},{3,11}... | collective-permute-start | bytes 393224 | tf_op jit(solution)/shard_map/ppermute | solution.py:208
  57.8 1.6 %collective-permute-done.12 = bf16[2,2,128,256]{3,2,1,0:T(8,128)(2,1)S(1)} collective-permute-done((bf16[2,2,128,256]{3,2,1,0:T(8,128)(2,1)}, bf16[2,2,128,256]{3,2,1,0:T(8,128)(2,1)S(1)}, u32[]{:S(2)}, u32[]{:S(2)}) %collective-permute-start.12) | collective-permute-done | bytes 262176 | tf_op jit(solution)/shard_map/ppermute | solution.py:205
  59.4 6.5 %collective-permute-done.13 = bf16[2,2,128,256]{3,2,1,0:T(8,128)(2,1)S(1)} collective-permute-done((bf16[2,2,128,256]{3,2,1,0:T(8,128)(2,1)}, bf16[2,2,128,256]{3,2,1,0:T(8,128)(2,1)S(1)}, u32[]{:S(2)}, u32[]{:S(2)}) %collective-permute-start.13) | collective-permute-done | bytes 262176 | tf_op jit(solution)/shard_map/ppermute | solution.py:205
  65.9 2.2 %collective-permute-done.14 = bf16[2,2,128,256]{3,2,1,0:T(8,128)(2,1)S(1)} collective-permute-done((bf16[2,2,128,256]{3,2,1,0:T(8,128)(2,1)}, bf16[2,2,128,256]{3,2,1,0:T(8,128)(2,1)S(1)}, u32[]{:S(2)}, u32[]{:S(2)}) %collective-permute-start.14) | collective-permute-done | bytes 262176 | tf_op jit(solution)/shard_map/ppermute | solution.py:205
  68.8 6.2 %collective-permute-done.15 = bf16[2,128,256]{2,1,0:T(8,128)(2,1)S(1)} collective-permute-done((bf16[2,128,256]{2,1,0:T(8,128)(2,1)S(1)}, bf16[2,128,256]{2,1,0:T(8,128)(2,1)S(1)}, u32[]{:S(2)}, u32[]{:S(2)}) %collective-permute-start.15) | collective-permute-done | bytes 131104 | tf_op jit(solution)/shard_map/ppermute | solution.py:208
  (58 shorter events, 5.9 us)
Async XLA Ops:
  1.6 9.0 %collective-permute-start = (bf16[128,512]{1,0:T(8,128)(2,1)S(1)}, bf16[128,512]{1,0:T(8,128)(2,1)S(1)}, u32[]{:S(2)}, u32[]{:S(2)}) collective-permute-start(bf16[128,512]{1,0:T(8,128)(2,1)S(1)} %get-tuple-element.41), channel_id=1, source_target_pairs={{0,8},{2,10},{4,12},{6,14},{8,0},{10,2},{12,4},{14,6},{1,9},{3,11}... | collective-permute-start | bytes 393224 | tf_op jit(solution)/shard_map/ppermute | solution.py:152
  10.6 8.7 %collective-permute-start.1 = (bf16[128,512]{1,0:T(8,128)(2,1)S(1)}, bf16[128,512]{1,0:T(8,128)(2,1)S(1)}, u32[]{:S(2)}, u32[]{:S(2)}) collective-permute-start(bf16[128,512]{1,0:T(8,128)(2,1)S(1)} %pad_maximum_fusion.3), channel_id=1, source_target_pairs={{0,8},{2,10},{4,12},{6,14},{8,0},{10,2},{12,4},{14,6},{1,9},{3,11}... | collective-permute-start | bytes 393224 | tf_op jit(solution)/shard_map/ppermute | solution.py:152
  11.1 8.2 %copy-start.1 = (bf16[2,128,512]{2,1,0:T(8,128)(2,1)}, bf16[2,128,512]{2,1,0:T(8,128)(2,1)S(1)}, u32[]{:S(2)}) copy-start(bf16[2,128,512]{2,1,0:T(8,128)(2,1)S(1)} %pad_maximum_fusion.1) | copy-start | bytes 786436
  11.1 12.5 %collective-permute-start.5 = (bf16[2,128,512]{2,1,0:T(8,128)(2,1)S(1)}, bf16[2,128,512]{2,1,0:T(8,128)(2,1)S(1)}, u32[]{:S(2)}, u32[]{:S(2)}) collective-permute-start(bf16[2,128,512]{2,1,0:T(8,128)(2,1)S(1)} %pad_maximum_fusion.1), channel_id=1, source_target_pairs={{0,2},{2,4},{4,6},{6,0},{8,10},{10,12},{12,14},{14,8},{1,3},{3,5},... | collective-permute-start | bytes 786440 | tf_op jit(solution)/shard_map/ppermute | solution.py:161
  15.1 14.2 %collective-permute-start.6 = (bf16[2,128,512]{2,1,0:T(8,128)(2,1)S(1)}, bf16[2,128,512]{2,1,0:T(8,128)(2,1)S(1)}, u32[]{:S(2)}, u32[]{:S(2)}) collective-permute-start(bf16[2,128,512]{2,1,0:T(8,128)(2,1)S(1)} %pad_maximum_fusion.1), channel_id=1, source_target_pairs={{0,4},{2,6},{4,0},{6,2},{8,12},{10,14},{12,8},{14,10},{1,5},{3,7},... | collective-permute-start | bytes 786440 | tf_op jit(solution)/shard_map/ppermute | solution.py:161
  15.3 15.1 %collective-permute-start.7 = (bf16[2,128,512]{2,1,0:T(8,128)(2,1)S(1)}, bf16[2,128,512]{2,1,0:T(8,128)(2,1)S(1)}, u32[]{:S(2)}, u32[]{:S(2)}) collective-permute-start(bf16[2,128,512]{2,1,0:T(8,128)(2,1)S(1)} %pad_maximum_fusion.1), channel_id=1, source_target_pairs={{0,6},{2,0},{4,2},{6,4},{8,14},{10,8},{12,10},{14,12},{1,7},{3,1},... | collective-permute-start | bytes 786440 | tf_op jit(solution)/shard_map/ppermute | solution.py:161
  19.3 19.4 %copy-start = (bf16[2,128,512]{2,1,0:T(8,128)(2,1)}, bf16[2,128,512]{2,1,0:T(8,128)(2,1)S(1)}, u32[]{:S(2)}) copy-start(bf16[2,128,512]{2,1,0:T(8,128)(2,1)S(1)} %pad_maximum_fusion) | copy-start | bytes 786436
  19.3 22.3 %collective-permute-start.2 = (bf16[2,128,512]{2,1,0:T(8,128)(2,1)S(1)}, bf16[2,128,512]{2,1,0:T(8,128)(2,1)S(1)}, u32[]{:S(2)}, u32[]{:S(2)}) collective-permute-start(bf16[2,128,512]{2,1,0:T(8,128)(2,1)S(1)} %pad_maximum_fusion), channel_id=1, source_target_pairs={{0,2},{2,4},{4,6},{6,0},{8,10},{10,12},{12,14},{14,8},{1,3},{3,5},... | collective-permute-start | bytes 786440 | tf_op jit(solution)/shard_map/ppermute | solution.py:161
  21.6 21.3 %collective-permute-start.3 = (bf16[2,128,512]{2,1,0:T(8,128)(2,1)S(1)}, bf16[2,128,512]{2,1,0:T(8,128)(2,1)S(1)}, u32[]{:S(2)}, u32[]{:S(2)}) collective-permute-start(bf16[2,128,512]{2,1,0:T(8,128)(2,1)S(1)} %pad_maximum_fusion), channel_id=1, source_target_pairs={{0,4},{2,6},{4,0},{6,2},{8,12},{10,14},{12,8},{14,10},{1,5},{3,7},... | collective-permute-start | bytes 786440 | tf_op jit(solution)/shard_map/ppermute | solution.py:161
  23.6 6.8 %copy-start.3 = (bf16[2,128,512]{2,1,0:T(8,128)(2,1)}, bf16[2,128,512]{2,1,0:T(8,128)(2,1)S(1)}, u32[]{:S(2)}) copy-start(bf16[2,128,512]{2,1,0:T(8,128)(2,1)S(1)} %collective-permute-done.5) | copy-start | bytes 786436
  23.6 19.3 %collective-permute-start.4 = (bf16[2,128,512]{2,1,0:T(8,128)(2,1)S(1)}, bf16[2,128,512]{2,1,0:T(8,128)(2,1)S(1)}, u32[]{:S(2)}, u32[]{:S(2)}) collective-permute-start(bf16[2,128,512]{2,1,0:T(8,128)(2,1)S(1)} %pad_maximum_fusion), channel_id=1, source_target_pairs={{0,6},{2,0},{4,2},{6,4},{8,14},{10,8},{12,10},{14,12},{1,7},{3,1},... | collective-permute-start | bytes 786440 | tf_op jit(solution)/shard_map/ppermute | solution.py:161
  29.3 1.0 %copy-start.4 = (bf16[2,128,512]{2,1,0:T(8,128)(2,1)}, bf16[2,128,512]{2,1,0:T(8,128)(2,1)S(1)}, u32[]{:S(2)}) copy-start(bf16[2,128,512]{2,1,0:T(8,128)(2,1)S(1)} %collective-permute-done.6) | copy-start | bytes 786436
  38.7 13.7 %collective-permute-start.10 = (bf16[2,2,128,256]{3,2,1,0:T(8,128)(2,1)}, bf16[2,2,128,256]{3,2,1,0:T(8,128)(2,1)S(1)}, u32[]{:S(2)}, u32[]{:S(2)}) collective-permute-start(bf16[2,2,128,256]{3,2,1,0:T(8,128)(2,1)} %bitcast.83), channel_id=1, source_target_pairs={{0,6},{2,0},{4,2},{6,4},{8,14},{10,8},{12,10},{14,12},{1,7},{3,1},... | collective-permute-start | bytes 786440 | tf_op jit(solution)/shard_map/ppermute | solution.py:205
  39.2 15.1 %collective-permute-start.8 = (bf16[2,2,128,256]{3,2,1,0:T(8,128)(2,1)}, bf16[2,2,128,256]{3,2,1,0:T(8,128)(2,1)S(1)}, u32[]{:S(2)}, u32[]{:S(2)}) collective-permute-start(bf16[2,2,128,256]{3,2,1,0:T(8,128)(2,1)} %bitcast.81), channel_id=1, source_target_pairs={{0,2},{2,4},{4,6},{6,0},{8,10},{10,12},{12,14},{14,8},{1,3},{3,5},... | collective-permute-start | bytes 786440 | tf_op jit(solution)/shard_map/ppermute | solution.py:205
  41.7 1.2 %copy-start.2 = (bf16[2,128,512]{2,1,0:T(8,128)(2,1)}, bf16[2,128,512]{2,1,0:T(8,128)(2,1)S(1)}, u32[]{:S(2)}) copy-start(bf16[2,128,512]{2,1,0:T(8,128)(2,1)S(1)} %collective-permute-done.2) | copy-start | bytes 786436
  41.7 12.7 %collective-permute-start.9 = (bf16[2,2,128,256]{3,2,1,0:T(8,128)(2,1)}, bf16[2,2,128,256]{3,2,1,0:T(8,128)(2,1)S(1)}, u32[]{:S(2)}, u32[]{:S(2)}) collective-permute-start(bf16[2,2,128,256]{3,2,1,0:T(8,128)(2,1)} %bitcast.80), channel_id=1, source_target_pairs={{0,4},{2,6},{4,0},{6,2},{8,12},{10,14},{12,8},{14,10},{1,5},{3,7},... | collective-permute-start | bytes 786440 | tf_op jit(solution)/shard_map/ppermute | solution.py:205
  42.9 0.8 %copy-start.7 = (bf16[2,128,512]{2,1,0:T(8,128)(2,1)}, bf16[2,128,512]{2,1,0:T(8,128)(2,1)S(1)}, u32[]{:S(2)}) copy-start(bf16[2,128,512]{2,1,0:T(8,128)(2,1)S(1)} %collective-permute-done.4) | copy-start | bytes 786436
  43.7 10.7 %copy-start.8 = (f32[2,2,2,64,256]{4,3,2,1,0:T(8,128)S(1)}, f32[2,2,2,64,256]{4,3,2,1,0:T(8,128)}, u32[]{:S(2)}) copy-start(f32[2,2,2,64,256]{4,3,2,1,0:T(8,128)} %get-tuple-element.24) | copy-start | bytes 1572868
  51.5 7.9 %collective-permute-start.12 = (bf16[2,2,128,256]{3,2,1,0:T(8,128)(2,1)}, bf16[2,2,128,256]{3,2,1,0:T(8,128)(2,1)S(1)}, u32[]{:S(2)}, u32[]{:S(2)}) collective-permute-start(bf16[2,2,128,256]{3,2,1,0:T(8,128)(2,1)} %bitcast.85), channel_id=1, source_target_pairs={{0,2},{2,4},{4,6},{6,0},{8,10},{10,12},{12,14},{14,8},{1,3},{3,5},... | collective-permute-start | bytes 786440 | tf_op jit(solution)/shard_map/ppermute | solution.py:205
  51.6 14.3 %collective-permute-start.13 = (bf16[2,2,128,256]{3,2,1,0:T(8,128)(2,1)}, bf16[2,2,128,256]{3,2,1,0:T(8,128)(2,1)S(1)}, u32[]{:S(2)}, u32[]{:S(2)}) collective-permute-start(bf16[2,2,128,256]{3,2,1,0:T(8,128)(2,1)} %bitcast.84), channel_id=1, source_target_pairs={{0,4},{2,6},{4,0},{6,2},{8,12},{10,14},{12,8},{14,10},{1,5},{3,7},... | collective-permute-start | bytes 786440 | tf_op jit(solution)/shard_map/ppermute | solution.py:205
  52.4 15.6 %collective-permute-start.14 = (bf16[2,2,128,256]{3,2,1,0:T(8,128)(2,1)}, bf16[2,2,128,256]{3,2,1,0:T(8,128)(2,1)S(1)}, u32[]{:S(2)}, u32[]{:S(2)}) collective-permute-start(bf16[2,2,128,256]{3,2,1,0:T(8,128)(2,1)} %bitcast.82), channel_id=1, source_target_pairs={{0,6},{2,0},{4,2},{6,4},{8,14},{10,8},{12,10},{14,12},{1,7},{3,1},... | collective-permute-start | bytes 786440 | tf_op jit(solution)/shard_map/ppermute | solution.py:205
  54.4 13.7 %copy-start.9 = (f32[2,2,2,64,256]{4,3,2,1,0:T(8,128)S(1)}, f32[2,2,2,64,256]{4,3,2,1,0:T(8,128)}, u32[]{:S(2)}) copy-start(f32[2,2,2,64,256]{4,3,2,1,0:T(8,128)} %get-tuple-element.28) | copy-start | bytes 1572868
  54.5 14.2 %collective-permute-start.11 = (bf16[2,128,256]{2,1,0:T(8,128)(2,1)S(1)}, bf16[2,128,256]{2,1,0:T(8,128)(2,1)S(1)}, u32[]{:S(2)}, u32[]{:S(2)}) collective-permute-start(bf16[2,128,256]{2,1,0:T(8,128)(2,1)S(1)} %fusion.8), channel_id=1, source_target_pairs={{0,8},{2,10},{4,12},{6,14},{8,0},{10,2},{12,4},{14,6},{1,9},{3,11}... | collective-permute-start | bytes 393224 | tf_op jit(solution)/shard_map/ppermute | solution.py:208
  68.2 6.8 %collective-permute-start.15 = (bf16[2,128,256]{2,1,0:T(8,128)(2,1)S(1)}, bf16[2,128,256]{2,1,0:T(8,128)(2,1)S(1)}, u32[]{:S(2)}, u32[]{:S(2)}) collective-permute-start(bf16[2,128,256]{2,1,0:T(8,128)(2,1)S(1)} %fusion.9), channel_id=1, source_target_pairs={{0,8},{2,10},{4,12},{6,14},{8,0},{10,2},{12,4},{14,6},{1,9},{3,11}... | collective-permute-start | bytes 393224 | tf_op jit(solution)/shard_map/ppermute | solution.py:208
  (4 other events, 2.7 us)

commit v14 on v11

--- a/solution.py
+++ b/solution.py
@@ -144,10 +144,13 @@
     query_grad = None
     key_grads = []
     value_grads = []
+    partner_keys = lax.ppermute(key_rows, "ctx", cross_pairs())
+    partner_values = lax.ppermute(value_rows, "ctx", cross_pairs())
     for chunk in range(chunks):
         cols = slice(chunk * chunk_cols, (chunk + 1) * chunk_cols)
         pair = jnp.concatenate([key_rows[:, cols], value_rows[:, cols]], axis=1)
-        both = jnp.stack([pair, lax.ppermute(pair, "ctx", cross_pairs())])
+        partner = jnp.concatenate([partner_keys[:, cols], partner_values[:, cols]], axis=1)
+        both = jnp.stack([pair, partner])
         pieces = [both]
         for shift in range(1, half):
             pieces.append(lax.ppermute(both, "ctx", half_pairs(shift)))

time: 76.8 us -> 79 us (1.029)
  waiting for transfers between devices: 28.1 us -> 29.2 us
  starting transfers between devices: 24.7 us -> 25.7 us
    ppermute x2, starting transfers between devices: 6.95 us -> 8.42 us  [local(): lax.ppermute(summed[1].astype(jnp.bfloat16), 'ctx', cross_pairs())]
    ppermute x2, waiting for transfers between devices: 8.66 us -> 9.92 us  [the longest x1 7.95 us: local(): partner_keys = lax.ppermute(key_rows, 'ctx', cross_pairs())]
    unnamed x24 -> x26, local copies, waits for them, and re-layouts: 2.82 us -> 2.82 us
  transfers between devices with their start and end apart: 16 -> 16, of which waited for: 6 -> 7; matrix products, arithmetic and copies ran while one was open for 3% -> 4% of each run, Pallas kernels for 20% -> 20%
where the time goes in v14:
time: 79 us; the launch traced here: 78.7 us
  waiting for transfers between devices  29.2 us (37%)
  starting transfers between devices  25.7 us (33%)
  Pallas kernels  15.4 us (19%)
  local copies, waits for them, and re-layouts  5.47 us (7%)
  other arithmetic  2.09 us (3%)
  between operations  0.85 us (1%)
    pallas_call x2, Pallas kernels, local(): attended, query_grad, own_pack, *send_packs = kernel(*operands)  15.4 us
    ppermute x2, starting transfers between devices, local(): lax.ppermute(summed[1].astype(jnp.bfloat16), 'ctx', cross_pairs())  8.42 us
    ppermute x1, waiting for transfers between devices, local(): partner_keys = lax.ppermute(key_rows, 'ctx', cross_pairs())  7.95 us
    ppermute x6, waiting for transfers between devices, local(): pieces.append(lax.ppermute(both, 'ctx', half_pairs(shift)))  7.94 us
    ppermute x6, starting transfers between devices, local(): lax.ppermute(send_packs[shift - 1].reshape(pack_shape), 'ctx', half_pairs...  7.39 us
    ppermute x6, waiting for transfers between devices, local(): lax.ppermute(send_packs[shift - 1].reshape(pack_shape), 'ctx', half_pairs...  6.62 us
    ppermute x6, starting transfers between devices, local(): pieces.append(lax.ppermute(both, 'ctx', half_pairs(shift)))  5.75 us
    ppermute x2, waiting for transfers between devices, local(): lax.ppermute(summed[1].astype(jnp.bfloat16), 'ctx', cross_pairs())  4.7 us
  transfers between devices with their start and end apart: 16, of which 7 were waited for; matrix products, arithmetic and copies ran while one was open for 4% of the time, Pallas kernels for 20%

profile of v14, /device:TPU:0, one launch (start us, length us, event | category | flops | bytes accessed | tf_op | source)
XLA Modules:
  0.0 78.7 jit_solution(7402372135840764035)
XLA Ops:
  0.6 4.1 %collective-permute-start = (bf16[128,512]{1,0:T(8,128)(2,1)}, bf16[128,512]{1,0:T(8,128)(2,1)S(1)}, u32[]{:S(2)}, u32[]{:S(2)}) collective-permute-start(bf16[128,512]{1,0:T(8,128)(2,1)} %param.7), channel_id=1, source_target_pairs={{0,8},{2,10},{4,12},{6,14},{8,0},{10,2},{12,4},{14,6},{1,9},{3,11}... | collective-permute-start | bytes 393224 | tf_op jit(solution)/shard_map/ppermute | solution.py:147
  4.8 0.9 %fusion.16 = (bf16[128,256]{1,0:T(8,128)(2,1)S(1)}, bf16[128,256]{1,0:T(8,128)(2,1)S(1)}) fusion(bf16[128,512]{1,0:T(8,128)(2,1)} %param.7), kind=kLoop, calls=%fused_computation.49 | loop fusion | bytes 262144 | tf_op jit(solution)/shard_map/slice | solution.py:151
  6.9 7.9 %collective-permute-done = bf16[128,512]{1,0:T(8,128)(2,1)S(1)} collective-permute-done((bf16[128,512]{1,0:T(8,128)(2,1)}, bf16[128,512]{1,0:T(8,128)(2,1)S(1)}, u32[]{:S(2)}, u32[]{:S(2)}) %collective-permute-start) | collective-permute-done | bytes 131104 | tf_op jit(solution)/shard_map/ppermute | solution.py:147
  14.9 2.0 %collective-permute-done.1 = bf16[128,512]{1,0:T(8,128)(2,1)S(1)} collective-permute-done((bf16[128,512]{1,0:T(8,128)(2,1)}, bf16[128,512]{1,0:T(8,128)(2,1)S(1)}, u32[]{:S(2)}, u32[]{:S(2)}) %collective-permute-start.1) | collective-permute-done | bytes 131104 | tf_op jit(solution)/shard_map/ppermute | solution.py:148
  17.0 1.6 %collective-permute-start.5 = (bf16[2,128,512]{2,1,0:T(8,128)(2,1)S(1)}, bf16[2,128,512]{2,1,0:T(8,128)(2,1)S(1)}, u32[]{:S(2)}, u32[]{:S(2)}) collective-permute-start(bf16[2,128,512]{2,1,0:T(8,128)(2,1)S(1)} %pad_maximum_fusion.1), channel_id=1, source_target_pairs={{0,2},{2,4},{4,6},{6,0},{8,10},{10,12},{12,14},{14,8},{1,3},{3,5},... | collective-permute-start | bytes 786440 | tf_op jit(solution)/shard_map/ppermute | solution.py:156
  18.6 0.8 collective-permute-start.6
  19.4 1.4 %collective-permute-start.7 = (bf16[2,128,512]{2,1,0:T(8,128)(2,1)S(1)}, bf16[2,128,512]{2,1,0:T(8,128)(2,1)S(1)}, u32[]{:S(2)}, u32[]{:S(2)}) collective-permute-start(bf16[2,128,512]{2,1,0:T(8,128)(2,1)S(1)} %pad_maximum_fusion.1), channel_id=1, source_target_pairs={{0,6},{2,0},{4,2},{6,4},{8,14},{10,8},{12,10},{14,12},{1,7},{3,1},... | collective-permute-start | bytes 786440 | tf_op jit(solution)/shard_map/ppermute | solution.py:156
  20.8 0.7 collective-permute-start.2
  22.2 0.8 %reshape.110.refs_1_ = s32[2,64,1]{2,1,0:T(8,128)} reshape(s32[128]{0:T(128)S(1)} %copy-done.12) | data formatting | bytes 1024 | tf_op jit(solution)/shard_map/reshape | solution.py:135
  23.7 1.2 %collective-permute-start.3 = (bf16[2,128,512]{2,1,0:T(8,128)(2,1)S(1)}, bf16[2,128,512]{2,1,0:T(8,128)(2,1)S(1)}, u32[]{:S(2)}, u32[]{:S(2)}) collective-permute-start(bf16[2,128,512]{2,1,0:T(8,128)(2,1)S(1)} %pad_maximum_fusion), channel_id=1, source_target_pairs={{0,4},{2,6},{4,0},{6,2},{8,12},{10,14},{12,8},{14,10},{1,5},{3,7},... | collective-permute-start | bytes 786440 | tf_op jit(solution)/shard_map/ppermute | solution.py:156
  24.9 4.0 %collective-permute-done.5 = bf16[2,128,512]{2,1,0:T(8,128)(2,1)S(1)} collective-permute-done((bf16[2,128,512]{2,1,0:T(8,128)(2,1)S(1)}, bf16[2,128,512]{2,1,0:T(8,128)(2,1)S(1)}, u32[]{:S(2)}, u32[]{:S(2)}) %collective-permute-start.5) | collective-permute-done | bytes 262176 | tf_op jit(solution)/shard_map/ppermute | solution.py:156
  29.0 3.9 %collective-permute-done.7 = bf16[2,128,512]{2,1,0:T(8,128)(2,1)S(1)} collective-permute-done((bf16[2,128,512]{2,1,0:T(8,128)(2,1)S(1)}, bf16[2,128,512]{2,1,0:T(8,128)(2,1)S(1)}, u32[]{:S(2)}, u32[]{:S(2)}) %collective-permute-start.7) | collective-permute-done | bytes 262176 | tf_op jit(solution)/shard_map/ppermute | solution.py:156
  32.9 0.7 copy-done.5
  33.6 7.6 %shard_map.93 = (bf16[128,4096]{1,0:T(8,128)(2,1)}, bf16[128,4096]{1,0:T(8,128)(2,1)}, f32[2,2,2,64,256]{4,3,2,1,0:T(8,128)}, bf16[2,2,2,64,256]{4,3,2,1,0:T(8,1...) custom-call(s32[34]{0:T(128)} %concatenate.23.refs_0_, s32[2,64,1]{2,1,0:T(8,128)} %reshape.110.refs_1_, ...), custom_call_target="tpu_custom_call" | custom-call | tf_op jit(solution)/shard_map/pallas_call | solution.py:195
  41.2 2.3 %collective-permute-start.10 = (bf16[2,2,128,256]{3,2,1,0:T(8,128)(2,1)}, bf16[2,2,128,256]{3,2,1,0:T(8,128)(2,1)S(1)}, u32[]{:S(2)}, u32[]{:S(2)}) collective-permute-start(bf16[2,2,128,256]{3,2,1,0:T(8,128)(2,1)} %bitcast.83), channel_id=1, source_target_pairs={{0,6},{2,0},{4,2},{6,4},{8,14},{10,8},{12,10},{14,12},{1,7},{3,1},... | collective-permute-start | bytes 786440 | tf_op jit(solution)/shard_map/ppermute | solution.py:200
  43.6 1.3 %collective-permute-start.9 = (bf16[2,2,128,256]{3,2,1,0:T(8,128)(2,1)}, bf16[2,2,128,256]{3,2,1,0:T(8,128)(2,1)S(1)}, u32[]{:S(2)}, u32[]{:S(2)}) collective-permute-start(bf16[2,2,128,256]{3,2,1,0:T(8,128)(2,1)} %bitcast.80), channel_id=1, source_target_pairs={{0,4},{2,6},{4,0},{6,2},{8,12},{10,14},{12,8},{14,10},{1,5},{3,7},... | collective-permute-start | bytes 786440 | tf_op jit(solution)/shard_map/ppermute | solution.py:200
  44.9 0.7 copy-done.6
  45.7 7.8 %shard_map.94 = (bf16[128,4096]{1,0:T(8,128)(2,1)}, bf16[128,4096]{1,0:T(8,128)(2,1)}, f32[2,2,2,64,256]{4,3,2,1,0:T(8,128)}, bf16[2,2,2,64,256]{4,3,2,1,0:T(8,1...) custom-call(s32[34]{0:T(128)} %concatenate.23.refs_0_, ...), custom_call_target="tpu_custom_call", output_to_operand_aliasing={{0}: (12, {}), {1}: (13, {})} | custom-call | tf_op jit(solution)/shard_map/pallas_call | solution.py:195
  53.5 2.2 %collective-permute-start.12 = (bf16[2,2,128,256]{3,2,1,0:T(8,128)(2,1)}, bf16[2,2,128,256]{3,2,1,0:T(8,128)(2,1)S(1)}, u32[]{:S(2)}, u32[]{:S(2)}) collective-permute-start(bf16[2,2,128,256]{3,2,1,0:T(8,128)(2,1)} %bitcast.85), channel_id=1, source_target_pairs={{0,2},{2,4},{4,6},{6,0},{8,10},{10,12},{12,14},{14,8},{1,3},{3,5},... | collective-permute-start | bytes 786440 | tf_op jit(solution)/shard_map/ppermute | solution.py:200
  55.7 1.3 %collective-permute-start.13 = (bf16[2,2,128,256]{3,2,1,0:T(8,128)(2,1)}, bf16[2,2,128,256]{3,2,1,0:T(8,128)(2,1)S(1)}, u32[]{:S(2)}, u32[]{:S(2)}) collective-permute-start(bf16[2,2,128,256]{3,2,1,0:T(8,128)(2,1)} %bitcast.84), channel_id=1, source_target_pairs={{0,4},{2,6},{4,0},{6,2},{8,12},{10,14},{12,8},{14,10},{1,5},{3,7},... | collective-permute-start | bytes 786440 | tf_op jit(solution)/shard_map/ppermute | solution.py:200
  57.4 3.3 %collective-permute-start.11 = (bf16[2,128,256]{2,1,0:T(8,128)(2,1)S(1)}, bf16[2,128,256]{2,1,0:T(8,128)(2,1)S(1)}, u32[]{:S(2)}, u32[]{:S(2)}) collective-permute-start(bf16[2,128,256]{2,1,0:T(8,128)(2,1)S(1)} %fusion.8), channel_id=1, source_target_pairs={{0,8},{2,10},{4,12},{6,14},{8,0},{10,2},{12,4},{14,6},{1,9},{3,11}... | collective-permute-start | bytes 393224 | tf_op jit(solution)/shard_map/ppermute | solution.py:203
  60.7 6.0 %collective-permute-done.12 = bf16[2,2,128,256]{3,2,1,0:T(8,128)(2,1)S(1)} collective-permute-done((bf16[2,2,128,256]{3,2,1,0:T(8,128)(2,1)}, bf16[2,2,128,256]{3,2,1,0:T(8,128)(2,1)S(1)}, u32[]{:S(2)}, u32[]{:S(2)}) %collective-permute-start.12) | collective-permute-done | bytes 262176 | tf_op jit(solution)/shard_map/ppermute | solution.py:200
  67.5 5.1 %collective-permute-start.15 = (bf16[2,128,256]{2,1,0:T(8,128)(2,1)S(1)}, bf16[2,128,256]{2,1,0:T(8,128)(2,1)S(1)}, u32[]{:S(2)}, u32[]{:S(2)}) collective-permute-start(bf16[2,128,256]{2,1,0:T(8,128)(2,1)S(1)} %fusion.9), channel_id=1, source_target_pairs={{0,8},{2,10},{4,12},{6,14},{8,0},{10,2},{12,4},{14,6},{1,9},{3,11}... | collective-permute-start | bytes 393224 | tf_op jit(solution)/shard_map/ppermute | solution.py:203
  72.6 4.7 %collective-permute-done.15 = bf16[2,128,256]{2,1,0:T(8,128)(2,1)S(1)} collective-permute-done((bf16[2,128,256]{2,1,0:T(8,128)(2,1)S(1)}, bf16[2,128,256]{2,1,0:T(8,128)(2,1)S(1)}, u32[]{:S(2)}, u32[]{:S(2)}) %collective-permute-start.15) | collective-permute-done | bytes 131104 | tf_op jit(solution)/shard_map/ppermute | solution.py:203
  (63 shorter events, 5.4 us)
Async XLA Ops:
  0.6 14.3 %collective-permute-start = (bf16[128,512]{1,0:T(8,128)(2,1)}, bf16[128,512]{1,0:T(8,128)(2,1)S(1)}, u32[]{:S(2)}, u32[]{:S(2)}) collective-permute-start(bf16[128,512]{1,0:T(8,128)(2,1)} %param.7), channel_id=1, source_target_pairs={{0,8},{2,10},{4,12},{6,14},{8,0},{10,2},{12,4},{14,6},{1,9},{3,11}... | collective-permute-start | bytes 393224 | tf_op jit(solution)/shard_map/ppermute | solution.py:147
  4.7 12.1 %collective-permute-start.1 = (bf16[128,512]{1,0:T(8,128)(2,1)}, bf16[128,512]{1,0:T(8,128)(2,1)S(1)}, u32[]{:S(2)}, u32[]{:S(2)}) collective-permute-start(bf16[128,512]{1,0:T(8,128)(2,1)} %param.8), channel_id=1, source_target_pairs={{0,8},{2,10},{4,12},{6,14},{8,0},{10,2},{12,4},{14,6},{1,9},{3,11}... | collective-permute-start | bytes 393224 | tf_op jit(solution)/shard_map/ppermute | solution.py:148
  4.8 2.1 %copy-start.10 = (bf16[128,512]{1,0:T(8,128)(2,1)S(1)}, bf16[128,512]{1,0:T(8,128)(2,1)}, u32[]{:S(2)}) copy-start(bf16[128,512]{1,0:T(8,128)(2,1)} %param.8) | copy-start | bytes 393220
  16.9 3.8 %copy-start.1 = (bf16[2,128,512]{2,1,0:T(8,128)(2,1)}, bf16[2,128,512]{2,1,0:T(8,128)(2,1)S(1)}, u32[]{:S(2)}) copy-start(bf16[2,128,512]{2,1,0:T(8,128)(2,1)S(1)} %pad_maximum_fusion.1) | copy-start | bytes 786436
  17.0 12.0 %collective-permute-start.5 = (bf16[2,128,512]{2,1,0:T(8,128)(2,1)S(1)}, bf16[2,128,512]{2,1,0:T(8,128)(2,1)S(1)}, u32[]{:S(2)}, u32[]{:S(2)}) collective-permute-start(bf16[2,128,512]{2,1,0:T(8,128)(2,1)S(1)} %pad_maximum_fusion.1), channel_id=1, source_target_pairs={{0,2},{2,4},{4,6},{6,0},{8,10},{10,12},{12,14},{14,8},{1,3},{3,5},... | collective-permute-start | bytes 786440 | tf_op jit(solution)/shard_map/ppermute | solution.py:156
  18.6 10.4 %collective-permute-start.6 = (bf16[2,128,512]{2,1,0:T(8,128)(2,1)S(1)}, bf16[2,128,512]{2,1,0:T(8,128)(2,1)S(1)}, u32[]{:S(2)}, u32[]{:S(2)}) collective-permute-start(bf16[2,128,512]{2,1,0:T(8,128)(2,1)S(1)} %pad_maximum_fusion.1), channel_id=1, source_target_pairs={{0,4},{2,6},{4,0},{6,2},{8,12},{10,14},{12,8},{14,10},{1,5},{3,7},... | collective-permute-start | bytes 786440 | tf_op jit(solution)/shard_map/ppermute | solution.py:156
  19.4 13.5 %collective-permute-start.7 = (bf16[2,128,512]{2,1,0:T(8,128)(2,1)S(1)}, bf16[2,128,512]{2,1,0:T(8,128)(2,1)S(1)}, u32[]{:S(2)}, u32[]{:S(2)}) collective-permute-start(bf16[2,128,512]{2,1,0:T(8,128)(2,1)S(1)} %pad_maximum_fusion.1), channel_id=1, source_target_pairs={{0,6},{2,0},{4,2},{6,4},{8,14},{10,8},{12,10},{14,12},{1,7},{3,1},... | collective-permute-start | bytes 786440 | tf_op jit(solution)/shard_map/ppermute | solution.py:156
  20.8 20.4 %copy-start = (bf16[2,128,512]{2,1,0:T(8,128)(2,1)}, bf16[2,128,512]{2,1,0:T(8,128)(2,1)S(1)}, u32[]{:S(2)}) copy-start(bf16[2,128,512]{2,1,0:T(8,128)(2,1)S(1)} %pad_maximum_fusion) | copy-start | bytes 786436
  20.8 22.7 %collective-permute-start.2 = (bf16[2,128,512]{2,1,0:T(8,128)(2,1)S(1)}, bf16[2,128,512]{2,1,0:T(8,128)(2,1)S(1)}, u32[]{:S(2)}, u32[]{:S(2)}) collective-permute-start(bf16[2,128,512]{2,1,0:T(8,128)(2,1)S(1)} %pad_maximum_fusion), channel_id=1, source_target_pairs={{0,2},{2,4},{4,6},{6,0},{8,10},{10,12},{12,14},{14,8},{1,3},{3,5},... | collective-permute-start | bytes 786440 | tf_op jit(solution)/shard_map/ppermute | solution.py:156
  23.7 21.3 %collective-permute-start.3 = (bf16[2,128,512]{2,1,0:T(8,128)(2,1)S(1)}, bf16[2,128,512]{2,1,0:T(8,128)(2,1)S(1)}, u32[]{:S(2)}, u32[]{:S(2)}) collective-permute-start(bf16[2,128,512]{2,1,0:T(8,128)(2,1)S(1)} %pad_maximum_fusion), channel_id=1, source_target_pairs={{0,4},{2,6},{4,0},{6,2},{8,12},{10,14},{12,8},{14,10},{1,5},{3,7},... | collective-permute-start | bytes 786440 | tf_op jit(solution)/shard_map/ppermute | solution.py:156
  28.9 3.9 %copy-start.3 = (bf16[2,128,512]{2,1,0:T(8,128)(2,1)}, bf16[2,128,512]{2,1,0:T(8,128)(2,1)S(1)}, u32[]{:S(2)}) copy-start(bf16[2,128,512]{2,1,0:T(8,128)(2,1)S(1)} %collective-permute-done.5) | copy-start | bytes 786436
  29.0 16.0 %collective-permute-start.4 = (bf16[2,128,512]{2,1,0:T(8,128)(2,1)S(1)}, bf16[2,128,512]{2,1,0:T(8,128)(2,1)S(1)}, u32[]{:S(2)}, u32[]{:S(2)}) collective-permute-start(bf16[2,128,512]{2,1,0:T(8,128)(2,1)S(1)} %pad_maximum_fusion), channel_id=1, source_target_pairs={{0,6},{2,0},{4,2},{6,4},{8,14},{10,8},{12,10},{14,12},{1,7},{3,1},... | collective-permute-start | bytes 786440 | tf_op jit(solution)/shard_map/ppermute | solution.py:156
  29.0 3.9 %copy-start.4 = (bf16[2,128,512]{2,1,0:T(8,128)(2,1)}, bf16[2,128,512]{2,1,0:T(8,128)(2,1)S(1)}, u32[]{:S(2)}) copy-start(bf16[2,128,512]{2,1,0:T(8,128)(2,1)S(1)} %collective-permute-done.6) | copy-start | bytes 786436
  41.2 15.7 %collective-permute-start.10 = (bf16[2,2,128,256]{3,2,1,0:T(8,128)(2,1)}, bf16[2,2,128,256]{3,2,1,0:T(8,128)(2,1)S(1)}, u32[]{:S(2)}, u32[]{:S(2)}) collective-permute-start(bf16[2,2,128,256]{3,2,1,0:T(8,128)(2,1)} %bitcast.83), channel_id=1, source_target_pairs={{0,6},{2,0},{4,2},{6,4},{8,14},{10,8},{12,10},{14,12},{1,7},{3,1},... | collective-permute-start | bytes 786440 | tf_op jit(solution)/shard_map/ppermute | solution.py:200
  43.6 13.7 %collective-permute-start.8 = (bf16[2,2,128,256]{3,2,1,0:T(8,128)(2,1)}, bf16[2,2,128,256]{3,2,1,0:T(8,128)(2,1)S(1)}, u32[]{:S(2)}, u32[]{:S(2)}) collective-permute-start(bf16[2,2,128,256]{3,2,1,0:T(8,128)(2,1)} %bitcast.81), channel_id=1, source_target_pairs={{0,2},{2,4},{4,6},{6,0},{8,10},{10,12},{12,14},{14,8},{1,3},{3,5},... | collective-permute-start | bytes 786440 | tf_op jit(solution)/shard_map/ppermute | solution.py:200
  43.6 1.4 %copy-start.2 = (bf16[2,128,512]{2,1,0:T(8,128)(2,1)}, bf16[2,128,512]{2,1,0:T(8,128)(2,1)S(1)}, u32[]{:S(2)}) copy-start(bf16[2,128,512]{2,1,0:T(8,128)(2,1)S(1)} %collective-permute-done.2) | copy-start | bytes 786436
  43.6 13.7 %collective-permute-start.9 = (bf16[2,2,128,256]{3,2,1,0:T(8,128)(2,1)}, bf16[2,2,128,256]{3,2,1,0:T(8,128)(2,1)S(1)}, u32[]{:S(2)}, u32[]{:S(2)}) collective-permute-start(bf16[2,2,128,256]{3,2,1,0:T(8,128)(2,1)} %bitcast.80), channel_id=1, source_target_pairs={{0,4},{2,6},{4,0},{6,2},{8,12},{10,14},{12,8},{14,10},{1,5},{3,7},... | collective-permute-start | bytes 786440 | tf_op jit(solution)/shard_map/ppermute | solution.py:200
  45.7 11.5 %copy-start.8 = (f32[2,2,2,64,256]{4,3,2,1,0:T(8,128)S(1)}, f32[2,2,2,64,256]{4,3,2,1,0:T(8,128)}, u32[]{:S(2)}) copy-start(f32[2,2,2,64,256]{4,3,2,1,0:T(8,128)} %get-tuple-element.20) | copy-start | bytes 1572868
  53.5 13.3 %collective-permute-start.12 = (bf16[2,2,128,256]{3,2,1,0:T(8,128)(2,1)}, bf16[2,2,128,256]{3,2,1,0:T(8,128)(2,1)S(1)}, u32[]{:S(2)}, u32[]{:S(2)}) collective-permute-start(bf16[2,2,128,256]{3,2,1,0:T(8,128)(2,1)} %bitcast.85), channel_id=1, source_target_pairs={{0,2},{2,4},{4,6},{6,0},{8,10},{10,12},{12,14},{14,8},{1,3},{3,5},... | collective-permute-start | bytes 786440 | tf_op jit(solution)/shard_map/ppermute | solution.py:200
  55.7 11.1 %collective-permute-start.13 = (bf16[2,2,128,256]{3,2,1,0:T(8,128)(2,1)}, bf16[2,2,128,256]{3,2,1,0:T(8,128)(2,1)S(1)}, u32[]{:S(2)}, u32[]{:S(2)}) collective-permute-start(bf16[2,2,128,256]{3,2,1,0:T(8,128)(2,1)} %bitcast.84), channel_id=1, source_target_pairs={{0,4},{2,6},{4,0},{6,2},{8,12},{10,14},{12,8},{14,10},{1,5},{3,7},... | collective-permute-start | bytes 786440 | tf_op jit(solution)/shard_map/ppermute | solution.py:200
  57.0 10.4 %collective-permute-start.14 = (bf16[2,2,128,256]{3,2,1,0:T(8,128)(2,1)}, bf16[2,2,128,256]{3,2,1,0:T(8,128)(2,1)S(1)}, u32[]{:S(2)}, u32[]{:S(2)}) collective-permute-start(bf16[2,2,128,256]{3,2,1,0:T(8,128)(2,1)} %bitcast.82), channel_id=1, source_target_pairs={{0,6},{2,0},{4,2},{6,4},{8,14},{10,8},{12,10},{14,12},{1,7},{3,1},... | collective-permute-start | bytes 786440 | tf_op jit(solution)/shard_map/ppermute | solution.py:200
  57.2 10.1 %copy-start.9 = (f32[2,2,2,64,256]{4,3,2,1,0:T(8,128)S(1)}, f32[2,2,2,64,256]{4,3,2,1,0:T(8,128)}, u32[]{:S(2)}) copy-start(f32[2,2,2,64,256]{4,3,2,1,0:T(8,128)} %get-tuple-element.24) | copy-start | bytes 1572868
  57.4 15.2 %collective-permute-start.11 = (bf16[2,128,256]{2,1,0:T(8,128)(2,1)S(1)}, bf16[2,128,256]{2,1,0:T(8,128)(2,1)S(1)}, u32[]{:S(2)}, u32[]{:S(2)}) collective-permute-start(bf16[2,128,256]{2,1,0:T(8,128)(2,1)S(1)} %fusion.8), channel_id=1, source_target_pairs={{0,8},{2,10},{4,12},{6,14},{8,0},{10,2},{12,4},{14,6},{1,9},{3,11}... | collective-permute-start | bytes 393224 | tf_op jit(solution)/shard_map/ppermute | solution.py:203
  67.5 9.8 %collective-permute-start.15 = (bf16[2,128,256]{2,1,0:T(8,128)(2,1)S(1)}, bf16[2,128,256]{2,1,0:T(8,128)(2,1)S(1)}, u32[]{:S(2)}, u32[]{:S(2)}) collective-permute-start(bf16[2,128,256]{2,1,0:T(8,128)(2,1)S(1)} %fusion.9), channel_id=1, source_target_pairs={{0,8},{2,10},{4,12},{6,14},{8,0},{10,2},{12,4},{14,6},{1,9},{3,11}... | collective-permute-start | bytes 393224 | tf_op jit(solution)/shard_map/ppermute | solution.py:203
  (5 other events, 3.5 us)

commit v15 on v11

--- a/solution.py
+++ b/solution.py
@@ -61,8 +61,7 @@
         masked = scores + bias
         row_max = jnp.max(masked, axis=1, keepdims=True)
         shifted = jnp.exp(masked - row_max)
-        log_totals = row_max + jnp.log(jnp.sum(shifted, axis=1, keepdims=True))
-        weights = jnp.exp(masked - log_totals)
+        weights = shifted * (1.0 / jnp.sum(shifted, axis=1, keepdims=True))
         weights_low = weights.astype(jnp.bfloat16)
         attended = jnp.dot(weights_low, value_block,
                            preferred_element_type=jnp.float32).astype(jnp.bfloat16)

time: 76.8 us -> 76.6 us (level)
  starting transfers between devices: 24.7 us -> 23.2 us
  waiting for transfers between devices: 28.1 us -> 29.6 us
    ppermute x2, starting transfers between devices: 6.95 us -> 5.45 us  [local(): lax.ppermute(summed[1].astype(jnp.bfloat16), 'ctx', cross_pairs())]
    ppermute x2, waiting for transfers between devices: 4.49 us -> 5.92 us  [local(): lax.ppermute(summed[1].astype(jnp.bfloat16), 'ctx', cross_pairs())]
where the time goes in v15:
time: 76.6 us; the launch traced here: 76.3 us
  waiting for transfers between devices  29.6 us (39%)
  starting transfers between devices  23.2 us (30%)
  Pallas kernels  15.1 us (20%)
  local copies, waits for them, and re-layouts  5.46 us (7%)
  other arithmetic  2.07 us (3%)
  between operations  0.84 us (1%)
    pallas_call x2, Pallas kernels, local(): attended, query_grad, own_pack, *send_packs = kernel(*operands)  15.1 us
    ppermute x2, waiting for transfers between devices, local(): both = jnp.stack([pair, lax.ppermute(pair, 'ctx', cross_pairs())])  8.66 us
    ppermute x6, waiting for transfers between devices, local(): pieces.append(lax.ppermute(both, 'ctx', half_pairs(shift)))  7.7 us
    ppermute x6, starting transfers between devices, local(): lax.ppermute(send_packs[shift - 1].reshape(pack_shape), 'ctx', half_pairs...  7.55 us
    ppermute x6, waiting for transfers between devices, local(): lax.ppermute(send_packs[shift - 1].reshape(pack_shape), 'ctx', half_pairs...  7.29 us
    ppermute x6, starting transfers between devices, local(): pieces.append(lax.ppermute(both, 'ctx', half_pairs(shift)))  6.03 us
    ppermute x2, waiting for transfers between devices, local(): lax.ppermute(summed[1].astype(jnp.bfloat16), 'ctx', cross_pairs())  5.92 us
    ppermute x2, starting transfers between devices, local(): lax.ppermute(summed[1].astype(jnp.bfloat16), 'ctx', cross_pairs())  5.45 us
  transfers between devices with their start and end apart: 16, of which 6 were waited for; matrix products, arithmetic and copies ran while one was open for 3% of the time, Pallas kernels for 20%

profile of v15, /device:TPU:0, one launch (start us, length us, event | category | flops | bytes accessed | tf_op | source)
XLA Modules:
  0.0 76.3 jit_solution(54636476839344662)
XLA Ops:
  0.6 1.0 %fusion.18 = (bf16[128,256]{1,0:T(8,128)(2,1)S(1)}, bf16[128,256]{1,0:T(8,128)(2,1)S(1)}, bf16[128,256]{1,0:T(8,128)(2,1)S(1)}, bf16[128,256]{1,0:T(8,128)(2,1)S(1)}) fusion(bf16[128,512]{1,0:T(8,128)(2,1)} %param.7, bf16[128,512]{1,0:T(8,128)(2,1)} %param.8), kind=kLoop, calls=%fused_computation.49 | loop fusion | bytes 524288 | tf_op jit(solution)/shard_map/slice | solution.py:148
  1.6 4.1 %collective-permute-start.4 = (bf16[128,512]{1,0:T(8,128)(2,1)S(1)}, bf16[128,512]{1,0:T(8,128)(2,1)S(1)}, u32[]{:S(2)}, u32[]{:S(2)}) collective-permute-start(bf16[128,512]{1,0:T(8,128)(2,1)S(1)} %get-tuple-element.37), channel_id=1, source_target_pairs={{0,8},{2,10},{4,12},{6,14},{8,0},{10,2},{12,4},{14,6},{1,9},{3,11}... | collective-permute-start | bytes 393224 | tf_op jit(solution)/shard_map/ppermute | solution.py:149
  7.0 8.7 %collective-permute-done.4 = bf16[128,512]{1,0:T(8,128)(2,1)S(1)} collective-permute-done((bf16[128,512]{1,0:T(8,128)(2,1)S(1)}, bf16[128,512]{1,0:T(8,128)(2,1)S(1)}, u32[]{:S(2)}, u32[]{:S(2)}) %collective-permute-start.4) | collective-permute-done | bytes 131104 | tf_op jit(solution)/shard_map/ppermute | solution.py:149
  15.7 1.9 %collective-permute-start.5 = (bf16[2,128,512]{2,1,0:T(8,128)(2,1)S(1)}, bf16[2,128,512]{2,1,0:T(8,128)(2,1)S(1)}, u32[]{:S(2)}, u32[]{:S(2)}) collective-permute-start(bf16[2,128,512]{2,1,0:T(8,128)(2,1)S(1)} %pad_maximum_fusion.1), channel_id=1, source_target_pairs={{0,2},{2,4},{4,6},{6,0},{8,10},{10,12},{12,14},{14,8},{1,3},{3,5},... | collective-permute-start | bytes 786440 | tf_op jit(solution)/shard_map/ppermute | solution.py:152
  17.6 1.5 %collective-permute-start.7 = (bf16[2,128,512]{2,1,0:T(8,128)(2,1)S(1)}, bf16[2,128,512]{2,1,0:T(8,128)(2,1)S(1)}, u32[]{:S(2)}, u32[]{:S(2)}) collective-permute-start(bf16[2,128,512]{2,1,0:T(8,128)(2,1)S(1)} %pad_maximum_fusion.1), channel_id=1, source_target_pairs={{0,6},{2,0},{4,2},{6,4},{8,14},{10,8},{12,10},{14,12},{1,7},{3,1},... | collective-permute-start | bytes 786440 | tf_op jit(solution)/shard_map/ppermute | solution.py:152
  20.4 0.8 %reshape.110.refs_1_ = s32[2,64,1]{2,1,0:T(8,128)} reshape(s32[128]{0:T(128)S(1)} %copy-done.11) | data formatting | bytes 1024 | tf_op jit(solution)/shard_map/reshape | solution.py:134
  21.9 2.0 %collective-permute-start.2 = (bf16[2,128,512]{2,1,0:T(8,128)(2,1)S(1)}, bf16[2,128,512]{2,1,0:T(8,128)(2,1)S(1)}, u32[]{:S(2)}, u32[]{:S(2)}) collective-permute-start(bf16[2,128,512]{2,1,0:T(8,128)(2,1)S(1)} %pad_maximum_fusion), channel_id=1, source_target_pairs={{0,4},{2,6},{4,0},{6,2},{8,12},{10,14},{12,8},{14,10},{1,5},{3,7},... | collective-permute-start | bytes 786440 | tf_op jit(solution)/shard_map/ppermute | solution.py:152
  23.9 4.1 %collective-permute-done.5 = bf16[2,128,512]{2,1,0:T(8,128)(2,1)S(1)} collective-permute-done((bf16[2,128,512]{2,1,0:T(8,128)(2,1)S(1)}, bf16[2,128,512]{2,1,0:T(8,128)(2,1)S(1)}, u32[]{:S(2)}, u32[]{:S(2)}) %collective-permute-start.5) | collective-permute-done | bytes 262176 | tf_op jit(solution)/shard_map/ppermute | solution.py:152
  28.1 3.6 %collective-permute-done.7 = bf16[2,128,512]{2,1,0:T(8,128)(2,1)S(1)} collective-permute-done((bf16[2,128,512]{2,1,0:T(8,128)(2,1)S(1)}, bf16[2,128,512]{2,1,0:T(8,128)(2,1)S(1)}, u32[]{:S(2)}, u32[]{:S(2)}) %collective-permute-start.7) | collective-permute-done | bytes 262176 | tf_op jit(solution)/shard_map/ppermute | solution.py:152
  31.6 0.7 copy-done.5
  32.3 7.5 %shard_map.93 = (bf16[128,4096]{1,0:T(8,128)(2,1)}, bf16[128,4096]{1,0:T(8,128)(2,1)}, f32[2,2,2,64,256]{4,3,2,1,0:T(8,128)}, bf16[2,2,2,64,256]{4,3,2,1,0:T(8,1...) custom-call(s32[34]{0:T(128)} %concatenate.17.refs_0_, s32[2,64,1]{2,1,0:T(8,128)} %reshape.110.refs_1_, ...), custom_call_target="tpu_custom_call" | custom-call | tf_op jit(solution)/shard_map/pallas_call | solution.py:191
  39.8 1.9 %collective-permute-start.10 = (bf16[2,2,128,256]{3,2,1,0:T(8,128)(2,1)}, bf16[2,2,128,256]{3,2,1,0:T(8,128)(2,1)S(1)}, u32[]{:S(2)}, u32[]{:S(2)}) collective-permute-start(bf16[2,2,128,256]{3,2,1,0:T(8,128)(2,1)} %bitcast.83), channel_id=1, source_target_pairs={{0,6},{2,0},{4,2},{6,4},{8,14},{10,8},{12,10},{14,12},{1,7},{3,1},... | collective-permute-start | bytes 786440 | tf_op jit(solution)/shard_map/ppermute | solution.py:196
  41.7 0.7 collective-permute-start.8
  42.4 1.5 %collective-permute-start.9 = (bf16[2,2,128,256]{3,2,1,0:T(8,128)(2,1)}, bf16[2,2,128,256]{3,2,1,0:T(8,128)(2,1)S(1)}, u32[]{:S(2)}, u32[]{:S(2)}) collective-permute-start(bf16[2,2,128,256]{3,2,1,0:T(8,128)(2,1)} %bitcast.80), channel_id=1, source_target_pairs={{0,4},{2,6},{4,0},{6,2},{8,12},{10,14},{12,8},{14,10},{1,5},{3,7},... | collective-permute-start | bytes 786440 | tf_op jit(solution)/shard_map/ppermute | solution.py:196
  43.9 0.7 copy-done.6
  44.7 7.6 %shard_map.94 = (bf16[128,4096]{1,0:T(8,128)(2,1)}, bf16[128,4096]{1,0:T(8,128)(2,1)}, f32[2,2,2,64,256]{4,3,2,1,0:T(8,128)}, bf16[2,2,2,64,256]{4,3,2,1,0:T(8,1...) custom-call(s32[34]{0:T(128)} %concatenate.17.refs_0_, ...), custom_call_target="tpu_custom_call", output_to_operand_aliasing={{0}: (12, {}), {1}: (13, {})} | custom-call | tf_op jit(solution)/shard_map/pallas_call | solution.py:191
  52.3 1.5 %collective-permute-start.12 = (bf16[2,2,128,256]{3,2,1,0:T(8,128)(2,1)}, bf16[2,2,128,256]{3,2,1,0:T(8,128)(2,1)S(1)}, u32[]{:S(2)}, u32[]{:S(2)}) collective-permute-start(bf16[2,2,128,256]{3,2,1,0:T(8,128)(2,1)} %bitcast.85), channel_id=1, source_target_pairs={{0,2},{2,4},{4,6},{6,0},{8,10},{10,12},{12,14},{14,8},{1,3},{3,5},... | collective-permute-start | bytes 786440 | tf_op jit(solution)/shard_map/ppermute | solution.py:196
  53.9 1.9 %collective-permute-start.13 = (bf16[2,2,128,256]{3,2,1,0:T(8,128)(2,1)}, bf16[2,2,128,256]{3,2,1,0:T(8,128)(2,1)S(1)}, u32[]{:S(2)}, u32[]{:S(2)}) collective-permute-start(bf16[2,2,128,256]{3,2,1,0:T(8,128)(2,1)} %bitcast.84), channel_id=1, source_target_pairs={{0,4},{2,6},{4,0},{6,2},{8,12},{10,14},{12,8},{14,10},{1,5},{3,7},... | collective-permute-start | bytes 786440 | tf_op jit(solution)/shard_map/ppermute | solution.py:196
  56.0 2.5 %collective-permute-start.11 = (bf16[2,128,256]{2,1,0:T(8,128)(2,1)S(1)}, bf16[2,128,256]{2,1,0:T(8,128)(2,1)S(1)}, u32[]{:S(2)}, u32[]{:S(2)}) collective-permute-start(bf16[2,128,256]{2,1,0:T(8,128)(2,1)S(1)} %fusion.8), channel_id=1, source_target_pairs={{0,8},{2,10},{4,12},{6,14},{8,0},{10,2},{12,4},{14,6},{1,9},{3,11}... | collective-permute-start | bytes 393224 | tf_op jit(solution)/shard_map/ppermute | solution.py:199
  58.5 7.1 %collective-permute-done.12 = bf16[2,2,128,256]{3,2,1,0:T(8,128)(2,1)S(1)} collective-permute-done((bf16[2,2,128,256]{3,2,1,0:T(8,128)(2,1)}, bf16[2,2,128,256]{3,2,1,0:T(8,128)(2,1)S(1)}, u32[]{:S(2)}, u32[]{:S(2)}) %collective-permute-start.12) | collective-permute-done | bytes 262176 | tf_op jit(solution)/shard_map/ppermute | solution.py:196
  65.9 3.0 %collective-permute-start.15 = (bf16[2,128,256]{2,1,0:T(8,128)(2,1)S(1)}, bf16[2,128,256]{2,1,0:T(8,128)(2,1)S(1)}, u32[]{:S(2)}, u32[]{:S(2)}) collective-permute-start(bf16[2,128,256]{2,1,0:T(8,128)(2,1)S(1)} %fusion.9), channel_id=1, source_target_pairs={{0,8},{2,10},{4,12},{6,14},{8,0},{10,2},{12,4},{14,6},{1,9},{3,11}... | collective-permute-start | bytes 393224 | tf_op jit(solution)/shard_map/ppermute | solution.py:199
  69.0 5.9 %collective-permute-done.15 = bf16[2,128,256]{2,1,0:T(8,128)(2,1)S(1)} collective-permute-done((bf16[2,128,256]{2,1,0:T(8,128)(2,1)S(1)}, bf16[2,128,256]{2,1,0:T(8,128)(2,1)S(1)}, u32[]{:S(2)}, u32[]{:S(2)}) %collective-permute-start.15) | collective-permute-done | bytes 131104 | tf_op jit(solution)/shard_map/ppermute | solution.py:199
  74.9 0.7 copy_bitcast_fusion
  75.6 0.7 copy_bitcast_fusion.1
  (58 shorter events, 3.9 us)
Async XLA Ops:
  1.6 14.0 %collective-permute-start.4 = (bf16[128,512]{1,0:T(8,128)(2,1)S(1)}, bf16[128,512]{1,0:T(8,128)(2,1)S(1)}, u32[]{:S(2)}, u32[]{:S(2)}) collective-permute-start(bf16[128,512]{1,0:T(8,128)(2,1)S(1)} %get-tuple-element.37), channel_id=1, source_target_pairs={{0,8},{2,10},{4,12},{6,14},{8,0},{10,2},{12,4},{14,6},{1,9},{3,11}... | collective-permute-start | bytes 393224 | tf_op jit(solution)/shard_map/ppermute | solution.py:149
  5.7 13.4 %collective-permute-start = (bf16[128,512]{1,0:T(8,128)(2,1)S(1)}, bf16[128,512]{1,0:T(8,128)(2,1)S(1)}, u32[]{:S(2)}, u32[]{:S(2)}) collective-permute-start(bf16[128,512]{1,0:T(8,128)(2,1)S(1)} %get-tuple-element.43), channel_id=1, source_target_pairs={{0,8},{2,10},{4,12},{6,14},{8,0},{10,2},{12,4},{14,6},{1,9},{3,11}... | collective-permute-start | bytes 393224 | tf_op jit(solution)/shard_map/ppermute | solution.py:149
  15.7 3.5 %copy-start.1 = (bf16[2,128,512]{2,1,0:T(8,128)(2,1)}, bf16[2,128,512]{2,1,0:T(8,128)(2,1)S(1)}, u32[]{:S(2)}) copy-start(bf16[2,128,512]{2,1,0:T(8,128)(2,1)S(1)} %pad_maximum_fusion.1) | copy-start | bytes 786436
  15.7 12.3 %collective-permute-start.5 = (bf16[2,128,512]{2,1,0:T(8,128)(2,1)S(1)}, bf16[2,128,512]{2,1,0:T(8,128)(2,1)S(1)}, u32[]{:S(2)}, u32[]{:S(2)}) collective-permute-start(bf16[2,128,512]{2,1,0:T(8,128)(2,1)S(1)} %pad_maximum_fusion.1), channel_id=1, source_target_pairs={{0,2},{2,4},{4,6},{6,0},{8,10},{10,12},{12,14},{14,8},{1,3},{3,5},... | collective-permute-start | bytes 786440 | tf_op jit(solution)/shard_map/ppermute | solution.py:152
  17.6 10.4 %collective-permute-start.6 = (bf16[2,128,512]{2,1,0:T(8,128)(2,1)S(1)}, bf16[2,128,512]{2,1,0:T(8,128)(2,1)S(1)}, u32[]{:S(2)}, u32[]{:S(2)}) collective-permute-start(bf16[2,128,512]{2,1,0:T(8,128)(2,1)S(1)} %pad_maximum_fusion.1), channel_id=1, source_target_pairs={{0,4},{2,6},{4,0},{6,2},{8,12},{10,14},{12,8},{14,10},{1,5},{3,7},... | collective-permute-start | bytes 786440 | tf_op jit(solution)/shard_map/ppermute | solution.py:152
  17.6 14.0 %collective-permute-start.7 = (bf16[2,128,512]{2,1,0:T(8,128)(2,1)S(1)}, bf16[2,128,512]{2,1,0:T(8,128)(2,1)S(1)}, u32[]{:S(2)}, u32[]{:S(2)}) collective-permute-start(bf16[2,128,512]{2,1,0:T(8,128)(2,1)S(1)} %pad_maximum_fusion.1), channel_id=1, source_target_pairs={{0,6},{2,0},{4,2},{6,4},{8,14},{10,8},{12,10},{14,12},{1,7},{3,1},... | collective-permute-start | bytes 786440 | tf_op jit(solution)/shard_map/ppermute | solution.py:152
  19.2 20.6 %copy-start = (bf16[2,128,512]{2,1,0:T(8,128)(2,1)}, bf16[2,128,512]{2,1,0:T(8,128)(2,1)S(1)}, u32[]{:S(2)}) copy-start(bf16[2,128,512]{2,1,0:T(8,128)(2,1)S(1)} %pad_maximum_fusion) | copy-start | bytes 786436
  19.2 23.2 %collective-permute-start.1 = (bf16[2,128,512]{2,1,0:T(8,128)(2,1)S(1)}, bf16[2,128,512]{2,1,0:T(8,128)(2,1)S(1)}, u32[]{:S(2)}, u32[]{:S(2)}) collective-permute-start(bf16[2,128,512]{2,1,0:T(8,128)(2,1)S(1)} %pad_maximum_fusion), channel_id=1, source_target_pairs={{0,2},{2,4},{4,6},{6,0},{8,10},{10,12},{12,14},{14,8},{1,3},{3,5},... | collective-permute-start | bytes 786440 | tf_op jit(solution)/shard_map/ppermute | solution.py:152
  21.9 22.0 %collective-permute-start.2 = (bf16[2,128,512]{2,1,0:T(8,128)(2,1)S(1)}, bf16[2,128,512]{2,1,0:T(8,128)(2,1)S(1)}, u32[]{:S(2)}, u32[]{:S(2)}) collective-permute-start(bf16[2,128,512]{2,1,0:T(8,128)(2,1)S(1)} %pad_maximum_fusion), channel_id=1, source_target_pairs={{0,4},{2,6},{4,0},{6,2},{8,12},{10,14},{12,8},{14,10},{1,5},{3,7},... | collective-permute-start | bytes 786440 | tf_op jit(solution)/shard_map/ppermute | solution.py:152
  28.0 3.6 %copy-start.3 = (bf16[2,128,512]{2,1,0:T(8,128)(2,1)}, bf16[2,128,512]{2,1,0:T(8,128)(2,1)S(1)}, u32[]{:S(2)}) copy-start(bf16[2,128,512]{2,1,0:T(8,128)(2,1)S(1)} %collective-permute-done.5) | copy-start | bytes 786436
  28.0 15.8 %collective-permute-start.3 = (bf16[2,128,512]{2,1,0:T(8,128)(2,1)S(1)}, bf16[2,128,512]{2,1,0:T(8,128)(2,1)S(1)}, u32[]{:S(2)}, u32[]{:S(2)}) collective-permute-start(bf16[2,128,512]{2,1,0:T(8,128)(2,1)S(1)} %pad_maximum_fusion), channel_id=1, source_target_pairs={{0,6},{2,0},{4,2},{6,4},{8,14},{10,8},{12,10},{14,12},{1,7},{3,1},... | collective-permute-start | bytes 786440 | tf_op jit(solution)/shard_map/ppermute | solution.py:152
  28.0 3.6 %copy-start.4 = (bf16[2,128,512]{2,1,0:T(8,128)(2,1)}, bf16[2,128,512]{2,1,0:T(8,128)(2,1)S(1)}, u32[]{:S(2)}) copy-start(bf16[2,128,512]{2,1,0:T(8,128)(2,1)S(1)} %collective-permute-done.6) | copy-start | bytes 786436
  39.8 15.9 %collective-permute-start.10 = (bf16[2,2,128,256]{3,2,1,0:T(8,128)(2,1)}, bf16[2,2,128,256]{3,2,1,0:T(8,128)(2,1)S(1)}, u32[]{:S(2)}, u32[]{:S(2)}) collective-permute-start(bf16[2,2,128,256]{3,2,1,0:T(8,128)(2,1)} %bitcast.83), channel_id=1, source_target_pairs={{0,6},{2,0},{4,2},{6,4},{8,14},{10,8},{12,10},{14,12},{1,7},{3,1},... | collective-permute-start | bytes 786440 | tf_op jit(solution)/shard_map/ppermute | solution.py:196
  41.7 14.1 %collective-permute-start.8 = (bf16[2,2,128,256]{3,2,1,0:T(8,128)(2,1)}, bf16[2,2,128,256]{3,2,1,0:T(8,128)(2,1)S(1)}, u32[]{:S(2)}, u32[]{:S(2)}) collective-permute-start(bf16[2,2,128,256]{3,2,1,0:T(8,128)(2,1)} %bitcast.81), channel_id=1, source_target_pairs={{0,2},{2,4},{4,6},{6,0},{8,10},{10,12},{12,14},{14,8},{1,3},{3,5},... | collective-permute-start | bytes 786440 | tf_op jit(solution)/shard_map/ppermute | solution.py:196
  42.4 1.5 %copy-start.2 = (bf16[2,128,512]{2,1,0:T(8,128)(2,1)}, bf16[2,128,512]{2,1,0:T(8,128)(2,1)S(1)}, u32[]{:S(2)}) copy-start(bf16[2,128,512]{2,1,0:T(8,128)(2,1)S(1)} %collective-permute-done.1) | copy-start | bytes 786436
  42.4 13.5 %collective-permute-start.9 = (bf16[2,2,128,256]{3,2,1,0:T(8,128)(2,1)}, bf16[2,2,128,256]{3,2,1,0:T(8,128)(2,1)S(1)}, u32[]{:S(2)}, u32[]{:S(2)}) collective-permute-start(bf16[2,2,128,256]{3,2,1,0:T(8,128)(2,1)} %bitcast.80), channel_id=1, source_target_pairs={{0,4},{2,6},{4,0},{6,2},{8,12},{10,14},{12,8},{14,10},{1,5},{3,7},... | collective-permute-start | bytes 786440 | tf_op jit(solution)/shard_map/ppermute | solution.py:196
  43.9 0.8 %copy-start.7 = (bf16[2,128,512]{2,1,0:T(8,128)(2,1)}, bf16[2,128,512]{2,1,0:T(8,128)(2,1)S(1)}, u32[]{:S(2)}) copy-start(bf16[2,128,512]{2,1,0:T(8,128)(2,1)S(1)} %collective-permute-done.3) | copy-start | bytes 786436
  44.7 11.2 %copy-start.8 = (f32[2,2,2,64,256]{4,3,2,1,0:T(8,128)S(1)}, f32[2,2,2,64,256]{4,3,2,1,0:T(8,128)}, u32[]{:S(2)}) copy-start(f32[2,2,2,64,256]{4,3,2,1,0:T(8,128)} %get-tuple-element.20) | copy-start | bytes 1572868
  52.3 13.2 %collective-permute-start.12 = (bf16[2,2,128,256]{3,2,1,0:T(8,128)(2,1)}, bf16[2,2,128,256]{3,2,1,0:T(8,128)(2,1)S(1)}, u32[]{:S(2)}, u32[]{:S(2)}) collective-permute-start(bf16[2,2,128,256]{3,2,1,0:T(8,128)(2,1)} %bitcast.85), channel_id=1, source_target_pairs={{0,2},{2,4},{4,6},{6,0},{8,10},{10,12},{12,14},{14,8},{1,3},{3,5},... | collective-permute-start | bytes 786440 | tf_op jit(solution)/shard_map/ppermute | solution.py:196
  53.9 11.7 %collective-permute-start.13 = (bf16[2,2,128,256]{3,2,1,0:T(8,128)(2,1)}, bf16[2,2,128,256]{3,2,1,0:T(8,128)(2,1)S(1)}, u32[]{:S(2)}, u32[]{:S(2)}) collective-permute-start(bf16[2,2,128,256]{3,2,1,0:T(8,128)(2,1)} %bitcast.84), channel_id=1, source_target_pairs={{0,4},{2,6},{4,0},{6,2},{8,12},{10,14},{12,8},{14,10},{1,5},{3,7},... | collective-permute-start | bytes 786440 | tf_op jit(solution)/shard_map/ppermute | solution.py:196
  55.8 10.0 %collective-permute-start.14 = (bf16[2,2,128,256]{3,2,1,0:T(8,128)(2,1)}, bf16[2,2,128,256]{3,2,1,0:T(8,128)(2,1)S(1)}, u32[]{:S(2)}, u32[]{:S(2)}) collective-permute-start(bf16[2,2,128,256]{3,2,1,0:T(8,128)(2,1)} %bitcast.82), channel_id=1, source_target_pairs={{0,6},{2,0},{4,2},{6,4},{8,14},{10,8},{12,10},{14,12},{1,7},{3,1},... | collective-permute-start | bytes 786440 | tf_op jit(solution)/shard_map/ppermute | solution.py:196
  55.9 9.9 %copy-start.9 = (f32[2,2,2,64,256]{4,3,2,1,0:T(8,128)S(1)}, f32[2,2,2,64,256]{4,3,2,1,0:T(8,128)}, u32[]{:S(2)}) copy-start(f32[2,2,2,64,256]{4,3,2,1,0:T(8,128)} %get-tuple-element.24) | copy-start | bytes 1572868
  56.0 12.9 %collective-permute-start.11 = (bf16[2,128,256]{2,1,0:T(8,128)(2,1)S(1)}, bf16[2,128,256]{2,1,0:T(8,128)(2,1)S(1)}, u32[]{:S(2)}, u32[]{:S(2)}) collective-permute-start(bf16[2,128,256]{2,1,0:T(8,128)(2,1)S(1)} %fusion.8), channel_id=1, source_target_pairs={{0,8},{2,10},{4,12},{6,14},{8,0},{10,2},{12,4},{14,6},{1,9},{3,11}... | collective-permute-start | bytes 393224 | tf_op jit(solution)/shard_map/ppermute | solution.py:199
  65.9 9.0 %collective-permute-start.15 = (bf16[2,128,256]{2,1,0:T(8,128)(2,1)S(1)}, bf16[2,128,256]{2,1,0:T(8,128)(2,1)S(1)}, u32[]{:S(2)}, u32[]{:S(2)}) collective-permute-start(bf16[2,128,256]{2,1,0:T(8,128)(2,1)S(1)} %fusion.9), channel_id=1, source_target_pairs={{0,8},{2,10},{4,12},{6,14},{8,0},{10,2},{12,4},{14,6},{1,9},{3,11}... | collective-permute-start | bytes 393224 | tf_op jit(solution)/shard_map/ppermute | solution.py:199
  (4 other events, 2.7 us)

commit v16 on v15

--- a/solution.py
+++ b/solution.py
@@ -146,10 +146,16 @@
     for chunk in range(chunks):
         cols = slice(chunk * chunk_cols, (chunk + 1) * chunk_cols)
         pair = jnp.concatenate([key_rows[:, cols], value_rows[:, cols]], axis=1)
-        both = jnp.stack([pair, lax.ppermute(pair, "ctx", cross_pairs())])
-        pieces = [both]
-        for shift in range(1, half):
-            pieces.append(lax.ppermute(both, "ctx", half_pairs(shift)))
+        if chunk == 0:
+            both = jnp.stack([pair, lax.ppermute(pair, "ctx", cross_pairs())])
+            pieces = [both]
+            for shift in range(1, half):
+                pieces.append(lax.ppermute(both, "ctx", half_pairs(shift)))
+        else:
+            around = [pair] + [lax.ppermute(pair, "ctx", half_pairs(shift))
+                               for shift in range(1, half)]
+            crossed = lax.ppermute(jnp.stack(around), "ctx", cross_pairs())
+            pieces = [jnp.stack([around[shift], crossed[shift]]) for shift in range(half)]
         pieces = [piece.reshape(2 * tiles, SPAN, 2 * chunk_cols) for piece in pieces]
 
         aliased = chunk > 0

time: 76.6 us -> 99.4 us (1.30)
  waiting for transfers between devices: 29.6 us -> 51.9 us
  other arithmetic: 2.07 us -> 5.05 us
  starting transfers between devices: 23.2 us -> 21.5 us
    ppermute x6, waiting for transfers between devices: 7.29 us -> 23.7 us  [local(): lax.ppermute(send_packs[shift - 1].reshape(pack_shape), 'ctx', half_pairs...]
    ppermute x0 -> x4, waiting for transfers between devices: none -> 7.84 us  [the longest x1 7.83 us: local(): crossed = lax.ppermute(jnp.stack(around), 'ctx', cross_pairs())]
    ppermute x0 -> x4, starting transfers between devices: none -> 6.58 us  [the longest x3 5.23 us: local(): lax.ppermute(pair, 'ctx', half_pairs(shift))]
    ppermute x2, starting transfers between devices: 5.45 us -> 0.58 us  [local(): lax.ppermute(summed[1].astype(jnp.bfloat16), 'ctx', cross_pairs())]
    ppermute x2 -> x1, waiting for transfers between devices: 8.66 us -> 5.1 us  [local(): both = jnp.stack([pair, lax.ppermute(pair, 'ctx', cross_pairs())])]
    another operation x2 -> x8, other arithmetic: 0.06 us -> 3.09 us  [the longest x5 2.96 us: local(): jnp.stack([around[shift], crossed[shift]])]
    ppermute x6 -> x3, starting transfers between devices: 6.03 us -> 3.48 us  [local(): pieces.append(lax.ppermute(both, 'ctx', half_pairs(shift)))]
    ppermute x2 -> x1, starting transfers between devices: 4.19 us -> 2.65 us  [local(): both = jnp.stack([pair, lax.ppermute(pair, 'ctx', cross_pairs())])]
  transfers between devices with their start and end apart: 16 -> 16, of which waited for: 6 -> 11; matrix products, arithmetic and copies ran while one was open for 3% -> 5% of each run, Pallas kernels for 20% -> 15%
where the time goes in v16:
time: 99.4 us; the launch traced here: 99.1 us
  waiting for transfers between devices  51.9 us (52%)
  starting transfers between devices  21.5 us (22%)
  Pallas kernels  15 us (15%)
  other arithmetic  5.05 us (5%)
  local copies, waits for them, and re-layouts  4.76 us (5%)
    ppermute x6, waiting for transfers between devices, local(): lax.ppermute(send_packs[shift - 1].reshape(pack_shape), 'ctx', half_pairs...  23.7 us
    pallas_call x2, Pallas kernels, local(): attended, query_grad, own_pack, *send_packs = kernel(*operands)  15 us
    ppermute x3, waiting for transfers between devices, local(): pieces.append(lax.ppermute(both, 'ctx', half_pairs(shift)))  8.47 us
    ppermute x6, starting transfers between devices, local(): lax.ppermute(send_packs[shift - 1].reshape(pack_shape), 'ctx', half_pairs...  8.25 us
    ppermute x1, waiting for transfers between devices, local(): crossed = lax.ppermute(jnp.stack(around), 'ctx', cross_pairs())  7.83 us
    ppermute x2, waiting for transfers between devices, local(): lax.ppermute(summed[1].astype(jnp.bfloat16), 'ctx', cross_pairs())  6.8 us
    ppermute x3, starting transfers between devices, local(): lax.ppermute(pair, 'ctx', half_pairs(shift))  5.23 us
    ppermute x1, waiting for transfers between devices, local(): both = jnp.stack([pair, lax.ppermute(pair, 'ctx', cross_pairs())])  5.1 us
  transfers between devices with their start and end apart: 16, of which 11 were waited for; matrix products, arithmetic and copies ran while one was open for 5% of the time, Pallas kernels for 15%

profile of v16, /device:TPU:0, one launch (start us, length us, event | category | flops | bytes accessed | tf_op | source)
XLA Modules:
  0.0 99.1 jit_solution(7267787808228082310)
XLA Ops:
  0.6 1.0 fusion.19
  1.6 3.0 %collective-permute-start = (bf16[128,512]{1,0:T(8,128)(2,1)S(1)}, bf16[128,512]{1,0:T(8,128)(2,1)S(1)}, u32[]{:S(2)}, u32[]{:S(2)}) collective-permute-start(bf16[128,512]{1,0:T(8,128)(2,1)S(1)} %get-tuple-element.47), channel_id=1, source_target_pairs={{0,2},{2,4},{4,6},{6,0},{8,10},{10,12},{12,14},{14,8},{1,3},{3,5},... | collective-permute-start | bytes 393224 | tf_op jit(solution)/shard_map/ppermute | solution.py:155
  4.6 1.6 %collective-permute-start.1 = (bf16[128,512]{1,0:T(8,128)(2,1)S(1)}, bf16[128,512]{1,0:T(8,128)(2,1)S(1)}, u32[]{:S(2)}, u32[]{:S(2)}) collective-permute-start(bf16[128,512]{1,0:T(8,128)(2,1)S(1)} %get-tuple-element.47), channel_id=1, source_target_pairs={{0,4},{2,6},{4,0},{6,2},{8,12},{10,14},{12,8},{14,10},{1,5},{3,7},... | collective-permute-start | bytes 393224 | tf_op jit(solution)/shard_map/ppermute | solution.py:155
  6.2 2.7 %collective-permute-start.4 = (bf16[128,512]{1,0:T(8,128)(2,1)S(1)}, bf16[128,512]{1,0:T(8,128)(2,1)S(1)}, u32[]{:S(2)}, u32[]{:S(2)}) collective-permute-start(bf16[128,512]{1,0:T(8,128)(2,1)S(1)} %get-tuple-element.41), channel_id=1, source_target_pairs={{0,8},{2,10},{4,12},{6,14},{8,0},{10,2},{12,4},{14,6},{1,9},{3,11}... | collective-permute-start | bytes 393224 | tf_op jit(solution)/shard_map/ppermute | solution.py:150
  9.6 5.1 %collective-permute-done.4 = bf16[128,512]{1,0:T(8,128)(2,1)S(1)} collective-permute-done((bf16[128,512]{1,0:T(8,128)(2,1)S(1)}, bf16[128,512]{1,0:T(8,128)(2,1)S(1)}, u32[]{:S(2)}, u32[]{:S(2)}) %collective-permute-start.4) | collective-permute-done | bytes 131104 | tf_op jit(solution)/shard_map/ppermute | solution.py:150
  15.3 3.4 %collective-permute-start.6 = (bf16[2,128,512]{2,1,0:T(8,128)(2,1)S(1)}, bf16[2,128,512]{2,1,0:T(8,128)(2,1)S(1)}, u32[]{:S(2)}, u32[]{:S(2)}) collective-permute-start(bf16[2,128,512]{2,1,0:T(8,128)(2,1)S(1)} %pad_maximum_fusion.5), channel_id=1, source_target_pairs={{0,4},{2,6},{4,0},{6,2},{8,12},{10,14},{12,8},{14,10},{1,5},{3,7},... | collective-permute-start | bytes 786440 | tf_op jit(solution)/shard_map/ppermute | solution.py:153
  18.7 6.2 %collective-permute-done.5 = bf16[2,128,512]{2,1,0:T(8,128)(2,1)S(1)} collective-permute-done((bf16[2,128,512]{2,1,0:T(8,128)(2,1)S(1)}, bf16[2,128,512]{2,1,0:T(8,128)(2,1)S(1)}, u32[]{:S(2)}, u32[]{:S(2)}) %collective-permute-start.5) | collective-permute-done | bytes 262176 | tf_op jit(solution)/shard_map/ppermute | solution.py:153
  26.3 0.8 reshape.110.refs_1_
  27.8 2.2 %collective-permute-done.7 = bf16[2,128,512]{2,1,0:T(8,128)(2,1)S(1)} collective-permute-done((bf16[2,128,512]{2,1,0:T(8,128)(2,1)S(1)}, bf16[2,128,512]{2,1,0:T(8,128)(2,1)S(1)}, u32[]{:S(2)}, u32[]{:S(2)}) %collective-permute-start.7) | collective-permute-done | bytes 262176 | tf_op jit(solution)/shard_map/ppermute | solution.py:153
  30.7 7.5 %shard_map.93 = (bf16[128,4096]{1,0:T(8,128)(2,1)}, bf16[128,4096]{1,0:T(8,128)(2,1)}, f32[2,2,2,64,256]{4,3,2,1,0:T(8,128)}, bf16[2,2,2,64,256]{4,3,2,1,0:T(8,1...) custom-call(s32[34]{0:T(128)} %concatenate.17.refs_0_, s32[2,64,1]{2,1,0:T(8,128)} %reshape.110.refs_1_, ...), custom_call_target="tpu_custom_call" | custom-call | tf_op jit(solution)/shard_map/pallas_call | solution.py:197
  38.2 3.4 %collective-permute-start.10 = (bf16[2,2,128,256]{3,2,1,0:T(8,128)(2,1)}, bf16[2,2,128,256]{3,2,1,0:T(8,128)(2,1)S(1)}, u32[]{:S(2)}, u32[]{:S(2)}) collective-permute-start(bf16[2,2,128,256]{3,2,1,0:T(8,128)(2,1)} %bitcast.90), channel_id=1, source_target_pairs={{0,6},{2,0},{4,2},{6,4},{8,14},{10,8},{12,10},{14,12},{1,7},{3,1},... | collective-permute-start | bytes 786440 | tf_op jit(solution)/shard_map/ppermute | solution.py:202
  42.4 1.4 %collective-permute-start.3 = (bf16[4,128,512]{2,1,0:T(8,128)(2,1)S(1)}, bf16[4,128,512]{2,1,0:T(8,128)(2,1)S(1)}, u32[]{:S(2)}, u32[]{:S(2)}) collective-permute-start(bf16[4,128,512]{2,1,0:T(8,128)(2,1)S(1)} %pad_maximum_fusion), channel_id=1, source_target_pairs={{0,8},{2,10},{4,12},{6,14},{8,0},{10,2},{12,4},{14,6},{1,9},{3,11}... | collective-permute-start | bytes 1572872 | tf_op jit(solution)/shard_map/ppermute | solution.py:157
  43.7 5.0 %collective-permute-done.10 = bf16[2,2,128,256]{3,2,1,0:T(8,128)(2,1)S(1)} collective-permute-done((bf16[2,2,128,256]{3,2,1,0:T(8,128)(2,1)}, bf16[2,2,128,256]{3,2,1,0:T(8,128)(2,1)S(1)}, u32[]{:S(2)}, u32[]{:S(2)}) %collective-permute-start.10) | collective-permute-done | bytes 262176 | tf_op jit(solution)/shard_map/ppermute | solution.py:202
  48.7 9.5 %collective-permute-done.8 = bf16[2,2,128,256]{3,2,1,0:T(8,128)(2,1)S(1)} collective-permute-done((bf16[2,2,128,256]{3,2,1,0:T(8,128)(2,1)}, bf16[2,2,128,256]{3,2,1,0:T(8,128)(2,1)S(1)}, u32[]{:S(2)}, u32[]{:S(2)}) %collective-permute-start.8) | collective-permute-done | bytes 262176 | tf_op jit(solution)/shard_map/ppermute | solution.py:202
  58.2 2.0 %collective-permute-done.9 = bf16[2,2,128,256]{3,2,1,0:T(8,128)(2,1)S(1)} collective-permute-done((bf16[2,2,128,256]{3,2,1,0:T(8,128)(2,1)}, bf16[2,2,128,256]{3,2,1,0:T(8,128)(2,1)S(1)}, u32[]{:S(2)}, u32[]{:S(2)}) %collective-permute-start.9) | collective-permute-done | bytes 262176 | tf_op jit(solution)/shard_map/ppermute | solution.py:202
  60.5 7.8 %collective-permute-done.3 = bf16[4,128,512]{2,1,0:T(8,128)(2,1)S(1)} collective-permute-done((bf16[4,128,512]{2,1,0:T(8,128)(2,1)S(1)}, bf16[4,128,512]{2,1,0:T(8,128)(2,1)S(1)}, u32[]{:S(2)}, u32[]{:S(2)}) %collective-permute-start.3) | collective-permute-done | bytes 524320 | tf_op jit(solution)/shard_map/ppermute | solution.py:157
  69.8 0.7 pad_maximum_fusion.2
  70.5 0.7 pad_maximum_fusion.1
  71.3 7.5 %shard_map.94 = (bf16[128,4096]{1,0:T(8,128)(2,1)}, bf16[128,4096]{1,0:T(8,128)(2,1)}, f32[2,2,2,64,256]{4,3,2,1,0:T(8,128)}, bf16[2,2,2,64,256]{4,3,2,1,0:T(8,1...) custom-call(s32[34]{0:T(128)} %concatenate.17.refs_0_, ...), custom_call_target="tpu_custom_call", output_to_operand_aliasing={{0}: (12, {}), {1}: (13, {})} | custom-call | tf_op jit(solution)/shard_map/pallas_call | solution.py:197
  78.8 2.6 %collective-permute-start.12 = (bf16[2,2,128,256]{3,2,1,0:T(8,128)(2,1)}, bf16[2,2,128,256]{3,2,1,0:T(8,128)(2,1)S(1)}, u32[]{:S(2)}, u32[]{:S(2)}) collective-permute-start(bf16[2,2,128,256]{3,2,1,0:T(8,128)(2,1)} %bitcast.92), channel_id=1, source_target_pairs={{0,2},{2,4},{4,6},{6,0},{8,10},{10,12},{12,14},{14,8},{1,3},{3,5},... | collective-permute-start | bytes 786440 | tf_op jit(solution)/shard_map/ppermute | solution.py:202
  81.5 1.5 %collective-permute-start.14 = (bf16[2,2,128,256]{3,2,1,0:T(8,128)(2,1)}, bf16[2,2,128,256]{3,2,1,0:T(8,128)(2,1)S(1)}, u32[]{:S(2)}, u32[]{:S(2)}) collective-permute-start(bf16[2,2,128,256]{3,2,1,0:T(8,128)(2,1)} %bitcast.89), channel_id=1, source_target_pairs={{0,6},{2,0},{4,2},{6,4},{8,14},{10,8},{12,10},{14,12},{1,7},{3,1},... | collective-permute-start | bytes 786440 | tf_op jit(solution)/shard_map/ppermute | solution.py:202
  83.0 4.8 %collective-permute-done.12 = bf16[2,2,128,256]{3,2,1,0:T(8,128)(2,1)S(1)} collective-permute-done((bf16[2,2,128,256]{3,2,1,0:T(8,128)(2,1)}, bf16[2,2,128,256]{3,2,1,0:T(8,128)(2,1)S(1)}, u32[]{:S(2)}, u32[]{:S(2)}) %collective-permute-start.12) | collective-permute-done | bytes 262176 | tf_op jit(solution)/shard_map/ppermute | solution.py:202
  88.2 2.1 %collective-permute-done.14 = bf16[2,2,128,256]{3,2,1,0:T(8,128)(2,1)S(1)} collective-permute-done((bf16[2,2,128,256]{3,2,1,0:T(8,128)(2,1)}, bf16[2,2,128,256]{3,2,1,0:T(8,128)(2,1)S(1)}, u32[]{:S(2)}, u32[]{:S(2)}) %collective-permute-start.14) | collective-permute-done | bytes 262176 | tf_op jit(solution)/shard_map/ppermute | solution.py:202
  90.9 6.8 %collective-permute-done.15 = bf16[2,128,256]{2,1,0:T(8,128)(2,1)S(1)} collective-permute-done((bf16[2,128,256]{2,1,0:T(8,128)(2,1)S(1)}, bf16[2,128,256]{2,1,0:T(8,128)(2,1)S(1)}, u32[]{:S(2)}, u32[]{:S(2)}) %collective-permute-start.15) | collective-permute-done | bytes 131104 | tf_op jit(solution)/shard_map/ppermute | solution.py:205
  (55 shorter events, 8.8 us)
Async XLA Ops:
  1.6 40.0 %collective-permute-start = (bf16[128,512]{1,0:T(8,128)(2,1)S(1)}, bf16[128,512]{1,0:T(8,128)(2,1)S(1)}, u32[]{:S(2)}, u32[]{:S(2)}) collective-permute-start(bf16[128,512]{1,0:T(8,128)(2,1)S(1)} %get-tuple-element.47), channel_id=1, source_target_pairs={{0,2},{2,4},{4,6},{6,0},{8,10},{10,12},{12,14},{14,8},{1,3},{3,5},... | collective-permute-start | bytes 393224 | tf_op jit(solution)/shard_map/ppermute | solution.py:155
  4.6 37.6 %collective-permute-start.1 = (bf16[128,512]{1,0:T(8,128)(2,1)S(1)}, bf16[128,512]{1,0:T(8,128)(2,1)S(1)}, u32[]{:S(2)}, u32[]{:S(2)}) collective-permute-start(bf16[128,512]{1,0:T(8,128)(2,1)S(1)} %get-tuple-element.47), channel_id=1, source_target_pairs={{0,4},{2,6},{4,0},{6,2},{8,12},{10,14},{12,8},{14,10},{1,5},{3,7},... | collective-permute-start | bytes 393224 | tf_op jit(solution)/shard_map/ppermute | solution.py:155
  6.2 8.5 %collective-permute-start.4 = (bf16[128,512]{1,0:T(8,128)(2,1)S(1)}, bf16[128,512]{1,0:T(8,128)(2,1)S(1)}, u32[]{:S(2)}, u32[]{:S(2)}) collective-permute-start(bf16[128,512]{1,0:T(8,128)(2,1)S(1)} %get-tuple-element.41), channel_id=1, source_target_pairs={{0,8},{2,10},{4,12},{6,14},{8,0},{10,2},{12,4},{14,6},{1,9},{3,11}... | collective-permute-start | bytes 393224 | tf_op jit(solution)/shard_map/ppermute | solution.py:150
  8.9 0.7 copy-start.6
  14.8 15.2 %copy-start = (bf16[2,128,512]{2,1,0:T(8,128)(2,1)}, bf16[2,128,512]{2,1,0:T(8,128)(2,1)S(1)}, u32[]{:S(2)}) copy-start(bf16[2,128,512]{2,1,0:T(8,128)(2,1)S(1)} %pad_maximum_fusion.5) | copy-start | bytes 786436
  14.8 10.2 %collective-permute-start.5 = (bf16[2,128,512]{2,1,0:T(8,128)(2,1)S(1)}, bf16[2,128,512]{2,1,0:T(8,128)(2,1)S(1)}, u32[]{:S(2)}, u32[]{:S(2)}) collective-permute-start(bf16[2,128,512]{2,1,0:T(8,128)(2,1)S(1)} %pad_maximum_fusion.5), channel_id=1, source_target_pairs={{0,2},{2,4},{4,6},{6,0},{8,10},{10,12},{12,14},{14,8},{1,3},{3,5},... | collective-permute-start | bytes 786440 | tf_op jit(solution)/shard_map/ppermute | solution.py:153
  15.3 12.5 %collective-permute-start.6 = (bf16[2,128,512]{2,1,0:T(8,128)(2,1)S(1)}, bf16[2,128,512]{2,1,0:T(8,128)(2,1)S(1)}, u32[]{:S(2)}, u32[]{:S(2)}) collective-permute-start(bf16[2,128,512]{2,1,0:T(8,128)(2,1)S(1)} %pad_maximum_fusion.5), channel_id=1, source_target_pairs={{0,4},{2,6},{4,0},{6,2},{8,12},{10,14},{12,8},{14,10},{1,5},{3,7},... | collective-permute-start | bytes 786440 | tf_op jit(solution)/shard_map/ppermute | solution.py:153
  18.7 11.3 %collective-permute-start.7 = (bf16[2,128,512]{2,1,0:T(8,128)(2,1)S(1)}, bf16[2,128,512]{2,1,0:T(8,128)(2,1)S(1)}, u32[]{:S(2)}, u32[]{:S(2)}) collective-permute-start(bf16[2,128,512]{2,1,0:T(8,128)(2,1)S(1)} %pad_maximum_fusion.5), channel_id=1, source_target_pairs={{0,6},{2,0},{4,2},{6,4},{8,14},{10,8},{12,10},{14,12},{1,7},{3,1},... | collective-permute-start | bytes 786440 | tf_op jit(solution)/shard_map/ppermute | solution.py:153
  25.0 5.0 %copy-start.1 = (bf16[2,128,512]{2,1,0:T(8,128)(2,1)}, bf16[2,128,512]{2,1,0:T(8,128)(2,1)S(1)}, u32[]{:S(2)}) copy-start(bf16[2,128,512]{2,1,0:T(8,128)(2,1)S(1)} %collective-permute-done.5) | copy-start | bytes 786436
  25.0 17.3 %collective-permute-start.2 = (bf16[128,512]{1,0:T(8,128)(2,1)S(1)}, bf16[128,512]{1,0:T(8,128)(2,1)S(1)}, u32[]{:S(2)}, u32[]{:S(2)}) collective-permute-start(bf16[128,512]{1,0:T(8,128)(2,1)S(1)} %get-tuple-element.47), channel_id=1, source_target_pairs={{0,6},{2,0},{4,2},{6,4},{8,14},{10,8},{12,10},{14,12},{1,7},{3,1},... | collective-permute-start | bytes 393224 | tf_op jit(solution)/shard_map/ppermute | solution.py:155
  25.6 0.7 copy-start.7
  27.8 2.2 %copy-start.2 = (bf16[2,128,512]{2,1,0:T(8,128)(2,1)}, bf16[2,128,512]{2,1,0:T(8,128)(2,1)S(1)}, u32[]{:S(2)}) copy-start(bf16[2,128,512]{2,1,0:T(8,128)(2,1)S(1)} %collective-permute-done.6) | copy-start | bytes 786436
  30.0 0.7 copy-start.3
  38.2 10.5 %collective-permute-start.10 = (bf16[2,2,128,256]{3,2,1,0:T(8,128)(2,1)}, bf16[2,2,128,256]{3,2,1,0:T(8,128)(2,1)S(1)}, u32[]{:S(2)}, u32[]{:S(2)}) collective-permute-start(bf16[2,2,128,256]{3,2,1,0:T(8,128)(2,1)} %bitcast.90), channel_id=1, source_target_pairs={{0,6},{2,0},{4,2},{6,4},{8,14},{10,8},{12,10},{14,12},{1,7},{3,1},... | collective-permute-start | bytes 786440 | tf_op jit(solution)/shard_map/ppermute | solution.py:202
  41.6 16.6 %collective-permute-start.8 = (bf16[2,2,128,256]{3,2,1,0:T(8,128)(2,1)}, bf16[2,2,128,256]{3,2,1,0:T(8,128)(2,1)S(1)}, u32[]{:S(2)}, u32[]{:S(2)}) collective-permute-start(bf16[2,2,128,256]{3,2,1,0:T(8,128)(2,1)} %bitcast.88), channel_id=1, source_target_pairs={{0,2},{2,4},{4,6},{6,0},{8,10},{10,12},{12,14},{14,8},{1,3},{3,5},... | collective-permute-start | bytes 786440 | tf_op jit(solution)/shard_map/ppermute | solution.py:202
  41.6 18.6 %collective-permute-start.9 = (bf16[2,2,128,256]{3,2,1,0:T(8,128)(2,1)}, bf16[2,2,128,256]{3,2,1,0:T(8,128)(2,1)S(1)}, u32[]{:S(2)}, u32[]{:S(2)}) collective-permute-start(bf16[2,2,128,256]{3,2,1,0:T(8,128)(2,1)} %bitcast.87), channel_id=1, source_target_pairs={{0,4},{2,6},{4,0},{6,2},{8,12},{10,14},{12,8},{14,10},{1,5},{3,7},... | collective-permute-start | bytes 786440 | tf_op jit(solution)/shard_map/ppermute | solution.py:202
  42.3 18.0 %copy-start.4 = (f32[2,2,2,64,256]{4,3,2,1,0:T(8,128)S(1)}, f32[2,2,2,64,256]{4,3,2,1,0:T(8,128)}, u32[]{:S(2)}) copy-start(f32[2,2,2,64,256]{4,3,2,1,0:T(8,128)} %get-tuple-element.20) | copy-start | bytes 1572868
  42.4 25.9 %collective-permute-start.3 = (bf16[4,128,512]{2,1,0:T(8,128)(2,1)S(1)}, bf16[4,128,512]{2,1,0:T(8,128)(2,1)S(1)}, u32[]{:S(2)}, u32[]{:S(2)}) collective-permute-start(bf16[4,128,512]{2,1,0:T(8,128)(2,1)S(1)} %pad_maximum_fusion), channel_id=1, source_target_pairs={{0,8},{2,10},{4,12},{6,14},{8,0},{10,2},{12,4},{14,6},{1,9},{3,11}... | collective-permute-start | bytes 1572872 | tf_op jit(solution)/shard_map/ppermute | solution.py:157
  60.4 22.6 %collective-permute-start.11 = (bf16[2,128,256]{2,1,0:T(8,128)(2,1)S(1)}, bf16[2,128,256]{2,1,0:T(8,128)(2,1)S(1)}, u32[]{:S(2)}, u32[]{:S(2)}) collective-permute-start(bf16[2,128,256]{2,1,0:T(8,128)(2,1)S(1)} %fusion.8), channel_id=1, source_target_pairs={{0,8},{2,10},{4,12},{6,14},{8,0},{10,2},{12,4},{14,6},{1,9},{3,11}... | collective-permute-start | bytes 393224 | tf_op jit(solution)/shard_map/ppermute | solution.py:205
  78.8 11.4 %copy-start.5 = (f32[2,2,2,64,256]{4,3,2,1,0:T(8,128)S(1)}, f32[2,2,2,64,256]{4,3,2,1,0:T(8,128)}, u32[]{:S(2)}) copy-start(f32[2,2,2,64,256]{4,3,2,1,0:T(8,128)} %get-tuple-element.24) | copy-start | bytes 1572868
  78.8 9.0 %collective-permute-start.12 = (bf16[2,2,128,256]{3,2,1,0:T(8,128)(2,1)}, bf16[2,2,128,256]{3,2,1,0:T(8,128)(2,1)S(1)}, u32[]{:S(2)}, u32[]{:S(2)}) collective-permute-start(bf16[2,2,128,256]{3,2,1,0:T(8,128)(2,1)} %bitcast.92), channel_id=1, source_target_pairs={{0,2},{2,4},{4,6},{6,0},{8,10},{10,12},{12,14},{14,8},{1,3},{3,5},... | collective-permute-start | bytes 786440 | tf_op jit(solution)/shard_map/ppermute | solution.py:202
  81.5 6.7 %collective-permute-start.13 = (bf16[2,2,128,256]{3,2,1,0:T(8,128)(2,1)}, bf16[2,2,128,256]{3,2,1,0:T(8,128)(2,1)S(1)}, u32[]{:S(2)}, u32[]{:S(2)}) collective-permute-start(bf16[2,2,128,256]{3,2,1,0:T(8,128)(2,1)} %bitcast.91), channel_id=1, source_target_pairs={{0,4},{2,6},{4,0},{6,2},{8,12},{10,14},{12,8},{14,10},{1,5},{3,7},... | collective-permute-start | bytes 786440 | tf_op jit(solution)/shard_map/ppermute | solution.py:202
  81.5 8.8 %collective-permute-start.14 = (bf16[2,2,128,256]{3,2,1,0:T(8,128)(2,1)}, bf16[2,2,128,256]{3,2,1,0:T(8,128)(2,1)S(1)}, u32[]{:S(2)}, u32[]{:S(2)}) collective-permute-start(bf16[2,2,128,256]{3,2,1,0:T(8,128)(2,1)} %bitcast.89), channel_id=1, source_target_pairs={{0,6},{2,0},{4,2},{6,4},{8,14},{10,8},{12,10},{14,12},{1,7},{3,1},... | collective-permute-start | bytes 786440 | tf_op jit(solution)/shard_map/ppermute | solution.py:202
  90.4 7.3 %collective-permute-start.15 = (bf16[2,128,256]{2,1,0:T(8,128)(2,1)S(1)}, bf16[2,128,256]{2,1,0:T(8,128)(2,1)S(1)}, u32[]{:S(2)}, u32[]{:S(2)}) collective-permute-start(bf16[2,128,256]{2,1,0:T(8,128)(2,1)S(1)} %fusion.9), channel_id=1, source_target_pairs={{0,8},{2,10},{4,12},{6,14},{8,0},{10,2},{12,4},{14,6},{1,9},{3,11}... | collective-permute-start | bytes 393224 | tf_op jit(solution)/shard_map/ppermute | solution.py:205

commit v17 on v15

--- a/solution.py
+++ b/solution.py
@@ -90,7 +90,7 @@
     my_half = index_ref[info]
     my_q = index_ref[info + 1]
     for shift, ref in enumerate((own_ref,) + tuple(send_refs)):
-        target = my_half * half + (my_q + shift) % half
+        target = my_half * half + (my_q ^ shift)
         other = (target + half) % (2 * half)
         for k, device in enumerate((target, other)):
             block = buf_ref[pl.ds(device * tiles, tiles)]
@@ -125,7 +125,7 @@
     my_half = my_index // half
     my_q = my_index % half
     window_owner = window_slot // tiles
-    owner_s = (my_q - window_owner % half) % half
+    owner_s = my_q ^ (window_owner % half)
     owner_k = (window_owner // half != my_half).astype(jnp.int32)
     window_row = owner_k * tiles + window_slot % tiles
     index_table = jnp.concatenate([owner_s.reshape(-1), window_slot.reshape(-1), my_spans,
@@ -137,7 +137,7 @@
         return [(i, i ^ half) for i in range(ctx_count)]
 
     def half_pairs(shift):
-        return [(i, (i // half) * half + (i % half + shift) % half) for i in range(ctx_count)]
+        return [(i, (i // half) * half + ((i % half) ^ shift)) for i in range(ctx_count)]
 
     attended = None
     query_grad = None

time: 76.6 us -> 76.3 us (level)
  starting transfers between devices: 23.2 us -> 19.1 us
  waiting for transfers between devices: 29.6 us -> 33.6 us
    ppermute x2, starting transfers between devices: 5.45 us -> 2.29 us  [local(): lax.ppermute(summed[1].astype(jnp.bfloat16), 'ctx', cross_pairs())]
    ppermute x6, waiting for transfers between devices: 7.29 us -> 10.4 us  [local(): lax.ppermute(send_packs[shift - 1].reshape(pack_shape), 'ctx', half_pairs...]
    ppermute x6, waiting for transfers between devices: 7.7 us -> 8.76 us  [local(): pieces.append(lax.ppermute(both, 'ctx', half_pairs(shift)))]
  transfers between devices with their start and end apart: 16 -> 16, of which waited for: 6 -> 7; matrix products, arithmetic and copies ran while one was open for 3% -> 3% of each run, Pallas kernels for 20% -> 20%
where the time goes in v17:
time: 76.3 us; the launch traced here: 76.1 us
  waiting for transfers between devices  33.6 us (44%)
  starting transfers between devices  19.1 us (25%)
  Pallas kernels  15 us (20%)
  local copies, waits for them, and re-layouts  5.46 us (7%)
  other arithmetic  2.06 us (3%)
  between operations  0.85 us (1%)
    pallas_call x2, Pallas kernels, local(): attended, query_grad, own_pack, *send_packs = kernel(*operands)  15 us
    ppermute x6, waiting for transfers between devices, local(): lax.ppermute(send_packs[shift - 1].reshape(pack_shape), 'ctx', half_pairs...  10.4 us
    ppermute x6, waiting for transfers between devices, local(): pieces.append(lax.ppermute(both, 'ctx', half_pairs(shift)))  8.76 us
    ppermute x2, waiting for transfers between devices, local(): both = jnp.stack([pair, lax.ppermute(pair, 'ctx', cross_pairs())])  8.66 us
    ppermute x6, starting transfers between devices, local(): lax.ppermute(send_packs[shift - 1].reshape(pack_shape), 'ctx', half_pairs...  7.11 us
    ppermute x2, waiting for transfers between devices, local(): lax.ppermute(summed[1].astype(jnp.bfloat16), 'ctx', cross_pairs())  5.75 us
    ppermute x6, starting transfers between devices, local(): pieces.append(lax.ppermute(both, 'ctx', half_pairs(shift)))  5.49 us
    ppermute x2, starting transfers between devices, local(): both = jnp.stack([pair, lax.ppermute(pair, 'ctx', cross_pairs())])  4.19 us
  transfers between devices with their start and end apart: 16, of which 7 were waited for; matrix products, arithmetic and copies ran while one was open for 3% of the time, Pallas kernels for 20%

profile of v17, /device:TPU:0, one launch (start us, length us, event | category | flops | bytes accessed | tf_op | source)
XLA Modules:
  0.0 76.1 jit_solution(9638255304861940709)
XLA Ops:
  0.6 1.0 %fusion.17 = (bf16[128,256]{1,0:T(8,128)(2,1)S(1)}, bf16[128,256]{1,0:T(8,128)(2,1)S(1)}, bf16[128,256]{1,0:T(8,128)(2,1)S(1)}, bf16[128,256]{1,0:T(8,128)(2,1)S(1)}) fusion(bf16[128,512]{1,0:T(8,128)(2,1)} %param.7, bf16[128,512]{1,0:T(8,128)(2,1)} %param.8), kind=kLoop, calls=%fused_computation.45 | loop fusion | bytes 524288 | tf_op jit(solution)/shard_map/slice | solution.py:148
  1.6 4.1 %collective-permute-start.4 = (bf16[128,512]{1,0:T(8,128)(2,1)S(1)}, bf16[128,512]{1,0:T(8,128)(2,1)S(1)}, u32[]{:S(2)}, u32[]{:S(2)}) collective-permute-start(bf16[128,512]{1,0:T(8,128)(2,1)S(1)} %get-tuple-element.37), channel_id=1, source_target_pairs={{0,8},{2,10},{4,12},{6,14},{8,0},{10,2},{12,4},{14,6},{1,9},{3,11}... | collective-permute-start | bytes 393224 | tf_op jit(solution)/shard_map/ppermute | solution.py:149
  7.0 8.7 %collective-permute-done.4 = bf16[128,512]{1,0:T(8,128)(2,1)S(1)} collective-permute-done((bf16[128,512]{1,0:T(8,128)(2,1)S(1)}, bf16[128,512]{1,0:T(8,128)(2,1)S(1)}, u32[]{:S(2)}, u32[]{:S(2)}) %collective-permute-start.4) | collective-permute-done | bytes 131104 | tf_op jit(solution)/shard_map/ppermute | solution.py:149
  15.7 1.9 %collective-permute-start.5 = (bf16[2,128,512]{2,1,0:T(8,128)(2,1)S(1)}, bf16[2,128,512]{2,1,0:T(8,128)(2,1)S(1)}, u32[]{:S(2)}, u32[]{:S(2)}) collective-permute-start(bf16[2,128,512]{2,1,0:T(8,128)(2,1)S(1)} %pad_maximum_fusion.1), channel_id=1, source_target_pairs={{0,2},{2,0},{4,6},{6,4},{8,10},{10,8},{12,14},{14,12},{1,3},{3,1},... | collective-permute-start | bytes 786440 | tf_op jit(solution)/shard_map/ppermute | solution.py:152
  17.6 1.6 %collective-permute-start.7 = (bf16[2,128,512]{2,1,0:T(8,128)(2,1)S(1)}, bf16[2,128,512]{2,1,0:T(8,128)(2,1)S(1)}, u32[]{:S(2)}, u32[]{:S(2)}) collective-permute-start(bf16[2,128,512]{2,1,0:T(8,128)(2,1)S(1)} %pad_maximum_fusion.1), channel_id=1, source_target_pairs={{0,6},{2,4},{4,2},{6,0},{8,14},{10,12},{12,10},{14,8},{1,7},{3,5},... | collective-permute-start | bytes 786440 | tf_op jit(solution)/shard_map/ppermute | solution.py:152
  19.3 1.9 %collective-permute-start.1 = (bf16[2,128,512]{2,1,0:T(8,128)(2,1)S(1)}, bf16[2,128,512]{2,1,0:T(8,128)(2,1)S(1)}, u32[]{:S(2)}, u32[]{:S(2)}) collective-permute-start(bf16[2,128,512]{2,1,0:T(8,128)(2,1)S(1)} %pad_maximum_fusion), channel_id=1, source_target_pairs={{0,2},{2,0},{4,6},{6,4},{8,10},{10,8},{12,14},{14,12},{1,3},{3,1},... | collective-permute-start | bytes 786440 | tf_op jit(solution)/shard_map/ppermute | solution.py:152
  21.9 0.8 %reshape.110.refs_1_ = s32[2,64,1]{2,1,0:T(8,128)} reshape(s32[128]{0:T(128)S(1)} %copy-done.11) | data formatting | bytes 1024 | tf_op jit(solution)/shard_map/reshape | solution.py:134
  23.4 5.7 %collective-permute-done.5 = bf16[2,128,512]{2,1,0:T(8,128)(2,1)S(1)} collective-permute-done((bf16[2,128,512]{2,1,0:T(8,128)(2,1)S(1)}, bf16[2,128,512]{2,1,0:T(8,128)(2,1)S(1)}, u32[]{:S(2)}, u32[]{:S(2)}) %collective-permute-start.5) | collective-permute-done | bytes 262176 | tf_op jit(solution)/shard_map/ppermute | solution.py:152
  29.1 3.0 %collective-permute-done.7 = bf16[2,128,512]{2,1,0:T(8,128)(2,1)S(1)} collective-permute-done((bf16[2,128,512]{2,1,0:T(8,128)(2,1)S(1)}, bf16[2,128,512]{2,1,0:T(8,128)(2,1)S(1)}, u32[]{:S(2)}, u32[]{:S(2)}) %collective-permute-start.7) | collective-permute-done | bytes 262176 | tf_op jit(solution)/shard_map/ppermute | solution.py:152
  32.1 0.7 copy-done.5
  32.9 7.5 %shard_map.93 = (bf16[128,4096]{1,0:T(8,128)(2,1)}, bf16[128,4096]{1,0:T(8,128)(2,1)}, f32[2,2,2,64,256]{4,3,2,1,0:T(8,128)}, bf16[2,2,2,64,256]{4,3,2,1,0:T(8,1...) custom-call(s32[34]{0:T(128)} %concatenate.17.refs_0_, s32[2,64,1]{2,1,0:T(8,128)} %reshape.110.refs_1_, ...), custom_call_target="tpu_custom_call" | custom-call | tf_op jit(solution)/shard_map/pallas_call | solution.py:191
  40.3 1.4 %collective-permute-start.10 = (bf16[2,2,128,256]{3,2,1,0:T(8,128)(2,1)}, bf16[2,2,128,256]{3,2,1,0:T(8,128)(2,1)S(1)}, u32[]{:S(2)}, u32[]{:S(2)}) collective-permute-start(bf16[2,2,128,256]{3,2,1,0:T(8,128)(2,1)} %bitcast.83), channel_id=1, source_target_pairs={{0,6},{2,4},{4,2},{6,0},{8,14},{10,12},{12,10},{14,8},{1,7},{3,5},... | collective-permute-start | bytes 786440 | tf_op jit(solution)/shard_map/ppermute | solution.py:196
  41.7 0.7 collective-permute-start.8
  42.4 1.5 %collective-permute-start.9 = (bf16[2,2,128,256]{3,2,1,0:T(8,128)(2,1)}, bf16[2,2,128,256]{3,2,1,0:T(8,128)(2,1)S(1)}, u32[]{:S(2)}, u32[]{:S(2)}) collective-permute-start(bf16[2,2,128,256]{3,2,1,0:T(8,128)(2,1)} %bitcast.80), channel_id=1, source_target_pairs={{0,4},{2,6},{4,0},{6,2},{8,12},{10,14},{12,8},{14,10},{1,5},{3,7},... | collective-permute-start | bytes 786440 | tf_op jit(solution)/shard_map/ppermute | solution.py:196
  43.9 0.7 copy-done.6
  44.7 7.6 %shard_map.94 = (bf16[128,4096]{1,0:T(8,128)(2,1)}, bf16[128,4096]{1,0:T(8,128)(2,1)}, f32[2,2,2,64,256]{4,3,2,1,0:T(8,128)}, bf16[2,2,2,64,256]{4,3,2,1,0:T(8,1...) custom-call(s32[34]{0:T(128)} %concatenate.17.refs_0_, ...), custom_call_target="tpu_custom_call", output_to_operand_aliasing={{0}: (12, {}), {1}: (13, {})} | custom-call | tf_op jit(solution)/shard_map/pallas_call | solution.py:191
  52.3 2.0 %collective-permute-start.12 = (bf16[2,2,128,256]{3,2,1,0:T(8,128)(2,1)}, bf16[2,2,128,256]{3,2,1,0:T(8,128)(2,1)S(1)}, u32[]{:S(2)}, u32[]{:S(2)}) collective-permute-start(bf16[2,2,128,256]{3,2,1,0:T(8,128)(2,1)} %bitcast.85), channel_id=1, source_target_pairs={{0,2},{2,0},{4,6},{6,4},{8,10},{10,8},{12,14},{14,12},{1,3},{3,1},... | collective-permute-start | bytes 786440 | tf_op jit(solution)/shard_map/ppermute | solution.py:196
  54.4 1.5 %collective-permute-start.14 = (bf16[2,2,128,256]{3,2,1,0:T(8,128)(2,1)}, bf16[2,2,128,256]{3,2,1,0:T(8,128)(2,1)S(1)}, u32[]{:S(2)}, u32[]{:S(2)}) collective-permute-start(bf16[2,2,128,256]{3,2,1,0:T(8,128)(2,1)} %bitcast.82), channel_id=1, source_target_pairs={{0,6},{2,4},{4,2},{6,0},{8,14},{10,12},{12,10},{14,8},{1,7},{3,5},... | collective-permute-start | bytes 786440 | tf_op jit(solution)/shard_map/ppermute | solution.py:196
  56.0 1.5 %collective-permute-start.11 = (bf16[2,128,256]{2,1,0:T(8,128)(2,1)S(1)}, bf16[2,128,256]{2,1,0:T(8,128)(2,1)S(1)}, u32[]{:S(2)}, u32[]{:S(2)}) collective-permute-start(bf16[2,128,256]{2,1,0:T(8,128)(2,1)S(1)} %fusion.8), channel_id=1, source_target_pairs={{0,8},{2,10},{4,12},{6,14},{8,0},{10,2},{12,4},{14,6},{1,9},{3,11}... | collective-permute-start | bytes 393224 | tf_op jit(solution)/shard_map/ppermute | solution.py:199
  57.5 3.2 %collective-permute-done.12 = bf16[2,2,128,256]{3,2,1,0:T(8,128)(2,1)S(1)} collective-permute-done((bf16[2,2,128,256]{3,2,1,0:T(8,128)(2,1)}, bf16[2,2,128,256]{3,2,1,0:T(8,128)(2,1)S(1)}, u32[]{:S(2)}, u32[]{:S(2)}) %collective-permute-start.12) | collective-permute-done | bytes 262176 | tf_op jit(solution)/shard_map/ppermute | solution.py:196
  60.8 2.1 %collective-permute-done.13 = bf16[2,2,128,256]{3,2,1,0:T(8,128)(2,1)S(1)} collective-permute-done((bf16[2,2,128,256]{3,2,1,0:T(8,128)(2,1)}, bf16[2,2,128,256]{3,2,1,0:T(8,128)(2,1)S(1)}, u32[]{:S(2)}, u32[]{:S(2)}) %collective-permute-start.13) | collective-permute-done | bytes 262176 | tf_op jit(solution)/shard_map/ppermute | solution.py:196
  62.9 5.1 %collective-permute-done.14 = bf16[2,2,128,256]{3,2,1,0:T(8,128)(2,1)S(1)} collective-permute-done((bf16[2,2,128,256]{3,2,1,0:T(8,128)(2,1)}, bf16[2,2,128,256]{3,2,1,0:T(8,128)(2,1)S(1)}, u32[]{:S(2)}, u32[]{:S(2)}) %collective-permute-start.14) | collective-permute-done | bytes 262176 | tf_op jit(solution)/shard_map/ppermute | solution.py:196
  68.1 0.8 %collective-permute-start.15 = (bf16[2,128,256]{2,1,0:T(8,128)(2,1)S(1)}, bf16[2,128,256]{2,1,0:T(8,128)(2,1)S(1)}, u32[]{:S(2)}, u32[]{:S(2)}) collective-permute-start(bf16[2,128,256]{2,1,0:T(8,128)(2,1)S(1)} %fusion.9), channel_id=1, source_target_pairs={{0,8},{2,10},{4,12},{6,14},{8,0},{10,2},{12,4},{14,6},{1,9},{3,11}... | collective-permute-start | bytes 393224 | tf_op jit(solution)/shard_map/ppermute | solution.py:199
  68.9 5.7 %collective-permute-done.15 = bf16[2,128,256]{2,1,0:T(8,128)(2,1)S(1)} collective-permute-done((bf16[2,128,256]{2,1,0:T(8,128)(2,1)S(1)}, bf16[2,128,256]{2,1,0:T(8,128)(2,1)S(1)}, u32[]{:S(2)}, u32[]{:S(2)}) %collective-permute-start.15) | collective-permute-done | bytes 131104 | tf_op jit(solution)/shard_map/ppermute | solution.py:199
  (58 shorter events, 4.5 us)
Async XLA Ops:
  1.6 14.0 %collective-permute-start.4 = (bf16[128,512]{1,0:T(8,128)(2,1)S(1)}, bf16[128,512]{1,0:T(8,128)(2,1)S(1)}, u32[]{:S(2)}, u32[]{:S(2)}) collective-permute-start(bf16[128,512]{1,0:T(8,128)(2,1)S(1)} %get-tuple-element.37), channel_id=1, source_target_pairs={{0,8},{2,10},{4,12},{6,14},{8,0},{10,2},{12,4},{14,6},{1,9},{3,11}... | collective-permute-start | bytes 393224 | tf_op jit(solution)/shard_map/ppermute | solution.py:149
  5.7 13.5 %collective-permute-start = (bf16[128,512]{1,0:T(8,128)(2,1)S(1)}, bf16[128,512]{1,0:T(8,128)(2,1)S(1)}, u32[]{:S(2)}, u32[]{:S(2)}) collective-permute-start(bf16[128,512]{1,0:T(8,128)(2,1)S(1)} %get-tuple-element.43), channel_id=1, source_target_pairs={{0,8},{2,10},{4,12},{6,14},{8,0},{10,2},{12,4},{14,6},{1,9},{3,11}... | collective-permute-start | bytes 393224 | tf_op jit(solution)/shard_map/ppermute | solution.py:149
  15.7 3.6 %copy-start.1 = (bf16[2,128,512]{2,1,0:T(8,128)(2,1)}, bf16[2,128,512]{2,1,0:T(8,128)(2,1)S(1)}, u32[]{:S(2)}) copy-start(bf16[2,128,512]{2,1,0:T(8,128)(2,1)S(1)} %pad_maximum_fusion.1) | copy-start | bytes 786436
  15.7 13.4 %collective-permute-start.5 = (bf16[2,128,512]{2,1,0:T(8,128)(2,1)S(1)}, bf16[2,128,512]{2,1,0:T(8,128)(2,1)S(1)}, u32[]{:S(2)}, u32[]{:S(2)}) collective-permute-start(bf16[2,128,512]{2,1,0:T(8,128)(2,1)S(1)} %pad_maximum_fusion.1), channel_id=1, source_target_pairs={{0,2},{2,0},{4,6},{6,4},{8,10},{10,8},{12,14},{14,12},{1,3},{3,1},... | collective-permute-start | bytes 786440 | tf_op jit(solution)/shard_map/ppermute | solution.py:152
  17.6 11.5 %collective-permute-start.6 = (bf16[2,128,512]{2,1,0:T(8,128)(2,1)S(1)}, bf16[2,128,512]{2,1,0:T(8,128)(2,1)S(1)}, u32[]{:S(2)}, u32[]{:S(2)}) collective-permute-start(bf16[2,128,512]{2,1,0:T(8,128)(2,1)S(1)} %pad_maximum_fusion.1), channel_id=1, source_target_pairs={{0,4},{2,6},{4,0},{6,2},{8,12},{10,14},{12,8},{14,10},{1,5},{3,7},... | collective-permute-start | bytes 786440 | tf_op jit(solution)/shard_map/ppermute | solution.py:152
  17.6 14.5 %collective-permute-start.7 = (bf16[2,128,512]{2,1,0:T(8,128)(2,1)S(1)}, bf16[2,128,512]{2,1,0:T(8,128)(2,1)S(1)}, u32[]{:S(2)}, u32[]{:S(2)}) collective-permute-start(bf16[2,128,512]{2,1,0:T(8,128)(2,1)S(1)} %pad_maximum_fusion.1), channel_id=1, source_target_pairs={{0,6},{2,4},{4,2},{6,0},{8,14},{10,12},{12,10},{14,8},{1,7},{3,5},... | collective-permute-start | bytes 786440 | tf_op jit(solution)/shard_map/ppermute | solution.py:152
  19.3 21.0 %copy-start = (bf16[2,128,512]{2,1,0:T(8,128)(2,1)}, bf16[2,128,512]{2,1,0:T(8,128)(2,1)S(1)}, u32[]{:S(2)}) copy-start(bf16[2,128,512]{2,1,0:T(8,128)(2,1)S(1)} %pad_maximum_fusion) | copy-start | bytes 786436
  19.3 23.1 %collective-permute-start.1 = (bf16[2,128,512]{2,1,0:T(8,128)(2,1)S(1)}, bf16[2,128,512]{2,1,0:T(8,128)(2,1)S(1)}, u32[]{:S(2)}, u32[]{:S(2)}) collective-permute-start(bf16[2,128,512]{2,1,0:T(8,128)(2,1)S(1)} %pad_maximum_fusion), channel_id=1, source_target_pairs={{0,2},{2,0},{4,6},{6,4},{8,10},{10,8},{12,14},{14,12},{1,3},{3,1},... | collective-permute-start | bytes 786440 | tf_op jit(solution)/shard_map/ppermute | solution.py:152
  23.4 20.5 %collective-permute-start.2 = (bf16[2,128,512]{2,1,0:T(8,128)(2,1)S(1)}, bf16[2,128,512]{2,1,0:T(8,128)(2,1)S(1)}, u32[]{:S(2)}, u32[]{:S(2)}) collective-permute-start(bf16[2,128,512]{2,1,0:T(8,128)(2,1)S(1)} %pad_maximum_fusion), channel_id=1, source_target_pairs={{0,4},{2,6},{4,0},{6,2},{8,12},{10,14},{12,8},{14,10},{1,5},{3,7},... | collective-permute-start | bytes 786440 | tf_op jit(solution)/shard_map/ppermute | solution.py:152
  29.1 3.0 %copy-start.3 = (bf16[2,128,512]{2,1,0:T(8,128)(2,1)}, bf16[2,128,512]{2,1,0:T(8,128)(2,1)S(1)}, u32[]{:S(2)}) copy-start(bf16[2,128,512]{2,1,0:T(8,128)(2,1)S(1)} %collective-permute-done.5) | copy-start | bytes 786436
  29.1 14.8 %collective-permute-start.3 = (bf16[2,128,512]{2,1,0:T(8,128)(2,1)S(1)}, bf16[2,128,512]{2,1,0:T(8,128)(2,1)S(1)}, u32[]{:S(2)}, u32[]{:S(2)}) collective-permute-start(bf16[2,128,512]{2,1,0:T(8,128)(2,1)S(1)} %pad_maximum_fusion), channel_id=1, source_target_pairs={{0,6},{2,4},{4,2},{6,0},{8,14},{10,12},{12,10},{14,8},{1,7},{3,5},... | collective-permute-start | bytes 786440 | tf_op jit(solution)/shard_map/ppermute | solution.py:152
  29.1 3.0 %copy-start.4 = (bf16[2,128,512]{2,1,0:T(8,128)(2,1)}, bf16[2,128,512]{2,1,0:T(8,128)(2,1)S(1)}, u32[]{:S(2)}) copy-start(bf16[2,128,512]{2,1,0:T(8,128)(2,1)S(1)} %collective-permute-done.6) | copy-start | bytes 786436
  40.3 14.0 %collective-permute-start.10 = (bf16[2,2,128,256]{3,2,1,0:T(8,128)(2,1)}, bf16[2,2,128,256]{3,2,1,0:T(8,128)(2,1)S(1)}, u32[]{:S(2)}, u32[]{:S(2)}) collective-permute-start(bf16[2,2,128,256]{3,2,1,0:T(8,128)(2,1)} %bitcast.83), channel_id=1, source_target_pairs={{0,6},{2,4},{4,2},{6,0},{8,14},{10,12},{12,10},{14,8},{1,7},{3,5},... | collective-permute-start | bytes 786440 | tf_op jit(solution)/shard_map/ppermute | solution.py:196
  41.7 14.2 %collective-permute-start.8 = (bf16[2,2,128,256]{3,2,1,0:T(8,128)(2,1)}, bf16[2,2,128,256]{3,2,1,0:T(8,128)(2,1)S(1)}, u32[]{:S(2)}, u32[]{:S(2)}) collective-permute-start(bf16[2,2,128,256]{3,2,1,0:T(8,128)(2,1)} %bitcast.81), channel_id=1, source_target_pairs={{0,2},{2,0},{4,6},{6,4},{8,10},{10,8},{12,14},{14,12},{1,3},{3,1},... | collective-permute-start | bytes 786440 | tf_op jit(solution)/shard_map/ppermute | solution.py:196
  42.4 1.5 %copy-start.2 = (bf16[2,128,512]{2,1,0:T(8,128)(2,1)}, bf16[2,128,512]{2,1,0:T(8,128)(2,1)S(1)}, u32[]{:S(2)}) copy-start(bf16[2,128,512]{2,1,0:T(8,128)(2,1)S(1)} %collective-permute-done.1) | copy-start | bytes 786436
  42.4 13.5 %collective-permute-start.9 = (bf16[2,2,128,256]{3,2,1,0:T(8,128)(2,1)}, bf16[2,2,128,256]{3,2,1,0:T(8,128)(2,1)S(1)}, u32[]{:S(2)}, u32[]{:S(2)}) collective-permute-start(bf16[2,2,128,256]{3,2,1,0:T(8,128)(2,1)} %bitcast.80), channel_id=1, source_target_pairs={{0,4},{2,6},{4,0},{6,2},{8,12},{10,14},{12,8},{14,10},{1,5},{3,7},... | collective-permute-start | bytes 786440 | tf_op jit(solution)/shard_map/ppermute | solution.py:196
  43.9 0.8 %copy-start.7 = (bf16[2,128,512]{2,1,0:T(8,128)(2,1)}, bf16[2,128,512]{2,1,0:T(8,128)(2,1)S(1)}, u32[]{:S(2)}) copy-start(bf16[2,128,512]{2,1,0:T(8,128)(2,1)S(1)} %collective-permute-done.3) | copy-start | bytes 786436
  44.7 11.2 %copy-start.8 = (f32[2,2,2,64,256]{4,3,2,1,0:T(8,128)S(1)}, f32[2,2,2,64,256]{4,3,2,1,0:T(8,128)}, u32[]{:S(2)}) copy-start(f32[2,2,2,64,256]{4,3,2,1,0:T(8,128)} %get-tuple-element.20) | copy-start | bytes 1572868
  52.3 8.5 %collective-permute-start.12 = (bf16[2,2,128,256]{3,2,1,0:T(8,128)(2,1)}, bf16[2,2,128,256]{3,2,1,0:T(8,128)(2,1)S(1)}, u32[]{:S(2)}, u32[]{:S(2)}) collective-permute-start(bf16[2,2,128,256]{3,2,1,0:T(8,128)(2,1)} %bitcast.85), channel_id=1, source_target_pairs={{0,2},{2,0},{4,6},{6,4},{8,10},{10,8},{12,14},{14,12},{1,3},{3,1},... | collective-permute-start | bytes 786440 | tf_op jit(solution)/shard_map/ppermute | solution.py:196
  54.3 8.6 %collective-permute-start.13 = (bf16[2,2,128,256]{3,2,1,0:T(8,128)(2,1)}, bf16[2,2,128,256]{3,2,1,0:T(8,128)(2,1)S(1)}, u32[]{:S(2)}, u32[]{:S(2)}) collective-permute-start(bf16[2,2,128,256]{3,2,1,0:T(8,128)(2,1)} %bitcast.84), channel_id=1, source_target_pairs={{0,4},{2,6},{4,0},{6,2},{8,12},{10,14},{12,8},{14,10},{1,5},{3,7},... | collective-permute-start | bytes 786440 | tf_op jit(solution)/shard_map/ppermute | solution.py:196
  54.4 13.6 %collective-permute-start.14 = (bf16[2,2,128,256]{3,2,1,0:T(8,128)(2,1)}, bf16[2,2,128,256]{3,2,1,0:T(8,128)(2,1)S(1)}, u32[]{:S(2)}, u32[]{:S(2)}) collective-permute-start(bf16[2,2,128,256]{3,2,1,0:T(8,128)(2,1)} %bitcast.82), channel_id=1, source_target_pairs={{0,6},{2,4},{4,2},{6,0},{8,14},{10,12},{12,10},{14,8},{1,7},{3,5},... | collective-permute-start | bytes 786440 | tf_op jit(solution)/shard_map/ppermute | solution.py:196
  55.9 12.1 %copy-start.9 = (f32[2,2,2,64,256]{4,3,2,1,0:T(8,128)S(1)}, f32[2,2,2,64,256]{4,3,2,1,0:T(8,128)}, u32[]{:S(2)}) copy-start(f32[2,2,2,64,256]{4,3,2,1,0:T(8,128)} %get-tuple-element.24) | copy-start | bytes 1572868
  56.0 12.8 %collective-permute-start.11 = (bf16[2,128,256]{2,1,0:T(8,128)(2,1)S(1)}, bf16[2,128,256]{2,1,0:T(8,128)(2,1)S(1)}, u32[]{:S(2)}, u32[]{:S(2)}) collective-permute-start(bf16[2,128,256]{2,1,0:T(8,128)(2,1)S(1)} %fusion.8), channel_id=1, source_target_pairs={{0,8},{2,10},{4,12},{6,14},{8,0},{10,2},{12,4},{14,6},{1,9},{3,11}... | collective-permute-start | bytes 393224 | tf_op jit(solution)/shard_map/ppermute | solution.py:199
  68.1 6.6 %collective-permute-start.15 = (bf16[2,128,256]{2,1,0:T(8,128)(2,1)S(1)}, bf16[2,128,256]{2,1,0:T(8,128)(2,1)S(1)}, u32[]{:S(2)}, u32[]{:S(2)}) collective-permute-start(bf16[2,128,256]{2,1,0:T(8,128)(2,1)S(1)} %fusion.9), channel_id=1, source_target_pairs={{0,8},{2,10},{4,12},{6,14},{8,0},{10,2},{12,4},{14,6},{1,9},{3,11}... | collective-permute-start | bytes 393224 | tf_op jit(solution)/shard_map/ppermute | solution.py:199
  (4 other events, 2.7 us)
